TPU v7x, 512 devices: a whole 4x8x8 slice. The times are simulated.
512 devices in a mesh: grp: 16 (over y, core), dev: 32 (over z, x).
Axes of the slice: x: 4, y: 8, z: 8, core: 2. Of those that a mesh axis runs over, the one named last changes fastest.
Arguments:
- panel_inverse: float32 [16, 32, 256, 256], P('grp', 'dev')
- coupling: float32 [16, 32, 256, 256], P('grp', 'dev'), may hold values from -0.875 to 0.875
- loads: float32 [16, 32, 16, 256], P('grp', 'dev'), may hold values from -6 to 6
- stiffness: float32 [24, 24], replicated
- element_substructure: int32 [16, 32, 1024], P('grp', 'dev'), may hold values from 0 to 31
- element_rows: int32 [16, 32, 24, 1024], P('grp', 'dev'), may hold values from 0 to 255
- element_density: float32 [16, 32, 1024], P('grp', 'dev'), may hold values from 0.2 to 1
- send_elements: int32 [16, 32, 32, 64], P('grp', 'dev'), may hold values from 0 to 1023
- receive_cells: int32 [16, 32, 32, 64], P('grp', 'dev'), may hold values from -1 to 16383, as said below
- design_density: float32 [16, 32, 128, 128], P('grp', 'dev'), may hold values from 0.3 to 1
- filter_offsets: int32 [8], replicated, may hold values from -3 to 3, as said below
- filter_weights: float32 [8], replicated, may hold values from 0.2 to 1
Outputs:
- interface: float32 [16, 32, 16, 256], P('grp', 'dev')
- filtered: float32 [16, 32, 128, 128], P('grp', 'dev')
Inputs may be any that keep to these rules, and one draw needn't show every extreme that they name: `receive_cells`: each receiver's slots from one source are filled in order: the first 64, 32, 16 or 8 hold a cell, the rest -1; in every group one owner is full from every source. `filter_offsets`: the offsets -3 and 3 are always among them; offsets may repeat.
All inputs are finite; a program needn't handle non-finite values.
Results may differ from a plain program's by a relative error of at most 0.0003.
Values sent between devices are 32-bit elements; how exact they have to be, the bound alone decides.
No kernel may reach another device: no remote copies, remote signals or barrier semaphores. Data moves between devices by JAX's collectives and lax.ppermute only.
A program may use at most 64 MiB of HBM per device.

v0:
```python
import jax
import jax.numpy as jnp
from jax import lax
from jax.sharding import PartitionSpec as P

NK = 8
RADIUS = 3


exact_mode = lax.Precision.HIGHEST
penalty = 3.0
energy_scale = 1.0 / 4096.0


def passed_along(value, axis, steps):
    count = lax.axis_size(axis)
    leading, last = (max(0, -steps), min(count, count - steps))
    return lax.ppermute(value, axis, [(source, source + steps) for source in range(leading, last)])


def padded_2(cells, sides, width):
    for axis, dim in sides:
        count = lax.axis_size(axis)
        ends = count - 1
        head = lax.slice_in_dim(cells, 0, width, axis=dim)
        tail = lax.slice_in_dim(cells, cells.shape[dim] - width, cells.shape[dim], axis=dim)
        cells = jnp.concatenate(
            [
                lax.ppermute(tail, axis, [(i, (i + 1) % count) for i in range(ends)]),
                cells,
                lax.ppermute(head, axis, [((i + 1) % count, i) for i in range(ends)]),
            ],
            axis=dim,
        )
    return cells


def product(left, right):
    return jnp.dot(left, right, precision=exact_mode, preferred_element_type=jnp.float32)


def on_device(
    panel_inverse,
    coupling,
    loads,
    stiffness,
    element_substructure,
    element_rows,
    element_density,
    send_elements,
    receive_cells,
    design_density,
    filter_offsets,
    filter_weights,
):
    inverse = panel_inverse[0, 0]
    couple = coupling[0, 0]
    rights = loads[0, 0]
    source = product(rights, inverse)

    def advance(level, current):
        previous = passed_along(current, "grp", 1)
        return product(rights - product(previous, couple), inverse)

    solved = lax.fori_loop(0, lax.axis_size("grp") - 1, advance, source)
    columns = lax.all_gather(solved, "dev", axis=1, tiled=True)
    panel_order = solved.shape[1]
    lookup = element_substructure[0, 0][None, :] * panel_order + element_rows[0, 0]
    motion = jnp.take(columns, lookup, axis=1)
    forces = jnp.einsum("ij,lje->lie", stiffness, motion, precision=exact_mode)
    energy = jnp.sum(motion * forces, axis=(0, 1))
    density = element_density[0, 0]
    sensitivity = -penalty * density * density * energy * energy_scale
    outgoing = jnp.take(sensitivity, send_elements[0, 0], axis=0)
    received = lax.all_to_all(outgoing, "dev", split_axis=0, concat_axis=0, tiled=True)
    owned = design_density[0, 0]
    row_count = owned.shape[0]
    cells = row_count * 128
    targets = receive_cells[0, 0]
    segment_ids = jnp.where(targets >= 0, targets, cells)
    collected = jax.ops.segment_sum(received.ravel(), segment_ids.ravel(), num_segments=cells + 1)[
        :cells
    ]
    weighted = owned * collected.reshape(row_count, 128)
    padded = padded_2(weighted, (("dev", 0),), RADIUS)
    total_rows = lax.axis_size("dev") * row_count
    global_rows = lax.axis_index("dev") * row_count + jnp.arange(row_count, dtype=jnp.int32)
    accum = jnp.zeros((row_count, 128), jnp.float32)
    weight_sum = jnp.zeros((row_count,), jnp.float32)
    for which in range(NK):
        offset = filter_offsets[which]
        window_rows = lax.dynamic_slice_in_dim(padded, RADIUS + offset, row_count, 0)
        inside = ((global_rows + offset >= 0) & (global_rows + offset < total_rows)).astype(
            jnp.float32
        )
        accum = accum + filter_weights[which] * window_rows
        weight_sum = weight_sum + filter_weights[which] * inside
    filtered = accum / (owned * weight_sum[:, None])
    return (solved[None, None], filtered[None, None])


def solution(mesh):
    placed = (
        P("grp", "dev", None, None),
        P("grp", "dev", None, None),
        P("grp", "dev", None, None),
        P(),
        P("grp", "dev", None),
        P("grp", "dev", None, None),
        P("grp", "dev", None),
        P("grp", "dev", None, None),
        P("grp", "dev", None, None),
        P("grp", "dev", None, None),
        P(),
        P(),
    )
    return jax.shard_map(
        on_device,
        mesh=mesh,
        in_specs=placed,
        out_specs=(P("grp", "dev", None, None), P("grp", "dev", None, None)),
        check_vma=False,
    )
```

profile of v0, /device:TPU:38, one launch (start us, length us, event | category | flops | bytes accessed | tf_op | source)
XLA Modules:
  0.0 357.5 jit_solution(10545197386665113381)
XLA Ops:
  4.4 129.7 %while.10 = (s32[]{:T(128)}, f32[16,256]{1,0:T(8,128)S(1)}, f32[256,256]{1,0:T(8,128)}, f32[16,256]{1,0:T(8,128)}, f32[256,256]{1,0:T(8,128)}, /*index=5*/s32[]{:T(128)}) while((s32[]{:T(128)}, f32[16,256]{1,0:T(8,128)S(1)}, f32[256,256]{1,0:T(8,128)}, f32[16,256]{1,0:T(8,128)}, f32[256,256]{1,0:T(8,128)}, /*index=5*/s32[]{:T(128)}) %tuple.42), condition=%wide.region_1.0_spmd, body=%wide.region_0.0_spmd.sunk | while | flops 25169920 | bytes 671853 | solution.py:65
  4.4 1.9 collective-permute-start
  6.3 4.3 %collective-permute-done = f32[16,256]{1,0:T(8,128)S(1)} collective-permute-done((f32[16,256]{1,0:T(8,128)S(1)}, f32[16,256]{1,0:T(8,128)S(1)}, u32[]{:S(2)}, u32[]{:S(2)}) %collective-permute-start) | collective-permute-done | bytes 16416 | tf_op jit(solution)/shard_map/while/body/eval_jaxpr/ppermute | solution.py:18
  10.7 1.2 convolution_subtract_fusion.2
  13.0 1.9 collective-permute-start
  15.0 4.3 %collective-permute-done = f32[16,256]{1,0:T(8,128)S(1)} collective-permute-done((f32[16,256]{1,0:T(8,128)S(1)}, f32[16,256]{1,0:T(8,128)S(1)}, u32[]{:S(2)}, u32[]{:S(2)}) %collective-permute-start) | collective-permute-done | bytes 16416 | tf_op jit(solution)/shard_map/while/body/eval_jaxpr/ppermute | solution.py:18
  19.3 1.2 convolution_subtract_fusion.2
  21.7 1.9 collective-permute-start
  23.6 4.3 %collective-permute-done = f32[16,256]{1,0:T(8,128)S(1)} collective-permute-done((f32[16,256]{1,0:T(8,128)S(1)}, f32[16,256]{1,0:T(8,128)S(1)}, u32[]{:S(2)}, u32[]{:S(2)}) %collective-permute-start) | collective-permute-done | bytes 16416 | tf_op jit(solution)/shard_map/while/body/eval_jaxpr/ppermute | solution.py:18
  27.9 1.2 convolution_subtract_fusion.2
  30.3 1.9 collective-permute-start
  32.3 4.3 %collective-permute-done = f32[16,256]{1,0:T(8,128)S(1)} collective-permute-done((f32[16,256]{1,0:T(8,128)S(1)}, f32[16,256]{1,0:T(8,128)S(1)}, u32[]{:S(2)}, u32[]{:S(2)}) %collective-permute-start) | collective-permute-done | bytes 16416 | tf_op jit(solution)/shard_map/while/body/eval_jaxpr/ppermute | solution.py:18
  36.6 1.2 convolution_subtract_fusion.2
  39.0 1.9 collective-permute-start
  40.9 4.3 %collective-permute-done = f32[16,256]{1,0:T(8,128)S(1)} collective-permute-done((f32[16,256]{1,0:T(8,128)S(1)}, f32[16,256]{1,0:T(8,128)S(1)}, u32[]{:S(2)}, u32[]{:S(2)}) %collective-permute-start) | collective-permute-done | bytes 16416 | tf_op jit(solution)/shard_map/while/body/eval_jaxpr/ppermute | solution.py:18
  45.2 1.2 convolution_subtract_fusion.2
  47.6 1.9 collective-permute-start
  49.5 4.3 %collective-permute-done = f32[16,256]{1,0:T(8,128)S(1)} collective-permute-done((f32[16,256]{1,0:T(8,128)S(1)}, f32[16,256]{1,0:T(8,128)S(1)}, u32[]{:S(2)}, u32[]{:S(2)}) %collective-permute-start) | collective-permute-done | bytes 16416 | tf_op jit(solution)/shard_map/while/body/eval_jaxpr/ppermute | solution.py:18
  53.9 1.2 convolution_subtract_fusion.2
  56.3 1.9 collective-permute-start
  58.2 4.3 %collective-permute-done = f32[16,256]{1,0:T(8,128)S(1)} collective-permute-done((f32[16,256]{1,0:T(8,128)S(1)}, f32[16,256]{1,0:T(8,128)S(1)}, u32[]{:S(2)}, u32[]{:S(2)}) %collective-permute-start) | collective-permute-done | bytes 16416 | tf_op jit(solution)/shard_map/while/body/eval_jaxpr/ppermute | solution.py:18
  64.9 1.9 collective-permute-start
  66.8 4.3 %collective-permute-done = f32[16,256]{1,0:T(8,128)S(1)} collective-permute-done((f32[16,256]{1,0:T(8,128)S(1)}, f32[16,256]{1,0:T(8,128)S(1)}, u32[]{:S(2)}, u32[]{:S(2)}) %collective-permute-start) | collective-permute-done | bytes 16416 | tf_op jit(solution)/shard_map/while/body/eval_jaxpr/ppermute | solution.py:18
  73.6 1.9 collective-permute-start
  75.5 4.3 %collective-permute-done = f32[16,256]{1,0:T(8,128)S(1)} collective-permute-done((f32[16,256]{1,0:T(8,128)S(1)}, f32[16,256]{1,0:T(8,128)S(1)}, u32[]{:S(2)}, u32[]{:S(2)}) %collective-permute-start) | collective-permute-done | bytes 16416 | tf_op jit(solution)/shard_map/while/body/eval_jaxpr/ppermute | solution.py:18
  82.2 1.9 collective-permute-start
  84.1 4.3 %collective-permute-done = f32[16,256]{1,0:T(8,128)S(1)} collective-permute-done((f32[16,256]{1,0:T(8,128)S(1)}, f32[16,256]{1,0:T(8,128)S(1)}, u32[]{:S(2)}, u32[]{:S(2)}) %collective-permute-start) | collective-permute-done | bytes 16416 | tf_op jit(solution)/shard_map/while/body/eval_jaxpr/ppermute | solution.py:18
  90.9 1.9 collective-permute-start
  92.8 4.3 %collective-permute-done = f32[16,256]{1,0:T(8,128)S(1)} collective-permute-done((f32[16,256]{1,0:T(8,128)S(1)}, f32[16,256]{1,0:T(8,128)S(1)}, u32[]{:S(2)}, u32[]{:S(2)}) %collective-permute-start) | collective-permute-done | bytes 16416 | tf_op jit(solution)/shard_map/while/body/eval_jaxpr/ppermute | solution.py:18
  99.5 1.9 collective-permute-start
  101.4 4.3 %collective-permute-done = f32[16,256]{1,0:T(8,128)S(1)} collective-permute-done((f32[16,256]{1,0:T(8,128)S(1)}, f32[16,256]{1,0:T(8,128)S(1)}, u32[]{:S(2)}, u32[]{:S(2)}) %collective-permute-start) | collective-permute-done | bytes 16416 | tf_op jit(solution)/shard_map/while/body/eval_jaxpr/ppermute | solution.py:18
  108.2 1.9 collective-permute-start
  110.1 4.3 %collective-permute-done = f32[16,256]{1,0:T(8,128)S(1)} collective-permute-done((f32[16,256]{1,0:T(8,128)S(1)}, f32[16,256]{1,0:T(8,128)S(1)}, u32[]{:S(2)}, u32[]{:S(2)}) %collective-permute-start) | collective-permute-done | bytes 16416 | tf_op jit(solution)/shard_map/while/body/eval_jaxpr/ppermute | solution.py:18
  116.8 1.9 collective-permute-start
  118.7 4.3 %collective-permute-done = f32[16,256]{1,0:T(8,128)S(1)} collective-permute-done((f32[16,256]{1,0:T(8,128)S(1)}, f32[16,256]{1,0:T(8,128)S(1)}, u32[]{:S(2)}, u32[]{:S(2)}) %collective-permute-start) | collective-permute-done | bytes 16416 | tf_op jit(solution)/shard_map/while/body/eval_jaxpr/ppermute | solution.py:18
  125.4 1.9 collective-permute-start
  127.4 4.3 %collective-permute-done = f32[16,256]{1,0:T(8,128)S(1)} collective-permute-done((f32[16,256]{1,0:T(8,128)S(1)}, f32[16,256]{1,0:T(8,128)S(1)}, u32[]{:S(2)}, u32[]{:S(2)}) %collective-permute-start) | collective-permute-done | bytes 16416 | tf_op jit(solution)/shard_map/while/body/eval_jaxpr/ppermute | solution.py:18
  134.2 64.9 %all_gather.3 = f32[16,8192]{0,1:T(8,128)} all-gather(f32[16,256]{0,1:T(8,128)S(1)} %copy.18), channel_id=1, replica_groups=mesh['grp'=16,'dev'=32] {'dev'}, dimensions={1}, use_global_device_ids=true | all-gather | bytes 540672 | tf_op jit(solution)/shard_map/all_gather | solution.py:66
  199.2 84.1 %gather_fusion = f32[24576,16]{1,0:T(8,128)} fusion(f32[16,8192]{0,1:T(8,128)} %all_gather.3, s32[24576]{0:T(1024)S(1)} %broadcast_clamp_fusion), kind=kCustom, calls=%fused_computation | custom fusion | bytes 3244032 | tf_op jit(solution)/shard_map/jit(_take)/gather | solution.py:69
  283.3 7.7 %copy.20 = f32[24,1024,16]{1,0,2:T(8,128)S(1)} copy(f32[24,1024,16]{2,1,0:T(8,128)} %bitcast.87) | data formatting | bytes 3145728 | tf_op jit(solution)/shard_map/jit(_take)/gather | solution.py:69
  291.1 1.7 fusion
  292.8 8.6 %gather_fusion.1 = f32[2048]{0:T(1024)S(1)} fusion(f32[1024]{0:T(1024)S(1)} %fusion.16, s32[2048]{0:T(1024)S(1)} %broadcast_clamp_fusion.1), kind=kCustom, calls=%fused_computation.1 | custom fusion | bytes 24576 | tf_op jit(solution)/shard_map/jit(_take)/gather | solution.py:74
  302.1 6.3 %all-to-all-start = ((f32[32,1,64]{2,1,0:T(1,128)}), f32[32,1,64]{2,1,0:T(1,128)S(1)}, u32[]{:S(2)}, u32[]{:S(2)}) async-start(f32[32,1,64]{2,1,0:T(1,128)} %and_select_fusion), calls=%async_computation | async-start | bytes 32768 | tf_op jit(solution)/shard_map/all_to_all | solution.py:75
  309.9 10.0 %fusion.23 = f32[128]{0:T(128)S(1)} fusion(f32[]{:T(128)} %bitcast.31, s32[]{:T(128)} %bitcast.32, f32[]{:T(128)} %bitcast.29, s32[]{:T(128)} %bitcast.30, f32[]{:T(128)} %bitcast.27, s32[]{:T(128)} %bitcast.28, f32[]{:T(128)} %bitcast.25, s32[]{:T(128)} %bitcast.26, f32[]{:T(128)} %bitcast.23, s32[]{:T(128)} %bitcast.24, f32[]{:T(128)} %bitcast.21, ...), kind=kLoop, calls=%fused_computation.50 | loop fusion | flops 6144 | bytes 580 | tf_op jit(solution)/shard_map/add | solution.py:97
  322.5 12.5 %scatter_custom_fusion = f32[16385]{0:T(1024)S(1)} fusion(s32[2048]{0:T(1024)S(1)} %bitcast.96, f32[2048]{0:T(1024)S(1)} %reshape.242, f32[]{:T(128)} %constant.61.clone.1), kind=kCustom, calls=%fused_computation.28 | custom fusion | flops 2048 | bytes 65544 | tf_op jit(solution)/shard_map/scatter-add | solution.py:81
  335.0 3.2 collective-permute-start.2
  338.2 4.8 %collective-permute-start.1 = (f32[3,128]{1,0:T(4,128)S(1)}, f32[3,128]{1,0:T(4,128)S(1)}, u32[]{:S(2)}, u32[]{:S(2)}) collective-permute-start(f32[3,128]{1,0:T(4,128)S(1)} %get-tuple-element.40), channel_id=1, source_target_pairs={{0,1},{1,2},{2,3},{3,4},{4,5},{5,6},{6,7},{7,8},{8,9},{9,10},{10,1... | collective-permute-start | bytes 4616 | tf_op jit(solution)/shard_map/ppermute | solution.py:29
  351.8 5.7 %fusion.11 = f32[1,1,128,128]{3,2,1,0:T(8,128)} fusion(f32[1,1,128,128]{3,2,1,0:T(8,128)S(1)} %copy-done.1, f32[134,128]{1,0:T(8,128)S(1)} %pad_maximum_fusion, s32[]{:T(128)S(6)} %select_n.103, s32[]{:T(128)S(6)} %select_n.102, s32[]{:T(128)S(6)} %select_n.101, s32[]{:T(128)S(6)} %select_n.100, s32[]{:T(128)S(6)} %select_n.99, s32[]{:T(128)S(6)} %select_n.98, ...), kind=kLoop, calls=%fused_computation.23 | loop fusion | flops 278528 | bytes 655936 | tf_op jit(solution)/shard_map/broadcast_in_dim | solution.py:99
  (66 shorter events, 35.3 us)
Async XLA Ops:
  0.6 290.4 %copy-start = (f32[24,24]{1,0:T(8,128)S(1)}, f32[24,24]{1,0:T(8,128)}, u32[]{:S(2)}) copy-start(f32[24,24]{1,0:T(8,128)} %param.17) | copy-start | bytes 6916
  4.4 6.3 %collective-permute-start = (f32[16,256]{1,0:T(8,128)S(1)}, f32[16,256]{1,0:T(8,128)S(1)}, u32[]{:S(2)}, u32[]{:S(2)}) collective-permute-start(f32[16,256]{1,0:T(8,128)S(1)} %get-tuple-element.96), channel_id=1, source_target_pairs={{0,32},{32,64},{64,96},{96,128},{128,160},{160,192},{192,224},{224... | collective-permute-start | bytes 49160 | tf_op jit(solution)/shard_map/while/body/eval_jaxpr/ppermute | solution.py:18
  13.0 6.3 %collective-permute-start = (f32[16,256]{1,0:T(8,128)S(1)}, f32[16,256]{1,0:T(8,128)S(1)}, u32[]{:S(2)}, u32[]{:S(2)}) collective-permute-start(f32[16,256]{1,0:T(8,128)S(1)} %get-tuple-element.96), channel_id=1, source_target_pairs={{0,32},{32,64},{64,96},{96,128},{128,160},{160,192},{192,224},{224... | collective-permute-start | bytes 49160 | tf_op jit(solution)/shard_map/while/body/eval_jaxpr/ppermute | solution.py:18
  21.7 6.3 %collective-permute-start = (f32[16,256]{1,0:T(8,128)S(1)}, f32[16,256]{1,0:T(8,128)S(1)}, u32[]{:S(2)}, u32[]{:S(2)}) collective-permute-start(f32[16,256]{1,0:T(8,128)S(1)} %get-tuple-element.96), channel_id=1, source_target_pairs={{0,32},{32,64},{64,96},{96,128},{128,160},{160,192},{192,224},{224... | collective-permute-start | bytes 49160 | tf_op jit(solution)/shard_map/while/body/eval_jaxpr/ppermute | solution.py:18
  30.3 6.3 %collective-permute-start = (f32[16,256]{1,0:T(8,128)S(1)}, f32[16,256]{1,0:T(8,128)S(1)}, u32[]{:S(2)}, u32[]{:S(2)}) collective-permute-start(f32[16,256]{1,0:T(8,128)S(1)} %get-tuple-element.96), channel_id=1, source_target_pairs={{0,32},{32,64},{64,96},{96,128},{128,160},{160,192},{192,224},{224... | collective-permute-start | bytes 49160 | tf_op jit(solution)/shard_map/while/body/eval_jaxpr/ppermute | solution.py:18
  39.0 6.3 %collective-permute-start = (f32[16,256]{1,0:T(8,128)S(1)}, f32[16,256]{1,0:T(8,128)S(1)}, u32[]{:S(2)}, u32[]{:S(2)}) collective-permute-start(f32[16,256]{1,0:T(8,128)S(1)} %get-tuple-element.96), channel_id=1, source_target_pairs={{0,32},{32,64},{64,96},{96,128},{128,160},{160,192},{192,224},{224... | collective-permute-start | bytes 49160 | tf_op jit(solution)/shard_map/while/body/eval_jaxpr/ppermute | solution.py:18
  47.6 6.3 %collective-permute-start = (f32[16,256]{1,0:T(8,128)S(1)}, f32[16,256]{1,0:T(8,128)S(1)}, u32[]{:S(2)}, u32[]{:S(2)}) collective-permute-start(f32[16,256]{1,0:T(8,128)S(1)} %get-tuple-element.96), channel_id=1, source_target_pairs={{0,32},{32,64},{64,96},{96,128},{128,160},{160,192},{192,224},{224... | collective-permute-start | bytes 49160 | tf_op jit(solution)/shard_map/while/body/eval_jaxpr/ppermute | solution.py:18
  56.3 6.3 %collective-permute-start = (f32[16,256]{1,0:T(8,128)S(1)}, f32[16,256]{1,0:T(8,128)S(1)}, u32[]{:S(2)}, u32[]{:S(2)}) collective-permute-start(f32[16,256]{1,0:T(8,128)S(1)} %get-tuple-element.96), channel_id=1, source_target_pairs={{0,32},{32,64},{64,96},{96,128},{128,160},{160,192},{192,224},{224... | collective-permute-start | bytes 49160 | tf_op jit(solution)/shard_map/while/body/eval_jaxpr/ppermute | solution.py:18
  64.9 6.3 %collective-permute-start = (f32[16,256]{1,0:T(8,128)S(1)}, f32[16,256]{1,0:T(8,128)S(1)}, u32[]{:S(2)}, u32[]{:S(2)}) collective-permute-start(f32[16,256]{1,0:T(8,128)S(1)} %get-tuple-element.96), channel_id=1, source_target_pairs={{0,32},{32,64},{64,96},{96,128},{128,160},{160,192},{192,224},{224... | collective-permute-start | bytes 49160 | tf_op jit(solution)/shard_map/while/body/eval_jaxpr/ppermute | solution.py:18
  73.6 6.3 %collective-permute-start = (f32[16,256]{1,0:T(8,128)S(1)}, f32[16,256]{1,0:T(8,128)S(1)}, u32[]{:S(2)}, u32[]{:S(2)}) collective-permute-start(f32[16,256]{1,0:T(8,128)S(1)} %get-tuple-element.96), channel_id=1, source_target_pairs={{0,32},{32,64},{64,96},{96,128},{128,160},{160,192},{192,224},{224... | collective-permute-start | bytes 49160 | tf_op jit(solution)/shard_map/while/body/eval_jaxpr/ppermute | solution.py:18
  82.2 6.3 %collective-permute-start = (f32[16,256]{1,0:T(8,128)S(1)}, f32[16,256]{1,0:T(8,128)S(1)}, u32[]{:S(2)}, u32[]{:S(2)}) collective-permute-start(f32[16,256]{1,0:T(8,128)S(1)} %get-tuple-element.96), channel_id=1, source_target_pairs={{0,32},{32,64},{64,96},{96,128},{128,160},{160,192},{192,224},{224... | collective-permute-start | bytes 49160 | tf_op jit(solution)/shard_map/while/body/eval_jaxpr/ppermute | solution.py:18
  90.9 6.3 %collective-permute-start = (f32[16,256]{1,0:T(8,128)S(1)}, f32[16,256]{1,0:T(8,128)S(1)}, u32[]{:S(2)}, u32[]{:S(2)}) collective-permute-start(f32[16,256]{1,0:T(8,128)S(1)} %get-tuple-element.96), channel_id=1, source_target_pairs={{0,32},{32,64},{64,96},{96,128},{128,160},{160,192},{192,224},{224... | collective-permute-start | bytes 49160 | tf_op jit(solution)/shard_map/while/body/eval_jaxpr/ppermute | solution.py:18
  99.5 6.3 %collective-permute-start = (f32[16,256]{1,0:T(8,128)S(1)}, f32[16,256]{1,0:T(8,128)S(1)}, u32[]{:S(2)}, u32[]{:S(2)}) collective-permute-start(f32[16,256]{1,0:T(8,128)S(1)} %get-tuple-element.96), channel_id=1, source_target_pairs={{0,32},{32,64},{64,96},{96,128},{128,160},{160,192},{192,224},{224... | collective-permute-start | bytes 49160 | tf_op jit(solution)/shard_map/while/body/eval_jaxpr/ppermute | solution.py:18
  108.2 6.3 %collective-permute-start = (f32[16,256]{1,0:T(8,128)S(1)}, f32[16,256]{1,0:T(8,128)S(1)}, u32[]{:S(2)}, u32[]{:S(2)}) collective-permute-start(f32[16,256]{1,0:T(8,128)S(1)} %get-tuple-element.96), channel_id=1, source_target_pairs={{0,32},{32,64},{64,96},{96,128},{128,160},{160,192},{192,224},{224... | collective-permute-start | bytes 49160 | tf_op jit(solution)/shard_map/while/body/eval_jaxpr/ppermute | solution.py:18
  116.8 6.3 %collective-permute-start = (f32[16,256]{1,0:T(8,128)S(1)}, f32[16,256]{1,0:T(8,128)S(1)}, u32[]{:S(2)}, u32[]{:S(2)}) collective-permute-start(f32[16,256]{1,0:T(8,128)S(1)} %get-tuple-element.96), channel_id=1, source_target_pairs={{0,32},{32,64},{64,96},{96,128},{128,160},{160,192},{192,224},{224... | collective-permute-start | bytes 49160 | tf_op jit(solution)/shard_map/while/body/eval_jaxpr/ppermute | solution.py:18
  125.4 6.3 %collective-permute-start = (f32[16,256]{1,0:T(8,128)S(1)}, f32[16,256]{1,0:T(8,128)S(1)}, u32[]{:S(2)}, u32[]{:S(2)}) collective-permute-start(f32[16,256]{1,0:T(8,128)S(1)} %get-tuple-element.96), channel_id=1, source_target_pairs={{0,32},{32,64},{64,96},{96,128},{128,160},{160,192},{192,224},{224... | collective-permute-start | bytes 49160 | tf_op jit(solution)/shard_map/while/body/eval_jaxpr/ppermute | solution.py:18
  134.1 65.0 %copy-start.2 = (f32[16,256]{1,0:T(8,128)}, f32[16,256]{1,0:T(8,128)S(1)}, u32[]{:S(2)}) copy-start(f32[16,256]{1,0:T(8,128)S(1)} %get-tuple-element.29) | copy-start | bytes 49156
  283.3 7.7 %copy-start.3 = (s32[1,1,32,64]{3,2,1,0:T(8,128)S(1)}, s32[1,1,32,64]{3,2,1,0:T(8,128)}, u32[]{:S(2)}) copy-start(s32[1,1,32,64]{3,2,1,0:T(8,128)} %param.21) | copy-start | bytes 24580
  290.9 1.8 copy-start.7
  292.8 15.7 %copy-start.6 = (s32[1,1,32,64]{3,2,1,0:T(8,128)S(1)}, s32[1,1,32,64]{3,2,1,0:T(8,128)}, u32[]{:S(2)}) copy-start(s32[1,1,32,64]{3,2,1,0:T(8,128)} %param.22) | copy-start | bytes 24580
  292.8 15.8 %copy-start.4 = (s32[8]{0:T(128)S(1)}, s32[8]{0:T(128)}, u32[]{:S(2)}) copy-start(s32[8]{0:T(128)} %param.24) | copy-start | bytes 100
  292.8 16.5 %copy-start.5 = (f32[8]{0:T(128)S(1)}, f32[8]{0:T(128)}, u32[]{:S(2)}) copy-start(f32[8]{0:T(128)} %param.25) | copy-start | bytes 100
  292.8 42.2 %copy-start.1 = (f32[1,1,128,128]{3,2,1,0:T(8,128)S(1)}, f32[1,1,128,128]{3,2,1,0:T(8,128)}, u32[]{:S(2)}) copy-start(f32[1,1,128,128]{3,2,1,0:T(8,128)} %param.23) | copy-start | bytes 196612
  302.1 19.0 %all-to-all-start = ((f32[32,1,64]{2,1,0:T(1,128)}), f32[32,1,64]{2,1,0:T(1,128)S(1)}, u32[]{:S(2)}, u32[]{:S(2)}) async-start(f32[32,1,64]{2,1,0:T(1,128)} %and_select_fusion), calls=%async_computation | async-start | bytes 32768 | tf_op jit(solution)/shard_map/all_to_all | solution.py:75
  335.0 16.8 %collective-permute-start.2 = (f32[3,128]{1,0:T(4,128)S(1)}, f32[3,128]{1,0:T(4,128)S(1)}, u32[]{:S(2)}, u32[]{:S(2)}) collective-permute-start(f32[3,128]{1,0:T(4,128)S(1)} %get-tuple-element.41), channel_id=1, source_target_pairs={{1,0},{2,1},{3,2},{4,3},{5,4},{6,5},{7,6},{8,7},{9,8},{10,9},{11,1... | collective-permute-start | bytes 4616 | tf_op jit(solution)/shard_map/ppermute | solution.py:31
  338.2 13.6 %collective-permute-start.1 = (f32[3,128]{1,0:T(4,128)S(1)}, f32[3,128]{1,0:T(4,128)S(1)}, u32[]{:S(2)}, u32[]{:S(2)}) collective-permute-start(f32[3,128]{1,0:T(4,128)S(1)} %get-tuple-element.40), channel_id=1, source_target_pairs={{0,1},{1,2},{2,3},{3,4},{4,5},{5,6},{6,7},{7,8},{8,9},{9,10},{10,1... | collective-permute-start | bytes 4616 | tf_op jit(solution)/shard_map/ppermute | solution.py:29
where the time goes:
time: 359 us; the launch traced here: 358 us
  local copies, waits for them, and re-layouts  103 us (29%)
  waiting for transfers between devices  65.1 us (18%)
  blocking collectives  64.9 us (18%)
  starting transfers between devices  43.1 us (12%)
  matrix products  37.8 us (11%)
  other arithmetic  32.2 us (9%)
  between operations  10.9 us (3%)
    gather x2, local copies, waits for them, and re-layouts, on_device(): motion = jnp.take(columns, lookup, axis=1)  91.8 us
    ppermute x15, waiting for transfers between devices, passed_along(): lax.ppermute(value, axis, [(source, source + steps) for source in range(l...  65.1 us
    all_gather x1, blocking collectives, on_device(): columns = lax.all_gather(solved, 'dev', axis=1, tiled=True)  64.9 us
    dot_general x31, matrix products, product(): jnp.dot(left, right, precision=exact_mode, preferred_element_type=jnp.flo...  36.1 us
    ppermute x15, starting transfers between devices, passed_along(): lax.ppermute(value, axis, [(source, source + steps) for source in range(l...  28.8 us
    scatter-add x1, other arithmetic, on_device(): jax.ops.segment_sum(received.ravel(), segment_ids.ravel(), num_segments=c...  12.5 us
    add x1, other arithmetic, on_device(): weight_sum = weight_sum + filter_weights[which] * inside  10 us
    gather x2, local copies, waits for them, and re-layouts, on_device(): outgoing = jnp.take(sensitivity, send_elements[0, 0], axis=0)  8.67 us
  transfers between devices with their start and end apart: 18, of which 15 were waited for; matrix products, arithmetic and copies ran while one was open for 3% of the time, Pallas kernels for 0%

commit v1 on v0

--- a/solution.py
+++ b/solution.py
@@ -39,6 +39,58 @@
     return jnp.dot(left, right, precision=exact_mode, preferred_element_type=jnp.float32)
 
 
+def interface_chain(inverse, couple, rights):
+    offset = product(rights, inverse)
+    step = -product(couple, inverse)
+    order = rights.shape[0]
+    levels = lax.axis_size("grp")
+    shift = 1
+    while shift < levels:
+        if 2 * shift < levels:
+            packed = passed_along(jnp.concatenate([offset, step], axis=0), "grp", shift)
+            earlier_offset, earlier_step = packed[:order], packed[order:]
+            offset = product(earlier_offset, step) + offset
+            step = product(earlier_step, step)
+        else:
+            earlier_offset = passed_along(offset, "grp", shift)
+            offset = product(earlier_offset, step) + offset
+        shift *= 2
+    return offset
+
+
+def picked(values, index):
+    lanes = 128
+    table = values.reshape(-1, lanes)
+    flat = index.reshape(-1)
+    high = flat // lanes
+    low = flat % lanes
+    rows = jnp.zeros((flat.shape[0], lanes), values.dtype)
+    for which in range(table.shape[0]):
+        rows = rows + jnp.where((high == which)[:, None], table[which][None, :], 0.0)
+    lane_ids = lax.broadcasted_iota(jnp.int32, (1, lanes), 1)
+    chosen = jnp.sum(jnp.where(lane_ids == low[:, None], rows, 0.0), axis=1)
+    return chosen.reshape(index.shape)
+
+
+def scattered(values, targets, row_count):
+    lanes = 128
+    flat_values = values.reshape(-1)
+    flat_targets = targets.reshape(-1)
+    row = jnp.where(flat_targets >= 0, flat_targets // lanes, -1)
+    col = flat_targets % lanes
+    row_ids = lax.broadcasted_iota(jnp.int32, (1, row_count), 1)
+    lane_ids = lax.broadcasted_iota(jnp.int32, (1, lanes), 1)
+    rows_hot = (row[:, None] == row_ids).astype(jnp.float32)
+    cols_hot = jnp.where(col[:, None] == lane_ids, flat_values[:, None], 0.0)
+    return lax.dot_general(
+        rows_hot,
+        cols_hot,
+        (((0,), (0,)), ((), ())),
+        precision=exact_mode,
+        preferred_element_type=jnp.float32,
+    )
+
+
 def on_device(
     panel_inverse,
     coupling,
@@ -56,32 +108,24 @@
     inverse = panel_inverse[0, 0]
     couple = coupling[0, 0]
     rights = loads[0, 0]
-    source = product(rights, inverse)
+    solved = interface_chain(inverse, couple, rights)
 
-    def advance(level, current):
-        previous = passed_along(current, "grp", 1)
-        return product(rights - product(previous, couple), inverse)
-
-    solved = lax.fori_loop(0, lax.axis_size("grp") - 1, advance, source)
-    columns = lax.all_gather(solved, "dev", axis=1, tiled=True)
-    panel_order = solved.shape[1]
+    panels = lax.all_gather(solved, "dev", axis=0, tiled=False)
+    slabs, order, panel_order = panels.shape
+    table = jnp.transpose(panels, (0, 2, 1)).reshape(slabs * panel_order, order)
     lookup = element_substructure[0, 0][None, :] * panel_order + element_rows[0, 0]
-    motion = jnp.take(columns, lookup, axis=1)
-    forces = jnp.einsum("ij,lje->lie", stiffness, motion, precision=exact_mode)
-    energy = jnp.sum(motion * forces, axis=(0, 1))
+    dofs, elements = lookup.shape
+    motion = jnp.take(table, lookup.reshape(-1), axis=0).reshape(dofs, elements, order)
+    forces = jnp.einsum("ij,jel->iel", stiffness, motion, precision=exact_mode)
+    energy = jnp.sum(motion * forces, axis=(0, 2))
     density = element_density[0, 0]
     sensitivity = -penalty * density * density * energy * energy_scale
-    outgoing = jnp.take(sensitivity, send_elements[0, 0], axis=0)
+    outgoing = picked(sensitivity, send_elements[0, 0])
     received = lax.all_to_all(outgoing, "dev", split_axis=0, concat_axis=0, tiled=True)
     owned = design_density[0, 0]
     row_count = owned.shape[0]
-    cells = row_count * 128
-    targets = receive_cells[0, 0]
-    segment_ids = jnp.where(targets >= 0, targets, cells)
-    collected = jax.ops.segment_sum(received.ravel(), segment_ids.ravel(), num_segments=cells + 1)[
-        :cells
-    ]
-    weighted = owned * collected.reshape(row_count, 128)
+    collected = scattered(received, receive_cells[0, 0], row_count)
+    weighted = owned * collected
     padded = padded_2(weighted, (("dev", 0),), RADIUS)
     total_rows = lax.axis_size("dev") * row_count
     global_rows = lax.axis_index("dev") * row_count + jnp.arange(row_count, dtype=jnp.int32)

time: 359 us -> 248 us (0.69)
  the two profiles are of different devices: /device:TPU:38 before, /device:TPU:96 now
where the time goes in v1:
time: 248 us; the launch traced here: 247 us
  local copies, waits for them, and re-layouts  97.9 us (39%)
  blocking collectives  54.4 us (22%)
  waiting for transfers between devices  35.5 us (14%)
  starting transfers between devices  20.8 us (8%)
  other arithmetic  19.9 us (8%)
  between operations  11.1 us (4%)
  matrix products  7.72 us (3%)
    gather x2, local copies, waits for them, and re-layouts, on_device(): jnp.take(table, lookup.reshape(-1), axis=0).reshape(dofs, elements, order)  91.3 us
    all_gather x1, blocking collectives, on_device(): panels = lax.all_gather(solved, 'dev', axis=0, tiled=False)  54.4 us
    ppermute x4, waiting for transfers between devices, passed_along(): lax.ppermute(value, axis, [(source, source + steps) for source in range(l...  35.5 us
    add x1, other arithmetic, on_device(): weight_sum = weight_sum + filter_weights[which] * inside  10 us
    ppermute x4, starting transfers between devices, passed_along(): lax.ppermute(value, axis, [(source, source + steps) for source in range(l...  7.07 us
    all_to_all x1, starting transfers between devices, on_device(): lax.all_to_all(outgoing, 'dev', split_axis=0, concat_axis=0, tiled=True)  5.79 us
    broadcast_in_dim x1, other arithmetic, on_device(): return (solved[None, None], filtered[None, None])  5.76 us
  transfers between devices with their start and end apart: 7, of which 4 were waited for; matrix products, arithmetic and copies ran while one was open for 5% of the time, Pallas kernels for 0%

profile of v1, /device:TPU:96, one launch (start us, length us, event | category | flops | bytes accessed | tf_op | source)
XLA Modules:
  0.0 247.4 jit_solution(13159419427163164165)
XLA Ops:
  0.6 0.0 copy-start
  0.7 0.9 copy-done
  1.6 1.3 convolution_negate_fusion
  2.9 0.9 fusion.17
  3.9 0.0 copy-start.4
  3.9 0.0 copy-start.7
  3.9 1.9 collective-permute-start
  5.9 0.1 copy.19
  6.0 0.1 copy.20
  6.1 0.1 compare_select_fusion
  6.3 0.1 reshape_squeeze.7
  6.4 0.0 copy-start.5
  6.4 6.6 %collective-permute-done = f32[272,256]{1,0:T(8,128)S(1)} collective-permute-done((f32[272,256]{1,0:T(8,128)S(1)}, f32[272,256]{1,0:T(8,128)S(1)}, u32[]{:S(2)}, u32[]{:S(2)}) %collective-permute-start) | collective-permute-done | bytes 278560 | tf_op jit(solution)/shard_map/ppermute | solution.py:18
  13.0 0.4 fusion.13
  13.4 0.2 convolution_add_fusion.3
  13.6 1.9 collective-permute-start.1
  15.6 0.7 fusion.45
  16.3 0.1 reshape_squeeze.6
  16.3 6.9 %collective-permute-done.1 = f32[272,256]{1,0:T(8,128)S(1)} collective-permute-done((f32[272,256]{1,0:T(8,128)S(1)}, f32[272,256]{1,0:T(8,128)S(1)}, u32[]{:S(2)}, u32[]{:S(2)}) %collective-permute-start.1) | collective-permute-done | bytes 278560 | tf_op jit(solution)/shard_map/ppermute | solution.py:18
  23.3 0.2 convolution_add_fusion.2
  23.5 0.4 fusion.11
  23.9 1.9 collective-permute-start.2
  25.9 0.7 fusion.44
  26.6 14.1 %collective-permute-done.2 = f32[272,256]{1,0:T(8,128)S(1)} collective-permute-done((f32[272,256]{1,0:T(8,128)S(1)}, f32[272,256]{1,0:T(8,128)S(1)}, u32[]{:S(2)}, u32[]{:S(2)}) %collective-permute-start.2) | collective-permute-done | bytes 278560 | tf_op jit(solution)/shard_map/ppermute | solution.py:18
  40.8 0.2 convolution_add_fusion.1
  41.0 1.3 collective-permute-start.3
  42.3 0.4 fusion.9
  42.7 7.9 %collective-permute-done.3 = f32[16,256]{1,0:T(8,128)S(1)} collective-permute-done((f32[16,256]{1,0:T(8,128)S(1)}, f32[16,256]{1,0:T(8,128)S(1)}, u32[]{:S(2)}, u32[]{:S(2)}) %collective-permute-start.3) | collective-permute-done | bytes 16416 | tf_op jit(solution)/shard_map/ppermute | solution.py:18
  50.5 0.2 convolution_add_fusion
  50.7 0.0 copy-start.3
  50.8 54.4 %all-gather = f32[512,256]{1,0:T(8,128)S(1)} all-gather(f32[16,256]{1,0:T(8,128)S(1)} %convolution_add_fusion), channel_id=2, replica_groups=mesh['grp'=16,'dev'=32] {'dev'}, dimensions={0}, use_global_device_ids=true | all-gather | bytes 540672 | tf_op jit(solution)/shard_map/all_gather | solution.py:113
  105.1 2.6 %copy.16 = f32[32,256,16]{2,1,0:T(8,128)} copy(f32[32,256,16]{1,2,0:T(8,128)S(1)} %bitcast.81) | data formatting | bytes 1048576 | tf_op jit(solution)/shard_map/transpose | solution.py:115
  107.7 83.7 %gather_fusion = f32[24576,16]{1,0:T(8,128)} fusion(f32[8192,16]{1,0:T(8,128)} %bitcast.79, s32[24576]{0:T(1024)S(1)} %broadcast_clamp_fusion), kind=kCustom, calls=%fused_computation | custom fusion | bytes 3244032 | tf_op jit(solution)/shard_map/jit(_take)/gather | solution.py:118
  191.4 7.7 %copy.18 = f32[24,1024,16]{1,0,2:T(8,128)S(1)} copy(f32[24,1024,16]{2,1,0:T(8,128)} %bitcast.80) | data formatting | bytes 3145728 | tf_op jit(solution)/shard_map/jit(_take)/gather | solution.py:118
  199.1 0.0 copy-start.8
  199.1 0.0 copy-start.2
  199.1 1.6 fusion
  200.8 3.1 %select_reduce_fusion = f32[2048]{0:T(1024)S(1)} fusion(f32[128]{0:T(128)S(1)} %get-tuple-element.16, f32[128]{0:T(128)S(1)} %get-tuple-element.17, f32[128]{0:T(128)S(1)} %get-tuple-element.18, f32[128]{0:T(128)S(1)} %get-tuple-element.19, f32[128]{0:T(128)S(1)} %get-tuple-element.20, f32[128]{0:T(128)S(1)} %get-tuple-element.21, ...), kind=kLoop, calls=%fused_computation.11 | loop fusion | flops 4716544 | bytes 36864 | tf_op jit(solution)/shard_map/reduce_sum | solution.py:71
  203.9 0.7 all_to_all.6
  204.6 5.8 %all-to-all-start = ((f32[32,1,64]{2,1,0:T(1,128)}), f32[32,1,64]{2,1,0:T(1,128)S(1)}, u32[]{:S(2)}, u32[]{:S(2)}) async-start(f32[32,1,64]{2,1,0:T(1,128)} %all_to_all.6), calls=%async_computation | async-start | bytes 32768 | tf_op jit(solution)/shard_map/all_to_all | solution.py:124
  210.4 10.0 %fusion.39 = f32[128]{0:T(128)S(1)} fusion(f32[]{:T(128)} %bitcast.29, s32[]{:T(128)} %bitcast.30, f32[]{:T(128)} %bitcast.27, s32[]{:T(128)} %bitcast.28, f32[]{:T(128)} %bitcast.25, s32[]{:T(128)} %bitcast.26, f32[]{:T(128)} %bitcast.23, s32[]{:T(128)} %bitcast.24, f32[]{:T(128)} %bitcast.21, s32[]{:T(128)} %bitcast.22, f32[]{:T(128)} %bitcast.19, ...), kind=kLoop, calls=%fused_computation.92 | loop fusion | flops 6144 | bytes 580 | tf_op jit(solution)/shard_map/add | solution.py:141
  222.4 0.5 broadcast.532
  222.9 0.7 reduce.3
  223.6 0.1 broadcast_in_dim.161
  223.7 1.9 convolution_multiply_fusion
  225.6 3.4 %collective-permute-start.4 = (f32[3,128]{1,0:T(4,128)S(1)}, f32[3,128]{1,0:T(4,128)S(1)}, u32[]{:S(2)}, u32[]{:S(2)}) collective-permute-start(f32[3,128]{1,0:T(4,128)S(1)} %get-tuple-element.4), channel_id=1, source_target_pairs={{0,1},{1,2},{2,3},{3,4},{4,5},{5,6},{6,7},{7,8},{8,9},{9,10},{10,1... | collective-permute-start | bytes 4616 | tf_op jit(solution)/shard_map/ppermute | solution.py:29
  229.0 4.6 %collective-permute-start.5 = (f32[3,128]{1,0:T(4,128)S(1)}, f32[3,128]{1,0:T(4,128)S(1)}, u32[]{:S(2)}, u32[]{:S(2)}) collective-permute-start(f32[3,128]{1,0:T(4,128)S(1)} %get-tuple-element.5), channel_id=1, source_target_pairs={{1,0},{2,1},{3,2},{4,3},{5,4},{6,5},{7,6},{8,7},{9,8},{10,9},{11,1... | collective-permute-start | bytes 4616 | tf_op jit(solution)/shard_map/ppermute | solution.py:31
  241.6 5.8 %fusion.20 = f32[1,1,128,128]{3,2,1,0:T(8,128)} fusion(f32[1,1,128,128]{3,2,1,0:T(8,128)S(1)} %copy-done.2, f32[134,128]{1,0:T(8,128)S(1)} %pad_maximum_fusion.3, s32[]{:T(128)S(6)} %select_n.168, s32[]{:T(128)S(6)} %select_n.167, s32[]{:T(128)S(6)} %select_n.166, s32[]{:T(128)S(6)} %select_n.165, s32[]{:T(128)S(6)} %select_n.164, s32[]{:T(128)S(6)} %select_n.163, ...), kind=kLoop, calls=%fused_computation.41 | loop fusion | flops 278528 | bytes 655936 | tf_op jit(solution)/shard_map/broadcast_in_dim | solution.py:143
  (32 shorter events, 0.3 us)
Async XLA Ops:
  0.6 1.0 copy-start
  0.6 5.2 %copy-start.9 = (s32[1,1,1024]{2,1,0:T(1,128)S(1)}, s32[1,1,1024]{2,1,0:T(1,128)}, u32[]{:S(2)}) copy-start(s32[1,1,1024]{2,1,0:T(1,128)} %param.16) | copy-start | bytes 12292
  0.7 5.3 %copy-start.1 = (s32[1,1,24,1024]{3,2,1,0:T(8,128)S(1)}, s32[1,1,24,1024]{3,2,1,0:T(8,128)}, u32[]{:S(2)}) copy-start(s32[1,1,24,1024]{3,2,1,0:T(8,128)} %param.17) | copy-start | bytes 294916
  0.7 5.6 %copy-start.6 = (s32[1,1,32,64]{3,2,1,0:T(8,128)S(1)}, s32[1,1,32,64]{3,2,1,0:T(8,128)}, u32[]{:S(2)}) copy-start(s32[1,1,32,64]{3,2,1,0:T(8,128)} %param.19) | copy-start | bytes 24580
  3.9 11.7 %copy-start.4 = (s32[8]{0:T(128)S(1)}, s32[8]{0:T(128)}, u32[]{:S(2)}) copy-start(s32[8]{0:T(128)} %param.22) | copy-start | bytes 100
  3.9 12.4 %copy-start.7 = (s32[1,1,32,64]{3,2,1,0:T(8,128)S(1)}, s32[1,1,32,64]{3,2,1,0:T(8,128)}, u32[]{:S(2)}) copy-start(s32[1,1,32,64]{3,2,1,0:T(8,128)} %param.20) | copy-start | bytes 24580
  3.9 9.1 %collective-permute-start = (f32[272,256]{1,0:T(8,128)S(1)}, f32[272,256]{1,0:T(8,128)S(1)}, u32[]{:S(2)}, u32[]{:S(2)}) collective-permute-start(f32[272,256]{1,0:T(8,128)S(1)} %pad_maximum_fusion), channel_id=1, source_target_pairs={{0,32},{32,64},{64,96},{96,128},{128,160},{160,192},{192,224},{224... | collective-permute-start | bytes 835592 | tf_op jit(solution)/shard_map/ppermute | solution.py:18
  6.4 19.4 %copy-start.5 = (f32[8]{0:T(128)S(1)}, f32[8]{0:T(128)}, u32[]{:S(2)}) copy-start(f32[8]{0:T(128)} %param.23) | copy-start | bytes 100
  13.6 9.7 %collective-permute-start.1 = (f32[272,256]{1,0:T(8,128)S(1)}, f32[272,256]{1,0:T(8,128)S(1)}, u32[]{:S(2)}, u32[]{:S(2)}) collective-permute-start(f32[272,256]{1,0:T(8,128)S(1)} %pad_maximum_fusion.1), channel_id=1, source_target_pairs={{0,64},{32,96},{64,128},{96,160},{128,192},{160,224},{192,256},{22... | collective-permute-start | bytes 835592 | tf_op jit(solution)/shard_map/ppermute | solution.py:18
  23.9 16.8 %collective-permute-start.2 = (f32[272,256]{1,0:T(8,128)S(1)}, f32[272,256]{1,0:T(8,128)S(1)}, u32[]{:S(2)}, u32[]{:S(2)}) collective-permute-start(f32[272,256]{1,0:T(8,128)S(1)} %pad_maximum_fusion.2), channel_id=1, source_target_pairs={{0,128},{32,160},{64,192},{96,224},{128,256},{160,288},{192,320},{... | collective-permute-start | bytes 835592 | tf_op jit(solution)/shard_map/ppermute | solution.py:18
  41.0 9.6 %collective-permute-start.3 = (f32[16,256]{1,0:T(8,128)S(1)}, f32[16,256]{1,0:T(8,128)S(1)}, u32[]{:S(2)}, u32[]{:S(2)}) collective-permute-start(f32[16,256]{1,0:T(8,128)S(1)} %convolution_add_fusion.1), channel_id=1, source_target_pairs={{0,256},{32,288},{64,320},{96,352},{128,384},{160,416},{192,448},{... | collective-permute-start | bytes 49160 | tf_op jit(solution)/shard_map/ppermute | solution.py:18
  50.7 57.0 %copy-start.3 = (f32[16,256]{1,0:T(8,128)}, f32[16,256]{1,0:T(8,128)S(1)}, u32[]{:S(2)}) copy-start(f32[16,256]{1,0:T(8,128)S(1)} %convolution_add_fusion) | copy-start | bytes 49156
  191.4 7.7 %copy-start.10 = (f32[24,24]{1,0:T(8,128)S(1)}, f32[24,24]{1,0:T(8,128)}, u32[]{:S(2)}) copy-start(f32[24,24]{1,0:T(8,128)} %param.15) | copy-start | bytes 6916
  199.1 1.7 copy-start.8
  199.1 24.6 %copy-start.2 = (f32[1,1,128,128]{3,2,1,0:T(8,128)S(1)}, f32[1,1,128,128]{3,2,1,0:T(8,128)}, u32[]{:S(2)}) copy-start(f32[1,1,128,128]{3,2,1,0:T(8,128)} %param.21) | copy-start | bytes 196612
  204.6 17.8 %all-to-all-start = ((f32[32,1,64]{2,1,0:T(1,128)}), f32[32,1,64]{2,1,0:T(1,128)S(1)}, u32[]{:S(2)}, u32[]{:S(2)}) async-start(f32[32,1,64]{2,1,0:T(1,128)} %all_to_all.6), calls=%async_computation | async-start | bytes 32768 | tf_op jit(solution)/shard_map/all_to_all | solution.py:124
  225.6 16.0 %collective-permute-start.4 = (f32[3,128]{1,0:T(4,128)S(1)}, f32[3,128]{1,0:T(4,128)S(1)}, u32[]{:S(2)}, u32[]{:S(2)}) collective-permute-start(f32[3,128]{1,0:T(4,128)S(1)} %get-tuple-element.4), channel_id=1, source_target_pairs={{0,1},{1,2},{2,3},{3,4},{4,5},{5,6},{6,7},{7,8},{8,9},{9,10},{10,1... | collective-permute-start | bytes 4616 | tf_op jit(solution)/shard_map/ppermute | solution.py:29
  229.0 12.6 %collective-permute-start.5 = (f32[3,128]{1,0:T(4,128)S(1)}, f32[3,128]{1,0:T(4,128)S(1)}, u32[]{:S(2)}, u32[]{:S(2)}) collective-permute-start(f32[3,128]{1,0:T(4,128)S(1)} %get-tuple-element.5), channel_id=1, source_target_pairs={{1,0},{2,1},{3,2},{4,3},{5,4},{6,5},{7,6},{8,7},{9,8},{10,9},{11,1... | collective-permute-start | bytes 4616 | tf_op jit(solution)/shard_map/ppermute | solution.py:31

commit v2 on v1

--- a/solution.py
+++ b/solution.py
@@ -2,6 +2,8 @@
 import jax.numpy as jnp
 from jax import lax
 from jax.sharding import PartitionSpec as P
+from jax.experimental import pallas as pl
+from jax.experimental.pallas import tpu as pltpu
 
 NK = 8
 RADIUS = 3
@@ -89,6 +91,45 @@
         precision=exact_mode,
         preferred_element_type=jnp.float32,
     )
+
+
+def gather_kernel(lookup_ref, table_ref, out_ref):
+    chunk = pl.program_id(0)
+    rows = out_ref.shape[0]
+    pack = out_ref.shape[1] // 16
+    group = lax.broadcasted_iota(jnp.int32, (1, out_ref.shape[1]), 1) // 16
+    base = chunk * rows * pack
+
+    def body(row, carry):
+        packed_row = jnp.zeros((1, out_ref.shape[1]), jnp.float32)
+        for part in range(pack):
+            where = lookup_ref[base + row * pack + part]
+            packed_row = jnp.where(group == part, table_ref[pl.ds(where, 1), :], packed_row)
+        out_ref[pl.ds(row, 1), :] = packed_row
+        return carry
+
+    lax.fori_loop(0, rows, body, 0, unroll=8)
+
+
+def gathered_rows(table, lookup):
+    width = table.shape[1]
+    pack = 128 // width
+    wide = jnp.tile(table, (1, pack))
+    total = lookup.shape[0]
+    out_rows = total // pack
+    chunks = 8
+    rows = out_rows // chunks
+    return pl.pallas_call(
+        gather_kernel,
+        out_shape=jax.ShapeDtypeStruct((out_rows, 128), jnp.float32),
+        grid_spec=pltpu.PrefetchScalarGridSpec(
+            num_scalar_prefetch=1,
+            grid=(chunks,),
+            in_specs=[pl.BlockSpec(wide.shape, lambda c, idx: (0, 0))],
+            out_specs=pl.BlockSpec((rows, 128), lambda c, idx: (c, 0)),
+        ),
+        cost_estimate=pl.CostEstimate(flops=0, bytes_accessed=wide.size * 4 + out_rows * 512, transcendentals=0),
+    )(lookup, wide)
 
 
 def on_device(
@@ -115,9 +156,11 @@
     table = jnp.transpose(panels, (0, 2, 1)).reshape(slabs * panel_order, order)
     lookup = element_substructure[0, 0][None, :] * panel_order + element_rows[0, 0]
     dofs, elements = lookup.shape
-    motion = jnp.take(table, lookup.reshape(-1), axis=0).reshape(dofs, elements, order)
-    forces = jnp.einsum("ij,jel->iel", stiffness, motion, precision=exact_mode)
-    energy = jnp.sum(motion * forces, axis=(0, 2))
+    pack = 128 // order
+    motion = gathered_rows(table, lookup.reshape(-1)).reshape(dofs, elements // pack, 128)
+    forces = jnp.einsum("ij,jab->iab", stiffness, motion, precision=exact_mode)
+    energy = jnp.sum(jnp.sum(motion * forces, axis=0).reshape(elements // pack, pack, order), axis=2)
+    energy = energy.reshape(elements)
     density = element_density[0, 0]
     sensitivity = -penalty * density * density * energy * energy_scale
     outgoing = picked(sensitivity, send_elements[0, 0])

time: 248 us -> 194 us (0.78)
  local copies, waits for them, and re-layouts: 97.9 us -> 12.1 us
  Pallas kernels: 0 us -> 27.5 us
  matrix products: 7.72 us -> 11.1 us
    gather x2 -> x0, local copies, waits for them, and re-layouts: 91.3 us -> none  [on_device(): jnp.take(table, lookup.reshape(-1), axis=0).reshape(dofs, elements, order)]
    pallas_call x0 -> x1, Pallas kernels: none -> 27.5 us  [gathered_rows(): pl.pallas_call(gather_kernel, out_shape=jax.ShapeDtypeStruct((out_rows, 1...]
    another operation x0 -> x2, local copies, waits for them, and re-layouts: none -> 7.96 us  [gathered_rows(): wide = jnp.tile(table, (1, pack))]
    dot_general x1, matrix products: 1.63 us -> 5.02 us  [on_device(): forces = jnp.einsum('ij,jab->iab', stiffness, motion, precision=exact_mode)]
    transpose x1 -> x0, local copies, waits for them, and re-layouts: 2.59 us -> none  [on_device(): table = jnp.transpose(panels, (0, 2, 1)).reshape(slabs * panel_order, order)]
  transfers between devices with their start and end apart: 7 -> 7, of which waited for: 4 -> 4; matrix products, arithmetic and copies ran while one was open for 5% -> 7% of each run, Pallas kernels for 0% -> 0%
where the time goes in v2:
time: 194 us; the launch traced here: 193 us
  blocking collectives  54.4 us (28%)
  waiting for transfers between devices  35.3 us (18%)
  Pallas kernels  27.5 us (14%)
  starting transfers between devices  20.8 us (11%)
  other arithmetic  20.3 us (10%)
  local copies, waits for them, and re-layouts  12.1 us (6%)
  matrix products  11.1 us (6%)
  between operations  11.1 us (6%)
    all_gather x1, blocking collectives, on_device(): panels = lax.all_gather(solved, 'dev', axis=0, tiled=False)  54.4 us
    ppermute x4, waiting for transfers between devices, passed_along(): lax.ppermute(value, axis, [(source, source + steps) for source in range(l...  35.2 us
    pallas_call x1, Pallas kernels, gathered_rows(): pl.pallas_call(gather_kernel, out_shape=jax.ShapeDtypeStruct((out_rows, 1...  27.5 us
    add x1, other arithmetic, on_device(): weight_sum = weight_sum + filter_weights[which] * inside  9.96 us
    another operation x2, local copies, waits for them, and re-layouts, gathered_rows(): wide = jnp.tile(table, (1, pack))  7.96 us
    ppermute x4, starting transfers between devices, passed_along(): lax.ppermute(value, axis, [(source, source + steps) for source in range(l...  7.07 us
    all_to_all x1, starting transfers between devices, on_device(): lax.all_to_all(outgoing, 'dev', split_axis=0, concat_axis=0, tiled=True)  5.79 us
    broadcast_in_dim x1, other arithmetic, on_device(): return (solved[None, None], filtered[None, None])  5.7 us
  transfers between devices with their start and end apart: 7, of which 4 were waited for; matrix products, arithmetic and copies ran while one was open for 7% of the time, Pallas kernels for 0%

profile of v2, /device:TPU:96, one launch (start us, length us, event | category | flops | bytes accessed | tf_op | source)
XLA Modules:
  0.0 192.6 jit_solution(13821558347277082686)
XLA Ops:
  0.6 0.0 copy-start
  0.7 0.9 copy-done
  1.6 1.3 convolution_negate_fusion
  2.9 0.9 fusion.15
  3.9 1.9 collective-permute-start
  5.8 0.1 reshape_squeeze.7
  6.0 0.0 copy-start.5
  6.0 7.0 %collective-permute-done = f32[272,256]{1,0:T(8,128)S(1)} collective-permute-done((f32[272,256]{1,0:T(8,128)S(1)}, f32[272,256]{1,0:T(8,128)S(1)}, u32[]{:S(2)}, u32[]{:S(2)}) %collective-permute-start) | collective-permute-done | bytes 278560 | tf_op jit(solution)/shard_map/ppermute | solution.py:20
  13.0 0.4 fusion.11
  13.4 0.0 copy-start.1
  13.4 0.0 copy-start.7
  13.4 0.2 convolution_add_fusion.3
  13.6 1.9 collective-permute-start.1
  15.6 0.7 fusion.42
  16.3 7.0 %collective-permute-done.1 = f32[272,256]{1,0:T(8,128)S(1)} collective-permute-done((f32[272,256]{1,0:T(8,128)S(1)}, f32[272,256]{1,0:T(8,128)S(1)}, u32[]{:S(2)}, u32[]{:S(2)}) %collective-permute-start.1) | collective-permute-done | bytes 278560 | tf_op jit(solution)/shard_map/ppermute | solution.py:20
  23.3 0.2 convolution_add_fusion.2
  23.5 0.4 fusion.9
  23.9 1.9 collective-permute-start.2
  25.9 0.7 fusion.41
  26.6 0.1 reshape_squeeze.6
  26.7 0.7 add.341.lookup_ref
  27.4 13.4 %collective-permute-done.2 = f32[272,256]{1,0:T(8,128)S(1)} collective-permute-done((f32[272,256]{1,0:T(8,128)S(1)}, f32[272,256]{1,0:T(8,128)S(1)}, u32[]{:S(2)}, u32[]{:S(2)}) %collective-permute-start.2) | collective-permute-done | bytes 278560 | tf_op jit(solution)/shard_map/ppermute | solution.py:20
  40.8 0.2 convolution_add_fusion.1
  41.0 1.3 collective-permute-start.3
  42.3 0.4 fusion.7
  42.7 7.9 %collective-permute-done.3 = f32[16,256]{1,0:T(8,128)S(1)} collective-permute-done((f32[16,256]{1,0:T(8,128)S(1)}, f32[16,256]{1,0:T(8,128)S(1)}, u32[]{:S(2)}, u32[]{:S(2)}) %collective-permute-start.3) | collective-permute-done | bytes 16416 | tf_op jit(solution)/shard_map/ppermute | solution.py:20
  50.5 0.2 convolution_add_fusion
  50.7 0.0 copy-start.3
  50.8 54.4 %all-gather = f32[512,256]{1,0:T(8,128)S(1)} all-gather(f32[16,256]{1,0:T(8,128)S(1)} %convolution_add_fusion), channel_id=2, replica_groups=mesh['grp'=16,'dev'=32] {'dev'}, dimensions={0}, use_global_device_ids=true | all-gather | bytes 540672 | tf_op jit(solution)/shard_map/all_gather | solution.py:154
  105.2 2.4 %tile.11 = f32[8192,8,16]{0,2,1:T(8,128)} broadcast(f32[8192,16]{0,1:T(8,128)S(1)} %bitcast.77), dimensions={0,2} | broadcast | bytes 4718592 | tf_op jit(solution)/shard_map/tile | solution.py:117
  107.6 5.6 %copy.27.table_ref = f32[8192,128]{1,0:T(8,128)} copy(f32[8192,128]{0,1:T(8,128)} %bitcast.75) | data formatting | bytes 8388608 | tf_op jit(solution)/shard_map/tile | solution.py:117
  113.2 27.5 %shard_map.131 = f32[3072,128]{1,0:T(8,128)} custom-call(s32[24576]{0:T(1024)} %add.341.lookup_ref, f32[8192,128]{1,0:T(8,128)} %copy.27.table_ref), custom_call_target="tpu_custom_call" | custom-call | bytes 5767168 | tf_op jit(solution)/shard_map/pallas_call | solution.py:122
  140.6 5.0 %fusion = f32[128,128]{1,0:T(8,128)S(1)} fusion(f32[24,128,128]{2,1,0:T(8,128)} %bitcast.76, f32[24,24]{1,0:T(8,128)S(1)} %copy-done.8), kind=kOutput, calls=%fused_computation.1 | convolution fusion | flops 114016256 | bytes 1640704 | tf_op jit(solution)/shard_map/ij,jab->iab/dot_general | solution.py:161
  145.7 0.1 copy.30
  145.8 0.1 copy.31
  145.9 0.1 reshape.279
  146.0 3.1 %select_reduce_fusion = f32[2048]{0:T(1024)S(1)} fusion(f32[128]{0:T(128)S(1)} %get-tuple-element.16, f32[128]{0:T(128)S(1)} %get-tuple-element.17, f32[128]{0:T(128)S(1)} %get-tuple-element.18, f32[128]{0:T(128)S(1)} %get-tuple-element.19, f32[128]{0:T(128)S(1)} %get-tuple-element.20, f32[128]{0:T(128)S(1)} %get-tuple-element.21, ...), kind=kLoop, calls=%fused_computation.10 | loop fusion | flops 4716544 | bytes 36864 | tf_op jit(solution)/shard_map/reduce_sum | solution.py:73
  149.2 0.7 all_to_all.6
  149.9 5.8 %all-to-all-start = ((f32[32,1,64]{2,1,0:T(1,128)}), f32[32,1,64]{2,1,0:T(1,128)S(1)}, u32[]{:S(2)}, u32[]{:S(2)}) async-start(f32[32,1,64]{2,1,0:T(1,128)} %all_to_all.6), calls=%async_computation | async-start | bytes 32768 | tf_op jit(solution)/shard_map/all_to_all | solution.py:167
  155.7 10.0 %fusion.37 = f32[128]{0:T(128)S(1)} fusion(f32[]{:T(128)} %bitcast.28, s32[]{:T(128)} %bitcast.29, f32[]{:T(128)} %bitcast.26, s32[]{:T(128)} %bitcast.27, f32[]{:T(128)} %bitcast.24, s32[]{:T(128)} %bitcast.25, f32[]{:T(128)} %bitcast.22, s32[]{:T(128)} %bitcast.23, f32[]{:T(128)} %bitcast.20, s32[]{:T(128)} %bitcast.21, f32[]{:T(128)} %bitcast.18, ...), kind=kLoop, calls=%fused_computation.85 | loop fusion | flops 6144 | bytes 580 | tf_op jit(solution)/shard_map/add | solution.py:184
  167.5 0.0 all-to-all-done
  167.5 0.5 broadcast.499
  168.0 0.7 reduce.3
  168.7 0.1 broadcast_in_dim.149
  168.8 1.9 convolution_multiply_fusion
  170.7 3.4 %collective-permute-start.4 = (f32[3,128]{1,0:T(4,128)S(1)}, f32[3,128]{1,0:T(4,128)S(1)}, u32[]{:S(2)}, u32[]{:S(2)}) collective-permute-start(f32[3,128]{1,0:T(4,128)S(1)} %get-tuple-element.4), channel_id=1, source_target_pairs={{0,1},{1,2},{2,3},{3,4},{4,5},{5,6},{6,7},{7,8},{8,9},{9,10},{10,1... | collective-permute-start | bytes 4616 | tf_op jit(solution)/shard_map/ppermute | solution.py:31
  174.1 4.6 %collective-permute-start.5 = (f32[3,128]{1,0:T(4,128)S(1)}, f32[3,128]{1,0:T(4,128)S(1)}, u32[]{:S(2)}, u32[]{:S(2)}) collective-permute-start(f32[3,128]{1,0:T(4,128)S(1)} %get-tuple-element.5), channel_id=1, source_target_pairs={{1,0},{2,1},{3,2},{4,3},{5,4},{6,5},{7,6},{8,7},{9,8},{10,9},{11,1... | collective-permute-start | bytes 4616 | tf_op jit(solution)/shard_map/ppermute | solution.py:33
  186.9 5.7 %fusion.18 = f32[1,1,128,128]{3,2,1,0:T(8,128)} fusion(f32[1,1,128,128]{3,2,1,0:T(8,128)S(1)} %copy-done.2, f32[134,128]{1,0:T(8,128)S(1)} %pad_maximum_fusion.3, s32[]{:T(128)S(6)} %select_n.143, s32[]{:T(128)S(6)} %select_n.142, s32[]{:T(128)S(6)} %select_n.141, s32[]{:T(128)S(6)} %select_n.140, s32[]{:T(128)S(6)} %select_n.139, s32[]{:T(128)S(6)} %select_n.138, ...), kind=kLoop, calls=%fused_computation.35 | loop fusion | flops 278528 | bytes 655936 | tf_op jit(solution)/shard_map/broadcast_in_dim | solution.py:186
  (35 shorter events, 0.3 us)
Async XLA Ops:
  0.6 1.0 copy-start
  0.6 5.2 %copy-start.6 = (s32[1,1,32,64]{3,2,1,0:T(8,128)S(1)}, s32[1,1,32,64]{3,2,1,0:T(8,128)}, u32[]{:S(2)}) copy-start(s32[1,1,32,64]{3,2,1,0:T(8,128)} %param.19) | copy-start | bytes 24580
  0.7 5.3 %copy-start.10 = (s32[1,1,1024]{2,1,0:T(1,128)S(1)}, s32[1,1,1024]{2,1,0:T(1,128)}, u32[]{:S(2)}) copy-start(s32[1,1,1024]{2,1,0:T(1,128)} %param.16) | copy-start | bytes 12292
  0.7 14.9 %copy-start.4 = (s32[8]{0:T(128)S(1)}, s32[8]{0:T(128)}, u32[]{:S(2)}) copy-start(s32[8]{0:T(128)} %param.22) | copy-start | bytes 100
  3.9 9.1 %collective-permute-start = (f32[272,256]{1,0:T(8,128)S(1)}, f32[272,256]{1,0:T(8,128)S(1)}, u32[]{:S(2)}, u32[]{:S(2)}) collective-permute-start(f32[272,256]{1,0:T(8,128)S(1)} %pad_maximum_fusion), channel_id=1, source_target_pairs={{0,32},{32,64},{64,96},{96,128},{128,160},{160,192},{192,224},{224... | collective-permute-start | bytes 835592 | tf_op jit(solution)/shard_map/ppermute | solution.py:20
  6.0 19.9 %copy-start.5 = (f32[8]{0:T(128)S(1)}, f32[8]{0:T(128)}, u32[]{:S(2)}) copy-start(f32[8]{0:T(128)} %param.23) | copy-start | bytes 100
  13.4 13.2 %copy-start.1 = (s32[1,1,24,1024]{3,2,1,0:T(8,128)S(1)}, s32[1,1,24,1024]{3,2,1,0:T(8,128)}, u32[]{:S(2)}) copy-start(s32[1,1,24,1024]{3,2,1,0:T(8,128)} %param.17) | copy-start | bytes 294916
  13.4 13.2 %copy-start.7 = (s32[1,1,32,64]{3,2,1,0:T(8,128)S(1)}, s32[1,1,32,64]{3,2,1,0:T(8,128)}, u32[]{:S(2)}) copy-start(s32[1,1,32,64]{3,2,1,0:T(8,128)} %param.20) | copy-start | bytes 24580
  13.6 9.7 %collective-permute-start.1 = (f32[272,256]{1,0:T(8,128)S(1)}, f32[272,256]{1,0:T(8,128)S(1)}, u32[]{:S(2)}, u32[]{:S(2)}) collective-permute-start(f32[272,256]{1,0:T(8,128)S(1)} %pad_maximum_fusion.1), channel_id=1, source_target_pairs={{0,64},{32,96},{64,128},{96,160},{128,192},{160,224},{192,256},{22... | collective-permute-start | bytes 835592 | tf_op jit(solution)/shard_map/ppermute | solution.py:20
  23.9 16.8 %collective-permute-start.2 = (f32[272,256]{1,0:T(8,128)S(1)}, f32[272,256]{1,0:T(8,128)S(1)}, u32[]{:S(2)}, u32[]{:S(2)}) collective-permute-start(f32[272,256]{1,0:T(8,128)S(1)} %pad_maximum_fusion.2), channel_id=1, source_target_pairs={{0,128},{32,160},{64,192},{96,224},{128,256},{160,288},{192,320},{... | collective-permute-start | bytes 835592 | tf_op jit(solution)/shard_map/ppermute | solution.py:20
  41.0 9.6 %collective-permute-start.3 = (f32[16,256]{1,0:T(8,128)S(1)}, f32[16,256]{1,0:T(8,128)S(1)}, u32[]{:S(2)}, u32[]{:S(2)}) collective-permute-start(f32[16,256]{1,0:T(8,128)S(1)} %convolution_add_fusion.1), channel_id=1, source_target_pairs={{0,256},{32,288},{64,320},{96,352},{128,384},{160,416},{192,448},{... | collective-permute-start | bytes 49160 | tf_op jit(solution)/shard_map/ppermute | solution.py:20
  50.7 56.8 %copy-start.3 = (f32[16,256]{1,0:T(8,128)}, f32[16,256]{1,0:T(8,128)S(1)}, u32[]{:S(2)}) copy-start(f32[16,256]{1,0:T(8,128)S(1)} %convolution_add_fusion) | copy-start | bytes 49156
  113.2 27.5 %copy-start.8 = (f32[24,24]{1,0:T(8,128)S(1)}, f32[24,24]{1,0:T(8,128)}, u32[]{:S(2)}) copy-start(f32[24,24]{1,0:T(8,128)} %param.15) | copy-start | bytes 6916
  140.6 5.4 %copy-start.9 = (f32[1,1,1024]{2,1,0:T(1,128)S(1)}, f32[1,1,1024]{2,1,0:T(1,128)}, u32[]{:S(2)}) copy-start(f32[1,1,1024]{2,1,0:T(1,128)} %param.18) | copy-start | bytes 12292
  140.6 28.1 %copy-start.2 = (f32[1,1,128,128]{3,2,1,0:T(8,128)S(1)}, f32[1,1,128,128]{3,2,1,0:T(8,128)}, u32[]{:S(2)}) copy-start(f32[1,1,128,128]{3,2,1,0:T(8,128)} %param.21) | copy-start | bytes 196612
  149.9 17.6 %all-to-all-start = ((f32[32,1,64]{2,1,0:T(1,128)}), f32[32,1,64]{2,1,0:T(1,128)S(1)}, u32[]{:S(2)}, u32[]{:S(2)}) async-start(f32[32,1,64]{2,1,0:T(1,128)} %all_to_all.6), calls=%async_computation | async-start | bytes 32768 | tf_op jit(solution)/shard_map/all_to_all | solution.py:167
  170.7 16.1 %collective-permute-start.4 = (f32[3,128]{1,0:T(4,128)S(1)}, f32[3,128]{1,0:T(4,128)S(1)}, u32[]{:S(2)}, u32[]{:S(2)}) collective-permute-start(f32[3,128]{1,0:T(4,128)S(1)} %get-tuple-element.4), channel_id=1, source_target_pairs={{0,1},{1,2},{2,3},{3,4},{4,5},{5,6},{6,7},{7,8},{8,9},{9,10},{10,1... | collective-permute-start | bytes 4616 | tf_op jit(solution)/shard_map/ppermute | solution.py:31
  174.1 12.8 %collective-permute-start.5 = (f32[3,128]{1,0:T(4,128)S(1)}, f32[3,128]{1,0:T(4,128)S(1)}, u32[]{:S(2)}, u32[]{:S(2)}) collective-permute-start(f32[3,128]{1,0:T(4,128)S(1)} %get-tuple-element.5), channel_id=1, source_target_pairs={{1,0},{2,1},{3,2},{4,3},{5,4},{6,5},{7,6},{8,7},{9,8},{10,9},{11,1... | collective-permute-start | bytes 4616 | tf_op jit(solution)/shard_map/ppermute | solution.py:33

commit v3 on v2

--- a/solution.py
+++ b/solution.py
@@ -132,6 +132,24 @@
     )(lookup, wide)
 
 
+def gathered_panels(solved):
+    count = lax.axis_size("dev")
+    me = lax.axis_index("dev")
+    bits = count.bit_length() - 1
+    order = [bits - 1, 1, bits - 2, bits - 3, 0] if bits == 5 else list(range(bits))
+    block = solved[None]
+    for bit in order:
+        partner = [(i, i ^ (1 << bit)) for i in range(count)]
+        other = lax.ppermute(block, "dev", partner)
+        high = ((me >> bit) & 1) == 1
+        block = jnp.where(high, jnp.concatenate([other, block], 0), jnp.concatenate([block, other], 0))
+    slab = jnp.arange(count, dtype=jnp.int32)
+    position = jnp.zeros_like(slab)
+    for place, bit in enumerate(order):
+        position = position + (((slab >> bit) & 1) << place)
+    return block, position
+
+
 def on_device(
     panel_inverse,
     coupling,
@@ -151,10 +169,11 @@
     rights = loads[0, 0]
     solved = interface_chain(inverse, couple, rights)
 
-    panels = lax.all_gather(solved, "dev", axis=0, tiled=False)
+    panels, position = gathered_panels(solved)
     slabs, order, panel_order = panels.shape
     table = jnp.transpose(panels, (0, 2, 1)).reshape(slabs * panel_order, order)
-    lookup = element_substructure[0, 0][None, :] * panel_order + element_rows[0, 0]
+    slab_place = jnp.take(position, element_substructure[0, 0], axis=0)
+    lookup = slab_place[None, :] * panel_order + element_rows[0, 0]
     dofs, elements = lookup.shape
     pack = 128 // order
     motion = gathered_rows(table, lookup.reshape(-1)).reshape(dofs, elements // pack, 128)

time: 194 us -> 189 us (0.974)
  the two profiles are of different devices: /device:TPU:96 before, /device:TPU:38 now
where the time goes in v3:
time: 189 us; the launch traced here: 187 us
  starting transfers between devices  50.9 us (27%)
  other arithmetic  40.4 us (21%)
  waiting for transfers between devices  32.3 us (17%)
  Pallas kernels  27.5 us (15%)
  local copies, waits for them, and re-layouts  13.6 us (7%)
  between operations  11.5 us (6%)
  matrix products  11.1 us (6%)
    pallas_call x1, Pallas kernels, gathered_rows(): pl.pallas_call(gather_kernel, out_shape=jax.ShapeDtypeStruct((out_rows, 1...  27.5 us
    ppermute x5, starting transfers between devices, gathered_panels(): other = lax.ppermute(block, 'dev', partner)  24.8 us
    ppermute x4, waiting for transfers between devices, passed_along(): lax.ppermute(value, axis, [(source, source + steps) for source in range(l...  17.3 us
    mul x1, other arithmetic, on_device(): lookup = slab_place[None, :] * panel_order + element_rows[0, 0]  15.6 us
    ppermute x5, waiting for transfers between devices, gathered_panels(): other = lax.ppermute(block, 'dev', partner)  15 us
    all_to_all x1, starting transfers between devices, on_device(): lax.all_to_all(outgoing, 'dev', split_axis=0, concat_axis=0, tiled=True)  11 us
    add x1, other arithmetic, on_device(): weight_sum = weight_sum + filter_weights[which] * inside  9.9 us
    another operation x3, local copies, waits for them, and re-layouts, gathered_rows(): wide = jnp.tile(table, (1, pack))  7.98 us
  transfers between devices with their start and end apart: 12, of which 8 were waited for; matrix products, arithmetic and copies ran while one was open for 18% of the time, Pallas kernels for 0%

profile of v3, /device:TPU:38, one launch (start us, length us, event | category | flops | bytes accessed | tf_op | source)
XLA Modules:
  0.0 187.2 jit_solution(17679289547328732683)
XLA Ops:
  0.7 0.9 copy-done
  1.6 1.3 convolution_negate_fusion
  2.9 0.9 fusion.16
  3.9 1.9 %collective-permute-start = (f32[272,256]{1,0:T(8,128)S(1)}, f32[272,256]{1,0:T(8,128)S(1)}, u32[]{:S(2)}, u32[]{:S(2)}) collective-permute-start(f32[272,256]{1,0:T(8,128)S(1)} %pad_maximum_fusion), channel_id=1, source_target_pairs={{0,32},{32,64},{64,96},{96,128},{128,160},{160,192},{192,224},{224... | collective-permute-start | bytes 835592 | tf_op jit(solution)/shard_map/ppermute | solution.py:20
  5.8 0.7 fusion.60
  6.5 6.4 %collective-permute-done = f32[272,256]{1,0:T(8,128)S(1)} collective-permute-done((f32[272,256]{1,0:T(8,128)S(1)}, f32[272,256]{1,0:T(8,128)S(1)}, u32[]{:S(2)}, u32[]{:S(2)}) %collective-permute-start) | collective-permute-done | bytes 278560 | tf_op jit(solution)/shard_map/ppermute | solution.py:20
  13.0 0.4 fusion.12
  13.4 0.2 convolution_add_fusion.3
  13.6 1.9 %collective-permute-start.1 = (f32[272,256]{1,0:T(8,128)S(1)}, f32[272,256]{1,0:T(8,128)S(1)}, u32[]{:S(2)}, u32[]{:S(2)}) collective-permute-start(f32[272,256]{1,0:T(8,128)S(1)} %pad_maximum_fusion.1), channel_id=1, source_target_pairs={{0,64},{32,96},{64,128},{96,160},{128,192},{160,224},{192,256},{22... | collective-permute-start | bytes 835592 | tf_op jit(solution)/shard_map/ppermute | solution.py:20
  15.6 4.4 %compare_select_fusion.1 = (s32[1024,1]{0,1:T(1,128)S(1)}, s32[1024,1]{0,1:T(1,128)S(1)}) fusion(s32[]{:T(128)} %bitcast.34, s32[]{:T(128)} %bitcast.35, s32[]{:T(128)} %bitcast.36, s32[]{:T(128)} %bitcast.37, s32[]{:T(128)} %bitcast.38, s32[]{:T(128)} %bitcast.40, s32[]{:T(128)} %bitcast.39, s32[1,1,1024]{2,1,0:T(1,128)S(1)} %copy-done.8), kind=kLoop, calls=%fused_computation.73 | loop fusion | flops 15360 | bytes 12316 | tf_op jit(solution)/shard_map/jit(_take)/gather | solution.py:175
  19.9 0.3 compare_reduce_fusion.24
  20.2 3.1 %collective-permute-done.1 = f32[272,256]{1,0:T(8,128)S(1)} collective-permute-done((f32[272,256]{1,0:T(8,128)S(1)}, f32[272,256]{1,0:T(8,128)S(1)}, u32[]{:S(2)}, u32[]{:S(2)}) %collective-permute-start.1) | collective-permute-done | bytes 278560 | tf_op jit(solution)/shard_map/ppermute | solution.py:20
  23.5 0.4 fusion.10
  24.0 2.1 %collective-permute-start.2 = (f32[272,256]{1,0:T(8,128)S(1)}, f32[272,256]{1,0:T(8,128)S(1)}, u32[]{:S(2)}, u32[]{:S(2)}) collective-permute-start(f32[272,256]{1,0:T(8,128)S(1)} %pad_maximum_fusion.2), channel_id=1, source_target_pairs={{0,128},{32,160},{64,192},{96,224},{128,256},{160,288},{192,320},{... | collective-permute-start | bytes 835592 | tf_op jit(solution)/shard_map/ppermute | solution.py:20
  26.0 0.7 fusion.59
  26.8 15.6 %fusion.32 = s32[1024]{0:T(1024)S(1)} fusion(pred[1024]{0:T(1024)(128)(4,1)S(1)} %get-tuple-element.26, pred[1024]{0:T(1024)(128)(4,1)S(1)} %get-tuple-element.25, pred[1024]{0:T(1024)(128)(4,1)S(1)} %get-tuple-element.24, pred[1024]{0:T(1024)(128)(4,1)S(1)} %get-tuple-element.23, pred[1024]{0:T(1024)(128)(4,1)S(1)} %get-tuple-element.22, ...), kind=kLoop, calls=%fused_computation.102 | loop fusion | flops 33792 | bytes 37988 | tf_op jit(solution)/shard_map/mul | solution.py:176
  42.4 0.2 convolution_add_fusion.1
  42.6 1.3 collective-permute-start.3
  43.9 0.4 fusion.8
  44.3 7.9 %collective-permute-done.3 = f32[16,256]{1,0:T(8,128)S(1)} collective-permute-done((f32[16,256]{1,0:T(8,128)S(1)}, f32[16,256]{1,0:T(8,128)S(1)}, u32[]{:S(2)}, u32[]{:S(2)}) %collective-permute-start.3) | collective-permute-done | bytes 16416 | tf_op jit(solution)/shard_map/ppermute | solution.py:20
  52.2 0.2 convolution_add_fusion
  52.4 10.9 %collective-permute-start.4 = (f32[1,16,256]{2,1,0:T(8,128)S(1)}, f32[1,16,256]{2,1,0:T(8,128)S(1)}, u32[]{:S(2)}, u32[]{:S(2)}) collective-permute-start(f32[1,16,256]{2,1,0:T(8,128)S(1)} %bitcast.114), channel_id=1, source_target_pairs={{0,16},{1,17},{2,18},{3,19},{4,20},{5,21},{6,22},{7,23},{8,24},{9,... | collective-permute-start | bytes 49160 | tf_op jit(solution)/shard_map/ppermute | solution.py:143
  63.4 1.6 collective-permute-done.4
  65.0 3.3 %collective-permute-start.5 = (f32[2,16,256]{2,1,0:T(8,128)S(1)}, f32[2,16,256]{2,1,0:T(8,128)S(1)}, u32[]{:S(2)}, u32[]{:S(2)}) collective-permute-start(f32[2,16,256]{2,1,0:T(8,128)S(1)} %maximum_select_fusion.4), channel_id=1, source_target_pairs={{0,2},{1,3},{2,0},{3,1},{4,6},{5,7},{6,4},{7,5},{8,10},{9,11},{10,... | collective-permute-start | bytes 98312 | tf_op jit(solution)/shard_map/ppermute | solution.py:143
  68.4 4.0 %collective-permute-done.5 = f32[2,16,256]{2,1,0:T(8,128)S(1)} collective-permute-done((f32[2,16,256]{2,1,0:T(8,128)S(1)}, f32[2,16,256]{2,1,0:T(8,128)S(1)}, u32[]{:S(2)}, u32[]{:S(2)}) %collective-permute-start.5) | collective-permute-done | bytes 32800 | tf_op jit(solution)/shard_map/ppermute | solution.py:143
  72.4 4.4 %collective-permute-start.6 = (f32[4,16,256]{2,1,0:T(8,128)S(1)}, f32[4,16,256]{2,1,0:T(8,128)S(1)}, u32[]{:S(2)}, u32[]{:S(2)}) collective-permute-start(f32[4,16,256]{2,1,0:T(8,128)S(1)} %maximum_select_fusion.3), channel_id=1, source_target_pairs={{0,8},{1,9},{2,10},{3,11},{4,12},{5,13},{6,14},{7,15},{8,0},{9,1},... | collective-permute-start | bytes 196616 | tf_op jit(solution)/shard_map/ppermute | solution.py:143
  76.8 2.6 %collective-permute-done.6 = f32[4,16,256]{2,1,0:T(8,128)S(1)} collective-permute-done((f32[4,16,256]{2,1,0:T(8,128)S(1)}, f32[4,16,256]{2,1,0:T(8,128)S(1)}, u32[]{:S(2)}, u32[]{:S(2)}) %collective-permute-start.6) | collective-permute-done | bytes 65568 | tf_op jit(solution)/shard_map/ppermute | solution.py:143
  79.4 3.4 %collective-permute-start.7 = (f32[8,16,256]{2,1,0:T(8,128)S(1)}, f32[8,16,256]{2,1,0:T(8,128)S(1)}, u32[]{:S(2)}, u32[]{:S(2)}) collective-permute-start(f32[8,16,256]{2,1,0:T(8,128)S(1)} %maximum_select_fusion.2), channel_id=1, source_target_pairs={{0,4},{1,5},{2,6},{3,7},{4,0},{5,1},{6,2},{7,3},{8,12},{9,13},{10,... | collective-permute-start | bytes 393224 | tf_op jit(solution)/shard_map/ppermute | solution.py:143
  82.8 0.7 fusion.58
  83.5 2.8 %collective-permute-done.7 = f32[8,16,256]{2,1,0:T(8,128)S(1)} collective-permute-done((f32[8,16,256]{2,1,0:T(8,128)S(1)}, f32[8,16,256]{2,1,0:T(8,128)S(1)}, u32[]{:S(2)}, u32[]{:S(2)}) %collective-permute-start.7) | collective-permute-done | bytes 131104 | tf_op jit(solution)/shard_map/ppermute | solution.py:143
  86.3 2.7 %collective-permute-start.8 = (f32[16,16,256]{2,1,0:T(8,128)S(1)}, f32[16,16,256]{2,1,0:T(8,128)S(1)}, u32[]{:S(2)}, u32[]{:S(2)}) collective-permute-start(f32[16,16,256]{2,1,0:T(8,128)S(1)} %maximum_select_fusion.1), channel_id=1, source_target_pairs={{0,1},{1,0},{2,3},{3,2},{4,5},{5,4},{6,7},{7,6},{8,9},{9,8},{10,11... | collective-permute-start | bytes 786440 | tf_op jit(solution)/shard_map/ppermute | solution.py:143
  89.1 0.7 fusion.57
  89.9 0.7 add.386.lookup_ref
  90.6 4.0 %collective-permute-done.8 = f32[16,16,256]{2,1,0:T(8,128)S(1)} collective-permute-done((f32[16,16,256]{2,1,0:T(8,128)S(1)}, f32[16,16,256]{2,1,0:T(8,128)S(1)}, u32[]{:S(2)}, u32[]{:S(2)}) %collective-permute-start.8) | collective-permute-done | bytes 262176 | tf_op jit(solution)/shard_map/ppermute | solution.py:143
  94.7 2.4 %tile.11 = f32[8192,8,16]{0,2,1:T(8,128)} broadcast(f32[8192,16]{0,1:T(8,128)S(1)} %bitcast.110), dimensions={0,2} | broadcast | bytes 4718592 | tf_op jit(solution)/shard_map/tile | solution.py:117
  97.1 5.6 %copy.27.table_ref = f32[8192,128]{1,0:T(8,128)} copy(f32[8192,128]{0,1:T(8,128)} %bitcast.108) | data formatting | bytes 8388608 | tf_op jit(solution)/shard_map/tile | solution.py:117
  102.6 27.5 %shard_map.131 = f32[3072,128]{1,0:T(8,128)} custom-call(s32[24576]{0:T(1024)} %add.386.lookup_ref, f32[8192,128]{1,0:T(8,128)} %copy.27.table_ref), custom_call_target="tpu_custom_call" | custom-call | bytes 5767168 | tf_op jit(solution)/shard_map/pallas_call | solution.py:122
  130.1 5.0 %fusion = f32[128,128]{1,0:T(8,128)S(1)} fusion(f32[24,128,128]{2,1,0:T(8,128)} %bitcast.109, f32[24,24]{1,0:T(8,128)S(1)} %copy-done.9), kind=kOutput, calls=%fused_computation.1 | convolution fusion | flops 114016256 | bytes 1640704 | tf_op jit(solution)/shard_map/ij,jab->iab/dot_general | solution.py:180
  135.5 3.1 %select_reduce_fusion = f32[2048]{0:T(1024)S(1)} fusion(f32[128]{0:T(128)S(1)} %get-tuple-element.43, f32[128]{0:T(128)S(1)} %get-tuple-element.44, f32[128]{0:T(128)S(1)} %get-tuple-element.45, f32[128]{0:T(128)S(1)} %get-tuple-element.46, f32[128]{0:T(128)S(1)} %get-tuple-element.47, f32[128]{0:T(128)S(1)} %get-tuple-element.48, ...), kind=kLoop, calls=%fused_computation.10 | loop fusion | flops 4716544 | bytes 36864 | tf_op jit(solution)/shard_map/reduce_sum | solution.py:73
  138.6 0.7 all_to_all.6
  139.3 11.0 %all-to-all-start = ((f32[32,1,64]{2,1,0:T(1,128)}), f32[32,1,64]{2,1,0:T(1,128)S(1)}, u32[]{:S(2)}, u32[]{:S(2)}) async-start(f32[32,1,64]{2,1,0:T(1,128)} %all_to_all.6), calls=%async_computation | async-start | bytes 32768 | tf_op jit(solution)/shard_map/all_to_all | solution.py:186
  150.3 9.9 %fusion.39 = f32[128]{0:T(128)S(1)} fusion(f32[]{:T(128)} %bitcast.62, s32[]{:T(128)} %bitcast.63, f32[]{:T(128)} %bitcast.60, s32[]{:T(128)} %bitcast.61, f32[]{:T(128)} %bitcast.58, s32[]{:T(128)} %bitcast.59, f32[]{:T(128)} %bitcast.56, s32[]{:T(128)} %bitcast.57, f32[]{:T(128)} %bitcast.54, s32[]{:T(128)} %bitcast.55, f32[]{:T(128)} %bitcast.52, ...), kind=kLoop, calls=%fused_computation.130 | loop fusion | flops 6144 | bytes 580 | tf_op jit(solution)/shard_map/add | solution.py:203
  161.5 0.5 broadcast.797
  162.0 0.7 reduce.53
  162.8 1.9 %convolution_multiply_fusion = f32[128,128]{1,0:T(8,128)S(1)} fusion(f32[2048]{0:T(1024)S(1)} %broadcast_in_dim.161, s32[2048]{0:T(1024)S(1)} %get-tuple-element.34, s32[2048]{0:T(1024)S(1)} %get-tuple-element.33, f32[1,1,128,128]{3,2,1,0:T(8,128)S(1)} %copy-done.2), kind=kOutput, calls=%fused_computation.4 | convolution fusion | flops 403456000 | bytes 155648 | tf_op jit(solution)/shard_map/dot_general | solution.py:87
  164.7 2.8 %collective-permute-start.10 = (f32[3,128]{1,0:T(4,128)S(1)}, f32[3,128]{1,0:T(4,128)S(1)}, u32[]{:S(2)}, u32[]{:S(2)}) collective-permute-start(f32[3,128]{1,0:T(4,128)S(1)} %get-tuple-element.32), channel_id=1, source_target_pairs={{1,0},{2,1},{3,2},{4,3},{5,4},{6,5},{7,6},{8,7},{9,8},{10,9},{11,1... | collective-permute-start | bytes 4616 | tf_op jit(solution)/shard_map/ppermute | solution.py:33
  167.5 5.2 %collective-permute-start.9 = (f32[3,128]{1,0:T(4,128)S(1)}, f32[3,128]{1,0:T(4,128)S(1)}, u32[]{:S(2)}, u32[]{:S(2)}) collective-permute-start(f32[3,128]{1,0:T(4,128)S(1)} %get-tuple-element.31), channel_id=1, source_target_pairs={{0,1},{1,2},{2,3},{3,4},{4,5},{5,6},{6,7},{7,8},{8,9},{9,10},{10,1... | collective-permute-start | bytes 4616 | tf_op jit(solution)/shard_map/ppermute | solution.py:31
  181.7 5.5 %fusion.19 = f32[1,1,128,128]{3,2,1,0:T(8,128)} fusion(f32[1,1,128,128]{3,2,1,0:T(8,128)S(1)} %copy-done.2, f32[134,128]{1,0:T(8,128)S(1)} %pad_maximum_fusion.3, s32[]{:T(128)S(6)} %select_n.224, s32[]{:T(128)S(6)} %select_n.223, s32[]{:T(128)S(6)} %select_n.222, s32[]{:T(128)S(6)} %select_n.221, s32[]{:T(128)S(6)} %select_n.220, s32[]{:T(128)S(6)} %select_n.219, ...), kind=kLoop, calls=%fused_computation.40 | loop fusion | flops 278528 | bytes 655936 | tf_op jit(solution)/shard_map/broadcast_in_dim | solution.py:205
  (54 shorter events, 1.2 us)
Async XLA Ops:
  0.6 1.0 copy-start
  0.6 14.9 %copy-start.8 = (s32[1,1,1024]{2,1,0:T(1,128)S(1)}, s32[1,1,1024]{2,1,0:T(1,128)}, u32[]{:S(2)}) copy-start(s32[1,1,1024]{2,1,0:T(1,128)} %param.16) | copy-start | bytes 12292
  3.9 9.1 %collective-permute-start = (f32[272,256]{1,0:T(8,128)S(1)}, f32[272,256]{1,0:T(8,128)S(1)}, u32[]{:S(2)}, u32[]{:S(2)}) collective-permute-start(f32[272,256]{1,0:T(8,128)S(1)} %pad_maximum_fusion), channel_id=1, source_target_pairs={{0,32},{32,64},{64,96},{96,128},{128,160},{160,192},{192,224},{224... | collective-permute-start | bytes 835592 | tf_op jit(solution)/shard_map/ppermute | solution.py:20
  13.6 9.7 %collective-permute-start.1 = (f32[272,256]{1,0:T(8,128)S(1)}, f32[272,256]{1,0:T(8,128)S(1)}, u32[]{:S(2)}, u32[]{:S(2)}) collective-permute-start(f32[272,256]{1,0:T(8,128)S(1)} %pad_maximum_fusion.1), channel_id=1, source_target_pairs={{0,64},{32,96},{64,128},{96,160},{128,192},{160,224},{192,256},{22... | collective-permute-start | bytes 835592 | tf_op jit(solution)/shard_map/ppermute | solution.py:20
  23.5 39.9 %copy-start.6 = (s32[1,1,32,64]{3,2,1,0:T(8,128)S(1)}, s32[1,1,32,64]{3,2,1,0:T(8,128)}, u32[]{:S(2)}) copy-start(s32[1,1,32,64]{3,2,1,0:T(8,128)} %param.19) | copy-start | bytes 24580
  23.9 58.9 %copy-start.4 = (s32[8]{0:T(128)S(1)}, s32[8]{0:T(128)}, u32[]{:S(2)}) copy-start(s32[8]{0:T(128)} %param.22) | copy-start | bytes 100
  23.9 65.2 %copy-start.5 = (f32[8]{0:T(128)S(1)}, f32[8]{0:T(128)}, u32[]{:S(2)}) copy-start(f32[8]{0:T(128)} %param.23) | copy-start | bytes 100
  23.9 65.8 %copy-start.1 = (s32[1,1,24,1024]{3,2,1,0:T(8,128)S(1)}, s32[1,1,24,1024]{3,2,1,0:T(8,128)}, u32[]{:S(2)}) copy-start(s32[1,1,24,1024]{3,2,1,0:T(8,128)} %param.17) | copy-start | bytes 294916
  24.0 18.4 %collective-permute-start.2 = (f32[272,256]{1,0:T(8,128)S(1)}, f32[272,256]{1,0:T(8,128)S(1)}, u32[]{:S(2)}, u32[]{:S(2)}) collective-permute-start(f32[272,256]{1,0:T(8,128)S(1)} %pad_maximum_fusion.2), channel_id=1, source_target_pairs={{0,128},{32,160},{64,192},{96,224},{128,256},{160,288},{192,320},{... | collective-permute-start | bytes 835592 | tf_op jit(solution)/shard_map/ppermute | solution.py:20
  26.8 63.0 %copy-start.7 = (s32[1,1,32,64]{3,2,1,0:T(8,128)S(1)}, s32[1,1,32,64]{3,2,1,0:T(8,128)}, u32[]{:S(2)}) copy-start(s32[1,1,32,64]{3,2,1,0:T(8,128)} %param.20) | copy-start | bytes 24580
  42.6 9.6 %collective-permute-start.3 = (f32[16,256]{1,0:T(8,128)S(1)}, f32[16,256]{1,0:T(8,128)S(1)}, u32[]{:S(2)}, u32[]{:S(2)}) collective-permute-start(f32[16,256]{1,0:T(8,128)S(1)} %convolution_add_fusion.1), channel_id=1, source_target_pairs={{0,256},{32,288},{64,320},{96,352},{128,384},{160,416},{192,448},{... | collective-permute-start | bytes 49160 | tf_op jit(solution)/shard_map/ppermute | solution.py:20
  52.4 42.3 %copy-start.3 = (f32[16,256]{1,0:T(8,128)}, f32[16,256]{1,0:T(8,128)S(1)}, u32[]{:S(2)}) copy-start(f32[16,256]{1,0:T(8,128)S(1)} %convolution_add_fusion) | copy-start | bytes 49156
  52.4 12.6 %collective-permute-start.4 = (f32[1,16,256]{2,1,0:T(8,128)S(1)}, f32[1,16,256]{2,1,0:T(8,128)S(1)}, u32[]{:S(2)}, u32[]{:S(2)}) collective-permute-start(f32[1,16,256]{2,1,0:T(8,128)S(1)} %bitcast.114), channel_id=1, source_target_pairs={{0,16},{1,17},{2,18},{3,19},{4,20},{5,21},{6,22},{7,23},{8,24},{9,... | collective-permute-start | bytes 49160 | tf_op jit(solution)/shard_map/ppermute | solution.py:143
  65.0 7.3 %collective-permute-start.5 = (f32[2,16,256]{2,1,0:T(8,128)S(1)}, f32[2,16,256]{2,1,0:T(8,128)S(1)}, u32[]{:S(2)}, u32[]{:S(2)}) collective-permute-start(f32[2,16,256]{2,1,0:T(8,128)S(1)} %maximum_select_fusion.4), channel_id=1, source_target_pairs={{0,2},{1,3},{2,0},{3,1},{4,6},{5,7},{6,4},{7,5},{8,10},{9,11},{10,... | collective-permute-start | bytes 98312 | tf_op jit(solution)/shard_map/ppermute | solution.py:143
  72.4 7.1 %collective-permute-start.6 = (f32[4,16,256]{2,1,0:T(8,128)S(1)}, f32[4,16,256]{2,1,0:T(8,128)S(1)}, u32[]{:S(2)}, u32[]{:S(2)}) collective-permute-start(f32[4,16,256]{2,1,0:T(8,128)S(1)} %maximum_select_fusion.3), channel_id=1, source_target_pairs={{0,8},{1,9},{2,10},{3,11},{4,12},{5,13},{6,14},{7,15},{8,0},{9,1},... | collective-permute-start | bytes 196616 | tf_op jit(solution)/shard_map/ppermute | solution.py:143
  79.4 6.9 %collective-permute-start.7 = (f32[8,16,256]{2,1,0:T(8,128)S(1)}, f32[8,16,256]{2,1,0:T(8,128)S(1)}, u32[]{:S(2)}, u32[]{:S(2)}) collective-permute-start(f32[8,16,256]{2,1,0:T(8,128)S(1)} %maximum_select_fusion.2), channel_id=1, source_target_pairs={{0,4},{1,5},{2,6},{3,7},{4,0},{5,1},{6,2},{7,3},{8,12},{9,13},{10,... | collective-permute-start | bytes 393224 | tf_op jit(solution)/shard_map/ppermute | solution.py:143
  86.3 8.3 %collective-permute-start.8 = (f32[16,16,256]{2,1,0:T(8,128)S(1)}, f32[16,16,256]{2,1,0:T(8,128)S(1)}, u32[]{:S(2)}, u32[]{:S(2)}) collective-permute-start(f32[16,16,256]{2,1,0:T(8,128)S(1)} %maximum_select_fusion.1), channel_id=1, source_target_pairs={{0,1},{1,0},{2,3},{3,2},{4,5},{5,4},{6,7},{7,6},{8,9},{9,8},{10,11... | collective-permute-start | bytes 786440 | tf_op jit(solution)/shard_map/ppermute | solution.py:143
  102.6 27.5 %copy-start.9 = (f32[24,24]{1,0:T(8,128)S(1)}, f32[24,24]{1,0:T(8,128)}, u32[]{:S(2)}) copy-start(f32[24,24]{1,0:T(8,128)} %param.15) | copy-start | bytes 6916
  130.1 5.3 %copy-start.10 = (f32[1,1,1024]{2,1,0:T(1,128)S(1)}, f32[1,1,1024]{2,1,0:T(1,128)}, u32[]{:S(2)}) copy-start(f32[1,1,1024]{2,1,0:T(1,128)} %param.18) | copy-start | bytes 12292
  130.1 32.7 %copy-start.2 = (f32[1,1,128,128]{3,2,1,0:T(8,128)S(1)}, f32[1,1,128,128]{3,2,1,0:T(8,128)}, u32[]{:S(2)}) copy-start(f32[1,1,128,128]{3,2,1,0:T(8,128)} %param.21) | copy-start | bytes 196612
  139.3 22.2 %all-to-all-start = ((f32[32,1,64]{2,1,0:T(1,128)}), f32[32,1,64]{2,1,0:T(1,128)S(1)}, u32[]{:S(2)}, u32[]{:S(2)}) async-start(f32[32,1,64]{2,1,0:T(1,128)} %all_to_all.6), calls=%async_computation | async-start | bytes 32768 | tf_op jit(solution)/shard_map/all_to_all | solution.py:186
  164.7 17.0 %collective-permute-start.10 = (f32[3,128]{1,0:T(4,128)S(1)}, f32[3,128]{1,0:T(4,128)S(1)}, u32[]{:S(2)}, u32[]{:S(2)}) collective-permute-start(f32[3,128]{1,0:T(4,128)S(1)} %get-tuple-element.32), channel_id=1, source_target_pairs={{1,0},{2,1},{3,2},{4,3},{5,4},{6,5},{7,6},{8,7},{9,8},{10,9},{11,1... | collective-permute-start | bytes 4616 | tf_op jit(solution)/shard_map/ppermute | solution.py:33
  167.5 14.2 %collective-permute-start.9 = (f32[3,128]{1,0:T(4,128)S(1)}, f32[3,128]{1,0:T(4,128)S(1)}, u32[]{:S(2)}, u32[]{:S(2)}) collective-permute-start(f32[3,128]{1,0:T(4,128)S(1)} %get-tuple-element.31), channel_id=1, source_target_pairs={{0,1},{1,2},{2,3},{3,4},{4,5},{5,6},{6,7},{7,8},{8,9},{9,10},{10,1... | collective-permute-start | bytes 4616 | tf_op jit(solution)/shard_map/ppermute | solution.py:31

commit v4 on v3

--- a/solution.py
+++ b/solution.py
@@ -143,11 +143,14 @@
         other = lax.ppermute(block, "dev", partner)
         high = ((me >> bit) & 1) == 1
         block = jnp.where(high, jnp.concatenate([other, block], 0), jnp.concatenate([block, other], 0))
-    slab = jnp.arange(count, dtype=jnp.int32)
+    return block, order
+
+
+def slab_position(slab, order):
     position = jnp.zeros_like(slab)
     for place, bit in enumerate(order):
         position = position + (((slab >> bit) & 1) << place)
-    return block, position
+    return position
 
 
 def on_device(
@@ -169,10 +172,10 @@
     rights = loads[0, 0]
     solved = interface_chain(inverse, couple, rights)
 
-    panels, position = gathered_panels(solved)
+    panels, bit_order = gathered_panels(solved)
     slabs, order, panel_order = panels.shape
     table = jnp.transpose(panels, (0, 2, 1)).reshape(slabs * panel_order, order)
-    slab_place = jnp.take(position, element_substructure[0, 0], axis=0)
+    slab_place = slab_position(element_substructure[0, 0], bit_order)
     lookup = slab_place[None, :] * panel_order + element_rows[0, 0]
     dofs, elements = lookup.shape
     pack = 128 // order
@@ -190,17 +193,19 @@
     weighted = owned * collected
     padded = padded_2(weighted, (("dev", 0),), RADIUS)
     total_rows = lax.axis_size("dev") * row_count
-    global_rows = lax.axis_index("dev") * row_count + jnp.arange(row_count, dtype=jnp.int32)
-    accum = jnp.zeros((row_count, 128), jnp.float32)
-    weight_sum = jnp.zeros((row_count,), jnp.float32)
-    for which in range(NK):
-        offset = filter_offsets[which]
-        window_rows = lax.dynamic_slice_in_dim(padded, RADIUS + offset, row_count, 0)
-        inside = ((global_rows + offset >= 0) & (global_rows + offset < total_rows)).astype(
-            jnp.float32
-        )
-        accum = accum + filter_weights[which] * window_rows
-        weight_sum = weight_sum + filter_weights[which] * inside
+    padded_rows = padded.shape[0]
+    reach = (
+        lax.broadcasted_iota(jnp.int32, (1, row_count, padded_rows), 2)
+        - lax.broadcasted_iota(jnp.int32, (1, row_count, padded_rows), 1)
+        - RADIUS
+    )
+    band = jnp.sum(
+        jnp.where(reach == filter_offsets[:, None, None], filter_weights[:, None, None], 0.0), axis=0
+    )
+    padded_global = lax.axis_index("dev") * row_count - RADIUS + jnp.arange(padded_rows, dtype=jnp.int32)
+    valid = ((padded_global >= 0) & (padded_global < total_rows)).astype(jnp.float32)
+    weight_sum = jnp.sum(band * valid[None, :], axis=1)
+    accum = product(band, padded)
     filtered = accum / (owned * weight_sum[:, None])
     return (solved[None, None], filtered[None, None])
 

time: 189 us -> 173 us (0.915)
  the two profiles are of different devices: /device:TPU:38 before, /device:TPU:96 now
where the time goes in v4:
time: 173 us; the launch traced here: 172 us
  waiting for transfers between devices  66.4 us (38%)
  starting transfers between devices  49.3 us (28%)
  Pallas kernels  27.5 us (16%)
  matrix products  12.2 us (7%)
  local copies, waits for them, and re-layouts  10.8 us (6%)
  other arithmetic  5.1 us (3%)
    ppermute x4, waiting for transfers between devices, passed_along(): lax.ppermute(value, axis, [(source, source + steps) for source in range(l...  37.6 us
    pallas_call x1, Pallas kernels, gathered_rows(): pl.pallas_call(gather_kernel, out_shape=jax.ShapeDtypeStruct((out_rows, 1...  27.5 us
    ppermute x5, starting transfers between devices, gathered_panels(): other = lax.ppermute(block, 'dev', partner)  25.1 us
    ppermute x5, waiting for transfers between devices, gathered_panels(): other = lax.ppermute(block, 'dev', partner)  14.8 us
    all_to_all x1, starting transfers between devices, on_device(): lax.all_to_all(outgoing, 'dev', split_axis=0, concat_axis=0, tiled=True)  11.1 us
    all_to_all x1, waiting for transfers between devices, on_device(): lax.all_to_all(outgoing, 'dev', split_axis=0, concat_axis=0, tiled=True)  8.47 us
    another operation x3, local copies, waits for them, and re-layouts, gathered_rows(): wide = jnp.tile(table, (1, pack))  8 us
    ppermute x4, starting transfers between devices, passed_along(): lax.ppermute(value, axis, [(source, source + steps) for source in range(l...  7.2 us
  transfers between devices with their start and end apart: 12, of which 11 were waited for; matrix products, arithmetic and copies ran while one was open for 1% of the time, Pallas kernels for 0%

profile of v4, /device:TPU:96, one launch (start us, length us, event | category | flops | bytes accessed | tf_op | source)
XLA Modules:
  0.0 172.4 jit_solution(11226614151605619517)
XLA Ops:
  0.6 0.9 copy-done
  1.6 1.3 convolution_negate_fusion
  2.9 0.9 fusion.17
  3.9 1.9 %collective-permute-start = (f32[272,256]{1,0:T(8,128)S(1)}, f32[272,256]{1,0:T(8,128)S(1)}, u32[]{:S(2)}, u32[]{:S(2)}) collective-permute-start(f32[272,256]{1,0:T(8,128)S(1)} %pad_maximum_fusion), channel_id=1, source_target_pairs={{0,32},{32,64},{64,96},{96,128},{128,160},{160,192},{192,224},{224... | collective-permute-start | bytes 835592 | tf_op jit(solution)/shard_map/ppermute | solution.py:20
  5.8 7.1 %collective-permute-done = f32[272,256]{1,0:T(8,128)S(1)} collective-permute-done((f32[272,256]{1,0:T(8,128)S(1)}, f32[272,256]{1,0:T(8,128)S(1)}, u32[]{:S(2)}, u32[]{:S(2)}) %collective-permute-start) | collective-permute-done | bytes 278560 | tf_op jit(solution)/shard_map/ppermute | solution.py:20
  13.0 0.4 fusion.13
  13.4 0.2 convolution_add_fusion.3
  13.6 1.9 %collective-permute-start.1 = (f32[272,256]{1,0:T(8,128)S(1)}, f32[272,256]{1,0:T(8,128)S(1)}, u32[]{:S(2)}, u32[]{:S(2)}) collective-permute-start(f32[272,256]{1,0:T(8,128)S(1)} %pad_maximum_fusion.1), channel_id=1, source_target_pairs={{0,64},{32,96},{64,128},{96,160},{128,192},{160,224},{192,256},{22... | collective-permute-start | bytes 835592 | tf_op jit(solution)/shard_map/ppermute | solution.py:20
  15.6 7.7 %collective-permute-done.1 = f32[272,256]{1,0:T(8,128)S(1)} collective-permute-done((f32[272,256]{1,0:T(8,128)S(1)}, f32[272,256]{1,0:T(8,128)S(1)}, u32[]{:S(2)}, u32[]{:S(2)}) %collective-permute-start.1) | collective-permute-done | bytes 278560 | tf_op jit(solution)/shard_map/ppermute | solution.py:20
  23.3 0.2 convolution_add_fusion.2
  23.5 0.4 fusion.11
  24.0 2.1 %collective-permute-start.2 = (f32[272,256]{1,0:T(8,128)S(1)}, f32[272,256]{1,0:T(8,128)S(1)}, u32[]{:S(2)}, u32[]{:S(2)}) collective-permute-start(f32[272,256]{1,0:T(8,128)S(1)} %pad_maximum_fusion.2), channel_id=1, source_target_pairs={{0,128},{32,160},{64,192},{96,224},{128,256},{160,288},{192,320},{... | collective-permute-start | bytes 835592 | tf_op jit(solution)/shard_map/ppermute | solution.py:20
  26.1 14.8 %collective-permute-done.2 = f32[272,256]{1,0:T(8,128)S(1)} collective-permute-done((f32[272,256]{1,0:T(8,128)S(1)}, f32[272,256]{1,0:T(8,128)S(1)}, u32[]{:S(2)}, u32[]{:S(2)}) %collective-permute-start.2) | collective-permute-done | bytes 278560 | tf_op jit(solution)/shard_map/ppermute | solution.py:20
  40.9 0.2 convolution_add_fusion.1
  41.1 1.3 collective-permute-start.3
  42.5 0.4 fusion.9
  42.8 7.9 %collective-permute-done.3 = f32[16,256]{1,0:T(8,128)S(1)} collective-permute-done((f32[16,256]{1,0:T(8,128)S(1)}, f32[16,256]{1,0:T(8,128)S(1)}, u32[]{:S(2)}, u32[]{:S(2)}) %collective-permute-start.3) | collective-permute-done | bytes 16416 | tf_op jit(solution)/shard_map/ppermute | solution.py:20
  50.7 0.2 convolution_add_fusion
  50.9 10.0 %collective-permute-start.4 = (f32[1,16,256]{2,1,0:T(8,128)S(1)}, f32[1,16,256]{2,1,0:T(8,128)S(1)}, u32[]{:S(2)}, u32[]{:S(2)}) collective-permute-start(f32[1,16,256]{2,1,0:T(8,128)S(1)} %bitcast.61), channel_id=1, source_target_pairs={{0,16},{1,17},{2,18},{3,19},{4,20},{5,21},{6,22},{7,23},{8,24},{9,... | collective-permute-start | bytes 49160 | tf_op jit(solution)/shard_map/ppermute | solution.py:143
  61.1 1.6 collective-permute-done.4
  62.7 4.9 %collective-permute-start.5 = (f32[2,16,256]{2,1,0:T(8,128)S(1)}, f32[2,16,256]{2,1,0:T(8,128)S(1)}, u32[]{:S(2)}, u32[]{:S(2)}) collective-permute-start(f32[2,16,256]{2,1,0:T(8,128)S(1)} %maximum_select_fusion.4), channel_id=1, source_target_pairs={{0,2},{1,3},{2,0},{3,1},{4,6},{5,7},{6,4},{7,5},{8,10},{9,11},{10,... | collective-permute-start | bytes 98312 | tf_op jit(solution)/shard_map/ppermute | solution.py:143
  67.6 2.3 %collective-permute-done.5 = f32[2,16,256]{2,1,0:T(8,128)S(1)} collective-permute-done((f32[2,16,256]{2,1,0:T(8,128)S(1)}, f32[2,16,256]{2,1,0:T(8,128)S(1)}, u32[]{:S(2)}, u32[]{:S(2)}) %collective-permute-start.5) | collective-permute-done | bytes 32800 | tf_op jit(solution)/shard_map/ppermute | solution.py:143
  70.0 4.3 %collective-permute-start.6 = (f32[4,16,256]{2,1,0:T(8,128)S(1)}, f32[4,16,256]{2,1,0:T(8,128)S(1)}, u32[]{:S(2)}, u32[]{:S(2)}) collective-permute-start(f32[4,16,256]{2,1,0:T(8,128)S(1)} %maximum_select_fusion.3), channel_id=1, source_target_pairs={{0,8},{1,9},{2,10},{3,11},{4,12},{5,13},{6,14},{7,15},{8,0},{9,1},... | collective-permute-start | bytes 196616 | tf_op jit(solution)/shard_map/ppermute | solution.py:143
  74.3 2.7 %collective-permute-done.6 = f32[4,16,256]{2,1,0:T(8,128)S(1)} collective-permute-done((f32[4,16,256]{2,1,0:T(8,128)S(1)}, f32[4,16,256]{2,1,0:T(8,128)S(1)}, u32[]{:S(2)}, u32[]{:S(2)}) %collective-permute-start.6) | collective-permute-done | bytes 65568 | tf_op jit(solution)/shard_map/ppermute | solution.py:143
  77.1 2.5 %collective-permute-start.7 = (f32[8,16,256]{2,1,0:T(8,128)S(1)}, f32[8,16,256]{2,1,0:T(8,128)S(1)}, u32[]{:S(2)}, u32[]{:S(2)}) collective-permute-start(f32[8,16,256]{2,1,0:T(8,128)S(1)} %maximum_select_fusion.2), channel_id=1, source_target_pairs={{0,4},{1,5},{2,6},{3,7},{4,0},{5,1},{6,2},{7,3},{8,12},{9,13},{10,... | collective-permute-start | bytes 393224 | tf_op jit(solution)/shard_map/ppermute | solution.py:143
  79.6 4.3 %collective-permute-done.7 = f32[8,16,256]{2,1,0:T(8,128)S(1)} collective-permute-done((f32[8,16,256]{2,1,0:T(8,128)S(1)}, f32[8,16,256]{2,1,0:T(8,128)S(1)}, u32[]{:S(2)}, u32[]{:S(2)}) %collective-permute-start.7) | collective-permute-done | bytes 131104 | tf_op jit(solution)/shard_map/ppermute | solution.py:143
  83.9 3.4 %collective-permute-start.8 = (f32[16,16,256]{2,1,0:T(8,128)S(1)}, f32[16,16,256]{2,1,0:T(8,128)S(1)}, u32[]{:S(2)}, u32[]{:S(2)}) collective-permute-start(f32[16,16,256]{2,1,0:T(8,128)S(1)} %maximum_select_fusion.1), channel_id=1, source_target_pairs={{0,1},{1,0},{2,3},{3,2},{4,5},{5,4},{6,7},{7,6},{8,9},{9,8},{10,11... | collective-permute-start | bytes 786440 | tf_op jit(solution)/shard_map/ppermute | solution.py:143
  87.4 0.2 select_reduce_fusion.1
  87.8 0.6 add.154.lookup_ref
  88.4 3.8 %collective-permute-done.8 = f32[16,16,256]{2,1,0:T(8,128)S(1)} collective-permute-done((f32[16,16,256]{2,1,0:T(8,128)S(1)}, f32[16,16,256]{2,1,0:T(8,128)S(1)}, u32[]{:S(2)}, u32[]{:S(2)}) %collective-permute-start.8) | collective-permute-done | bytes 262176 | tf_op jit(solution)/shard_map/ppermute | solution.py:143
  92.3 2.4 %tile.11 = f32[8192,8,16]{0,2,1:T(8,128)} broadcast(f32[8192,16]{0,1:T(8,128)S(1)} %bitcast.57), dimensions={0,2} | broadcast | bytes 4718592 | tf_op jit(solution)/shard_map/tile | solution.py:117
  94.7 5.6 %copy.27.table_ref = f32[8192,128]{1,0:T(8,128)} copy(f32[8192,128]{0,1:T(8,128)} %bitcast.55) | data formatting | bytes 8388608 | tf_op jit(solution)/shard_map/tile | solution.py:117
  100.3 27.5 %shard_map.131 = f32[3072,128]{1,0:T(8,128)} custom-call(s32[24576]{0:T(1024)} %add.154.lookup_ref, f32[8192,128]{1,0:T(8,128)} %copy.27.table_ref), custom_call_target="tpu_custom_call" | custom-call | bytes 5767168 | tf_op jit(solution)/shard_map/pallas_call | solution.py:122
  127.8 5.0 %fusion = f32[128,128]{1,0:T(8,128)S(1)} fusion(f32[24,128,128]{2,1,0:T(8,128)} %bitcast.56, f32[24,24]{1,0:T(8,128)S(1)} %copy-done.5), kind=kOutput, calls=%fused_computation.1 | convolution fusion | flops 114016256 | bytes 1640704 | tf_op jit(solution)/shard_map/ij,jab->iab/dot_general | solution.py:183
  132.9 0.1 copy.31
  133.0 0.1 reshape.308
  133.1 3.1 %select_reduce_fusion = f32[2048]{0:T(1024)S(1)} fusion(f32[128]{0:T(128)S(1)} %get-tuple-element.16, f32[128]{0:T(128)S(1)} %get-tuple-element.17, f32[128]{0:T(128)S(1)} %get-tuple-element.18, f32[128]{0:T(128)S(1)} %get-tuple-element.19, f32[128]{0:T(128)S(1)} %get-tuple-element.20, f32[128]{0:T(128)S(1)} %get-tuple-element.21, ...), kind=kLoop, calls=%fused_computation.12 | loop fusion | flops 4716544 | bytes 36864 | tf_op jit(solution)/shard_map/reduce_sum | solution.py:73
  136.3 0.7 all_to_all.6
  137.0 11.1 %all-to-all-start = ((f32[32,1,64]{2,1,0:T(1,128)}), f32[32,1,64]{2,1,0:T(1,128)S(1)}, u32[]{:S(2)}, u32[]{:S(2)}) async-start(f32[32,1,64]{2,1,0:T(1,128)} %all_to_all.6), calls=%async_computation | async-start | bytes 32768 | tf_op jit(solution)/shard_map/all_to_all | solution.py:189
  148.1 8.5 %all-to-all-done = f32[32,1,64]{2,1,0:T(1,128)S(1)} async-done(((f32[32,1,64]{2,1,0:T(1,128)}), f32[32,1,64]{2,1,0:T(1,128)S(1)}, u32[]{:S(2)}, u32[]{:S(2)}) %all-to-all-start) | async-done | bytes 8224 | tf_op jit(solution)/shard_map/all_to_all | solution.py:189
  156.6 0.5 broadcast.450
  157.1 0.7 reduce.3
  157.8 1.9 %convolution_multiply_fusion = f32[128,128]{1,0:T(8,128)S(1)} fusion(f32[2048]{0:T(1024)S(1)} %broadcast_in_dim.171, s32[2048]{0:T(1024)S(1)} %get-tuple-element.7, s32[2048]{0:T(1024)S(1)} %get-tuple-element.6, f32[1,1,128,128]{3,2,1,0:T(8,128)S(1)} %copy-done.10), kind=kOutput, calls=%fused_computation.6 | convolution fusion | flops 403456000 | bytes 155648 | tf_op jit(solution)/shard_map/dot_general | solution.py:87
  159.7 4.0 %collective-permute-start.10 = (f32[3,128]{1,0:T(4,128)S(1)}, f32[3,128]{1,0:T(4,128)S(1)}, u32[]{:S(2)}, u32[]{:S(2)}) collective-permute-start(f32[3,128]{1,0:T(4,128)S(1)} %get-tuple-element.5), channel_id=1, source_target_pairs={{1,0},{2,1},{3,2},{4,3},{5,4},{6,5},{7,6},{8,7},{9,8},{10,9},{11,1... | collective-permute-start | bytes 4616 | tf_op jit(solution)/shard_map/ppermute | solution.py:33
  163.7 1.9 %collective-permute-start.9 = (f32[3,128]{1,0:T(4,128)S(1)}, f32[3,128]{1,0:T(4,128)S(1)}, u32[]{:S(2)}, u32[]{:S(2)}) collective-permute-start(f32[3,128]{1,0:T(4,128)S(1)} %get-tuple-element.4), channel_id=1, source_target_pairs={{0,1},{1,2},{2,3},{3,4},{4,5},{5,6},{6,7},{7,8},{8,9},{9,10},{10,1... | collective-permute-start | bytes 4616 | tf_op jit(solution)/shard_map/ppermute | solution.py:31
  165.7 0.1 multiply_reduce_fusion
  165.8 5.6 %collective-permute-done.9 = f32[3,128]{1,0:T(4,128)S(1)} collective-permute-done((f32[3,128]{1,0:T(4,128)S(1)}, f32[3,128]{1,0:T(4,128)S(1)}, u32[]{:S(2)}, u32[]{:S(2)}) %collective-permute-start.9) | collective-permute-done | bytes 1568 | tf_op jit(solution)/shard_map/ppermute | solution.py:31
  171.3 1.0 fusion.2
  (49 shorter events, 0.8 us)
Async XLA Ops:
  0.6 1.0 copy-start
  3.9 22.1 %copy-start.7 = (s32[1,1,1024]{2,1,0:T(1,128)S(1)}, s32[1,1,1024]{2,1,0:T(1,128)}, u32[]{:S(2)}) copy-start(s32[1,1,1024]{2,1,0:T(1,128)} %param.16) | copy-start | bytes 12292
  3.9 9.1 %collective-permute-start = (f32[272,256]{1,0:T(8,128)S(1)}, f32[272,256]{1,0:T(8,128)S(1)}, u32[]{:S(2)}, u32[]{:S(2)}) collective-permute-start(f32[272,256]{1,0:T(8,128)S(1)} %pad_maximum_fusion), channel_id=1, source_target_pairs={{0,32},{32,64},{64,96},{96,128},{128,160},{160,192},{192,224},{224... | collective-permute-start | bytes 835592 | tf_op jit(solution)/shard_map/ppermute | solution.py:20
  13.6 47.3 %copy-start.3 = (s32[1,1,32,64]{3,2,1,0:T(8,128)S(1)}, s32[1,1,32,64]{3,2,1,0:T(8,128)}, u32[]{:S(2)}) copy-start(s32[1,1,32,64]{3,2,1,0:T(8,128)} %param.19) | copy-start | bytes 24580
  13.6 9.7 %collective-permute-start.1 = (f32[272,256]{1,0:T(8,128)S(1)}, f32[272,256]{1,0:T(8,128)S(1)}, u32[]{:S(2)}, u32[]{:S(2)}) collective-permute-start(f32[272,256]{1,0:T(8,128)S(1)} %pad_maximum_fusion.1), channel_id=1, source_target_pairs={{0,64},{32,96},{64,128},{96,160},{128,192},{160,224},{192,256},{22... | collective-permute-start | bytes 835592 | tf_op jit(solution)/shard_map/ppermute | solution.py:20
  23.9 63.4 %copy-start.8 = (f32[8]{0:T(128)S(1)}, f32[8]{0:T(128)}, u32[]{:S(2)}) copy-start(f32[8]{0:T(128)} %param.23) | copy-start | bytes 100
  23.9 63.4 %copy-start.9 = (s32[8]{0:T(128)S(1)}, s32[8]{0:T(128)}, u32[]{:S(2)}) copy-start(s32[8]{0:T(128)} %param.22) | copy-start | bytes 100
  24.0 63.7 %copy-start.1 = (s32[1,1,24,1024]{3,2,1,0:T(8,128)S(1)}, s32[1,1,24,1024]{3,2,1,0:T(8,128)}, u32[]{:S(2)}) copy-start(s32[1,1,24,1024]{3,2,1,0:T(8,128)} %param.17) | copy-start | bytes 294916
  24.0 17.0 %collective-permute-start.2 = (f32[272,256]{1,0:T(8,128)S(1)}, f32[272,256]{1,0:T(8,128)S(1)}, u32[]{:S(2)}, u32[]{:S(2)}) collective-permute-start(f32[272,256]{1,0:T(8,128)S(1)} %pad_maximum_fusion.2), channel_id=1, source_target_pairs={{0,128},{32,160},{64,192},{96,224},{128,256},{160,288},{192,320},{... | collective-permute-start | bytes 835592 | tf_op jit(solution)/shard_map/ppermute | solution.py:20
  26.1 61.6 %copy-start.4 = (s32[1,1,32,64]{3,2,1,0:T(8,128)S(1)}, s32[1,1,32,64]{3,2,1,0:T(8,128)}, u32[]{:S(2)}) copy-start(s32[1,1,32,64]{3,2,1,0:T(8,128)} %param.20) | copy-start | bytes 24580
  41.1 9.6 %collective-permute-start.3 = (f32[16,256]{1,0:T(8,128)S(1)}, f32[16,256]{1,0:T(8,128)S(1)}, u32[]{:S(2)}, u32[]{:S(2)}) collective-permute-start(f32[16,256]{1,0:T(8,128)S(1)} %convolution_add_fusion.1), channel_id=1, source_target_pairs={{0,256},{32,288},{64,320},{96,352},{128,384},{160,416},{192,448},{... | collective-permute-start | bytes 49160 | tf_op jit(solution)/shard_map/ppermute | solution.py:20
  50.9 41.4 %copy-start.2 = (f32[16,256]{1,0:T(8,128)}, f32[16,256]{1,0:T(8,128)S(1)}, u32[]{:S(2)}) copy-start(f32[16,256]{1,0:T(8,128)S(1)} %convolution_add_fusion) | copy-start | bytes 49156
  50.9 11.7 %collective-permute-start.4 = (f32[1,16,256]{2,1,0:T(8,128)S(1)}, f32[1,16,256]{2,1,0:T(8,128)S(1)}, u32[]{:S(2)}, u32[]{:S(2)}) collective-permute-start(f32[1,16,256]{2,1,0:T(8,128)S(1)} %bitcast.61), channel_id=1, source_target_pairs={{0,16},{1,17},{2,18},{3,19},{4,20},{5,21},{6,22},{7,23},{8,24},{9,... | collective-permute-start | bytes 49160 | tf_op jit(solution)/shard_map/ppermute | solution.py:143
  62.7 7.3 %collective-permute-start.5 = (f32[2,16,256]{2,1,0:T(8,128)S(1)}, f32[2,16,256]{2,1,0:T(8,128)S(1)}, u32[]{:S(2)}, u32[]{:S(2)}) collective-permute-start(f32[2,16,256]{2,1,0:T(8,128)S(1)} %maximum_select_fusion.4), channel_id=1, source_target_pairs={{0,2},{1,3},{2,0},{3,1},{4,6},{5,7},{6,4},{7,5},{8,10},{9,11},{10,... | collective-permute-start | bytes 98312 | tf_op jit(solution)/shard_map/ppermute | solution.py:143
  70.0 7.1 %collective-permute-start.6 = (f32[4,16,256]{2,1,0:T(8,128)S(1)}, f32[4,16,256]{2,1,0:T(8,128)S(1)}, u32[]{:S(2)}, u32[]{:S(2)}) collective-permute-start(f32[4,16,256]{2,1,0:T(8,128)S(1)} %maximum_select_fusion.3), channel_id=1, source_target_pairs={{0,8},{1,9},{2,10},{3,11},{4,12},{5,13},{6,14},{7,15},{8,0},{9,1},... | collective-permute-start | bytes 196616 | tf_op jit(solution)/shard_map/ppermute | solution.py:143
  77.1 6.9 %collective-permute-start.7 = (f32[8,16,256]{2,1,0:T(8,128)S(1)}, f32[8,16,256]{2,1,0:T(8,128)S(1)}, u32[]{:S(2)}, u32[]{:S(2)}) collective-permute-start(f32[8,16,256]{2,1,0:T(8,128)S(1)} %maximum_select_fusion.2), channel_id=1, source_target_pairs={{0,4},{1,5},{2,6},{3,7},{4,0},{5,1},{6,2},{7,3},{8,12},{9,13},{10,... | collective-permute-start | bytes 393224 | tf_op jit(solution)/shard_map/ppermute | solution.py:143
  83.9 8.3 %collective-permute-start.8 = (f32[16,16,256]{2,1,0:T(8,128)S(1)}, f32[16,16,256]{2,1,0:T(8,128)S(1)}, u32[]{:S(2)}, u32[]{:S(2)}) collective-permute-start(f32[16,16,256]{2,1,0:T(8,128)S(1)} %maximum_select_fusion.1), channel_id=1, source_target_pairs={{0,1},{1,0},{2,3},{3,2},{4,5},{5,4},{6,7},{7,6},{8,9},{9,8},{10,11... | collective-permute-start | bytes 786440 | tf_op jit(solution)/shard_map/ppermute | solution.py:143
  100.3 27.5 %copy-start.5 = (f32[24,24]{1,0:T(8,128)S(1)}, f32[24,24]{1,0:T(8,128)}, u32[]{:S(2)}) copy-start(f32[24,24]{1,0:T(8,128)} %param.15) | copy-start | bytes 6916
  127.7 5.3 %copy-start.6 = (f32[1,1,1024]{2,1,0:T(1,128)S(1)}, f32[1,1,1024]{2,1,0:T(1,128)}, u32[]{:S(2)}) copy-start(f32[1,1,1024]{2,1,0:T(1,128)} %param.18) | copy-start | bytes 12292
  127.8 30.1 %copy-start.10 = (f32[1,1,128,128]{3,2,1,0:T(8,128)S(1)}, f32[1,1,128,128]{3,2,1,0:T(8,128)}, u32[]{:S(2)}) copy-start(f32[1,1,128,128]{3,2,1,0:T(8,128)} %param.21) | copy-start | bytes 196612
  137.0 19.6 %all-to-all-start = ((f32[32,1,64]{2,1,0:T(1,128)}), f32[32,1,64]{2,1,0:T(1,128)S(1)}, u32[]{:S(2)}, u32[]{:S(2)}) async-start(f32[32,1,64]{2,1,0:T(1,128)} %all_to_all.6), calls=%async_computation | async-start | bytes 32768 | tf_op jit(solution)/shard_map/all_to_all | solution.py:189
  159.7 6.0 %collective-permute-start.10 = (f32[3,128]{1,0:T(4,128)S(1)}, f32[3,128]{1,0:T(4,128)S(1)}, u32[]{:S(2)}, u32[]{:S(2)}) collective-permute-start(f32[3,128]{1,0:T(4,128)S(1)} %get-tuple-element.5), channel_id=1, source_target_pairs={{1,0},{2,1},{3,2},{4,3},{5,4},{6,5},{7,6},{8,7},{9,8},{10,9},{11,1... | collective-permute-start | bytes 4616 | tf_op jit(solution)/shard_map/ppermute | solution.py:33
  163.7 7.6 %collective-permute-start.9 = (f32[3,128]{1,0:T(4,128)S(1)}, f32[3,128]{1,0:T(4,128)S(1)}, u32[]{:S(2)}, u32[]{:S(2)}) collective-permute-start(f32[3,128]{1,0:T(4,128)S(1)} %get-tuple-element.4), channel_id=1, source_target_pairs={{0,1},{1,2},{2,3},{3,4},{4,5},{5,6},{6,7},{7,8},{8,9},{9,10},{10,1... | collective-permute-start | bytes 4616 | tf_op jit(solution)/shard_map/ppermute | solution.py:31

commit v5 on v4

--- a/solution.py
+++ b/solution.py
@@ -172,10 +172,11 @@
     rights = loads[0, 0]
     solved = interface_chain(inverse, couple, rights)
 
-    panels, bit_order = gathered_panels(solved)
+    copies = jnp.broadcast_to(solved[None], (lax.axis_size("dev"),) + solved.shape)
+    panels = lax.all_to_all(copies, "dev", split_axis=0, concat_axis=0, tiled=True)
     slabs, order, panel_order = panels.shape
     table = jnp.transpose(panels, (0, 2, 1)).reshape(slabs * panel_order, order)
-    slab_place = slab_position(element_substructure[0, 0], bit_order)
+    slab_place = element_substructure[0, 0]
     lookup = slab_place[None, :] * panel_order + element_rows[0, 0]
     dofs, elements = lookup.shape
     pack = 128 // order

time: 173 us -> 154 us (0.89)
  the two profiles are of different devices: /device:TPU:96 before, /device:TPU:46 now
where the time goes in v5:
time: 154 us; the launch traced here: 153 us
  waiting for transfers between devices  62.7 us (41%)
  starting transfers between devices  32.8 us (21%)
  Pallas kernels  27.5 us (18%)
  matrix products  12.1 us (8%)
  local copies, waits for them, and re-layouts  11.6 us (8%)
  other arithmetic  4.99 us (3%)
    ppermute x4, waiting for transfers between devices, passed_along(): lax.ppermute(value, axis, [(source, source + steps) for source in range(l...  33.7 us
    pallas_call x1, Pallas kernels, gathered_rows(): pl.pallas_call(gather_kernel, out_shape=jax.ShapeDtypeStruct((out_rows, 1...  27.5 us
    all_to_all x1, waiting for transfers between devices, on_device(): lax.all_to_all(copies, 'dev', split_axis=0, concat_axis=0, tiled=True)  15.5 us
    all_to_all x1, starting transfers between devices, on_device(): lax.all_to_all(copies, 'dev', split_axis=0, concat_axis=0, tiled=True)  13.4 us
    another operation x3, local copies, waits for them, and re-layouts, gathered_rows(): wide = jnp.tile(table, (1, pack))  7.99 us
    ppermute x4, starting transfers between devices, passed_along(): lax.ppermute(value, axis, [(source, source + steps) for source in range(l...  7.97 us
    all_to_all x1, waiting for transfers between devices, on_device(): lax.all_to_all(outgoing, 'dev', split_axis=0, concat_axis=0, tiled=True)  7.87 us
    all_to_all x1, starting transfers between devices, on_device(): lax.all_to_all(outgoing, 'dev', split_axis=0, concat_axis=0, tiled=True)  5.57 us
  transfers between devices with their start and end apart: 8, of which 7 were waited for; matrix products, arithmetic and copies ran while one was open for 1% of the time, Pallas kernels for 0%

profile of v5, /device:TPU:46, one launch (start us, length us, event | category | flops | bytes accessed | tf_op | source)
XLA Modules:
  0.0 152.8 jit_solution(13742037763394631523)
XLA Ops:
  0.6 0.0 copy-start
  0.7 0.9 copy-done
  1.6 1.3 convolution_negate_fusion
  2.9 0.9 fusion.16
  3.9 1.9 %collective-permute-start = (f32[272,256]{1,0:T(8,128)S(1)}, f32[272,256]{1,0:T(8,128)S(1)}, u32[]{:S(2)}, u32[]{:S(2)}) collective-permute-start(f32[272,256]{1,0:T(8,128)S(1)} %pad_maximum_fusion), channel_id=1, source_target_pairs={{0,32},{32,64},{64,96},{96,128},{128,160},{160,192},{192,224},{224... | collective-permute-start | bytes 835592 | tf_op jit(solution)/shard_map/ppermute | solution.py:20
  5.8 5.9 %collective-permute-done = f32[272,256]{1,0:T(8,128)S(1)} collective-permute-done((f32[272,256]{1,0:T(8,128)S(1)}, f32[272,256]{1,0:T(8,128)S(1)}, u32[]{:S(2)}, u32[]{:S(2)}) %collective-permute-start) | collective-permute-done | bytes 278560 | tf_op jit(solution)/shard_map/ppermute | solution.py:20
  11.8 0.4 fusion.12
  12.1 0.0 copy-start.1
  12.2 0.2 convolution_add_fusion.3
  12.4 2.6 %collective-permute-start.1 = (f32[272,256]{1,0:T(8,128)S(1)}, f32[272,256]{1,0:T(8,128)S(1)}, u32[]{:S(2)}, u32[]{:S(2)}) collective-permute-start(f32[272,256]{1,0:T(8,128)S(1)} %pad_maximum_fusion.1), channel_id=1, source_target_pairs={{0,64},{32,96},{64,128},{96,160},{128,192},{160,224},{192,256},{22... | collective-permute-start | bytes 835592 | tf_op jit(solution)/shard_map/ppermute | solution.py:20
  15.1 6.4 %collective-permute-done.1 = f32[272,256]{1,0:T(8,128)S(1)} collective-permute-done((f32[272,256]{1,0:T(8,128)S(1)}, f32[272,256]{1,0:T(8,128)S(1)}, u32[]{:S(2)}, u32[]{:S(2)}) %collective-permute-start.1) | collective-permute-done | bytes 278560 | tf_op jit(solution)/shard_map/ppermute | solution.py:20
  21.4 0.2 convolution_add_fusion.2
  21.6 0.4 fusion.10
  22.1 2.2 %collective-permute-start.2 = (f32[272,256]{1,0:T(8,128)S(1)}, f32[272,256]{1,0:T(8,128)S(1)}, u32[]{:S(2)}, u32[]{:S(2)}) collective-permute-start(f32[272,256]{1,0:T(8,128)S(1)} %pad_maximum_fusion.2), channel_id=1, source_target_pairs={{0,128},{32,160},{64,192},{96,224},{128,256},{160,288},{192,320},{... | collective-permute-start | bytes 835592 | tf_op jit(solution)/shard_map/ppermute | solution.py:20
  24.3 0.1 reshape_squeeze.7
  24.4 0.1 reshape_squeeze.6
  24.5 0.6 add.118.lookup_ref
  25.1 13.6 %collective-permute-done.2 = f32[272,256]{1,0:T(8,128)S(1)} collective-permute-done((f32[272,256]{1,0:T(8,128)S(1)}, f32[272,256]{1,0:T(8,128)S(1)}, u32[]{:S(2)}, u32[]{:S(2)}) %collective-permute-start.2) | collective-permute-done | bytes 278560 | tf_op jit(solution)/shard_map/ppermute | solution.py:20
  38.7 0.2 convolution_add_fusion.1
  38.9 1.3 collective-permute-start.3
  40.2 0.4 fusion.8
  40.6 7.9 %collective-permute-done.3 = f32[16,256]{1,0:T(8,128)S(1)} collective-permute-done((f32[16,256]{1,0:T(8,128)S(1)}, f32[16,256]{1,0:T(8,128)S(1)}, u32[]{:S(2)}, u32[]{:S(2)}) %collective-permute-start.3) | collective-permute-done | bytes 16416 | tf_op jit(solution)/shard_map/ppermute | solution.py:20
  48.5 0.2 convolution_add_fusion
  48.7 0.0 copy-start.2
  48.7 0.9 broadcast_in_dim.156
  49.6 13.4 %all-to-all-start = ((f32[32,16,256]{2,1,0:T(8,128)}), f32[32,16,256]{2,1,0:T(8,128)S(1)}, u32[]{:S(2)}, u32[]{:S(2)}) async-start(f32[32,16,256]{2,1,0:T(8,128)} %broadcast_in_dim.156), calls=%async_computation | async-start | bytes 1048576 | tf_op jit(solution)/shard_map/all_to_all | solution.py:176
  63.0 0.2 select_reduce_fusion.1
  63.3 15.5 %all-to-all-done = f32[32,16,256]{2,1,0:T(8,128)S(1)} async-done(((f32[32,16,256]{2,1,0:T(8,128)}), f32[32,16,256]{2,1,0:T(8,128)S(1)}, u32[]{:S(2)}, u32[]{:S(2)}) %all-to-all-start) | async-done | bytes 524320 | tf_op jit(solution)/shard_map/all_to_all | solution.py:176
  78.9 2.4 %tile.11 = f32[8192,8,16]{0,2,1:T(8,128)} broadcast(f32[8192,16]{0,1:T(8,128)S(1)} %bitcast.55), dimensions={0,2} | broadcast | bytes 4718592 | tf_op jit(solution)/shard_map/tile | solution.py:117
  81.3 5.6 %copy.32.table_ref = f32[8192,128]{1,0:T(8,128)} copy(f32[8192,128]{0,1:T(8,128)} %bitcast.53) | data formatting | bytes 8388608 | tf_op jit(solution)/shard_map/tile | solution.py:117
  86.9 27.5 %shard_map.131 = f32[3072,128]{1,0:T(8,128)} custom-call(s32[24576]{0:T(1024)} %add.118.lookup_ref, f32[8192,128]{1,0:T(8,128)} %copy.32.table_ref), custom_call_target="tpu_custom_call" | custom-call | bytes 5767168 | tf_op jit(solution)/shard_map/pallas_call | solution.py:122
  114.4 5.0 %fusion = f32[128,128]{1,0:T(8,128)S(1)} fusion(f32[24,128,128]{2,1,0:T(8,128)} %bitcast.54, f32[24,24]{1,0:T(8,128)S(1)} %copy-done.5), kind=kOutput, calls=%fused_computation.1 | convolution fusion | flops 114016256 | bytes 1640704 | tf_op jit(solution)/shard_map/ij,jab->iab/dot_general | solution.py:184
  119.4 0.1 copy.35
  119.5 0.1 copy.36
  119.6 0.1 reshape.250
  119.7 3.1 %select_reduce_fusion = f32[2048]{0:T(1024)S(1)} fusion(f32[128]{0:T(128)S(1)} %get-tuple-element.16, f32[128]{0:T(128)S(1)} %get-tuple-element.17, f32[128]{0:T(128)S(1)} %get-tuple-element.18, f32[128]{0:T(128)S(1)} %get-tuple-element.19, f32[128]{0:T(128)S(1)} %get-tuple-element.20, f32[128]{0:T(128)S(1)} %get-tuple-element.21, ...), kind=kLoop, calls=%fused_computation.12 | loop fusion | flops 4716544 | bytes 36864 | tf_op jit(solution)/shard_map/reduce_sum | solution.py:73
  122.9 0.7 all_to_all.10
  123.6 5.6 %all-to-all-start.1 = ((f32[32,1,64]{2,1,0:T(1,128)}), f32[32,1,64]{2,1,0:T(1,128)S(1)}, u32[]{:S(2)}, u32[]{:S(2)}) async-start(f32[32,1,64]{2,1,0:T(1,128)} %all_to_all.10), calls=%async_computation.1 | async-start | bytes 32768 | tf_op jit(solution)/shard_map/all_to_all | solution.py:190
  129.2 7.9 %all-to-all-done.1 = f32[32,1,64]{2,1,0:T(1,128)S(1)} async-done(((f32[32,1,64]{2,1,0:T(1,128)}), f32[32,1,64]{2,1,0:T(1,128)S(1)}, u32[]{:S(2)}, u32[]{:S(2)}) %all-to-all-start.1) | async-done | bytes 8224 | tf_op jit(solution)/shard_map/all_to_all | solution.py:190
  137.0 0.5 broadcast.339
  137.5 0.7 reduce.3
  138.2 0.1 broadcast_in_dim.173
  138.3 1.9 %convolution_multiply_fusion = f32[128,128]{1,0:T(8,128)S(1)} fusion(f32[2048]{0:T(1024)S(1)} %broadcast_in_dim.173, s32[2048]{0:T(1024)S(1)} %get-tuple-element.7, s32[2048]{0:T(1024)S(1)} %get-tuple-element.6, f32[1,1,128,128]{3,2,1,0:T(8,128)S(1)} %copy-done.10), kind=kOutput, calls=%fused_computation.6 | convolution fusion | flops 403456000 | bytes 155648 | tf_op jit(solution)/shard_map/dot_general | solution.py:87
  140.2 4.0 %collective-permute-start.4 = (f32[3,128]{1,0:T(4,128)S(1)}, f32[3,128]{1,0:T(4,128)S(1)}, u32[]{:S(2)}, u32[]{:S(2)}) collective-permute-start(f32[3,128]{1,0:T(4,128)S(1)} %get-tuple-element.4), channel_id=1, source_target_pairs={{0,1},{1,2},{2,3},{3,4},{4,5},{5,6},{6,7},{7,8},{8,9},{9,10},{10,1... | collective-permute-start | bytes 4616 | tf_op jit(solution)/shard_map/ppermute | solution.py:31
  144.2 1.9 %collective-permute-start.5 = (f32[3,128]{1,0:T(4,128)S(1)}, f32[3,128]{1,0:T(4,128)S(1)}, u32[]{:S(2)}, u32[]{:S(2)}) collective-permute-start(f32[3,128]{1,0:T(4,128)S(1)} %get-tuple-element.5), channel_id=1, source_target_pairs={{1,0},{2,1},{3,2},{4,3},{5,4},{6,5},{7,6},{8,7},{9,8},{10,9},{11,1... | collective-permute-start | bytes 4616 | tf_op jit(solution)/shard_map/ppermute | solution.py:33
  146.1 0.1 multiply_reduce_fusion
  146.2 5.6 %collective-permute-done.5 = f32[3,128]{1,0:T(4,128)S(1)} collective-permute-done((f32[3,128]{1,0:T(4,128)S(1)}, f32[3,128]{1,0:T(4,128)S(1)}, u32[]{:S(2)}, u32[]{:S(2)}) %collective-permute-start.5) | collective-permute-done | bytes 1568 | tf_op jit(solution)/shard_map/ppermute | solution.py:33
  151.8 1.0 fusion.2
  (37 shorter events, 0.3 us)
Async XLA Ops:
  0.6 1.0 copy-start
  0.6 14.4 %copy-start.7 = (s32[1,1,1024]{2,1,0:T(1,128)S(1)}, s32[1,1,1024]{2,1,0:T(1,128)}, u32[]{:S(2)}) copy-start(s32[1,1,1024]{2,1,0:T(1,128)} %param.16) | copy-start | bytes 12292
  3.9 7.9 %collective-permute-start = (f32[272,256]{1,0:T(8,128)S(1)}, f32[272,256]{1,0:T(8,128)S(1)}, u32[]{:S(2)}, u32[]{:S(2)}) collective-permute-start(f32[272,256]{1,0:T(8,128)S(1)} %pad_maximum_fusion), channel_id=1, source_target_pairs={{0,32},{32,64},{64,96},{96,128},{128,160},{160,192},{192,224},{224... | collective-permute-start | bytes 835592 | tf_op jit(solution)/shard_map/ppermute | solution.py:20
  12.1 12.1 %copy-start.1 = (s32[1,1,24,1024]{3,2,1,0:T(8,128)S(1)}, s32[1,1,24,1024]{3,2,1,0:T(8,128)}, u32[]{:S(2)}) copy-start(s32[1,1,24,1024]{3,2,1,0:T(8,128)} %param.17) | copy-start | bytes 294916
  12.2 12.2 %copy-start.3 = (s32[1,1,32,64]{3,2,1,0:T(8,128)S(1)}, s32[1,1,32,64]{3,2,1,0:T(8,128)}, u32[]{:S(2)}) copy-start(s32[1,1,32,64]{3,2,1,0:T(8,128)} %param.19) | copy-start | bytes 24580
  12.2 12.2 %copy-start.4 = (s32[1,1,32,64]{3,2,1,0:T(8,128)S(1)}, s32[1,1,32,64]{3,2,1,0:T(8,128)}, u32[]{:S(2)}) copy-start(s32[1,1,32,64]{3,2,1,0:T(8,128)} %param.20) | copy-start | bytes 24580
  12.4 9.0 %collective-permute-start.1 = (f32[272,256]{1,0:T(8,128)S(1)}, f32[272,256]{1,0:T(8,128)S(1)}, u32[]{:S(2)}, u32[]{:S(2)}) collective-permute-start(f32[272,256]{1,0:T(8,128)S(1)} %pad_maximum_fusion.1), channel_id=1, source_target_pairs={{0,64},{32,96},{64,128},{96,160},{128,192},{160,224},{192,256},{22... | collective-permute-start | bytes 835592 | tf_op jit(solution)/shard_map/ppermute | solution.py:20
  22.1 16.6 %collective-permute-start.2 = (f32[272,256]{1,0:T(8,128)S(1)}, f32[272,256]{1,0:T(8,128)S(1)}, u32[]{:S(2)}, u32[]{:S(2)}) collective-permute-start(f32[272,256]{1,0:T(8,128)S(1)} %pad_maximum_fusion.2), channel_id=1, source_target_pairs={{0,128},{32,160},{64,192},{96,224},{128,256},{160,288},{192,320},{... | collective-permute-start | bytes 835592 | tf_op jit(solution)/shard_map/ppermute | solution.py:20
  25.1 37.9 %copy-start.8 = (f32[8]{0:T(128)S(1)}, f32[8]{0:T(128)}, u32[]{:S(2)}) copy-start(f32[8]{0:T(128)} %param.23) | copy-start | bytes 100
  25.1 37.9 %copy-start.9 = (s32[8]{0:T(128)S(1)}, s32[8]{0:T(128)}, u32[]{:S(2)}) copy-start(s32[8]{0:T(128)} %param.22) | copy-start | bytes 100
  38.9 9.6 %collective-permute-start.3 = (f32[16,256]{1,0:T(8,128)S(1)}, f32[16,256]{1,0:T(8,128)S(1)}, u32[]{:S(2)}, u32[]{:S(2)}) collective-permute-start(f32[16,256]{1,0:T(8,128)S(1)} %convolution_add_fusion.1), channel_id=1, source_target_pairs={{0,256},{32,288},{64,320},{96,352},{128,384},{160,416},{192,448},{... | collective-permute-start | bytes 49160 | tf_op jit(solution)/shard_map/ppermute | solution.py:20
  48.7 32.6 %copy-start.2 = (f32[16,256]{1,0:T(8,128)}, f32[16,256]{1,0:T(8,128)S(1)}, u32[]{:S(2)}) copy-start(f32[16,256]{1,0:T(8,128)S(1)} %convolution_add_fusion) | copy-start | bytes 49156
  49.6 29.3 %all-to-all-start = ((f32[32,16,256]{2,1,0:T(8,128)}), f32[32,16,256]{2,1,0:T(8,128)S(1)}, u32[]{:S(2)}, u32[]{:S(2)}) async-start(f32[32,16,256]{2,1,0:T(8,128)} %broadcast_in_dim.156), calls=%async_computation | async-start | bytes 1048576 | tf_op jit(solution)/shard_map/all_to_all | solution.py:176
  86.9 27.5 %copy-start.5 = (f32[24,24]{1,0:T(8,128)S(1)}, f32[24,24]{1,0:T(8,128)}, u32[]{:S(2)}) copy-start(f32[24,24]{1,0:T(8,128)} %param.15) | copy-start | bytes 6916
  114.4 5.3 %copy-start.6 = (f32[1,1,1024]{2,1,0:T(1,128)S(1)}, f32[1,1,1024]{2,1,0:T(1,128)}, u32[]{:S(2)}) copy-start(f32[1,1,1024]{2,1,0:T(1,128)} %param.18) | copy-start | bytes 12292
  114.4 24.0 %copy-start.10 = (f32[1,1,128,128]{3,2,1,0:T(8,128)S(1)}, f32[1,1,128,128]{3,2,1,0:T(8,128)}, u32[]{:S(2)}) copy-start(f32[1,1,128,128]{3,2,1,0:T(8,128)} %param.21) | copy-start | bytes 196612
  123.6 13.5 %all-to-all-start.1 = ((f32[32,1,64]{2,1,0:T(1,128)}), f32[32,1,64]{2,1,0:T(1,128)S(1)}, u32[]{:S(2)}, u32[]{:S(2)}) async-start(f32[32,1,64]{2,1,0:T(1,128)} %all_to_all.10), calls=%async_computation.1 | async-start | bytes 32768 | tf_op jit(solution)/shard_map/all_to_all | solution.py:190
  140.2 6.0 %collective-permute-start.4 = (f32[3,128]{1,0:T(4,128)S(1)}, f32[3,128]{1,0:T(4,128)S(1)}, u32[]{:S(2)}, u32[]{:S(2)}) collective-permute-start(f32[3,128]{1,0:T(4,128)S(1)} %get-tuple-element.4), channel_id=1, source_target_pairs={{0,1},{1,2},{2,3},{3,4},{4,5},{5,6},{6,7},{7,8},{8,9},{9,10},{10,1... | collective-permute-start | bytes 4616 | tf_op jit(solution)/shard_map/ppermute | solution.py:31
  144.2 7.6 %collective-permute-start.5 = (f32[3,128]{1,0:T(4,128)S(1)}, f32[3,128]{1,0:T(4,128)S(1)}, u32[]{:S(2)}, u32[]{:S(2)}) collective-permute-start(f32[3,128]{1,0:T(4,128)S(1)} %get-tuple-element.5), channel_id=1, source_target_pairs={{1,0},{2,1},{3,2},{4,3},{5,4},{6,5},{7,6},{8,7},{9,8},{10,9},{11,1... | collective-permute-start | bytes 4616 | tf_op jit(solution)/shard_map/ppermute | solution.py:33

commit v6 on v5

--- a/solution.py
+++ b/solution.py
@@ -46,18 +46,27 @@
     step = -product(couple, inverse)
     order = rights.shape[0]
     levels = lax.axis_size("grp")
-    shift = 1
+
+    def combine(pairs, with_step):
+        nonlocal offset, composite
+        if with_step:
+            packed = lax.ppermute(jnp.concatenate([offset, composite], axis=0), "grp", pairs)
+            earlier_offset, earlier_step = packed[:order], packed[order:]
+            offset = product(earlier_offset, composite) + offset
+            composite = product(earlier_step, composite)
+        else:
+            earlier_offset = lax.ppermute(offset, "grp", pairs)
+            offset = product(earlier_offset, composite) + offset
+
+    composite = step
+    combine([(g, g + 1) for g in range(0, levels - 1, 2)], True)
+    shift = 2
     while shift < levels:
-        if 2 * shift < levels:
-            packed = passed_along(jnp.concatenate([offset, step], axis=0), "grp", shift)
-            earlier_offset, earlier_step = packed[:order], packed[order:]
-            offset = product(earlier_offset, step) + offset
-            step = product(earlier_step, step)
-        else:
-            earlier_offset = passed_along(offset, "grp", shift)
-            offset = product(earlier_offset, step) + offset
+        pairs = [(g, g + shift) for g in range(1, levels - shift, 2)]
+        combine(pairs, 2 * shift < levels)
         shift *= 2
-    return offset
+    earlier_offset = lax.ppermute(offset, "grp", [(g, g + 1) for g in range(1, levels - 1, 2)])
+    return product(earlier_offset, step) + offset
 
 
 def picked(values, index):

time: 154 us -> 145 us (0.942)
  the two profiles are of different devices: /device:TPU:46 before, /device:TPU:54 now
where the time goes in v6:
time: 145 us; the launch traced here: 144 us
  waiting for transfers between devices  56.7 us (39%)
  starting transfers between devices  30 us (21%)
  Pallas kernels  27.5 us (19%)
  matrix products  12.3 us (8%)
  local copies, waits for them, and re-layouts  11.7 us (8%)
  other arithmetic  4.99 us (3%)
    pallas_call x1, Pallas kernels, gathered_rows(): pl.pallas_call(gather_kernel, out_shape=jax.ShapeDtypeStruct((out_rows, 1...  27.5 us
    ppermute x1, waiting for transfers between devices, interface_chain(): lax.ppermute(offset, 'grp', [(g, g + 1) for g in range(1, levels - 1, 2)])  24.9 us
    all_to_all x1, waiting for transfers between devices, on_device(): lax.all_to_all(copies, 'dev', split_axis=0, concat_axis=0, tiled=True)  17.2 us
    all_to_all x1, starting transfers between devices, on_device(): lax.all_to_all(copies, 'dev', split_axis=0, concat_axis=0, tiled=True)  13.4 us
    another operation x3, local copies, waits for them, and re-layouts, gathered_rows(): wide = jnp.tile(table, (1, pack))  8 us
    all_to_all x1, waiting for transfers between devices, on_device(): lax.all_to_all(outgoing, 'dev', split_axis=0, concat_axis=0, tiled=True)  7.87 us
    all_to_all x1, starting transfers between devices, on_device(): lax.all_to_all(outgoing, 'dev', split_axis=0, concat_axis=0, tiled=True)  5.57 us
    ppermute x1, waiting for transfers between devices, padded_2(): lax.ppermute(head, axis, [((i + 1) % count, i) for i in range(ends)])  5.55 us
  transfers between devices with their start and end apart: 9, of which 5 were waited for; matrix products, arithmetic and copies ran while one was open for 1% of the time, Pallas kernels for 0%

profile of v6, /device:TPU:54, one launch (start us, length us, event | category | flops | bytes accessed | tf_op | source)
XLA Modules:
  0.0 144.2 jit_solution(2841212389544378038)
XLA Ops:
  0.6 0.0 copy-start
  0.6 0.9 copy-done
  1.6 1.3 convolution_negate_fusion
  2.9 0.9 fusion.16
  3.9 1.8 %collective-permute-start = (f32[272,256]{1,0:T(8,128)S(1)}, f32[272,256]{1,0:T(8,128)S(1)}, u32[]{:S(2)}, u32[]{:S(2)}) collective-permute-start(f32[272,256]{1,0:T(8,128)S(1)} %pad_maximum_fusion), channel_id=1, source_target_pairs={{0,32},{64,96},{128,160},{192,224},{256,288},{320,352},{384,416},{... | collective-permute-start | bytes 835592 | tf_op jit(solution)/shard_map/ppermute | solution.py:53
  5.7 1.2 collective-permute-done
  6.8 0.4 fusion.12
  7.2 0.2 convolution_add_fusion.4
  7.5 0.7 collective-permute-start.1
  8.2 0.2 convolution_add_fusion.3
  8.4 0.0 copy-start.1
  8.4 0.4 fusion.10
  8.8 0.7 collective-permute-start.2
  9.6 0.2 convolution_add_fusion.2
  9.8 0.7 collective-permute-start.3
  10.5 0.4 fusion.8
  10.9 0.2 convolution_add_fusion.1
  11.1 1.3 collective-permute-start.4
  12.5 0.1 reshape_squeeze.7
  12.6 0.1 reshape_squeeze.6
  12.7 0.6 add.122.lookup_ref
  13.3 24.9 %collective-permute-done.4 = f32[16,256]{1,0:T(8,128)S(1)} collective-permute-done((f32[16,256]{1,0:T(8,128)S(1)}, f32[16,256]{1,0:T(8,128)S(1)}, u32[]{:S(2)}, u32[]{:S(2)}) %collective-permute-start.4) | collective-permute-done | bytes 16416 | tf_op jit(solution)/shard_map/ppermute | solution.py:68
  38.2 0.2 convolution_add_fusion
  38.4 0.0 copy-start.2
  38.5 0.9 broadcast_in_dim.156
  39.3 13.4 %all-to-all-start = ((f32[32,16,256]{2,1,0:T(8,128)}), f32[32,16,256]{2,1,0:T(8,128)S(1)}, u32[]{:S(2)}, u32[]{:S(2)}) async-start(f32[32,16,256]{2,1,0:T(8,128)} %broadcast_in_dim.156), calls=%async_computation | async-start | bytes 1048576 | tf_op jit(solution)/shard_map/all_to_all | solution.py:185
  52.8 0.2 select_reduce_fusion.1
  53.1 17.2 %all-to-all-done = f32[32,16,256]{2,1,0:T(8,128)S(1)} async-done(((f32[32,16,256]{2,1,0:T(8,128)}), f32[32,16,256]{2,1,0:T(8,128)S(1)}, u32[]{:S(2)}, u32[]{:S(2)}) %all-to-all-start) | async-done | bytes 524320 | tf_op jit(solution)/shard_map/all_to_all | solution.py:185
  70.3 2.4 %tile.11 = f32[8192,8,16]{0,2,1:T(8,128)} broadcast(f32[8192,16]{0,1:T(8,128)S(1)} %bitcast.57), dimensions={0,2} | broadcast | bytes 4718592 | tf_op jit(solution)/shard_map/tile | solution.py:126
  72.7 5.6 %copy.32.table_ref = f32[8192,128]{1,0:T(8,128)} copy(f32[8192,128]{0,1:T(8,128)} %bitcast.55) | data formatting | bytes 8388608 | tf_op jit(solution)/shard_map/tile | solution.py:126
  78.3 27.5 %shard_map.131 = f32[3072,128]{1,0:T(8,128)} custom-call(s32[24576]{0:T(1024)} %add.122.lookup_ref, f32[8192,128]{1,0:T(8,128)} %copy.32.table_ref), custom_call_target="tpu_custom_call" | custom-call | bytes 5767168 | tf_op jit(solution)/shard_map/pallas_call | solution.py:131
  105.8 5.0 %fusion = f32[128,128]{1,0:T(8,128)S(1)} fusion(f32[24,128,128]{2,1,0:T(8,128)} %bitcast.56, f32[24,24]{1,0:T(8,128)S(1)} %copy-done.5), kind=kOutput, calls=%fused_computation.1 | convolution fusion | flops 114016256 | bytes 1640704 | tf_op jit(solution)/shard_map/ij,jab->iab/dot_general | solution.py:193
  110.8 0.1 copy.35
  110.9 0.1 copy.36
  111.0 0.1 reshape.250
  111.1 3.1 %select_reduce_fusion = f32[2048]{0:T(1024)S(1)} fusion(f32[128]{0:T(128)S(1)} %get-tuple-element.16, f32[128]{0:T(128)S(1)} %get-tuple-element.17, f32[128]{0:T(128)S(1)} %get-tuple-element.18, f32[128]{0:T(128)S(1)} %get-tuple-element.19, f32[128]{0:T(128)S(1)} %get-tuple-element.20, f32[128]{0:T(128)S(1)} %get-tuple-element.21, ...), kind=kLoop, calls=%fused_computation.13 | loop fusion | flops 4716544 | bytes 36864 | tf_op jit(solution)/shard_map/reduce_sum | solution.py:82
  114.3 0.7 all_to_all.10
  115.0 5.6 %all-to-all-start.1 = ((f32[32,1,64]{2,1,0:T(1,128)}), f32[32,1,64]{2,1,0:T(1,128)S(1)}, u32[]{:S(2)}, u32[]{:S(2)}) async-start(f32[32,1,64]{2,1,0:T(1,128)} %all_to_all.10), calls=%async_computation.1 | async-start | bytes 32768 | tf_op jit(solution)/shard_map/all_to_all | solution.py:199
  120.6 7.9 %all-to-all-done.1 = f32[32,1,64]{2,1,0:T(1,128)S(1)} async-done(((f32[32,1,64]{2,1,0:T(1,128)}), f32[32,1,64]{2,1,0:T(1,128)S(1)}, u32[]{:S(2)}, u32[]{:S(2)}) %all-to-all-start.1) | async-done | bytes 8224 | tf_op jit(solution)/shard_map/all_to_all | solution.py:199
  128.4 0.5 broadcast.339
  128.9 0.7 reduce.3
  129.6 0.1 broadcast_in_dim.173
  129.7 1.9 %convolution_multiply_fusion = f32[128,128]{1,0:T(8,128)S(1)} fusion(f32[2048]{0:T(1024)S(1)} %broadcast_in_dim.173, s32[2048]{0:T(1024)S(1)} %get-tuple-element.7, s32[2048]{0:T(1024)S(1)} %get-tuple-element.6, f32[1,1,128,128]{3,2,1,0:T(8,128)S(1)} %copy-done.10), kind=kOutput, calls=%fused_computation.6 | convolution fusion | flops 403456000 | bytes 155648 | tf_op jit(solution)/shard_map/dot_general | solution.py:96
  131.6 4.0 %collective-permute-start.5 = (f32[3,128]{1,0:T(4,128)S(1)}, f32[3,128]{1,0:T(4,128)S(1)}, u32[]{:S(2)}, u32[]{:S(2)}) collective-permute-start(f32[3,128]{1,0:T(4,128)S(1)} %get-tuple-element.4), channel_id=1, source_target_pairs={{0,1},{1,2},{2,3},{3,4},{4,5},{5,6},{6,7},{7,8},{8,9},{9,10},{10,1... | collective-permute-start | bytes 4616 | tf_op jit(solution)/shard_map/ppermute | solution.py:31
  135.6 1.9 %collective-permute-start.6 = (f32[3,128]{1,0:T(4,128)S(1)}, f32[3,128]{1,0:T(4,128)S(1)}, u32[]{:S(2)}, u32[]{:S(2)}) collective-permute-start(f32[3,128]{1,0:T(4,128)S(1)} %get-tuple-element.5), channel_id=1, source_target_pairs={{1,0},{2,1},{3,2},{4,3},{5,4},{6,5},{7,6},{8,7},{9,8},{10,9},{11,1... | collective-permute-start | bytes 4616 | tf_op jit(solution)/shard_map/ppermute | solution.py:33
  137.5 0.1 multiply_reduce_fusion
  137.6 5.6 %collective-permute-done.6 = f32[3,128]{1,0:T(4,128)S(1)} collective-permute-done((f32[3,128]{1,0:T(4,128)S(1)}, f32[3,128]{1,0:T(4,128)S(1)}, u32[]{:S(2)}, u32[]{:S(2)}) %collective-permute-start.6) | collective-permute-done | bytes 1568 | tf_op jit(solution)/shard_map/ppermute | solution.py:33
  143.2 1.0 fusion.2
  (40 shorter events, 0.3 us)
Async XLA Ops:
  0.6 1.0 copy-start
  3.9 5.6 %copy-start.7 = (s32[1,1,1024]{2,1,0:T(1,128)S(1)}, s32[1,1,1024]{2,1,0:T(1,128)}, u32[]{:S(2)}) copy-start(s32[1,1,1024]{2,1,0:T(1,128)} %param.16) | copy-start | bytes 12292
  3.9 2.9 %collective-permute-start = (f32[272,256]{1,0:T(8,128)S(1)}, f32[272,256]{1,0:T(8,128)S(1)}, u32[]{:S(2)}, u32[]{:S(2)}) collective-permute-start(f32[272,256]{1,0:T(8,128)S(1)} %pad_maximum_fusion), channel_id=1, source_target_pairs={{0,32},{64,96},{128,160},{192,224},{256,288},{320,352},{384,416},{... | collective-permute-start | bytes 835592 | tf_op jit(solution)/shard_map/ppermute | solution.py:53
  7.5 0.7 collective-permute-start.1
  8.4 4.1 %copy-start.1 = (s32[1,1,24,1024]{3,2,1,0:T(8,128)S(1)}, s32[1,1,24,1024]{3,2,1,0:T(8,128)}, u32[]{:S(2)}) copy-start(s32[1,1,24,1024]{3,2,1,0:T(8,128)} %param.17) | copy-start | bytes 294916
  8.4 4.1 %copy-start.3 = (s32[1,1,32,64]{3,2,1,0:T(8,128)S(1)}, s32[1,1,32,64]{3,2,1,0:T(8,128)}, u32[]{:S(2)}) copy-start(s32[1,1,32,64]{3,2,1,0:T(8,128)} %param.19) | copy-start | bytes 24580
  8.4 4.2 %copy-start.4 = (s32[1,1,32,64]{3,2,1,0:T(8,128)S(1)}, s32[1,1,32,64]{3,2,1,0:T(8,128)}, u32[]{:S(2)}) copy-start(s32[1,1,32,64]{3,2,1,0:T(8,128)} %param.20) | copy-start | bytes 24580
  8.8 0.7 collective-permute-start.2
  9.8 1.1 collective-permute-start.3
  10.9 41.9 %copy-start.8 = (f32[8]{0:T(128)S(1)}, f32[8]{0:T(128)}, u32[]{:S(2)}) copy-start(f32[8]{0:T(128)} %param.23) | copy-start | bytes 100
  10.9 41.9 %copy-start.9 = (s32[8]{0:T(128)S(1)}, s32[8]{0:T(128)}, u32[]{:S(2)}) copy-start(s32[8]{0:T(128)} %param.22) | copy-start | bytes 100
  11.1 27.1 %collective-permute-start.4 = (f32[16,256]{1,0:T(8,128)S(1)}, f32[16,256]{1,0:T(8,128)S(1)}, u32[]{:S(2)}, u32[]{:S(2)}) collective-permute-start(f32[16,256]{1,0:T(8,128)S(1)} %convolution_add_fusion.1), channel_id=1, source_target_pairs={{32,64},{96,128},{160,192},{224,256},{288,320},{352,384},{416,448}... | collective-permute-start | bytes 49160 | tf_op jit(solution)/shard_map/ppermute | solution.py:68
  38.4 34.3 %copy-start.2 = (f32[16,256]{1,0:T(8,128)}, f32[16,256]{1,0:T(8,128)S(1)}, u32[]{:S(2)}) copy-start(f32[16,256]{1,0:T(8,128)S(1)} %convolution_add_fusion) | copy-start | bytes 49156
  39.3 30.9 %all-to-all-start = ((f32[32,16,256]{2,1,0:T(8,128)}), f32[32,16,256]{2,1,0:T(8,128)S(1)}, u32[]{:S(2)}, u32[]{:S(2)}) async-start(f32[32,16,256]{2,1,0:T(8,128)} %broadcast_in_dim.156), calls=%async_computation | async-start | bytes 1048576 | tf_op jit(solution)/shard_map/all_to_all | solution.py:185
  78.3 27.5 %copy-start.5 = (f32[24,24]{1,0:T(8,128)S(1)}, f32[24,24]{1,0:T(8,128)}, u32[]{:S(2)}) copy-start(f32[24,24]{1,0:T(8,128)} %param.15) | copy-start | bytes 6916
  105.8 5.3 %copy-start.6 = (f32[1,1,1024]{2,1,0:T(1,128)S(1)}, f32[1,1,1024]{2,1,0:T(1,128)}, u32[]{:S(2)}) copy-start(f32[1,1,1024]{2,1,0:T(1,128)} %param.18) | copy-start | bytes 12292
  105.8 24.0 %copy-start.10 = (f32[1,1,128,128]{3,2,1,0:T(8,128)S(1)}, f32[1,1,128,128]{3,2,1,0:T(8,128)}, u32[]{:S(2)}) copy-start(f32[1,1,128,128]{3,2,1,0:T(8,128)} %param.21) | copy-start | bytes 196612
  115.0 13.5 %all-to-all-start.1 = ((f32[32,1,64]{2,1,0:T(1,128)}), f32[32,1,64]{2,1,0:T(1,128)S(1)}, u32[]{:S(2)}, u32[]{:S(2)}) async-start(f32[32,1,64]{2,1,0:T(1,128)} %all_to_all.10), calls=%async_computation.1 | async-start | bytes 32768 | tf_op jit(solution)/shard_map/all_to_all | solution.py:199
  131.6 6.0 %collective-permute-start.5 = (f32[3,128]{1,0:T(4,128)S(1)}, f32[3,128]{1,0:T(4,128)S(1)}, u32[]{:S(2)}, u32[]{:S(2)}) collective-permute-start(f32[3,128]{1,0:T(4,128)S(1)} %get-tuple-element.4), channel_id=1, source_target_pairs={{0,1},{1,2},{2,3},{3,4},{4,5},{5,6},{6,7},{7,8},{8,9},{9,10},{10,1... | collective-permute-start | bytes 4616 | tf_op jit(solution)/shard_map/ppermute | solution.py:31
  135.6 7.6 %collective-permute-start.6 = (f32[3,128]{1,0:T(4,128)S(1)}, f32[3,128]{1,0:T(4,128)S(1)}, u32[]{:S(2)}, u32[]{:S(2)}) collective-permute-start(f32[3,128]{1,0:T(4,128)S(1)} %get-tuple-element.5), channel_id=1, source_target_pairs={{1,0},{2,1},{3,2},{4,3},{5,4},{6,5},{7,6},{8,7},{9,8},{10,9},{11,1... | collective-permute-start | bytes 4616 | tf_op jit(solution)/shard_map/ppermute | solution.py:33

commit v7 on v6

--- a/solution.py
+++ b/solution.py
@@ -120,10 +120,16 @@
     lax.fori_loop(0, rows, body, 0, unroll=8)
 
 
-def gathered_rows(table, lookup):
-    width = table.shape[1]
+def gathered_rows(panels, lookup):
+    slabs, width, panel_order = panels.shape
     pack = 128 // width
-    wide = jnp.tile(table, (1, pack))
+    spread = (
+        lax.broadcasted_iota(jnp.int32, (width, 128), 0)
+        == lax.broadcasted_iota(jnp.int32, (width, 128), 1) % width
+    ).astype(jnp.float32)
+    wide = lax.dot_general(
+        panels, spread, (((1,), (0,)), ((), ())), precision=exact_mode, preferred_element_type=jnp.float32
+    ).reshape(slabs * panel_order, 128)
     total = lookup.shape[0]
     out_rows = total // pack
     chunks = 8
@@ -184,12 +190,11 @@
     copies = jnp.broadcast_to(solved[None], (lax.axis_size("dev"),) + solved.shape)
     panels = lax.all_to_all(copies, "dev", split_axis=0, concat_axis=0, tiled=True)
     slabs, order, panel_order = panels.shape
-    table = jnp.transpose(panels, (0, 2, 1)).reshape(slabs * panel_order, order)
     slab_place = element_substructure[0, 0]
     lookup = slab_place[None, :] * panel_order + element_rows[0, 0]
     dofs, elements = lookup.shape
     pack = 128 // order
-    motion = gathered_rows(table, lookup.reshape(-1)).reshape(dofs, elements // pack, 128)
+    motion = gathered_rows(panels, lookup.reshape(-1)).reshape(dofs, elements // pack, 128)
     forces = jnp.einsum("ij,jab->iab", stiffness, motion, precision=exact_mode)
     energy = jnp.sum(jnp.sum(motion * forces, axis=0).reshape(elements // pack, pack, order), axis=2)
     energy = energy.reshape(elements)

time: 145 us -> 142 us (0.979)
  local copies, waits for them, and re-layouts: 11.7 us -> 3.64 us
  matrix products: 12.3 us -> 17.3 us
    another operation x3 -> x0, local copies, waits for them, and re-layouts: 8 us -> none  [gathered_rows(): wide = jnp.tile(table, (1, pack))]
    dot_general x0 -> x1, matrix products: none -> 4.99 us  [gathered_rows(): lax.dot_general(panels, spread, (((1,), (0,)), ((), ())), precision=exact...]
where the time goes in v7:
time: 142 us; the launch traced here: 141 us
  waiting for transfers between devices  56.6 us (40%)
  starting transfers between devices  30.1 us (21%)
  Pallas kernels  27.5 us (19%)
  matrix products  17.3 us (12%)
  other arithmetic  5.02 us (4%)
  local copies, waits for them, and re-layouts  3.64 us (3%)
    pallas_call x1, Pallas kernels, gathered_rows(): pl.pallas_call(gather_kernel, out_shape=jax.ShapeDtypeStruct((out_rows, 1...  27.5 us
    ppermute x1, waiting for transfers between devices, interface_chain(): lax.ppermute(offset, 'grp', [(g, g + 1) for g in range(1, levels - 1, 2)])  25.5 us
    all_to_all x1, waiting for transfers between devices, on_device(): lax.all_to_all(copies, 'dev', split_axis=0, concat_axis=0, tiled=True)  16.5 us
    all_to_all x1, starting transfers between devices, on_device(): lax.all_to_all(copies, 'dev', split_axis=0, concat_axis=0, tiled=True)  13.4 us
    all_to_all x1, waiting for transfers between devices, on_device(): lax.all_to_all(outgoing, 'dev', split_axis=0, concat_axis=0, tiled=True)  7.87 us
    all_to_all x1, starting transfers between devices, on_device(): lax.all_to_all(outgoing, 'dev', split_axis=0, concat_axis=0, tiled=True)  5.57 us
    ppermute x1, waiting for transfers between devices, padded_2(): lax.ppermute(head, axis, [((i + 1) % count, i) for i in range(ends)])  5.55 us
    dot_general x11, matrix products, product(): jnp.dot(left, right, precision=exact_mode, preferred_element_type=jnp.flo...  5.43 us
  transfers between devices with their start and end apart: 9, of which 5 were waited for; matrix products, arithmetic and copies ran while one was open for 1% of the time, Pallas kernels for 0%

profile of v7, /device:TPU:54, one launch (start us, length us, event | category | flops | bytes accessed | tf_op | source)
XLA Modules:
  0.0 141.3 jit_solution(14361211059077583462)
XLA Ops:
  0.6 0.0 copy-start
  0.7 0.9 copy-done
  1.6 1.3 convolution_negate_fusion
  2.9 0.9 fusion.16
  3.9 1.8 %collective-permute-start = (f32[272,256]{1,0:T(8,128)S(1)}, f32[272,256]{1,0:T(8,128)S(1)}, u32[]{:S(2)}, u32[]{:S(2)}) collective-permute-start(f32[272,256]{1,0:T(8,128)S(1)} %pad_maximum_fusion), channel_id=1, source_target_pairs={{0,32},{64,96},{128,160},{192,224},{256,288},{320,352},{384,416},{... | collective-permute-start | bytes 835592 | tf_op jit(solution)/shard_map/ppermute | solution.py:53
  5.7 1.2 collective-permute-done
  6.8 0.4 fusion.12
  7.2 0.2 convolution_add_fusion.4
  7.5 0.7 collective-permute-start.1
  8.2 0.0 copy-start.9
  8.2 0.2 convolution_add_fusion.3
  8.4 0.4 fusion.10
  8.8 0.7 collective-permute-start.2
  9.6 0.2 convolution_add_fusion.2
  9.8 0.0 copy-start.1
  9.8 0.8 collective-permute-start.3
  10.6 0.4 fusion.8
  11.0 0.2 convolution_add_fusion.1
  11.3 1.3 collective-permute-start.4
  12.6 0.2 select_reduce_fusion.1
  12.8 25.5 %collective-permute-done.4 = f32[16,256]{1,0:T(8,128)S(1)} collective-permute-done((f32[16,256]{1,0:T(8,128)S(1)}, f32[16,256]{1,0:T(8,128)S(1)}, u32[]{:S(2)}, u32[]{:S(2)}) %collective-permute-start.4) | collective-permute-done | bytes 16416 | tf_op jit(solution)/shard_map/ppermute | solution.py:68
  38.4 0.2 convolution_add_fusion
  38.6 0.0 copy-start.2
  38.6 0.9 broadcast_in_dim.156
  39.5 13.4 %all-to-all-start = ((f32[32,16,256]{2,1,0:T(8,128)}), f32[32,16,256]{2,1,0:T(8,128)S(1)}, u32[]{:S(2)}, u32[]{:S(2)}) async-start(f32[32,16,256]{2,1,0:T(8,128)} %broadcast_in_dim.156), calls=%async_computation | async-start | bytes 1048576 | tf_op jit(solution)/shard_map/all_to_all | solution.py:191
  53.0 0.1 reshape_squeeze.7
  53.0 0.1 reshape_squeeze.6
  53.1 0.7 add.129.lookup_ref
  53.8 16.5 %all-to-all-done = f32[32,16,256]{2,1,0:T(8,128)S(1)} async-done(((f32[32,16,256]{2,1,0:T(8,128)}), f32[32,16,256]{2,1,0:T(8,128)S(1)}, u32[]{:S(2)}, u32[]{:S(2)}) %all-to-all-start) | async-done | bytes 524320 | tf_op jit(solution)/shard_map/all_to_all | solution.py:191
  70.4 5.0 %fusion.32 = f32[32,256,128]{2,1,0:T(8,128)} fusion(f32[32,16,256]{2,1,0:T(8,128)S(1)} %all-to-all-done, s32[128]{0:T(128)S(1)} %get-tuple-element.23, s32[128]{0:T(128)S(1)} %get-tuple-element.24, pred[128]{0:T(512)(128)(4,1)S(1)} %compare_and_fusion), kind=kOutput, calls=%fused_computation.67 | convolution fusion | flops 201330688 | bytes 4719744 | tf_op jit(solution)/shard_map/dot_general | solution.py:130
  75.4 27.5 %shard_map.131 = f32[3072,128]{1,0:T(8,128)} custom-call(s32[24576]{0:T(1024)} %add.129.lookup_ref, f32[8192,128]{1,0:T(8,128)} %bitcast.56), custom_call_target="tpu_custom_call" | custom-call | bytes 5767168 | tf_op jit(solution)/shard_map/pallas_call | solution.py:137
  102.8 5.0 %fusion = f32[128,128]{1,0:T(8,128)S(1)} fusion(f32[24,128,128]{2,1,0:T(8,128)} %bitcast.57, f32[24,24]{1,0:T(8,128)S(1)} %copy-done.5), kind=kOutput, calls=%fused_computation.1 | convolution fusion | flops 114016256 | bytes 1640704 | tf_op jit(solution)/shard_map/ij,jab->iab/dot_general | solution.py:198
  107.9 0.1 copy.24
  108.0 0.1 copy.25
  108.1 0.1 reshape.250
  108.2 3.1 %select_reduce_fusion = f32[2048]{0:T(1024)S(1)} fusion(f32[128]{0:T(128)S(1)} %get-tuple-element.16, f32[128]{0:T(128)S(1)} %get-tuple-element.17, f32[128]{0:T(128)S(1)} %get-tuple-element.18, f32[128]{0:T(128)S(1)} %get-tuple-element.19, f32[128]{0:T(128)S(1)} %get-tuple-element.20, f32[128]{0:T(128)S(1)} %get-tuple-element.21, ...), kind=kLoop, calls=%fused_computation.13 | loop fusion | flops 4716544 | bytes 36864 | tf_op jit(solution)/shard_map/reduce_sum | solution.py:82
  111.4 0.7 all_to_all.10
  112.1 5.6 %all-to-all-start.1 = ((f32[32,1,64]{2,1,0:T(1,128)}), f32[32,1,64]{2,1,0:T(1,128)S(1)}, u32[]{:S(2)}, u32[]{:S(2)}) async-start(f32[32,1,64]{2,1,0:T(1,128)} %all_to_all.10), calls=%async_computation.1 | async-start | bytes 32768 | tf_op jit(solution)/shard_map/all_to_all | solution.py:204
  117.6 7.9 %all-to-all-done.1 = f32[32,1,64]{2,1,0:T(1,128)S(1)} async-done(((f32[32,1,64]{2,1,0:T(1,128)}), f32[32,1,64]{2,1,0:T(1,128)S(1)}, u32[]{:S(2)}, u32[]{:S(2)}) %all-to-all-start.1) | async-done | bytes 8224 | tf_op jit(solution)/shard_map/all_to_all | solution.py:204
  125.5 0.5 broadcast.351
  126.0 0.7 reduce.3
  126.7 0.1 broadcast_in_dim.173
  126.8 1.9 %convolution_multiply_fusion = f32[128,128]{1,0:T(8,128)S(1)} fusion(f32[2048]{0:T(1024)S(1)} %broadcast_in_dim.173, s32[2048]{0:T(1024)S(1)} %get-tuple-element.7, s32[2048]{0:T(1024)S(1)} %get-tuple-element.6, f32[1,1,128,128]{3,2,1,0:T(8,128)S(1)} %copy-done.10), kind=kOutput, calls=%fused_computation.6 | convolution fusion | flops 403456000 | bytes 155648 | tf_op jit(solution)/shard_map/dot_general | solution.py:96
  128.7 4.0 %collective-permute-start.5 = (f32[3,128]{1,0:T(4,128)S(1)}, f32[3,128]{1,0:T(4,128)S(1)}, u32[]{:S(2)}, u32[]{:S(2)}) collective-permute-start(f32[3,128]{1,0:T(4,128)S(1)} %get-tuple-element.4), channel_id=1, source_target_pairs={{0,1},{1,2},{2,3},{3,4},{4,5},{5,6},{6,7},{7,8},{8,9},{9,10},{10,1... | collective-permute-start | bytes 4616 | tf_op jit(solution)/shard_map/ppermute | solution.py:31
  132.7 1.9 %collective-permute-start.6 = (f32[3,128]{1,0:T(4,128)S(1)}, f32[3,128]{1,0:T(4,128)S(1)}, u32[]{:S(2)}, u32[]{:S(2)}) collective-permute-start(f32[3,128]{1,0:T(4,128)S(1)} %get-tuple-element.5), channel_id=1, source_target_pairs={{1,0},{2,1},{3,2},{4,3},{5,4},{6,5},{7,6},{8,7},{9,8},{10,9},{11,1... | collective-permute-start | bytes 4616 | tf_op jit(solution)/shard_map/ppermute | solution.py:33
  134.6 0.1 multiply_reduce_fusion
  134.7 5.6 %collective-permute-done.6 = f32[3,128]{1,0:T(4,128)S(1)} collective-permute-done((f32[3,128]{1,0:T(4,128)S(1)}, f32[3,128]{1,0:T(4,128)S(1)}, u32[]{:S(2)}, u32[]{:S(2)}) %collective-permute-start.6) | collective-permute-done | bytes 1568 | tf_op jit(solution)/shard_map/ppermute | solution.py:33
  140.3 1.0 fusion.2
  (40 shorter events, 0.3 us)
Async XLA Ops:
  0.6 1.0 copy-start
  0.6 7.5 %copy-start.7 = (s32[1,1,1024]{2,1,0:T(1,128)S(1)}, s32[1,1,1024]{2,1,0:T(1,128)}, u32[]{:S(2)}) copy-start(s32[1,1,1024]{2,1,0:T(1,128)} %param.16) | copy-start | bytes 12292
  3.9 2.9 %collective-permute-start = (f32[272,256]{1,0:T(8,128)S(1)}, f32[272,256]{1,0:T(8,128)S(1)}, u32[]{:S(2)}, u32[]{:S(2)}) collective-permute-start(f32[272,256]{1,0:T(8,128)S(1)} %pad_maximum_fusion), channel_id=1, source_target_pairs={{0,32},{64,96},{128,160},{192,224},{256,288},{320,352},{384,416},{... | collective-permute-start | bytes 835592 | tf_op jit(solution)/shard_map/ppermute | solution.py:53
  7.5 0.7 collective-permute-start.1
  8.2 4.4 %copy-start.8 = (f32[8]{0:T(128)S(1)}, f32[8]{0:T(128)}, u32[]{:S(2)}) copy-start(f32[8]{0:T(128)} %param.23) | copy-start | bytes 100
  8.2 4.4 %copy-start.9 = (s32[8]{0:T(128)S(1)}, s32[8]{0:T(128)}, u32[]{:S(2)}) copy-start(s32[8]{0:T(128)} %param.22) | copy-start | bytes 100
  8.8 0.7 collective-permute-start.2
  9.8 43.1 %copy-start.1 = (s32[1,1,24,1024]{3,2,1,0:T(8,128)S(1)}, s32[1,1,24,1024]{3,2,1,0:T(8,128)}, u32[]{:S(2)}) copy-start(s32[1,1,24,1024]{3,2,1,0:T(8,128)} %param.17) | copy-start | bytes 294916
  9.8 43.1 %copy-start.3 = (s32[1,1,32,64]{3,2,1,0:T(8,128)S(1)}, s32[1,1,32,64]{3,2,1,0:T(8,128)}, u32[]{:S(2)}) copy-start(s32[1,1,32,64]{3,2,1,0:T(8,128)} %param.19) | copy-start | bytes 24580
  9.8 1.2 collective-permute-start.3
  11.0 42.0 %copy-start.4 = (s32[1,1,32,64]{3,2,1,0:T(8,128)S(1)}, s32[1,1,32,64]{3,2,1,0:T(8,128)}, u32[]{:S(2)}) copy-start(s32[1,1,32,64]{3,2,1,0:T(8,128)} %param.20) | copy-start | bytes 24580
  11.3 27.1 %collective-permute-start.4 = (f32[16,256]{1,0:T(8,128)S(1)}, f32[16,256]{1,0:T(8,128)S(1)}, u32[]{:S(2)}, u32[]{:S(2)}) collective-permute-start(f32[16,256]{1,0:T(8,128)S(1)} %convolution_add_fusion.1), channel_id=1, source_target_pairs={{32,64},{96,128},{160,192},{224,256},{288,320},{352,384},{416,448}... | collective-permute-start | bytes 49160 | tf_op jit(solution)/shard_map/ppermute | solution.py:68
  38.6 36.8 %copy-start.2 = (f32[16,256]{1,0:T(8,128)}, f32[16,256]{1,0:T(8,128)S(1)}, u32[]{:S(2)}) copy-start(f32[16,256]{1,0:T(8,128)S(1)} %convolution_add_fusion) | copy-start | bytes 49156
  39.5 30.9 %all-to-all-start = ((f32[32,16,256]{2,1,0:T(8,128)}), f32[32,16,256]{2,1,0:T(8,128)S(1)}, u32[]{:S(2)}, u32[]{:S(2)}) async-start(f32[32,16,256]{2,1,0:T(8,128)} %broadcast_in_dim.156), calls=%async_computation | async-start | bytes 1048576 | tf_op jit(solution)/shard_map/all_to_all | solution.py:191
  75.4 27.5 %copy-start.5 = (f32[24,24]{1,0:T(8,128)S(1)}, f32[24,24]{1,0:T(8,128)}, u32[]{:S(2)}) copy-start(f32[24,24]{1,0:T(8,128)} %param.15) | copy-start | bytes 6916
  102.8 5.4 %copy-start.6 = (f32[1,1,1024]{2,1,0:T(1,128)S(1)}, f32[1,1,1024]{2,1,0:T(1,128)}, u32[]{:S(2)}) copy-start(f32[1,1,1024]{2,1,0:T(1,128)} %param.18) | copy-start | bytes 12292
  102.8 24.0 %copy-start.10 = (f32[1,1,128,128]{3,2,1,0:T(8,128)S(1)}, f32[1,1,128,128]{3,2,1,0:T(8,128)}, u32[]{:S(2)}) copy-start(f32[1,1,128,128]{3,2,1,0:T(8,128)} %param.21) | copy-start | bytes 196612
  112.1 13.5 %all-to-all-start.1 = ((f32[32,1,64]{2,1,0:T(1,128)}), f32[32,1,64]{2,1,0:T(1,128)S(1)}, u32[]{:S(2)}, u32[]{:S(2)}) async-start(f32[32,1,64]{2,1,0:T(1,128)} %all_to_all.10), calls=%async_computation.1 | async-start | bytes 32768 | tf_op jit(solution)/shard_map/all_to_all | solution.py:204
  128.7 6.0 %collective-permute-start.5 = (f32[3,128]{1,0:T(4,128)S(1)}, f32[3,128]{1,0:T(4,128)S(1)}, u32[]{:S(2)}, u32[]{:S(2)}) collective-permute-start(f32[3,128]{1,0:T(4,128)S(1)} %get-tuple-element.4), channel_id=1, source_target_pairs={{0,1},{1,2},{2,3},{3,4},{4,5},{5,6},{6,7},{7,8},{8,9},{9,10},{10,1... | collective-permute-start | bytes 4616 | tf_op jit(solution)/shard_map/ppermute | solution.py:31
  132.7 7.6 %collective-permute-start.6 = (f32[3,128]{1,0:T(4,128)S(1)}, f32[3,128]{1,0:T(4,128)S(1)}, u32[]{:S(2)}, u32[]{:S(2)}) collective-permute-start(f32[3,128]{1,0:T(4,128)S(1)} %get-tuple-element.5), channel_id=1, source_target_pairs={{1,0},{2,1},{3,2},{4,3},{5,4},{6,5},{7,6},{8,7},{9,8},{10,9},{11,1... | collective-permute-start | bytes 4616 | tf_op jit(solution)/shard_map/ppermute | solution.py:33

commit v8 on v7

--- a/solution.py
+++ b/solution.py
@@ -50,7 +50,11 @@
     def combine(pairs, with_step):
         nonlocal offset, composite
         if with_step:
-            packed = lax.ppermute(jnp.concatenate([offset, composite], axis=0), "grp", pairs)
+            packed = jnp.concatenate([offset, composite], axis=0)
+            half = packed.shape[0] // 2
+            packed = jnp.concatenate(
+                [lax.ppermute(packed[:half], "grp", pairs), lax.ppermute(packed[half:], "grp", pairs)], axis=0
+            )
             earlier_offset, earlier_step = packed[:order], packed[order:]
             offset = product(earlier_offset, composite) + offset
             composite = product(earlier_step, composite)

time: 142 us -> 141 us (level)
  the two profiles are of different devices: /device:TPU:54 before, /device:TPU:46 now
where the time goes in v8:
time: 141 us; the launch traced here: 140 us
  waiting for transfers between devices  52.6 us (37%)
  starting transfers between devices  32.7 us (23%)
  Pallas kernels  27.5 us (20%)
  matrix products  17.3 us (12%)
  other arithmetic  4.99 us (4%)
  local copies, waits for them, and re-layouts  3.68 us (3%)
    pallas_call x1, Pallas kernels, gathered_rows(): pl.pallas_call(gather_kernel, out_shape=jax.ShapeDtypeStruct((out_rows, 1...  27.5 us
    ppermute x1, waiting for transfers between devices, interface_chain(): lax.ppermute(offset, 'grp', [(g, g + 1) for g in range(1, levels - 1, 2)])  26.9 us
    all_to_all x1, starting transfers between devices, on_device(): lax.all_to_all(copies, 'dev', split_axis=0, concat_axis=0, tiled=True)  13.4 us
    all_to_all x1, waiting for transfers between devices, on_device(): lax.all_to_all(copies, 'dev', split_axis=0, concat_axis=0, tiled=True)  11.5 us
    all_to_all x1, waiting for transfers between devices, on_device(): lax.all_to_all(outgoing, 'dev', split_axis=0, concat_axis=0, tiled=True)  7.87 us
    all_to_all x1, starting transfers between devices, on_device(): lax.all_to_all(outgoing, 'dev', split_axis=0, concat_axis=0, tiled=True)  5.57 us
    ppermute x1, waiting for transfers between devices, padded_2(): lax.ppermute(head, axis, [((i + 1) % count, i) for i in range(ends)])  5.55 us
    dot_general x11, matrix products, product(): jnp.dot(left, right, precision=exact_mode, preferred_element_type=jnp.flo...  5.41 us
  transfers between devices with their start and end apart: 12, of which 5 were waited for; matrix products, arithmetic and copies ran while one was open for 2% of the time, Pallas kernels for 0%

profile of v8, /device:TPU:46, one launch (start us, length us, event | category | flops | bytes accessed | tf_op | source)
XLA Modules:
  0.0 139.9 jit_solution(4930541307506631725)
XLA Ops:
  0.6 0.9 copy-done
  1.6 1.3 convolution_negate_fusion
  2.9 0.9 fusion.16
  3.9 1.7 %collective-permute-start = (f32[136,256]{1,0:T(8,128)S(1)}, f32[136,256]{1,0:T(8,128)S(1)}, u32[]{:S(2)}, u32[]{:S(2)}) collective-permute-start(f32[136,256]{1,0:T(8,128)S(1)} %get-tuple-element.9), channel_id=1, source_target_pairs={{0,32},{64,96},{128,160},{192,224},{256,288},{320,352},{384,416},{... | collective-permute-start | bytes 417800 | tf_op jit(solution)/shard_map/ppermute | solution.py:56
  5.7 1.3 collective-permute-start.1
  7.0 0.2 convolution_add_fusion.4
  7.2 0.8 collective-permute-done.1
  7.9 0.4 fusion.12
  8.4 0.7 collective-permute-start.2
  9.1 0.7 collective-permute-start.3
  9.7 0.2 convolution_add_fusion.3
  10.0 0.4 fusion.10
  10.4 0.7 collective-permute-start.4
  11.1 0.7 collective-permute-start.6
  11.8 0.2 convolution_add_fusion.2
  12.1 0.8 collective-permute-start.5
  12.9 0.4 fusion.8
  13.3 0.2 convolution_add_fusion.1
  13.5 1.3 collective-permute-start.7
  14.8 0.2 select_reduce_fusion.1
  15.1 26.9 %collective-permute-done.7 = f32[16,256]{1,0:T(8,128)S(1)} collective-permute-done((f32[16,256]{1,0:T(8,128)S(1)}, f32[16,256]{1,0:T(8,128)S(1)}, u32[]{:S(2)}, u32[]{:S(2)}) %collective-permute-start.7) | collective-permute-done | bytes 16416 | tf_op jit(solution)/shard_map/ppermute | solution.py:72
  42.0 0.2 convolution_add_fusion
  42.2 0.0 copy-start.2
  42.2 0.9 broadcast_in_dim.156
  43.1 13.4 %all-to-all-start = ((f32[32,16,256]{2,1,0:T(8,128)}), f32[32,16,256]{2,1,0:T(8,128)S(1)}, u32[]{:S(2)}, u32[]{:S(2)}) async-start(f32[32,16,256]{2,1,0:T(8,128)} %broadcast_in_dim.156), calls=%async_computation | async-start | bytes 1048576 | tf_op jit(solution)/shard_map/all_to_all | solution.py:195
  56.6 0.1 reshape_squeeze.7
  56.6 0.1 reshape_squeeze.6
  56.7 0.7 add.129.lookup_ref
  57.5 11.5 %all-to-all-done = f32[32,16,256]{2,1,0:T(8,128)S(1)} async-done(((f32[32,16,256]{2,1,0:T(8,128)}), f32[32,16,256]{2,1,0:T(8,128)S(1)}, u32[]{:S(2)}, u32[]{:S(2)}) %all-to-all-start) | async-done | bytes 524320 | tf_op jit(solution)/shard_map/all_to_all | solution.py:195
  68.9 5.0 %fusion.32 = f32[32,256,128]{2,1,0:T(8,128)} fusion(f32[32,16,256]{2,1,0:T(8,128)S(1)} %all-to-all-done, s32[128]{0:T(128)S(1)} %get-tuple-element.29, s32[128]{0:T(128)S(1)} %get-tuple-element.30, pred[128]{0:T(512)(128)(4,1)S(1)} %compare_and_fusion), kind=kOutput, calls=%fused_computation.70 | convolution fusion | flops 201330688 | bytes 4719744 | tf_op jit(solution)/shard_map/dot_general | solution.py:134
  73.9 27.5 %shard_map.131 = f32[3072,128]{1,0:T(8,128)} custom-call(s32[24576]{0:T(1024)} %add.129.lookup_ref, f32[8192,128]{1,0:T(8,128)} %bitcast.56), custom_call_target="tpu_custom_call" | custom-call | bytes 5767168 | tf_op jit(solution)/shard_map/pallas_call | solution.py:141
  101.4 5.0 %fusion = f32[128,128]{1,0:T(8,128)S(1)} fusion(f32[24,128,128]{2,1,0:T(8,128)} %bitcast.57, f32[24,24]{1,0:T(8,128)S(1)} %copy-done.5), kind=kOutput, calls=%fused_computation.1 | convolution fusion | flops 114016256 | bytes 1640704 | tf_op jit(solution)/shard_map/ij,jab->iab/dot_general | solution.py:202
  106.4 0.1 copy.24
  106.5 0.1 copy.25
  106.6 0.1 reshape.250
  106.8 3.1 %select_reduce_fusion = f32[2048]{0:T(1024)S(1)} fusion(f32[128]{0:T(128)S(1)} %get-tuple-element.22, f32[128]{0:T(128)S(1)} %get-tuple-element.23, f32[128]{0:T(128)S(1)} %get-tuple-element.24, f32[128]{0:T(128)S(1)} %get-tuple-element.25, f32[128]{0:T(128)S(1)} %get-tuple-element.26, f32[128]{0:T(128)S(1)} %get-tuple-element.27, ...), kind=kLoop, calls=%fused_computation.13 | loop fusion | flops 4716544 | bytes 36864 | tf_op jit(solution)/shard_map/reduce_sum | solution.py:86
  109.9 0.7 all_to_all.10
  110.6 5.6 %all-to-all-start.1 = ((f32[32,1,64]{2,1,0:T(1,128)}), f32[32,1,64]{2,1,0:T(1,128)S(1)}, u32[]{:S(2)}, u32[]{:S(2)}) async-start(f32[32,1,64]{2,1,0:T(1,128)} %all_to_all.10), calls=%async_computation.1 | async-start | bytes 32768 | tf_op jit(solution)/shard_map/all_to_all | solution.py:208
  116.2 7.9 %all-to-all-done.1 = f32[32,1,64]{2,1,0:T(1,128)S(1)} async-done(((f32[32,1,64]{2,1,0:T(1,128)}), f32[32,1,64]{2,1,0:T(1,128)S(1)}, u32[]{:S(2)}, u32[]{:S(2)}) %all-to-all-start.1) | async-done | bytes 8224 | tf_op jit(solution)/shard_map/all_to_all | solution.py:208
  124.1 0.5 broadcast.351
  124.6 0.7 reduce.3
  125.3 0.1 broadcast_in_dim.173
  125.4 1.9 %convolution_multiply_fusion = f32[128,128]{1,0:T(8,128)S(1)} fusion(f32[2048]{0:T(1024)S(1)} %broadcast_in_dim.173, s32[2048]{0:T(1024)S(1)} %get-tuple-element.13, s32[2048]{0:T(1024)S(1)} %get-tuple-element.12, f32[1,1,128,128]{3,2,1,0:T(8,128)S(1)} %copy-done.10), kind=kOutput, calls=%fused_computation.6 | convolution fusion | flops 403456000 | bytes 155648 | tf_op jit(solution)/shard_map/dot_general | solution.py:100
  127.3 4.0 %collective-permute-start.8 = (f32[3,128]{1,0:T(4,128)S(1)}, f32[3,128]{1,0:T(4,128)S(1)}, u32[]{:S(2)}, u32[]{:S(2)}) collective-permute-start(f32[3,128]{1,0:T(4,128)S(1)} %get-tuple-element.10), channel_id=1, source_target_pairs={{0,1},{1,2},{2,3},{3,4},{4,5},{5,6},{6,7},{7,8},{8,9},{9,10},{10,1... | collective-permute-start | bytes 4616 | tf_op jit(solution)/shard_map/ppermute | solution.py:31
  131.2 1.9 %collective-permute-start.9 = (f32[3,128]{1,0:T(4,128)S(1)}, f32[3,128]{1,0:T(4,128)S(1)}, u32[]{:S(2)}, u32[]{:S(2)}) collective-permute-start(f32[3,128]{1,0:T(4,128)S(1)} %get-tuple-element.11), channel_id=1, source_target_pairs={{1,0},{2,1},{3,2},{4,3},{5,4},{6,5},{7,6},{8,7},{9,8},{10,9},{11,1... | collective-permute-start | bytes 4616 | tf_op jit(solution)/shard_map/ppermute | solution.py:33
  133.2 0.1 multiply_reduce_fusion
  133.3 5.6 %collective-permute-done.9 = f32[3,128]{1,0:T(4,128)S(1)} collective-permute-done((f32[3,128]{1,0:T(4,128)S(1)}, f32[3,128]{1,0:T(4,128)S(1)}, u32[]{:S(2)}, u32[]{:S(2)}) %collective-permute-start.9) | collective-permute-done | bytes 1568 | tf_op jit(solution)/shard_map/ppermute | solution.py:33
  138.8 1.0 fusion.2
  (46 shorter events, 0.4 us)
Async XLA Ops:
  0.6 1.0 copy-start
  2.9 6.1 %copy-start.7 = (s32[1,1,1024]{2,1,0:T(1,128)S(1)}, s32[1,1,1024]{2,1,0:T(1,128)}, u32[]{:S(2)}) copy-start(s32[1,1,1024]{2,1,0:T(1,128)} %param.16) | copy-start | bytes 12292
  3.9 3.1 %collective-permute-start = (f32[136,256]{1,0:T(8,128)S(1)}, f32[136,256]{1,0:T(8,128)S(1)}, u32[]{:S(2)}, u32[]{:S(2)}) collective-permute-start(f32[136,256]{1,0:T(8,128)S(1)} %get-tuple-element.9), channel_id=1, source_target_pairs={{0,32},{64,96},{128,160},{192,224},{256,288},{320,352},{384,416},{... | collective-permute-start | bytes 417800 | tf_op jit(solution)/shard_map/ppermute | solution.py:56
  5.7 2.3 %collective-permute-start.1 = (f32[136,256]{1,0:T(8,128)S(1)}, f32[136,256]{1,0:T(8,128)S(1)}, u32[]{:S(2)}, u32[]{:S(2)}) collective-permute-start(f32[136,256]{1,0:T(8,128)S(1)} %get-tuple-element.8), channel_id=1, source_target_pairs={{0,32},{64,96},{128,160},{192,224},{256,288},{320,352},{384,416},{... | collective-permute-start | bytes 417800 | tf_op jit(solution)/shard_map/ppermute | solution.py:56
  8.4 1.4 collective-permute-start.2
  9.1 0.9 collective-permute-start.3
  10.0 4.9 %copy-start.8 = (f32[8]{0:T(128)S(1)}, f32[8]{0:T(128)}, u32[]{:S(2)}) copy-start(f32[8]{0:T(128)} %param.23) | copy-start | bytes 100
  10.0 4.8 %copy-start.9 = (s32[8]{0:T(128)S(1)}, s32[8]{0:T(128)}, u32[]{:S(2)}) copy-start(s32[8]{0:T(128)} %param.22) | copy-start | bytes 100
  10.4 1.4 collective-permute-start.4
  11.1 1.7 %collective-permute-start.6 = (f32[136,256]{1,0:T(8,128)S(1)}, f32[136,256]{1,0:T(8,128)S(1)}, u32[]{:S(2)}, u32[]{:S(2)}) collective-permute-start(f32[136,256]{1,0:T(8,128)S(1)} %get-tuple-element.4), channel_id=1, source_target_pairs={{32,160},{96,224},{160,288},{224,352},{288,416},{352,480},{33,161}... | collective-permute-start | bytes 417800 | tf_op jit(solution)/shard_map/ppermute | solution.py:56
  12.0 44.5 %copy-start.1 = (s32[1,1,24,1024]{3,2,1,0:T(8,128)S(1)}, s32[1,1,24,1024]{3,2,1,0:T(8,128)}, u32[]{:S(2)}) copy-start(s32[1,1,24,1024]{3,2,1,0:T(8,128)} %param.17) | copy-start | bytes 294916
  12.1 1.2 collective-permute-start.5
  13.3 43.3 %copy-start.3 = (s32[1,1,32,64]{3,2,1,0:T(8,128)S(1)}, s32[1,1,32,64]{3,2,1,0:T(8,128)}, u32[]{:S(2)}) copy-start(s32[1,1,32,64]{3,2,1,0:T(8,128)} %param.19) | copy-start | bytes 24580
  13.3 43.4 %copy-start.4 = (s32[1,1,32,64]{3,2,1,0:T(8,128)S(1)}, s32[1,1,32,64]{3,2,1,0:T(8,128)}, u32[]{:S(2)}) copy-start(s32[1,1,32,64]{3,2,1,0:T(8,128)} %param.20) | copy-start | bytes 24580
  13.5 28.5 %collective-permute-start.7 = (f32[16,256]{1,0:T(8,128)S(1)}, f32[16,256]{1,0:T(8,128)S(1)}, u32[]{:S(2)}, u32[]{:S(2)}) collective-permute-start(f32[16,256]{1,0:T(8,128)S(1)} %convolution_add_fusion.1), channel_id=1, source_target_pairs={{32,64},{96,128},{160,192},{224,256},{288,320},{352,384},{416,448}... | collective-permute-start | bytes 49160 | tf_op jit(solution)/shard_map/ppermute | solution.py:72
  42.2 31.7 %copy-start.2 = (f32[16,256]{1,0:T(8,128)}, f32[16,256]{1,0:T(8,128)S(1)}, u32[]{:S(2)}) copy-start(f32[16,256]{1,0:T(8,128)S(1)} %convolution_add_fusion) | copy-start | bytes 49156
  43.1 25.9 %all-to-all-start = ((f32[32,16,256]{2,1,0:T(8,128)}), f32[32,16,256]{2,1,0:T(8,128)S(1)}, u32[]{:S(2)}, u32[]{:S(2)}) async-start(f32[32,16,256]{2,1,0:T(8,128)} %broadcast_in_dim.156), calls=%async_computation | async-start | bytes 1048576 | tf_op jit(solution)/shard_map/all_to_all | solution.py:195
  73.9 27.5 %copy-start.5 = (f32[24,24]{1,0:T(8,128)S(1)}, f32[24,24]{1,0:T(8,128)}, u32[]{:S(2)}) copy-start(f32[24,24]{1,0:T(8,128)} %param.15) | copy-start | bytes 6916
  101.4 5.3 %copy-start.6 = (f32[1,1,1024]{2,1,0:T(1,128)S(1)}, f32[1,1,1024]{2,1,0:T(1,128)}, u32[]{:S(2)}) copy-start(f32[1,1,1024]{2,1,0:T(1,128)} %param.18) | copy-start | bytes 12292
  101.4 24.0 %copy-start.10 = (f32[1,1,128,128]{3,2,1,0:T(8,128)S(1)}, f32[1,1,128,128]{3,2,1,0:T(8,128)}, u32[]{:S(2)}) copy-start(f32[1,1,128,128]{3,2,1,0:T(8,128)} %param.21) | copy-start | bytes 196612
  110.6 13.5 %all-to-all-start.1 = ((f32[32,1,64]{2,1,0:T(1,128)}), f32[32,1,64]{2,1,0:T(1,128)S(1)}, u32[]{:S(2)}, u32[]{:S(2)}) async-start(f32[32,1,64]{2,1,0:T(1,128)} %all_to_all.10), calls=%async_computation.1 | async-start | bytes 32768 | tf_op jit(solution)/shard_map/all_to_all | solution.py:208
  127.3 6.0 %collective-permute-start.8 = (f32[3,128]{1,0:T(4,128)S(1)}, f32[3,128]{1,0:T(4,128)S(1)}, u32[]{:S(2)}, u32[]{:S(2)}) collective-permute-start(f32[3,128]{1,0:T(4,128)S(1)} %get-tuple-element.10), channel_id=1, source_target_pairs={{0,1},{1,2},{2,3},{3,4},{4,5},{5,6},{6,7},{7,8},{8,9},{9,10},{10,1... | collective-permute-start | bytes 4616 | tf_op jit(solution)/shard_map/ppermute | solution.py:31
  131.2 7.6 %collective-permute-start.9 = (f32[3,128]{1,0:T(4,128)S(1)}, f32[3,128]{1,0:T(4,128)S(1)}, u32[]{:S(2)}, u32[]{:S(2)}) collective-permute-start(f32[3,128]{1,0:T(4,128)S(1)} %get-tuple-element.11), channel_id=1, source_target_pairs={{1,0},{2,1},{3,2},{4,3},{5,4},{6,5},{7,6},{8,7},{9,8},{10,9},{11,1... | collective-permute-start | bytes 4616 | tf_op jit(solution)/shard_map/ppermute | solution.py:33

commit v9 on v8

--- a/solution.py
+++ b/solution.py
@@ -87,16 +87,12 @@
     return chosen.reshape(index.shape)
 
 
-def scattered(values, targets, row_count):
+def scattered(values, rows, cols, row_count):
     lanes = 128
-    flat_values = values.reshape(-1)
-    flat_targets = targets.reshape(-1)
-    row = jnp.where(flat_targets >= 0, flat_targets // lanes, -1)
-    col = flat_targets % lanes
     row_ids = lax.broadcasted_iota(jnp.int32, (1, row_count), 1)
     lane_ids = lax.broadcasted_iota(jnp.int32, (1, lanes), 1)
-    rows_hot = (row[:, None] == row_ids).astype(jnp.float32)
-    cols_hot = jnp.where(col[:, None] == lane_ids, flat_values[:, None], 0.0)
+    rows_hot = (rows[:, None] == row_ids).astype(jnp.float32)
+    cols_hot = jnp.where(cols[:, None] == lane_ids, values[:, None], 0.0)
     return lax.dot_general(
         rows_hot,
         cols_hot,
@@ -104,6 +100,12 @@
         precision=exact_mode,
         preferred_element_type=jnp.float32,
     )
+
+
+def padded_targets(cells, first, last, shift):
+    row = cells // 128
+    keep = (cells >= 0) & (row >= first) & (row < last)
+    return jnp.where(keep, row + shift, -1).reshape(-1), (cells % 128).reshape(-1)
 
 
 def gather_kernel(lookup_ref, table_ref, out_ref):
@@ -204,13 +206,39 @@
     energy = energy.reshape(elements)
     density = element_density[0, 0]
     sensitivity = -penalty * density * density * energy * energy_scale
-    outgoing = picked(sensitivity, send_elements[0, 0])
-    received = lax.all_to_all(outgoing, "dev", split_axis=0, concat_axis=0, tiled=True)
     owned = design_density[0, 0]
     row_count = owned.shape[0]
-    collected = scattered(received, receive_cells[0, 0], row_count)
-    weighted = owned * collected
-    padded = padded_2(weighted, (("dev", 0),), RADIUS)
+    count = lax.axis_size("dev")
+    cells = receive_cells[0, 0]
+    sources, slots = cells.shape
+    shared = cells.astype(jnp.float32).reshape(-1, 128)
+    from_left = lax.ppermute(
+        jnp.concatenate([shared, owned[row_count - RADIUS :]], axis=0), "dev", [(i, i + 1) for i in range(count - 1)]
+    )
+    from_right = lax.ppermute(
+        jnp.concatenate([shared, owned[:RADIUS]], axis=0), "dev", [(i + 1, i) for i in range(count - 1)]
+    )
+    list_rows = shared.shape[0]
+    cells_left = from_left[:list_rows].astype(jnp.int32).reshape(sources, slots)
+    cells_right = from_right[:list_rows].astype(jnp.int32).reshape(sources, slots)
+    density_rows = jnp.concatenate([from_left[list_rows:], owned, from_right[list_rows:]], axis=0)
+
+    outgoing = picked(sensitivity, send_elements[0, 0])
+    edge = jnp.zeros((1, slots), jnp.float32)
+    spread_out = jnp.concatenate([edge, outgoing, edge], axis=0)
+    owners = outgoing.shape[0]
+    triple = jnp.stack([spread_out[0:owners], spread_out[1 : owners + 1], spread_out[2 : owners + 2]], axis=1)
+    received = lax.all_to_all(triple, "dev", split_axis=0, concat_axis=0, tiled=True)
+    left_rows, left_cols = padded_targets(cells_left, row_count - RADIUS, row_count, RADIUS - row_count)
+    own_rows, own_cols = padded_targets(cells, 0, row_count, RADIUS)
+    right_rows, right_cols = padded_targets(cells_right, 0, RADIUS, row_count + RADIUS)
+    collected = scattered(
+        jnp.concatenate([received[:, 0].reshape(-1), received[:, 1].reshape(-1), received[:, 2].reshape(-1)]),
+        jnp.concatenate([left_rows, own_rows, right_rows]),
+        jnp.concatenate([left_cols, own_cols, right_cols]),
+        row_count + 2 * RADIUS,
+    )
+    padded = density_rows * collected
     total_rows = lax.axis_size("dev") * row_count
     padded_rows = padded.shape[0]
     reach = (

time: 141 us -> 141 us (level)
  the two profiles are of different devices: /device:TPU:46 before, /device:TPU:40 now
where the time goes in v9:
time: 141 us; the launch traced here: 140 us
  waiting for transfers between devices  48.2 us (34%)
  starting transfers between devices  31.6 us (22%)
  Pallas kernels  27.5 us (20%)
  matrix products  18.2 us (13%)
  other arithmetic  6.57 us (5%)
  local copies, waits for them, and re-layouts  6.37 us (5%)
    pallas_call x1, Pallas kernels, gathered_rows(): pl.pallas_call(gather_kernel, out_shape=jax.ShapeDtypeStruct((out_rows, 1...  27.5 us
    ppermute x1, waiting for transfers between devices, interface_chain(): lax.ppermute(offset, 'grp', [(g, g + 1) for g in range(1, levels - 1, 2)])  25.6 us
    all_to_all x1, starting transfers between devices, on_device(): lax.all_to_all(copies, 'dev', split_axis=0, concat_axis=0, tiled=True)  14.9 us
    all_to_all x1, waiting for transfers between devices, on_device(): lax.all_to_all(copies, 'dev', split_axis=0, concat_axis=0, tiled=True)  13 us
    all_to_all x1, waiting for transfers between devices, on_device(): lax.all_to_all(triple, 'dev', split_axis=0, concat_axis=0, tiled=True)  9.61 us
    dot_general x11, matrix products, product(): jnp.dot(left, right, precision=exact_mode, preferred_element_type=jnp.flo...  5.41 us
    dot_general x1, matrix products, on_device(): forces = jnp.einsum('ij,jab->iab', stiffness, motion, precision=exact_mode)  5.02 us
    dot_general x1, matrix products, gathered_rows(): lax.dot_general(panels, spread, (((1,), (0,)), ((), ())), precision=exact...  4.97 us
  transfers between devices with their start and end apart: 12, of which 3 were waited for; matrix products, arithmetic and copies ran while one was open for 6% of the time, Pallas kernels for 0%

profile of v9, /device:TPU:40, one launch (start us, length us, event | category | flops | bytes accessed | tf_op | source)
XLA Modules:
  0.0 139.7 jit_solution(846800121153518392)
XLA Ops:
  0.7 0.9 copy-done
  1.6 1.3 convolution_negate_fusion
  2.9 0.9 fusion.17
  3.9 1.7 %collective-permute-start = (f32[136,256]{1,0:T(8,128)S(1)}, f32[136,256]{1,0:T(8,128)S(1)}, u32[]{:S(2)}, u32[]{:S(2)}) collective-permute-start(f32[136,256]{1,0:T(8,128)S(1)} %get-tuple-element.16), channel_id=1, source_target_pairs={{0,32},{64,96},{128,160},{192,224},{256,288},{320,352},{384,416},{... | collective-permute-start | bytes 417800 | tf_op jit(solution)/shard_map/ppermute | solution.py:56
  5.7 1.3 collective-permute-start.1
  7.0 0.7 slice_bitcast_fusion.1
  7.7 0.7 convert_element_type.22
  8.5 3.4 %collective-permute-start.8 = (f32[19,128]{1,0:T(8,128)S(1)}, f32[19,128]{1,0:T(8,128)S(1)}, u32[]{:S(2)}, u32[]{:S(2)}) collective-permute-start(f32[19,128]{1,0:T(8,128)S(1)} %get-tuple-element.30), channel_id=1, source_target_pairs={{0,1},{1,2},{2,3},{3,4},{4,5},{5,6},{6,7},{7,8},{8,9},{9,10},{10,1... | collective-permute-start | bytes 29192 | tf_op jit(solution)/shard_map/ppermute | solution.py:215
  11.9 1.3 collective-permute-start.9
  13.2 0.8 squeeze.25
  14.0 0.7 broadcast_multiply_fusion
  14.7 0.8 reshape_squeeze.12
  15.5 0.2 convolution_add_fusion.4
  15.8 0.4 fusion.13
  16.2 0.7 collective-permute-start.2
  16.9 0.7 collective-permute-start.3
  17.6 0.2 convolution_add_fusion.3
  17.8 0.4 fusion.11
  18.2 0.7 collective-permute-start.4
  19.0 0.2 select_reduce_fusion.1
  19.2 0.7 collective-permute-start.6
  19.9 0.2 convolution_add_fusion.2
  20.1 0.7 collective-permute-start.5
  20.8 0.4 fusion.9
  21.2 0.2 convolution_add_fusion.1
  21.4 1.3 collective-permute-start.7
  22.7 0.1 multiply_reduce_fusion
  22.8 25.6 %collective-permute-done.7 = f32[16,256]{1,0:T(8,128)S(1)} collective-permute-done((f32[16,256]{1,0:T(8,128)S(1)}, f32[16,256]{1,0:T(8,128)S(1)}, u32[]{:S(2)}, u32[]{:S(2)}) %collective-permute-start.7) | collective-permute-done | bytes 16416 | tf_op jit(solution)/shard_map/ppermute | solution.py:72
  48.4 0.2 convolution_add_fusion
  48.6 0.9 broadcast_in_dim.160
  49.5 14.9 %all-to-all-start = ((f32[32,16,256]{2,1,0:T(8,128)}), f32[32,16,256]{2,1,0:T(8,128)S(1)}, u32[]{:S(2)}, u32[]{:S(2)}) async-start(f32[32,16,256]{2,1,0:T(8,128)} %broadcast_in_dim.160), calls=%async_computation | async-start | bytes 1048576 | tf_op jit(solution)/shard_map/all_to_all | solution.py:197
  64.5 0.7 add.168.lookup_ref
  65.2 13.0 %all-to-all-done = f32[32,16,256]{2,1,0:T(8,128)S(1)} async-done(((f32[32,16,256]{2,1,0:T(8,128)}), f32[32,16,256]{2,1,0:T(8,128)S(1)}, u32[]{:S(2)}, u32[]{:S(2)}) %all-to-all-start) | async-done | bytes 524320 | tf_op jit(solution)/shard_map/all_to_all | solution.py:197
  78.2 5.0 %fusion.35 = f32[32,256,128]{2,1,0:T(8,128)} fusion(f32[32,16,256]{2,1,0:T(8,128)S(1)} %all-to-all-done, s32[128]{0:T(128)S(1)} %get-tuple-element.42, s32[128]{0:T(128)S(1)} %get-tuple-element.43, pred[128]{0:T(512)(128)(4,1)S(1)} %compare_and_fusion), kind=kOutput, calls=%fused_computation.100 | convolution fusion | flops 201330688 | bytes 4719744 | tf_op jit(solution)/shard_map/dot_general | solution.py:136
  83.2 27.5 %shard_map.131 = f32[3072,128]{1,0:T(8,128)} custom-call(s32[24576]{0:T(1024)} %add.168.lookup_ref, f32[8192,128]{1,0:T(8,128)} %bitcast.104), custom_call_target="tpu_custom_call" | custom-call | bytes 5767168 | tf_op jit(solution)/shard_map/pallas_call | solution.py:143
  110.7 5.0 %fusion.3 = f32[128,128]{1,0:T(8,128)S(1)} fusion(f32[24,128,128]{2,1,0:T(8,128)} %bitcast.105, f32[24,24]{1,0:T(8,128)S(1)} %copy-done.5), kind=kOutput, calls=%fused_computation.6 | convolution fusion | flops 114016256 | bytes 1640704 | tf_op jit(solution)/shard_map/ij,jab->iab/dot_general | solution.py:204
  115.7 0.1 copy.25
  115.8 0.1 copy.26
  115.9 0.1 reshape.221
  116.1 3.1 %select_reduce_fusion = f32[2048]{0:T(1024)S(1)} fusion(f32[128]{0:T(128)S(1)} %get-tuple-element.33, f32[128]{0:T(128)S(1)} %get-tuple-element.34, f32[128]{0:T(128)S(1)} %get-tuple-element.35, f32[128]{0:T(128)S(1)} %get-tuple-element.36, f32[128]{0:T(128)S(1)} %get-tuple-element.37, f32[128]{0:T(128)S(1)} %get-tuple-element.38, ...), kind=kLoop, calls=%fused_computation.19 | loop fusion | flops 4716544 | bytes 36864 | tf_op jit(solution)/shard_map/reduce_sum | solution.py:86
  119.4 0.7 reshape.242
  120.1 4.4 %all-to-all-start.1 = ((f32[32,1,192]{2,1,0:T(1,128)}), f32[32,1,192]{2,1,0:T(1,128)S(1)}, u32[]{:S(2)}, u32[]{:S(2)}) async-start(f32[32,1,192]{2,1,0:T(1,128)} %reshape.242), calls=%async_computation.1 | async-start | bytes 65536 | tf_op jit(solution)/shard_map/all_to_all | solution.py:231
  124.6 9.6 %all-to-all-done.1 = f32[32,1,192]{2,1,0:T(1,128)S(1)} async-done(((f32[32,1,192]{2,1,0:T(1,128)}), f32[32,1,192]{2,1,0:T(1,128)S(1)}, u32[]{:S(2)}, u32[]{:S(2)}) %all-to-all-start.1) | async-done | bytes 24608 | tf_op jit(solution)/shard_map/all_to_all | solution.py:231
  134.2 0.5 broadcast.407
  134.7 0.7 reduce.12
  135.5 0.1 slice_reduce_fusion.2
  135.9 2.8 %fusion = f32[134,128]{1,0:T(8,128)S(1)} fusion(s32[6144]{0:T(1024)S(1)} %get-tuple-element.40, f32[6144]{0:T(1024)S(1)} %pad_maximum_fusion.10, s32[6144]{0:T(1024)S(1)} %get-tuple-element.41), kind=kOutput, calls=%fused_computation.1 | convolution fusion | flops 1266978816 | bytes 142336 | tf_op jit(solution)/shard_map/dot_general | solution.py:96
  138.7 1.0 fusion.8
  (65 shorter events, 1.0 us)
Async XLA Ops:
  0.6 1.0 copy-start
  0.6 18.3 %copy-start.8 = (s32[8]{0:T(128)S(1)}, s32[8]{0:T(128)}, u32[]{:S(2)}) copy-start(s32[8]{0:T(128)} %param.22) | copy-start | bytes 100
  0.7 18.3 %copy-start.7 = (f32[8]{0:T(128)S(1)}, f32[8]{0:T(128)}, u32[]{:S(2)}) copy-start(f32[8]{0:T(128)} %param.23) | copy-start | bytes 100
  3.9 11.6 %collective-permute-start = (f32[136,256]{1,0:T(8,128)S(1)}, f32[136,256]{1,0:T(8,128)S(1)}, u32[]{:S(2)}, u32[]{:S(2)}) collective-permute-start(f32[136,256]{1,0:T(8,128)S(1)} %get-tuple-element.16), channel_id=1, source_target_pairs={{0,32},{64,96},{128,160},{192,224},{256,288},{320,352},{384,416},{... | collective-permute-start | bytes 417800 | tf_op jit(solution)/shard_map/ppermute | solution.py:56
  5.7 10.1 %collective-permute-start.1 = (f32[136,256]{1,0:T(8,128)S(1)}, f32[136,256]{1,0:T(8,128)S(1)}, u32[]{:S(2)}, u32[]{:S(2)}) collective-permute-start(f32[136,256]{1,0:T(8,128)S(1)} %get-tuple-element.15), channel_id=1, source_target_pairs={{0,32},{64,96},{128,160},{192,224},{256,288},{320,352},{384,416},{... | collective-permute-start | bytes 417800 | tf_op jit(solution)/shard_map/ppermute | solution.py:56
  8.5 56.7 %collective-permute-start.8 = (f32[19,128]{1,0:T(8,128)S(1)}, f32[19,128]{1,0:T(8,128)S(1)}, u32[]{:S(2)}, u32[]{:S(2)}) collective-permute-start(f32[19,128]{1,0:T(8,128)S(1)} %get-tuple-element.30), channel_id=1, source_target_pairs={{0,1},{1,2},{2,3},{3,4},{4,5},{5,6},{6,7},{7,8},{8,9},{9,10},{10,1... | collective-permute-start | bytes 29192 | tf_op jit(solution)/shard_map/ppermute | solution.py:215
  11.9 53.3 %collective-permute-start.9 = (f32[19,128]{1,0:T(8,128)S(1)}, f32[19,128]{1,0:T(8,128)S(1)}, u32[]{:S(2)}, u32[]{:S(2)}) collective-permute-start(f32[19,128]{1,0:T(8,128)S(1)} %get-tuple-element.31), channel_id=1, source_target_pairs={{1,0},{2,1},{3,2},{4,3},{5,4},{6,5},{7,6},{8,7},{9,8},{10,9},{11,1... | collective-permute-start | bytes 29192 | tf_op jit(solution)/shard_map/ppermute | solution.py:218
  16.1 48.3 %copy-start.1 = (s32[1,1,24,1024]{3,2,1,0:T(8,128)S(1)}, s32[1,1,24,1024]{3,2,1,0:T(8,128)}, u32[]{:S(2)}) copy-start(s32[1,1,24,1024]{3,2,1,0:T(8,128)} %param.17) | copy-start | bytes 294916
  16.2 1.4 collective-permute-start.2
  16.9 0.9 collective-permute-start.3
  18.2 1.6 %collective-permute-start.4 = (f32[136,256]{1,0:T(8,128)S(1)}, f32[136,256]{1,0:T(8,128)S(1)}, u32[]{:S(2)}, u32[]{:S(2)}) collective-permute-start(f32[136,256]{1,0:T(8,128)S(1)} %get-tuple-element.12), channel_id=1, source_target_pairs={{32,160},{96,224},{160,288},{224,352},{288,416},{352,480},{33,161}... | collective-permute-start | bytes 417800 | tf_op jit(solution)/shard_map/ppermute | solution.py:56
  19.2 1.6 %collective-permute-start.6 = (f32[136,256]{1,0:T(8,128)S(1)}, f32[136,256]{1,0:T(8,128)S(1)}, u32[]{:S(2)}, u32[]{:S(2)}) collective-permute-start(f32[136,256]{1,0:T(8,128)S(1)} %get-tuple-element.11), channel_id=1, source_target_pairs={{32,160},{96,224},{160,288},{224,352},{288,416},{352,480},{33,161}... | collective-permute-start | bytes 417800 | tf_op jit(solution)/shard_map/ppermute | solution.py:56
  20.1 1.1 collective-permute-start.5
  21.4 27.0 %collective-permute-start.7 = (f32[16,256]{1,0:T(8,128)S(1)}, f32[16,256]{1,0:T(8,128)S(1)}, u32[]{:S(2)}, u32[]{:S(2)}) collective-permute-start(f32[16,256]{1,0:T(8,128)S(1)} %convolution_add_fusion.1), channel_id=1, source_target_pairs={{32,64},{96,128},{160,192},{224,256},{288,320},{352,384},{416,448}... | collective-permute-start | bytes 49160 | tf_op jit(solution)/shard_map/ppermute | solution.py:72
  48.6 34.6 %copy-start.2 = (f32[16,256]{1,0:T(8,128)}, f32[16,256]{1,0:T(8,128)S(1)}, u32[]{:S(2)}) copy-start(f32[16,256]{1,0:T(8,128)S(1)} %convolution_add_fusion) | copy-start | bytes 49156
  49.5 28.7 %all-to-all-start = ((f32[32,16,256]{2,1,0:T(8,128)}), f32[32,16,256]{2,1,0:T(8,128)S(1)}, u32[]{:S(2)}, u32[]{:S(2)}) async-start(f32[32,16,256]{2,1,0:T(8,128)} %broadcast_in_dim.160), calls=%async_computation | async-start | bytes 1048576 | tf_op jit(solution)/shard_map/all_to_all | solution.py:197
  65.1 59.4 %copy-start.3 = (f32[19,128]{1,0:T(8,128)}, f32[19,128]{1,0:T(8,128)S(1)}, u32[]{:S(2)}) copy-start(f32[19,128]{1,0:T(8,128)S(1)} %collective-permute-done.8) | copy-start | bytes 29188
  65.2 59.4 %copy-start.4 = (f32[19,128]{1,0:T(8,128)}, f32[19,128]{1,0:T(8,128)S(1)}, u32[]{:S(2)}) copy-start(f32[19,128]{1,0:T(8,128)S(1)} %collective-permute-done.9) | copy-start | bytes 29188
  83.2 27.5 %copy-start.5 = (f32[24,24]{1,0:T(8,128)S(1)}, f32[24,24]{1,0:T(8,128)}, u32[]{:S(2)}) copy-start(f32[24,24]{1,0:T(8,128)} %param.15) | copy-start | bytes 6916
  83.2 32.8 %copy-start.6 = (f32[1,1,1024]{2,1,0:T(1,128)S(1)}, f32[1,1,1024]{2,1,0:T(1,128)}, u32[]{:S(2)}) copy-start(f32[1,1,1024]{2,1,0:T(1,128)} %param.18) | copy-start | bytes 12292
  110.7 28.0 %copy-start.9 = (f32[1,1,128,128]{3,2,1,0:T(8,128)S(1)}, f32[1,1,128,128]{3,2,1,0:T(8,128)}, u32[]{:S(2)}) copy-start(f32[1,1,128,128]{3,2,1,0:T(8,128)} %param.21) | copy-start | bytes 196612
  120.1 14.0 %all-to-all-start.1 = ((f32[32,1,192]{2,1,0:T(1,128)}), f32[32,1,192]{2,1,0:T(1,128)S(1)}, u32[]{:S(2)}, u32[]{:S(2)}) async-start(f32[32,1,192]{2,1,0:T(1,128)} %reshape.242), calls=%async_computation.1 | async-start | bytes 65536 | tf_op jit(solution)/shard_map/all_to_all | solution.py:231
  124.5 14.1 %slice-start = ((f32[19,128]{1,0:T(8,128)}), f32[3,128]{1,0:T(4,128)S(1)}, s32[]{:S(2)}) async-start(f32[19,128]{1,0:T(8,128)} %copy-done.3), calls=%async_computation.2 | async-start | bytes 4096 | tf_op jit(solution)/shard_map/slice | solution.py:224
  124.6 14.1 %slice-start.1 = ((f32[19,128]{1,0:T(8,128)}), f32[3,128]{1,0:T(4,128)S(1)}, s32[]{:S(2)}) async-start(f32[19,128]{1,0:T(8,128)} %copy-done.4), calls=%async_computation.3 | async-start | bytes 4096 | tf_op jit(solution)/shard_map/slice | solution.py:224

commit v10 on v9

--- a/solution.py
+++ b/solution.py
@@ -212,12 +212,11 @@
     cells = receive_cells[0, 0]
     sources, slots = cells.shape
     shared = cells.astype(jnp.float32).reshape(-1, 128)
-    from_left = lax.ppermute(
-        jnp.concatenate([shared, owned[row_count - RADIUS :]], axis=0), "dev", [(i, i + 1) for i in range(count - 1)]
-    )
-    from_right = lax.ppermute(
-        jnp.concatenate([shared, owned[:RADIUS]], axis=0), "dev", [(i + 1, i) for i in range(count - 1)]
-    )
+    to_right = jnp.concatenate([shared, owned[row_count - RADIUS :]], axis=0)
+    to_left = jnp.concatenate([shared, owned[:RADIUS]], axis=0)
+    to_right, to_left, _ = lax.optimization_barrier((to_right, to_left, solved))
+    from_left = lax.ppermute(to_right, "dev", [(i, i + 1) for i in range(count - 1)])
+    from_right = lax.ppermute(to_left, "dev", [(i + 1, i) for i in range(count - 1)])
     list_rows = shared.shape[0]
     cells_left = from_left[:list_rows].astype(jnp.int32).reshape(sources, slots)
     cells_right = from_right[:list_rows].astype(jnp.int32).reshape(sources, slots)

time: 141 us -> 138 us (0.979)
  waiting for transfers between devices: 48.2 us -> 43.7 us
  starting transfers between devices: 31.6 us -> 33.9 us
    all_to_all x1, waiting for transfers between devices: 13 us -> 3.77 us  [on_device(): lax.all_to_all(copies, 'dev', split_axis=0, concat_axis=0, tiled=True)]
    ppermute x2, waiting for transfers between devices: 0.01 us -> 4.23 us  [the longest x1 4.23 us: on_device(): lax.ppermute(to_left, 'dev', [(i + 1, i) for i in range(count - 1)])]
    all_to_all x1, starting transfers between devices: 4.36 us -> 8.02 us  [on_device(): lax.all_to_all(triple, 'dev', split_axis=0, concat_axis=0, tiled=True)]
    all_to_all x1, starting transfers between devices: 14.9 us -> 13.2 us  [on_device(): lax.all_to_all(copies, 'dev', split_axis=0, concat_axis=0, tiled=True)]
  transfers between devices with their start and end apart: 12 -> 12, of which waited for: 3 -> 4; matrix products, arithmetic and copies ran while one was open for 6% -> 4% of each run, Pallas kernels for 0% -> 0%
where the time goes in v10:
time: 138 us; the launch traced here: 137 us
  waiting for transfers between devices  43.7 us (32%)
  starting transfers between devices  33.9 us (25%)
  Pallas kernels  27.5 us (20%)
  matrix products  18.2 us (13%)
  local copies, waits for them, and re-layouts  6.39 us (5%)
  other arithmetic  5.85 us (4%)
    pallas_call x1, Pallas kernels, gathered_rows(): pl.pallas_call(gather_kernel, out_shape=jax.ShapeDtypeStruct((out_rows, 1...  27.5 us
    ppermute x1, waiting for transfers between devices, interface_chain(): lax.ppermute(offset, 'grp', [(g, g + 1) for g in range(1, levels - 1, 2)])  26 us
    all_to_all x1, starting transfers between devices, on_device(): lax.all_to_all(copies, 'dev', split_axis=0, concat_axis=0, tiled=True)  13.2 us
    all_to_all x1, waiting for transfers between devices, on_device(): lax.all_to_all(triple, 'dev', split_axis=0, concat_axis=0, tiled=True)  9.61 us
    all_to_all x1, starting transfers between devices, on_device(): lax.all_to_all(triple, 'dev', split_axis=0, concat_axis=0, tiled=True)  8.02 us
    dot_general x11, matrix products, product(): jnp.dot(left, right, precision=exact_mode, preferred_element_type=jnp.flo...  5.4 us
    dot_general x1, matrix products, on_device(): forces = jnp.einsum('ij,jab->iab', stiffness, motion, precision=exact_mode)  5.02 us
    dot_general x1, matrix products, gathered_rows(): lax.dot_general(panels, spread, (((1,), (0,)), ((), ())), precision=exact...  4.99 us
  transfers between devices with their start and end apart: 12, of which 4 were waited for; matrix products, arithmetic and copies ran while one was open for 4% of the time, Pallas kernels for 0%

profile of v10, /device:TPU:40, one launch (start us, length us, event | category | flops | bytes accessed | tf_op | source)
XLA Modules:
  0.0 136.8 jit_solution(5676237972766064980)
XLA Ops:
  0.7 0.9 copy-done
  1.6 1.3 convolution_negate_fusion
  3.0 0.9 fusion.17
  3.9 1.7 %collective-permute-start = (f32[136,256]{1,0:T(8,128)S(1)}, f32[136,256]{1,0:T(8,128)S(1)}, u32[]{:S(2)}, u32[]{:S(2)}) collective-permute-start(f32[136,256]{1,0:T(8,128)S(1)} %get-tuple-element.20), channel_id=1, source_target_pairs={{0,32},{64,96},{128,160},{192,224},{256,288},{320,352},{384,416},{... | collective-permute-start | bytes 417800 | tf_op jit(solution)/shard_map/ppermute | solution.py:56
  5.7 1.3 collective-permute-start.1
  7.0 0.8 reshape_squeeze.12
  7.8 0.7 broadcast_multiply_fusion
  8.5 0.8 squeeze.25
  9.3 0.7 slice_bitcast_fusion
  10.1 0.2 convolution_add_fusion.4
  10.3 0.4 fusion.13
  10.7 0.7 collective-permute-start.2
  11.4 0.2 select_reduce_fusion.1
  11.7 0.7 collective-permute-start.3
  12.4 0.2 convolution_add_fusion.3
  12.6 0.4 fusion.11
  13.0 0.7 collective-permute-start.4
  13.8 0.1 multiply_reduce_fusion
  13.9 0.7 collective-permute-start.6
  14.6 0.2 convolution_add_fusion.2
  14.8 0.7 collective-permute-start.5
  15.5 0.4 fusion.9
  15.9 0.2 convolution_add_fusion.1
  16.1 1.3 collective-permute-start.7
  17.4 26.0 %collective-permute-done.7 = f32[16,256]{1,0:T(8,128)S(1)} collective-permute-done((f32[16,256]{1,0:T(8,128)S(1)}, f32[16,256]{1,0:T(8,128)S(1)}, u32[]{:S(2)}, u32[]{:S(2)}) %collective-permute-start.7) | collective-permute-done | bytes 16416 | tf_op jit(solution)/shard_map/ppermute | solution.py:72
  43.5 0.2 convolution_add_fusion
  43.7 0.8 broadcast_in_dim.160
  44.6 13.2 %all-to-all-start = ((f32[32,16,256]{2,1,0:T(8,128)}), f32[32,16,256]{2,1,0:T(8,128)S(1)}, u32[]{:S(2)}, u32[]{:S(2)}) async-start(f32[32,16,256]{2,1,0:T(8,128)} %broadcast_in_dim.160), calls=%async_computation | async-start | bytes 1048576 | tf_op jit(solution)/shard_map/all_to_all | solution.py:197
  57.7 3.7 %collective-permute-start.8 = (f32[19,128]{1,0:T(8,128)S(1)}, f32[19,128]{1,0:T(8,128)S(1)}, u32[]{:S(2)}, u32[]{:S(2)}) collective-permute-start(f32[19,128]{1,0:T(8,128)S(1)} %get-tuple-element.4), channel_id=1, source_target_pairs={{0,1},{1,2},{2,3},{3,4},{4,5},{5,6},{6,7},{7,8},{8,9},{9,10},{10,1... | collective-permute-start | bytes 29192 | tf_op jit(solution)/shard_map/ppermute | solution.py:218
  61.5 0.7 add.168.lookup_ref
  62.2 1.3 collective-permute-start.9
  63.5 4.2 %collective-permute-done.9 = f32[19,128]{1,0:T(8,128)S(1)} collective-permute-done((f32[19,128]{1,0:T(8,128)S(1)}, f32[19,128]{1,0:T(8,128)S(1)}, u32[]{:S(2)}, u32[]{:S(2)}) %collective-permute-start.9) | collective-permute-done | bytes 9760 | tf_op jit(solution)/shard_map/ppermute | solution.py:219
  67.8 3.8 %all-to-all-done = f32[32,16,256]{2,1,0:T(8,128)S(1)} async-done(((f32[32,16,256]{2,1,0:T(8,128)}), f32[32,16,256]{2,1,0:T(8,128)S(1)}, u32[]{:S(2)}, u32[]{:S(2)}) %all-to-all-start) | async-done | bytes 524320 | tf_op jit(solution)/shard_map/all_to_all | solution.py:197
  71.6 5.0 %fusion.35 = f32[32,256,128]{2,1,0:T(8,128)} fusion(f32[32,16,256]{2,1,0:T(8,128)S(1)} %all-to-all-done, s32[128]{0:T(128)S(1)} %get-tuple-element.46, s32[128]{0:T(128)S(1)} %get-tuple-element.47, pred[128]{0:T(512)(128)(4,1)S(1)} %compare_and_fusion), kind=kOutput, calls=%fused_computation.100 | convolution fusion | flops 201330688 | bytes 4719744 | tf_op jit(solution)/shard_map/dot_general | solution.py:136
  76.6 27.5 %shard_map.131 = f32[3072,128]{1,0:T(8,128)} custom-call(s32[24576]{0:T(1024)} %add.168.lookup_ref, f32[8192,128]{1,0:T(8,128)} %bitcast.104), custom_call_target="tpu_custom_call" | custom-call | bytes 5767168 | tf_op jit(solution)/shard_map/pallas_call | solution.py:143
  104.0 5.0 %fusion.3 = f32[128,128]{1,0:T(8,128)S(1)} fusion(f32[24,128,128]{2,1,0:T(8,128)} %bitcast.105, f32[24,24]{1,0:T(8,128)S(1)} %copy-done.6), kind=kOutput, calls=%fused_computation.6 | convolution fusion | flops 114016256 | bytes 1640704 | tf_op jit(solution)/shard_map/ij,jab->iab/dot_general | solution.py:204
  109.1 0.1 copy.25
  109.2 0.1 copy.26
  109.3 0.1 reshape.221
  109.4 3.1 %select_reduce_fusion = f32[2048]{0:T(1024)S(1)} fusion(f32[128]{0:T(128)S(1)} %get-tuple-element.37, f32[128]{0:T(128)S(1)} %get-tuple-element.38, f32[128]{0:T(128)S(1)} %get-tuple-element.39, f32[128]{0:T(128)S(1)} %get-tuple-element.40, f32[128]{0:T(128)S(1)} %get-tuple-element.41, f32[128]{0:T(128)S(1)} %get-tuple-element.42, ...), kind=kLoop, calls=%fused_computation.19 | loop fusion | flops 4716544 | bytes 36864 | tf_op jit(solution)/shard_map/reduce_sum | solution.py:86
  112.8 0.7 reshape.242
  113.5 8.0 %all-to-all-start.1 = ((f32[32,1,192]{2,1,0:T(1,128)}), f32[32,1,192]{2,1,0:T(1,128)S(1)}, u32[]{:S(2)}, u32[]{:S(2)}) async-start(f32[32,1,192]{2,1,0:T(1,128)} %reshape.242), calls=%async_computation.1 | async-start | bytes 65536 | tf_op jit(solution)/shard_map/all_to_all | solution.py:230
  121.6 9.6 %all-to-all-done.1 = f32[32,1,192]{2,1,0:T(1,128)S(1)} async-done(((f32[32,1,192]{2,1,0:T(1,128)}), f32[32,1,192]{2,1,0:T(1,128)S(1)}, u32[]{:S(2)}, u32[]{:S(2)}) %all-to-all-start.1) | async-done | bytes 24608 | tf_op jit(solution)/shard_map/all_to_all | solution.py:230
  131.2 0.5 broadcast.407
  131.7 0.7 reduce.12
  132.5 0.1 slice_reduce_fusion.2
  132.9 2.8 %fusion = f32[134,128]{1,0:T(8,128)S(1)} fusion(s32[6144]{0:T(1024)S(1)} %get-tuple-element.44, f32[6144]{0:T(1024)S(1)} %pad_maximum_fusion.10, s32[6144]{0:T(1024)S(1)} %get-tuple-element.45), kind=kOutput, calls=%fused_computation.1 | convolution fusion | flops 1266978816 | bytes 142336 | tf_op jit(solution)/shard_map/dot_general | solution.py:96
  135.7 1.0 fusion.8
  (67 shorter events, 1.0 us)
Async XLA Ops:
  0.6 1.0 copy-start
  0.6 13.1 %copy-start.3 = (s32[1,1,32,64]{3,2,1,0:T(8,128)S(1)}, s32[1,1,32,64]{3,2,1,0:T(8,128)}, u32[]{:S(2)}) copy-start(s32[1,1,32,64]{3,2,1,0:T(8,128)} %param.20) | copy-start | bytes 24580
  0.7 10.8 %copy-start.9 = (s32[8]{0:T(128)S(1)}, s32[8]{0:T(128)}, u32[]{:S(2)}) copy-start(s32[8]{0:T(128)} %param.22) | copy-start | bytes 100
  0.7 10.8 %copy-start.8 = (f32[8]{0:T(128)S(1)}, f32[8]{0:T(128)}, u32[]{:S(2)}) copy-start(f32[8]{0:T(128)} %param.23) | copy-start | bytes 100
  3.9 6.1 %collective-permute-start = (f32[136,256]{1,0:T(8,128)S(1)}, f32[136,256]{1,0:T(8,128)S(1)}, u32[]{:S(2)}, u32[]{:S(2)}) collective-permute-start(f32[136,256]{1,0:T(8,128)S(1)} %get-tuple-element.20), channel_id=1, source_target_pairs={{0,32},{64,96},{128,160},{192,224},{256,288},{320,352},{384,416},{... | collective-permute-start | bytes 417800 | tf_op jit(solution)/shard_map/ppermute | solution.py:56
  5.7 4.6 %collective-permute-start.1 = (f32[136,256]{1,0:T(8,128)S(1)}, f32[136,256]{1,0:T(8,128)S(1)}, u32[]{:S(2)}, u32[]{:S(2)}) collective-permute-start(f32[136,256]{1,0:T(8,128)S(1)} %get-tuple-element.19), channel_id=1, source_target_pairs={{0,32},{64,96},{128,160},{192,224},{256,288},{320,352},{384,416},{... | collective-permute-start | bytes 417800 | tf_op jit(solution)/shard_map/ppermute | solution.py:56
  10.7 50.8 %copy-start.1 = (s32[1,1,24,1024]{3,2,1,0:T(8,128)S(1)}, s32[1,1,24,1024]{3,2,1,0:T(8,128)}, u32[]{:S(2)}) copy-start(s32[1,1,24,1024]{3,2,1,0:T(8,128)} %param.17) | copy-start | bytes 294916
  10.7 1.6 %collective-permute-start.2 = (f32[136,256]{1,0:T(8,128)S(1)}, f32[136,256]{1,0:T(8,128)S(1)}, u32[]{:S(2)}, u32[]{:S(2)}) collective-permute-start(f32[136,256]{1,0:T(8,128)S(1)} %get-tuple-element.18), channel_id=1, source_target_pairs={{32,96},{96,160},{160,224},{224,288},{288,352},{352,416},{416,480}... | collective-permute-start | bytes 417800 | tf_op jit(solution)/shard_map/ppermute | solution.py:56
  11.7 0.9 collective-permute-start.3
  13.0 1.6 %collective-permute-start.4 = (f32[136,256]{1,0:T(8,128)S(1)}, f32[136,256]{1,0:T(8,128)S(1)}, u32[]{:S(2)}, u32[]{:S(2)}) collective-permute-start(f32[136,256]{1,0:T(8,128)S(1)} %get-tuple-element.16), channel_id=1, source_target_pairs={{32,160},{96,224},{160,288},{224,352},{288,416},{352,480},{33,161}... | collective-permute-start | bytes 417800 | tf_op jit(solution)/shard_map/ppermute | solution.py:56
  13.9 1.6 %collective-permute-start.6 = (f32[136,256]{1,0:T(8,128)S(1)}, f32[136,256]{1,0:T(8,128)S(1)}, u32[]{:S(2)}, u32[]{:S(2)}) collective-permute-start(f32[136,256]{1,0:T(8,128)S(1)} %get-tuple-element.15), channel_id=1, source_target_pairs={{32,160},{96,224},{160,288},{224,352},{288,416},{352,480},{33,161}... | collective-permute-start | bytes 417800 | tf_op jit(solution)/shard_map/ppermute | solution.py:56
  14.8 1.1 collective-permute-start.5
  16.1 27.4 %collective-permute-start.7 = (f32[16,256]{1,0:T(8,128)S(1)}, f32[16,256]{1,0:T(8,128)S(1)}, u32[]{:S(2)}, u32[]{:S(2)}) collective-permute-start(f32[16,256]{1,0:T(8,128)S(1)} %convolution_add_fusion.1), channel_id=1, source_target_pairs={{32,64},{96,128},{160,192},{224,256},{288,320},{352,384},{416,448}... | collective-permute-start | bytes 49160 | tf_op jit(solution)/shard_map/ppermute | solution.py:72
  43.7 32.9 %copy-start.2 = (f32[16,256]{1,0:T(8,128)}, f32[16,256]{1,0:T(8,128)S(1)}, u32[]{:S(2)}) copy-start(f32[16,256]{1,0:T(8,128)S(1)} %convolution_add_fusion) | copy-start | bytes 49156
  44.6 27.0 %all-to-all-start = ((f32[32,16,256]{2,1,0:T(8,128)}), f32[32,16,256]{2,1,0:T(8,128)S(1)}, u32[]{:S(2)}, u32[]{:S(2)}) async-start(f32[32,16,256]{2,1,0:T(8,128)} %broadcast_in_dim.160), calls=%async_computation | async-start | bytes 1048576 | tf_op jit(solution)/shard_map/all_to_all | solution.py:197
  57.7 5.7 %collective-permute-start.8 = (f32[19,128]{1,0:T(8,128)S(1)}, f32[19,128]{1,0:T(8,128)S(1)}, u32[]{:S(2)}, u32[]{:S(2)}) collective-permute-start(f32[19,128]{1,0:T(8,128)S(1)} %get-tuple-element.4), channel_id=1, source_target_pairs={{0,1},{1,2},{2,3},{3,4},{4,5},{5,6},{6,7},{7,8},{8,9},{9,10},{10,1... | collective-permute-start | bytes 29192 | tf_op jit(solution)/shard_map/ppermute | solution.py:218
  62.2 5.6 %collective-permute-start.9 = (f32[19,128]{1,0:T(8,128)S(1)}, f32[19,128]{1,0:T(8,128)S(1)}, u32[]{:S(2)}, u32[]{:S(2)}) collective-permute-start(f32[19,128]{1,0:T(8,128)S(1)} %get-tuple-element.5), channel_id=1, source_target_pairs={{1,0},{2,1},{3,2},{4,3},{5,4},{6,5},{7,6},{8,7},{9,8},{10,9},{11,1... | collective-permute-start | bytes 29192 | tf_op jit(solution)/shard_map/ppermute | solution.py:219
  63.5 58.1 %copy-start.4 = (f32[19,128]{1,0:T(8,128)}, f32[19,128]{1,0:T(8,128)S(1)}, u32[]{:S(2)}) copy-start(f32[19,128]{1,0:T(8,128)S(1)} %collective-permute-done.8) | copy-start | bytes 29188
  67.8 53.8 %copy-start.5 = (f32[19,128]{1,0:T(8,128)}, f32[19,128]{1,0:T(8,128)S(1)}, u32[]{:S(2)}) copy-start(f32[19,128]{1,0:T(8,128)S(1)} %collective-permute-done.9) | copy-start | bytes 29188
  76.6 27.5 %copy-start.6 = (f32[24,24]{1,0:T(8,128)S(1)}, f32[24,24]{1,0:T(8,128)}, u32[]{:S(2)}) copy-start(f32[24,24]{1,0:T(8,128)} %param.15) | copy-start | bytes 6916
  76.6 32.8 %copy-start.7 = (f32[1,1,1024]{2,1,0:T(1,128)S(1)}, f32[1,1,1024]{2,1,0:T(1,128)}, u32[]{:S(2)}) copy-start(f32[1,1,1024]{2,1,0:T(1,128)} %param.18) | copy-start | bytes 12292
  104.0 31.7 %copy-start.10 = (f32[1,1,128,128]{3,2,1,0:T(8,128)S(1)}, f32[1,1,128,128]{3,2,1,0:T(8,128)}, u32[]{:S(2)}) copy-start(f32[1,1,128,128]{3,2,1,0:T(8,128)} %param.21) | copy-start | bytes 196612
  113.5 17.7 %all-to-all-start.1 = ((f32[32,1,192]{2,1,0:T(1,128)}), f32[32,1,192]{2,1,0:T(1,128)S(1)}, u32[]{:S(2)}, u32[]{:S(2)}) async-start(f32[32,1,192]{2,1,0:T(1,128)} %reshape.242), calls=%async_computation.1 | async-start | bytes 65536 | tf_op jit(solution)/shard_map/all_to_all | solution.py:230
  121.6 14.1 %slice-start = ((f32[19,128]{1,0:T(8,128)}), f32[3,128]{1,0:T(4,128)S(1)}, s32[]{:S(2)}) async-start(f32[19,128]{1,0:T(8,128)} %copy-done.4), calls=%async_computation.2 | async-start | bytes 4096 | tf_op jit(solution)/shard_map/slice | solution.py:223
  121.6 14.1 %slice-start.1 = ((f32[19,128]{1,0:T(8,128)}), f32[3,128]{1,0:T(4,128)S(1)}, s32[]{:S(2)}) async-start(f32[19,128]{1,0:T(8,128)} %copy-done.5), calls=%async_computation.3 | async-start | bytes 4096 | tf_op jit(solution)/shard_map/slice | solution.py:223

commit v11 on v10

--- a/solution.py
+++ b/solution.py
@@ -41,7 +41,7 @@
     return jnp.dot(left, right, precision=exact_mode, preferred_element_type=jnp.float32)
 
 
-def interface_chain(inverse, couple, rights):
+def interface_chain(inverse, couple, rights, held):
     offset = product(rights, inverse)
     step = -product(couple, inverse)
     order = rights.shape[0]
@@ -68,9 +68,11 @@
     while shift < levels:
         pairs = [(g, g + shift) for g in range(1, levels - shift, 2)]
         combine(pairs, 2 * shift < levels)
+        if shift == 2:
+            held, offset = lax.optimization_barrier((held, offset))
         shift *= 2
     earlier_offset = lax.ppermute(offset, "grp", [(g, g + 1) for g in range(1, levels - 1, 2)])
-    return product(earlier_offset, step) + offset
+    return product(earlier_offset, step) + offset, held
 
 
 def picked(values, index):
@@ -133,12 +135,19 @@
         lax.broadcasted_iota(jnp.int32, (width, 128), 0)
         == lax.broadcasted_iota(jnp.int32, (width, 128), 1) % width
     ).astype(jnp.float32)
-    wide = lax.dot_general(
-        panels, spread, (((1,), (0,)), ((), ())), precision=exact_mode, preferred_element_type=jnp.float32
-    ).reshape(slabs * panel_order, 128)
+    spread = spread.astype(jnp.bfloat16)
+    rest = panels
+    wide = None
+    for _ in range(3):
+        rounded = lax.reduce_precision(rest, exponent_bits=8, mantissa_bits=7)
+        rest = rest - rounded
+        part = rounded.astype(jnp.bfloat16)
+        term = lax.dot_general(part, spread, (((1,), (0,)), ((), ())), preferred_element_type=jnp.float32)
+        wide = term if wide is None else wide + term
+    wide = wide.reshape(slabs * panel_order, 128)
     total = lookup.shape[0]
     out_rows = total // pack
-    chunks = 8
+    chunks = 2
     rows = out_rows // chunks
     return pl.pallas_call(
         gather_kernel,
@@ -191,7 +200,9 @@
     inverse = panel_inverse[0, 0]
     couple = coupling[0, 0]
     rights = loads[0, 0]
-    solved = interface_chain(inverse, couple, rights)
+    held = (element_substructure, element_rows, element_density, send_elements, receive_cells, design_density)
+    solved, held = interface_chain(inverse, couple, rights, held)
+    element_substructure, element_rows, element_density, send_elements, receive_cells, design_density = held
 
     copies = jnp.broadcast_to(solved[None], (lax.axis_size("dev"),) + solved.shape)
     panels = lax.all_to_all(copies, "dev", split_axis=0, concat_axis=0, tiled=True)

time: 138 us -> 135 us (0.978)
  local copies, waits for them, and re-layouts: 6.39 us -> 4.25 us
    dot_general x1 -> x3, matrix products: 4.99 us -> 4.28 us  [gathered_rows(): lax.dot_general(part, spread, (((1,), (0,)), ((), ())), preferred_element...]
  transfers between devices with their start and end apart: 12 -> 12, of which waited for: 4 -> 4; matrix products, arithmetic and copies ran while one was open for 4% -> 2% of each run, Pallas kernels for 0% -> 0%
where the time goes in v11:
time: 135 us
  waiting for transfers between devices  44.3 us (33%)
  starting transfers between devices  33.8 us (25%)
  Pallas kernels  27.6 us (20%)
  matrix products  17.5 us (13%)
  other arithmetic  5.85 us (4%)
  local copies, waits for them, and re-layouts  4.25 us (3%)
    pallas_call x1, Pallas kernels, gathered_rows(): pl.pallas_call(gather_kernel, out_shape=jax.ShapeDtypeStruct((out_rows, 1...  27.6 us
    ppermute x1, waiting for transfers between devices, interface_chain(): lax.ppermute(offset, 'grp', [(g, g + 1) for g in range(1, levels - 1, 2)])  26.6 us
    all_to_all x1, starting transfers between devices, on_device(): lax.all_to_all(copies, 'dev', split_axis=0, concat_axis=0, tiled=True)  13.2 us
    all_to_all x1, waiting for transfers between devices, on_device(): lax.all_to_all(triple, 'dev', split_axis=0, concat_axis=0, tiled=True)  9.61 us
    all_to_all x1, starting transfers between devices, on_device(): lax.all_to_all(triple, 'dev', split_axis=0, concat_axis=0, tiled=True)  7.99 us
    dot_general x11, matrix products, product(): jnp.dot(left, right, precision=exact_mode, preferred_element_type=jnp.flo...  5.41 us
    dot_general x1, matrix products, on_device(): forces = jnp.einsum('ij,jab->iab', stiffness, motion, precision=exact_mode)  5.01 us
    dot_general x3, matrix products, gathered_rows(): lax.dot_general(part, spread, (((1,), (0,)), ((), ())), preferred_element...  4.28 us
  transfers between devices with their start and end apart: 12, of which 4 were waited for; matrix products, arithmetic and copies ran while one was open for 2% of the time, Pallas kernels for 0%

profile of v11, /device:TPU:40, one launch (start us, length us, event | category | flops | bytes accessed | tf_op | source)
XLA Modules:
  0.0 134.6 jit_solution(15010581102679579815)
XLA Ops:
  0.7 0.9 copy-done
  1.6 1.3 convolution_negate_fusion
  2.9 0.9 fusion.22
  3.9 1.7 %collective-permute-start = (f32[136,256]{1,0:T(8,128)S(1)}, f32[136,256]{1,0:T(8,128)S(1)}, u32[]{:S(2)}, u32[]{:S(2)}) collective-permute-start(f32[136,256]{1,0:T(8,128)S(1)} %get-tuple-element.34), channel_id=1, source_target_pairs={{0,32},{64,96},{128,160},{192,224},{256,288},{320,352},{384,416},{... | collective-permute-start | bytes 417800 | tf_op jit(solution)/shard_map/ppermute | solution.py:56
  5.7 1.3 collective-permute-start.1
  7.0 0.9 select_reduce_fusion.1
  8.0 0.2 convolution_add_fusion.4
  8.2 0.4 fusion.18
  8.6 0.7 collective-permute-start.2
  9.3 0.1 multiply_reduce_fusion
  9.4 0.7 collective-permute-start.3
  10.1 0.2 convolution_add_fusion.3
  10.4 0.4 fusion.16
  10.8 0.7 collective-permute-start.4
  11.5 0.7 collective-permute-start.6
  12.5 0.2 convolution_add_fusion.2
  12.7 0.7 collective-permute-start.5
  13.4 0.4 fusion.14
  13.8 0.2 convolution_add_fusion.1
  14.0 1.3 collective-permute-start.7
  15.3 26.6 %collective-permute-done.7 = f32[16,256]{1,0:T(8,128)S(1)} collective-permute-done((f32[16,256]{1,0:T(8,128)S(1)}, f32[16,256]{1,0:T(8,128)S(1)}, u32[]{:S(2)}, u32[]{:S(2)}) %collective-permute-start.7) | collective-permute-done | bytes 16416 | tf_op jit(solution)/shard_map/ppermute | solution.py:74
  41.9 0.2 convolution_add_fusion
  42.2 0.9 broadcast_in_dim.160
  43.0 13.2 %all-to-all-start = ((f32[32,16,256]{2,1,0:T(8,128)}), f32[32,16,256]{2,1,0:T(8,128)S(1)}, u32[]{:S(2)}, u32[]{:S(2)}) async-start(f32[32,16,256]{2,1,0:T(8,128)} %broadcast_in_dim.160), calls=%async_computation | async-start | bytes 1048576 | tf_op jit(solution)/shard_map/all_to_all | solution.py:208
  56.2 3.7 %collective-permute-start.8 = (f32[19,128]{1,0:T(8,128)S(1)}, f32[19,128]{1,0:T(8,128)S(1)}, u32[]{:S(2)}, u32[]{:S(2)}) collective-permute-start(f32[19,128]{1,0:T(8,128)S(1)} %get-tuple-element.14), channel_id=1, source_target_pairs={{0,1},{1,2},{2,3},{3,4},{4,5},{5,6},{6,7},{7,8},{8,9},{9,10},{10,1... | collective-permute-start | bytes 29192 | tf_op jit(solution)/shard_map/ppermute | solution.py:229
  60.0 0.7 add.178.lookup_ref
  60.6 1.3 collective-permute-start.9
  62.0 4.2 %collective-permute-done.9 = f32[19,128]{1,0:T(8,128)S(1)} collective-permute-done((f32[19,128]{1,0:T(8,128)S(1)}, f32[19,128]{1,0:T(8,128)S(1)}, u32[]{:S(2)}, u32[]{:S(2)}) %collective-permute-start.9) | collective-permute-done | bytes 9760 | tf_op jit(solution)/shard_map/ppermute | solution.py:230
  66.2 3.8 %all-to-all-done = f32[32,16,256]{2,1,0:T(8,128)S(1)} async-done(((f32[32,16,256]{2,1,0:T(8,128)}), f32[32,16,256]{2,1,0:T(8,128)S(1)}, u32[]{:S(2)}, u32[]{:S(2)}) %all-to-all-start) | async-done | bytes 524320 | tf_op jit(solution)/shard_map/all_to_all | solution.py:208
  70.0 0.8 fusion.12
  70.8 0.8 fusion.13
  71.6 2.8 %add_add_fusion = f32[32,256,128]{2,1,0:T(8,128)} fusion(f32[32,256,128]{2,1,0:T(8,128)S(1)} %fusion.12, f32[32,256,128]{2,1,0:T(8,128)S(1)} %fusion.13, f32[32,16,256]{2,1,0:T(8,128)S(1)} %all-to-all-done, s32[128]{0:T(128)S(1)} %iota_and_fusion, s32[128]{0:T(128)S(1)} %broadcast_add_fusion, pred[128]{0:T(512)(128)(4,1)S(1)} %compare_and_fusion), kind=kOutput, calls=%fused_computation | convolution fusion | flops 36446208 | bytes 13108352 | tf_op jit(solution)/shard_map/dot_general | solution.py:145
  74.3 27.6 %shard_map.131 = f32[3072,128]{1,0:T(8,128)} custom-call(s32[24576]{0:T(1024)} %add.178.lookup_ref, f32[8192,128]{1,0:T(8,128)} %bitcast.105), custom_call_target="tpu_custom_call" | custom-call | bytes 5767168 | tf_op jit(solution)/shard_map/pallas_call | solution.py:152
  101.9 5.0 %fusion.3 = f32[128,128]{1,0:T(8,128)S(1)} fusion(f32[24,128,128]{2,1,0:T(8,128)} %bitcast.106, f32[24,24]{1,0:T(8,128)S(1)} %copy-done.7), kind=kOutput, calls=%fused_computation.7 | convolution fusion | flops 114016256 | bytes 1640704 | tf_op jit(solution)/shard_map/ij,jab->iab/dot_general | solution.py:215
  106.9 0.1 copy.25
  107.0 0.1 copy.26
  107.1 0.1 reshape.221
  107.3 3.1 %select_reduce_fusion = f32[2048]{0:T(1024)S(1)} fusion(f32[128]{0:T(128)S(1)} %get-tuple-element.51, f32[128]{0:T(128)S(1)} %get-tuple-element.52, f32[128]{0:T(128)S(1)} %get-tuple-element.53, f32[128]{0:T(128)S(1)} %get-tuple-element.54, f32[128]{0:T(128)S(1)} %get-tuple-element.55, f32[128]{0:T(128)S(1)} %get-tuple-element.56, ...), kind=kLoop, calls=%fused_computation.20 | loop fusion | flops 4716544 | bytes 36864 | tf_op jit(solution)/shard_map/reduce_sum | solution.py:88
  110.5 0.1 stack_reshape.3
  110.7 0.7 reshape.242
  111.4 8.0 %all-to-all-start.1 = ((f32[32,1,192]{2,1,0:T(1,128)}), f32[32,1,192]{2,1,0:T(1,128)S(1)}, u32[]{:S(2)}, u32[]{:S(2)}) async-start(f32[32,1,192]{2,1,0:T(1,128)} %reshape.242), calls=%async_computation.1 | async-start | bytes 65536 | tf_op jit(solution)/shard_map/all_to_all | solution.py:241
  119.4 9.6 %all-to-all-done.1 = f32[32,1,192]{2,1,0:T(1,128)S(1)} async-done(((f32[32,1,192]{2,1,0:T(1,128)}), f32[32,1,192]{2,1,0:T(1,128)S(1)}, u32[]{:S(2)}, u32[]{:S(2)}) %all-to-all-start.1) | async-done | bytes 24608 | tf_op jit(solution)/shard_map/all_to_all | solution.py:241
  129.0 0.5 broadcast.407
  129.5 0.7 reduce.12
  130.3 0.1 reshape.243
  130.4 0.1 slice_reduce_fusion.2
  130.7 2.8 %fusion = f32[134,128]{1,0:T(8,128)S(1)} fusion(s32[6144]{0:T(1024)S(1)} %get-tuple-element.58, f32[6144]{0:T(1024)S(1)} %pad_maximum_fusion.10, s32[6144]{0:T(1024)S(1)} %get-tuple-element.59), kind=kOutput, calls=%fused_computation.2 | convolution fusion | flops 1266978816 | bytes 142336 | tf_op jit(solution)/shard_map/dot_general | solution.py:98
  133.5 1.0 fusion.8
  (70 shorter events, 1.0 us)
Async XLA Ops:
  0.6 1.0 copy-start
  0.6 11.6 %copy-start.9 = (s32[1,1,1024]{2,1,0:T(1,128)S(1)}, s32[1,1,1024]{2,1,0:T(1,128)}, u32[]{:S(2)}) copy-start(s32[1,1,1024]{2,1,0:T(1,128)} %param.16) | copy-start | bytes 12292
  0.7 11.6 %copy-start.6 = (s32[1,1,32,64]{3,2,1,0:T(8,128)S(1)}, s32[1,1,32,64]{3,2,1,0:T(8,128)}, u32[]{:S(2)}) copy-start(s32[1,1,32,64]{3,2,1,0:T(8,128)} %param.19) | copy-start | bytes 24580
  0.7 9.7 %copy-start.3 = (s32[1,1,32,64]{3,2,1,0:T(8,128)S(1)}, s32[1,1,32,64]{3,2,1,0:T(8,128)}, u32[]{:S(2)}) copy-start(s32[1,1,32,64]{3,2,1,0:T(8,128)} %param.20) | copy-start | bytes 24580
  0.7 11.8 %copy-start.10 = (f32[1,1,128,128]{3,2,1,0:T(8,128)S(1)}, f32[1,1,128,128]{3,2,1,0:T(8,128)}, u32[]{:S(2)}) copy-start(f32[1,1,128,128]{3,2,1,0:T(8,128)} %param.21) | copy-start | bytes 196612
  3.9 4.0 %collective-permute-start = (f32[136,256]{1,0:T(8,128)S(1)}, f32[136,256]{1,0:T(8,128)S(1)}, u32[]{:S(2)}, u32[]{:S(2)}) collective-permute-start(f32[136,256]{1,0:T(8,128)S(1)} %get-tuple-element.34), channel_id=1, source_target_pairs={{0,32},{64,96},{128,160},{192,224},{256,288},{320,352},{384,416},{... | collective-permute-start | bytes 417800 | tf_op jit(solution)/shard_map/ppermute | solution.py:56
  5.7 2.5 %collective-permute-start.1 = (f32[136,256]{1,0:T(8,128)S(1)}, f32[136,256]{1,0:T(8,128)S(1)}, u32[]{:S(2)}, u32[]{:S(2)}) collective-permute-start(f32[136,256]{1,0:T(8,128)S(1)} %get-tuple-element.33), channel_id=1, source_target_pairs={{0,32},{64,96},{128,160},{192,224},{256,288},{320,352},{384,416},{... | collective-permute-start | bytes 417800 | tf_op jit(solution)/shard_map/ppermute | solution.py:56
  8.6 51.3 %copy-start.1 = (s32[1,1,24,1024]{3,2,1,0:T(8,128)S(1)}, s32[1,1,24,1024]{3,2,1,0:T(8,128)}, u32[]{:S(2)}) copy-start(s32[1,1,24,1024]{3,2,1,0:T(8,128)} %param.17) | copy-start | bytes 294916
  8.6 1.5 %collective-permute-start.2 = (f32[136,256]{1,0:T(8,128)S(1)}, f32[136,256]{1,0:T(8,128)S(1)}, u32[]{:S(2)}, u32[]{:S(2)}) collective-permute-start(f32[136,256]{1,0:T(8,128)S(1)} %get-tuple-element.32), channel_id=1, source_target_pairs={{32,96},{96,160},{160,224},{224,288},{288,352},{352,416},{416,480}... | collective-permute-start | bytes 417800 | tf_op jit(solution)/shard_map/ppermute | solution.py:56
  9.4 1.0 collective-permute-start.3
  10.8 1.6 %collective-permute-start.4 = (f32[136,256]{1,0:T(8,128)S(1)}, f32[136,256]{1,0:T(8,128)S(1)}, u32[]{:S(2)}, u32[]{:S(2)}) collective-permute-start(f32[136,256]{1,0:T(8,128)S(1)} %get-tuple-element.30), channel_id=1, source_target_pairs={{32,160},{96,224},{160,288},{224,352},{288,416},{352,480},{33,161}... | collective-permute-start | bytes 417800 | tf_op jit(solution)/shard_map/ppermute | solution.py:56
  11.5 1.9 %collective-permute-start.6 = (f32[136,256]{1,0:T(8,128)S(1)}, f32[136,256]{1,0:T(8,128)S(1)}, u32[]{:S(2)}, u32[]{:S(2)}) collective-permute-start(f32[136,256]{1,0:T(8,128)S(1)} %get-tuple-element.29), channel_id=1, source_target_pairs={{32,160},{96,224},{160,288},{224,352},{288,416},{352,480},{33,161}... | collective-permute-start | bytes 417800 | tf_op jit(solution)/shard_map/ppermute | solution.py:56
  12.7 1.1 collective-permute-start.5
  14.0 27.9 %collective-permute-start.7 = (f32[16,256]{1,0:T(8,128)S(1)}, f32[16,256]{1,0:T(8,128)S(1)}, u32[]{:S(2)}, u32[]{:S(2)}) collective-permute-start(f32[16,256]{1,0:T(8,128)S(1)} %convolution_add_fusion.1), channel_id=1, source_target_pairs={{32,64},{96,128},{160,192},{224,256},{288,320},{352,384},{416,448}... | collective-permute-start | bytes 49160 | tf_op jit(solution)/shard_map/ppermute | solution.py:74
  42.1 28.7 %copy-start.2 = (f32[16,256]{1,0:T(8,128)}, f32[16,256]{1,0:T(8,128)S(1)}, u32[]{:S(2)}) copy-start(f32[16,256]{1,0:T(8,128)S(1)} %convolution_add_fusion) | copy-start | bytes 49156
  43.0 27.0 %all-to-all-start = ((f32[32,16,256]{2,1,0:T(8,128)}), f32[32,16,256]{2,1,0:T(8,128)S(1)}, u32[]{:S(2)}, u32[]{:S(2)}) async-start(f32[32,16,256]{2,1,0:T(8,128)} %broadcast_in_dim.160), calls=%async_computation | async-start | bytes 1048576 | tf_op jit(solution)/shard_map/all_to_all | solution.py:208
  56.2 5.7 %collective-permute-start.8 = (f32[19,128]{1,0:T(8,128)S(1)}, f32[19,128]{1,0:T(8,128)S(1)}, u32[]{:S(2)}, u32[]{:S(2)}) collective-permute-start(f32[19,128]{1,0:T(8,128)S(1)} %get-tuple-element.14), channel_id=1, source_target_pairs={{0,1},{1,2},{2,3},{3,4},{4,5},{5,6},{6,7},{7,8},{8,9},{9,10},{10,1... | collective-permute-start | bytes 29192 | tf_op jit(solution)/shard_map/ppermute | solution.py:229
  60.6 5.6 %collective-permute-start.9 = (f32[19,128]{1,0:T(8,128)S(1)}, f32[19,128]{1,0:T(8,128)S(1)}, u32[]{:S(2)}, u32[]{:S(2)}) collective-permute-start(f32[19,128]{1,0:T(8,128)S(1)} %get-tuple-element.15), channel_id=1, source_target_pairs={{1,0},{2,1},{3,2},{4,3},{5,4},{6,5},{7,6},{8,7},{9,8},{10,9},{11,1... | collective-permute-start | bytes 29192 | tf_op jit(solution)/shard_map/ppermute | solution.py:230
  61.9 57.4 %copy-start.4 = (f32[19,128]{1,0:T(8,128)}, f32[19,128]{1,0:T(8,128)S(1)}, u32[]{:S(2)}) copy-start(f32[19,128]{1,0:T(8,128)S(1)} %collective-permute-done.8) | copy-start | bytes 29188
  66.2 53.2 %copy-start.5 = (f32[19,128]{1,0:T(8,128)}, f32[19,128]{1,0:T(8,128)S(1)}, u32[]{:S(2)}) copy-start(f32[19,128]{1,0:T(8,128)S(1)} %collective-permute-done.9) | copy-start | bytes 29188
  74.3 27.6 %copy-start.7 = (f32[24,24]{1,0:T(8,128)S(1)}, f32[24,24]{1,0:T(8,128)}, u32[]{:S(2)}) copy-start(f32[24,24]{1,0:T(8,128)} %param.15) | copy-start | bytes 6916
  74.3 32.9 %copy-start.8 = (f32[1,1,1024]{2,1,0:T(1,128)S(1)}, f32[1,1,1024]{2,1,0:T(1,128)}, u32[]{:S(2)}) copy-start(f32[1,1,1024]{2,1,0:T(1,128)} %param.18) | copy-start | bytes 12292
  111.4 17.7 %all-to-all-start.1 = ((f32[32,1,192]{2,1,0:T(1,128)}), f32[32,1,192]{2,1,0:T(1,128)S(1)}, u32[]{:S(2)}, u32[]{:S(2)}) async-start(f32[32,1,192]{2,1,0:T(1,128)} %reshape.242), calls=%async_computation.1 | async-start | bytes 65536 | tf_op jit(solution)/shard_map/all_to_all | solution.py:241
  119.4 14.1 %slice-start = ((f32[19,128]{1,0:T(8,128)}), f32[3,128]{1,0:T(4,128)S(1)}, s32[]{:S(2)}) async-start(f32[19,128]{1,0:T(8,128)} %copy-done.4), calls=%async_computation.2 | async-start | bytes 4096 | tf_op jit(solution)/shard_map/slice | solution.py:234
  119.4 14.1 %slice-start.1 = ((f32[19,128]{1,0:T(8,128)}), f32[3,128]{1,0:T(4,128)S(1)}, s32[]{:S(2)}) async-start(f32[19,128]{1,0:T(8,128)} %copy-done.5), calls=%async_computation.3 | async-start | bytes 4096 | tf_op jit(solution)/shard_map/slice | solution.py:234

commit v12 on v11

--- a/solution.py
+++ b/solution.py
@@ -75,17 +75,23 @@
     return product(earlier_offset, step) + offset, held
 
 
+def split_product(hot, values, dimensions):
+    hot = hot.astype(jnp.bfloat16)
+    rest = values
+    total = None
+    for _ in range(3):
+        rounded = lax.reduce_precision(rest, exponent_bits=8, mantissa_bits=7)
+        rest = rest - rounded
+        term = lax.dot_general(hot, rounded.astype(jnp.bfloat16), dimensions, preferred_element_type=jnp.float32)
+        total = term if total is None else total + term
+    return total
+
+
 def picked(values, index):
-    lanes = 128
-    table = values.reshape(-1, lanes)
     flat = index.reshape(-1)
-    high = flat // lanes
-    low = flat % lanes
-    rows = jnp.zeros((flat.shape[0], lanes), values.dtype)
-    for which in range(table.shape[0]):
-        rows = rows + jnp.where((high == which)[:, None], table[which][None, :], 0.0)
-    lane_ids = lax.broadcasted_iota(jnp.int32, (1, lanes), 1)
-    chosen = jnp.sum(jnp.where(lane_ids == low[:, None], rows, 0.0), axis=1)
+    ids = lax.broadcasted_iota(jnp.int32, (1, values.shape[0]), 1)
+    hot = flat[:, None] == ids
+    chosen = split_product(hot, values[:, None], (((1,), (0,)), ((), ())))
     return chosen.reshape(index.shape)
 
 
@@ -93,15 +99,9 @@
     lanes = 128
     row_ids = lax.broadcasted_iota(jnp.int32, (1, row_count), 1)
     lane_ids = lax.broadcasted_iota(jnp.int32, (1, lanes), 1)
-    rows_hot = (rows[:, None] == row_ids).astype(jnp.float32)
+    rows_hot = rows[:, None] == row_ids
     cols_hot = jnp.where(cols[:, None] == lane_ids, values[:, None], 0.0)
-    return lax.dot_general(
-        rows_hot,
-        cols_hot,
-        (((0,), (0,)), ((), ())),
-        precision=exact_mode,
-        preferred_element_type=jnp.float32,
-    )
+    return split_product(rows_hot, cols_hot, (((0,), (0,)), ((), ())))
 
 
 def padded_targets(cells, first, last, shift):

time: 135 us -> 141 us (1.044)
  matrix products: 17.5 us -> 25.7 us
  other arithmetic: 5.85 us -> 2.68 us
    dot_general x1 -> x6, matrix products: 2.8 us -> 11 us  [split_product(): lax.dot_general(hot, rounded.astype(jnp.bfloat16), dimensions, preferred_...]
    reduce_sum x1 -> x0, other arithmetic: 3.14 us -> none  [picked(): chosen = jnp.sum(jnp.where(lane_ids == low[:, None], rows, 0.0), axis=1)]
where the time goes in v12:
time: 141 us; the launch traced here: 140 us
  waiting for transfers between devices  44.1 us (31%)
  starting transfers between devices  34.3 us (24%)
  Pallas kernels  27.6 us (20%)
  matrix products  25.7 us (18%)
  local copies, waits for them, and re-layouts  4.23 us (3%)
  other arithmetic  2.68 us (2%)
    pallas_call x1, Pallas kernels, gathered_rows(): pl.pallas_call(gather_kernel, out_shape=jax.ShapeDtypeStruct((out_rows, 1...  27.6 us
    ppermute x1, waiting for transfers between devices, interface_chain(): lax.ppermute(offset, 'grp', [(g, g + 1) for g in range(1, levels - 1, 2)])  26.8 us
    all_to_all x1, starting transfers between devices, on_device(): lax.all_to_all(copies, 'dev', split_axis=0, concat_axis=0, tiled=True)  13.2 us
    dot_general x6, matrix products, split_product(): lax.dot_general(hot, rounded.astype(jnp.bfloat16), dimensions, preferred_...  11 us
    all_to_all x1, waiting for transfers between devices, on_device(): lax.all_to_all(triple, 'dev', split_axis=0, concat_axis=0, tiled=True)  9.59 us
    all_to_all x1, starting transfers between devices, on_device(): lax.all_to_all(triple, 'dev', split_axis=0, concat_axis=0, tiled=True)  8.11 us
    dot_general x11, matrix products, product(): jnp.dot(left, right, precision=exact_mode, preferred_element_type=jnp.flo...  5.41 us
    dot_general x1, matrix products, on_device(): forces = jnp.einsum('ij,jab->iab', stiffness, motion, precision=exact_mode)  5.01 us
  transfers between devices with their start and end apart: 12, of which 4 were waited for; matrix products, arithmetic and copies ran while one was open for 2% of the time, Pallas kernels for 0%

profile of v12, /device:TPU:40, one launch (start us, length us, event | category | flops | bytes accessed | tf_op | source)
XLA Modules:
  0.0 139.9 jit_solution(1999657408913295996)
XLA Ops:
  0.7 0.9 copy-done
  1.6 1.3 convolution_negate_fusion
  2.9 0.9 fusion.42
  3.9 1.7 %collective-permute-start = (f32[136,256]{1,0:T(8,128)S(1)}, f32[136,256]{1,0:T(8,128)S(1)}, u32[]{:S(2)}, u32[]{:S(2)}) collective-permute-start(f32[136,256]{1,0:T(8,128)S(1)} %get-tuple-element.32), channel_id=1, source_target_pairs={{0,32},{64,96},{128,160},{192,224},{256,288},{320,352},{384,416},{... | collective-permute-start | bytes 417800 | tf_op jit(solution)/shard_map/ppermute | solution.py:56
  5.7 1.3 collective-permute-start.1
  7.0 0.9 select_reduce_fusion
  7.9 0.2 convolution_add_fusion.4
  8.2 0.4 fusion.38
  8.6 0.8 collective-permute-start.2
  9.4 0.1 multiply_reduce_fusion
  9.5 0.7 collective-permute-start.3
  10.2 0.2 convolution_add_fusion.3
  10.5 0.4 fusion.36
  10.9 0.7 collective-permute-start.4
  11.6 0.7 collective-permute-start.6
  12.4 0.2 convolution_add_fusion.2
  12.6 0.7 collective-permute-start.5
  13.3 0.4 fusion.34
  13.7 0.2 convolution_add_fusion.1
  13.9 1.3 collective-permute-start.7
  15.3 26.8 %collective-permute-done.7 = f32[16,256]{1,0:T(8,128)S(1)} collective-permute-done((f32[16,256]{1,0:T(8,128)S(1)}, f32[16,256]{1,0:T(8,128)S(1)}, u32[]{:S(2)}, u32[]{:S(2)}) %collective-permute-start.7) | collective-permute-done | bytes 16416 | tf_op jit(solution)/shard_map/ppermute | solution.py:74
  42.1 0.2 convolution_add_fusion
  42.3 0.8 broadcast_in_dim.52
  43.1 13.2 %all-to-all-start = ((f32[32,16,256]{2,1,0:T(8,128)}), f32[32,16,256]{2,1,0:T(8,128)S(1)}, u32[]{:S(2)}, u32[]{:S(2)}) async-start(f32[32,16,256]{2,1,0:T(8,128)} %broadcast_in_dim.52), calls=%async_computation | async-start | bytes 1048576 | tf_op jit(solution)/shard_map/all_to_all | solution.py:208
  56.3 3.7 %collective-permute-start.8 = (f32[19,128]{1,0:T(8,128)S(1)}, f32[19,128]{1,0:T(8,128)S(1)}, u32[]{:S(2)}, u32[]{:S(2)}) collective-permute-start(f32[19,128]{1,0:T(8,128)S(1)} %get-tuple-element.14), channel_id=1, source_target_pairs={{0,1},{1,2},{2,3},{3,4},{4,5},{5,6},{6,7},{7,8},{8,9},{9,10},{10,1... | collective-permute-start | bytes 29192 | tf_op jit(solution)/shard_map/ppermute | solution.py:229
  60.2 0.7 add.134.lookup_ref
  60.8 1.5 %collective-permute-start.9 = (f32[19,128]{1,0:T(8,128)S(1)}, f32[19,128]{1,0:T(8,128)S(1)}, u32[]{:S(2)}, u32[]{:S(2)}) collective-permute-start(f32[19,128]{1,0:T(8,128)S(1)} %get-tuple-element.15), channel_id=1, source_target_pairs={{1,0},{2,1},{3,2},{4,3},{5,4},{6,5},{7,6},{8,7},{9,8},{10,9},{11,1... | collective-permute-start | bytes 29192 | tf_op jit(solution)/shard_map/ppermute | solution.py:230
  62.4 4.1 %collective-permute-done.9 = f32[19,128]{1,0:T(8,128)S(1)} collective-permute-done((f32[19,128]{1,0:T(8,128)S(1)}, f32[19,128]{1,0:T(8,128)S(1)}, u32[]{:S(2)}, u32[]{:S(2)}) %collective-permute-start.9) | collective-permute-done | bytes 9760 | tf_op jit(solution)/shard_map/ppermute | solution.py:230
  66.5 3.7 %all-to-all-done = f32[32,16,256]{2,1,0:T(8,128)S(1)} async-done(((f32[32,16,256]{2,1,0:T(8,128)}), f32[32,16,256]{2,1,0:T(8,128)S(1)}, u32[]{:S(2)}, u32[]{:S(2)}) %all-to-all-start) | async-done | bytes 524320 | tf_op jit(solution)/shard_map/all_to_all | solution.py:208
  70.1 0.8 fusion.32
  70.9 0.8 fusion.33
  71.7 2.7 %add_add_fusion = f32[32,256,128]{2,1,0:T(8,128)} fusion(f32[32,256,128]{2,1,0:T(8,128)S(1)} %fusion.32, f32[32,256,128]{2,1,0:T(8,128)S(1)} %fusion.33, f32[32,16,256]{2,1,0:T(8,128)S(1)} %all-to-all-done, s32[128]{0:T(128)S(1)} %iota_and_fusion, s32[128]{0:T(128)S(1)} %broadcast_add_fusion, pred[128]{0:T(512)(128)(4,1)S(1)} %compare_and_fusion), kind=kOutput, calls=%fused_computation.8 | convolution fusion | flops 36446208 | bytes 13108352 | tf_op jit(solution)/shard_map/dot_general | solution.py:145
  74.4 27.6 %shard_map.131 = f32[3072,128]{1,0:T(8,128)} custom-call(s32[24576]{0:T(1024)} %add.134.lookup_ref, f32[8192,128]{1,0:T(8,128)} %bitcast.111), custom_call_target="tpu_custom_call" | custom-call | bytes 5767168 | tf_op jit(solution)/shard_map/pallas_call | solution.py:152
  102.0 5.0 %fusion.15 = f32[128,128]{1,0:T(8,128)S(1)} fusion(f32[24,128,128]{2,1,0:T(8,128)} %bitcast.112, f32[24,24]{1,0:T(8,128)S(1)} %copy-done.7), kind=kOutput, calls=%fused_computation.23 | convolution fusion | flops 114016256 | bytes 1640704 | tf_op jit(solution)/shard_map/ij,jab->iab/dot_general | solution.py:215
  107.2 0.1 copy.26
  107.4 1.8 %fusion.1 = f32[1,2048]{1,0:T(1,128)S(1)} fusion(bf16[1024,1]{0,1:T(2,128)(2,1)S(1)} %reshape.121, s32[2048]{0:T(1024)S(1)} %eq.76), kind=kOutput, calls=%fused_computation.2 | convolution fusion | flops 6291456 | bytes 18432 | tf_op jit(solution)/shard_map/dot_general | solution.py:85
  109.2 1.8 %fusion.2 = f32[1,2048]{1,0:T(1,128)S(1)} fusion(bf16[1024,1]{0,1:T(2,128)(2,1)S(1)} %reshape.119, s32[2048]{0:T(1024)S(1)} %eq.76), kind=kOutput, calls=%fused_computation.3 | convolution fusion | flops 6291456 | bytes 18432 | tf_op jit(solution)/shard_map/dot_general | solution.py:85
  111.0 1.8 %fusion = f32[1,2048]{1,0:T(1,128)S(1)} fusion(bf16[1024,1]{0,1:T(2,128)(2,1)S(1)} %reshape.123, s32[2048]{0:T(1024)S(1)} %eq.76), kind=kOutput, calls=%fused_computation.1 | convolution fusion | flops 6291456 | bytes 18432 | tf_op jit(solution)/shard_map/dot_general | solution.py:85
  113.0 0.7 reshape.142
  113.7 8.1 %all-to-all-start.1 = ((f32[32,1,192]{2,1,0:T(1,128)}), f32[32,1,192]{2,1,0:T(1,128)S(1)}, u32[]{:S(2)}, u32[]{:S(2)}) async-start(f32[32,1,192]{2,1,0:T(1,128)} %reshape.142), calls=%async_computation.1 | async-start | bytes 65536 | tf_op jit(solution)/shard_map/all_to_all | solution.py:241
  121.9 9.6 %all-to-all-done.1 = f32[32,1,192]{2,1,0:T(1,128)S(1)} async-done(((f32[32,1,192]{2,1,0:T(1,128)}), f32[32,1,192]{2,1,0:T(1,128)S(1)}, u32[]{:S(2)}, u32[]{:S(2)}) %all-to-all-start.1) | async-done | bytes 24608 | tf_op jit(solution)/shard_map/all_to_all | solution.py:241
  131.5 0.5 broadcast.180
  132.0 0.7 reduce.12
  132.8 0.1 slice_reduce_fusion.2
  133.2 1.9 %fusion.7 = f32[134,128]{1,0:T(8,128)S(1)} fusion(s32[6144]{0:T(1024)S(1)} %get-tuple-element.44, f32[6144]{0:T(1024)S(1)} %pad_maximum_fusion.10, s32[6144]{0:T(1024)S(1)} %get-tuple-element.45), kind=kOutput, calls=%fused_computation.14 | convolution fusion | flops 216305664 | bytes 142336 | tf_op jit(solution)/shard_map/dot_general | solution.py:85
  135.1 1.9 %fusion.6 = f32[134,128]{1,0:T(8,128)S(1)} fusion(s32[6144]{0:T(1024)S(1)} %get-tuple-element.44, f32[6144]{0:T(1024)S(1)} %pad_maximum_fusion.10, s32[6144]{0:T(1024)S(1)} %get-tuple-element.45), kind=kOutput, calls=%fused_computation.13 | convolution fusion | flops 217878528 | bytes 142336 | tf_op jit(solution)/shard_map/dot_general | solution.py:85
  137.0 1.9 %fusion.28 = f32[134,128]{1,0:T(8,128)S(1)} fusion(f32[134,128]{1,0:T(8,128)S(1)} %fusion.6, f32[134,128]{1,0:T(8,128)S(1)} %fusion.7, f32[6144]{0:T(1024)S(1)} %pad_maximum_fusion.10, s32[6144]{0:T(1024)S(1)} %get-tuple-element.45, s32[6144]{0:T(1024)S(1)} %get-tuple-element.44), kind=kOutput, calls=%fused_computation.38 | convolution fusion | flops 214767104 | bytes 279552 | tf_op jit(solution)/shard_map/dot_general | solution.py:85
  138.9 1.0 fusion.26
  (74 shorter events, 1.4 us)
Async XLA Ops:
  0.6 1.0 copy-start
  0.6 11.6 %copy-start.9 = (s32[1,1,1024]{2,1,0:T(1,128)S(1)}, s32[1,1,1024]{2,1,0:T(1,128)}, u32[]{:S(2)}) copy-start(s32[1,1,1024]{2,1,0:T(1,128)} %param.16) | copy-start | bytes 12292
  0.7 11.6 %copy-start.3 = (s32[1,1,32,64]{3,2,1,0:T(8,128)S(1)}, s32[1,1,32,64]{3,2,1,0:T(8,128)}, u32[]{:S(2)}) copy-start(s32[1,1,32,64]{3,2,1,0:T(8,128)} %param.20) | copy-start | bytes 24580
  0.7 11.7 %copy-start.10 = (f32[1,1,128,128]{3,2,1,0:T(8,128)S(1)}, f32[1,1,128,128]{3,2,1,0:T(8,128)}, u32[]{:S(2)}) copy-start(f32[1,1,128,128]{3,2,1,0:T(8,128)} %param.21) | copy-start | bytes 196612
  3.9 4.0 %collective-permute-start = (f32[136,256]{1,0:T(8,128)S(1)}, f32[136,256]{1,0:T(8,128)S(1)}, u32[]{:S(2)}, u32[]{:S(2)}) collective-permute-start(f32[136,256]{1,0:T(8,128)S(1)} %get-tuple-element.32), channel_id=1, source_target_pairs={{0,32},{64,96},{128,160},{192,224},{256,288},{320,352},{384,416},{... | collective-permute-start | bytes 417800 | tf_op jit(solution)/shard_map/ppermute | solution.py:56
  5.7 2.5 %collective-permute-start.1 = (f32[136,256]{1,0:T(8,128)S(1)}, f32[136,256]{1,0:T(8,128)S(1)}, u32[]{:S(2)}, u32[]{:S(2)}) collective-permute-start(f32[136,256]{1,0:T(8,128)S(1)} %get-tuple-element.31), channel_id=1, source_target_pairs={{0,32},{64,96},{128,160},{192,224},{256,288},{320,352},{384,416},{... | collective-permute-start | bytes 417800 | tf_op jit(solution)/shard_map/ppermute | solution.py:56
  8.6 51.5 %copy-start.1 = (s32[1,1,24,1024]{3,2,1,0:T(8,128)S(1)}, s32[1,1,24,1024]{3,2,1,0:T(8,128)}, u32[]{:S(2)}) copy-start(s32[1,1,24,1024]{3,2,1,0:T(8,128)} %param.17) | copy-start | bytes 294916
  8.6 51.5 %copy-start.6 = (s32[1,1,32,64]{3,2,1,0:T(8,128)S(1)}, s32[1,1,32,64]{3,2,1,0:T(8,128)}, u32[]{:S(2)}) copy-start(s32[1,1,32,64]{3,2,1,0:T(8,128)} %param.19) | copy-start | bytes 24580
  8.6 1.6 %collective-permute-start.2 = (f32[136,256]{1,0:T(8,128)S(1)}, f32[136,256]{1,0:T(8,128)S(1)}, u32[]{:S(2)}, u32[]{:S(2)}) collective-permute-start(f32[136,256]{1,0:T(8,128)S(1)} %get-tuple-element.30), channel_id=1, source_target_pairs={{32,96},{96,160},{160,224},{224,288},{288,352},{352,416},{416,480}... | collective-permute-start | bytes 417800 | tf_op jit(solution)/shard_map/ppermute | solution.py:56
  9.5 0.9 collective-permute-start.3
  10.9 1.5 %collective-permute-start.4 = (f32[136,256]{1,0:T(8,128)S(1)}, f32[136,256]{1,0:T(8,128)S(1)}, u32[]{:S(2)}, u32[]{:S(2)}) collective-permute-start(f32[136,256]{1,0:T(8,128)S(1)} %get-tuple-element.28), channel_id=1, source_target_pairs={{32,160},{96,224},{160,288},{224,352},{288,416},{352,480},{33,161}... | collective-permute-start | bytes 417800 | tf_op jit(solution)/shard_map/ppermute | solution.py:56
  11.6 1.7 %collective-permute-start.6 = (f32[136,256]{1,0:T(8,128)S(1)}, f32[136,256]{1,0:T(8,128)S(1)}, u32[]{:S(2)}, u32[]{:S(2)}) collective-permute-start(f32[136,256]{1,0:T(8,128)S(1)} %get-tuple-element.27), channel_id=1, source_target_pairs={{32,160},{96,224},{160,288},{224,352},{288,416},{352,480},{33,161}... | collective-permute-start | bytes 417800 | tf_op jit(solution)/shard_map/ppermute | solution.py:56
  12.6 1.1 collective-permute-start.5
  13.9 28.2 %collective-permute-start.7 = (f32[16,256]{1,0:T(8,128)S(1)}, f32[16,256]{1,0:T(8,128)S(1)}, u32[]{:S(2)}, u32[]{:S(2)}) collective-permute-start(f32[16,256]{1,0:T(8,128)S(1)} %convolution_add_fusion.1), channel_id=1, source_target_pairs={{32,64},{96,128},{160,192},{224,256},{288,320},{352,384},{416,448}... | collective-permute-start | bytes 49160 | tf_op jit(solution)/shard_map/ppermute | solution.py:74
  42.3 28.6 %copy-start.2 = (f32[16,256]{1,0:T(8,128)}, f32[16,256]{1,0:T(8,128)S(1)}, u32[]{:S(2)}) copy-start(f32[16,256]{1,0:T(8,128)S(1)} %convolution_add_fusion) | copy-start | bytes 49156
  43.1 27.0 %all-to-all-start = ((f32[32,16,256]{2,1,0:T(8,128)}), f32[32,16,256]{2,1,0:T(8,128)S(1)}, u32[]{:S(2)}, u32[]{:S(2)}) async-start(f32[32,16,256]{2,1,0:T(8,128)} %broadcast_in_dim.52), calls=%async_computation | async-start | bytes 1048576 | tf_op jit(solution)/shard_map/all_to_all | solution.py:208
  56.3 6.0 %collective-permute-start.8 = (f32[19,128]{1,0:T(8,128)S(1)}, f32[19,128]{1,0:T(8,128)S(1)}, u32[]{:S(2)}, u32[]{:S(2)}) collective-permute-start(f32[19,128]{1,0:T(8,128)S(1)} %get-tuple-element.14), channel_id=1, source_target_pairs={{0,1},{1,2},{2,3},{3,4},{4,5},{5,6},{6,7},{7,8},{8,9},{9,10},{10,1... | collective-permute-start | bytes 29192 | tf_op jit(solution)/shard_map/ppermute | solution.py:229
  60.8 5.6 %collective-permute-start.9 = (f32[19,128]{1,0:T(8,128)S(1)}, f32[19,128]{1,0:T(8,128)S(1)}, u32[]{:S(2)}, u32[]{:S(2)}) collective-permute-start(f32[19,128]{1,0:T(8,128)S(1)} %get-tuple-element.15), channel_id=1, source_target_pairs={{1,0},{2,1},{3,2},{4,3},{5,4},{6,5},{7,6},{8,7},{9,8},{10,9},{11,1... | collective-permute-start | bytes 29192 | tf_op jit(solution)/shard_map/ppermute | solution.py:230
  62.3 59.6 %copy-start.4 = (f32[19,128]{1,0:T(8,128)}, f32[19,128]{1,0:T(8,128)S(1)}, u32[]{:S(2)}) copy-start(f32[19,128]{1,0:T(8,128)S(1)} %collective-permute-done.8) | copy-start | bytes 29188
  66.4 55.5 %copy-start.5 = (f32[19,128]{1,0:T(8,128)}, f32[19,128]{1,0:T(8,128)S(1)}, u32[]{:S(2)}) copy-start(f32[19,128]{1,0:T(8,128)S(1)} %collective-permute-done.9) | copy-start | bytes 29188
  74.4 27.6 %copy-start.7 = (f32[24,24]{1,0:T(8,128)S(1)}, f32[24,24]{1,0:T(8,128)}, u32[]{:S(2)}) copy-start(f32[24,24]{1,0:T(8,128)} %param.15) | copy-start | bytes 6916
  74.4 32.9 %copy-start.8 = (f32[1,1,1024]{2,1,0:T(1,128)S(1)}, f32[1,1,1024]{2,1,0:T(1,128)}, u32[]{:S(2)}) copy-start(f32[1,1,1024]{2,1,0:T(1,128)} %param.18) | copy-start | bytes 12292
  113.7 17.7 %all-to-all-start.1 = ((f32[32,1,192]{2,1,0:T(1,128)}), f32[32,1,192]{2,1,0:T(1,128)S(1)}, u32[]{:S(2)}, u32[]{:S(2)}) async-start(f32[32,1,192]{2,1,0:T(1,128)} %reshape.142), calls=%async_computation.1 | async-start | bytes 65536 | tf_op jit(solution)/shard_map/all_to_all | solution.py:241
  136.9 1.9 %slice-start = ((f32[19,128]{1,0:T(8,128)}), f32[3,128]{1,0:T(4,128)S(1)}, s32[]{:S(2)}) async-start(f32[19,128]{1,0:T(8,128)} %copy-done.4), calls=%async_computation.2 | async-start | bytes 4096 | tf_op jit(solution)/shard_map/slice | solution.py:234
  136.9 1.9 %slice-start.1 = ((f32[19,128]{1,0:T(8,128)}), f32[3,128]{1,0:T(4,128)S(1)}, s32[]{:S(2)}) async-start(f32[19,128]{1,0:T(8,128)} %copy-done.5), calls=%async_computation.3 | async-start | bytes 4096 | tf_op jit(solution)/shard_map/slice | solution.py:234

commit v13 on v11

--- a/solution.py
+++ b/solution.py
@@ -137,14 +137,15 @@
     ).astype(jnp.float32)
     spread = spread.astype(jnp.bfloat16)
     rest = panels
-    wide = None
+    parts = []
     for _ in range(3):
         rounded = lax.reduce_precision(rest, exponent_bits=8, mantissa_bits=7)
         rest = rest - rounded
-        part = rounded.astype(jnp.bfloat16)
-        term = lax.dot_general(part, spread, (((1,), (0,)), ((), ())), preferred_element_type=jnp.float32)
-        wide = term if wide is None else wide + term
-    wide = wide.reshape(slabs * panel_order, 128)
+        parts.append(rounded.astype(jnp.bfloat16))
+    terms = lax.dot_general(
+        jnp.concatenate(parts, axis=0), spread, (((1,), (0,)), ((), ())), preferred_element_type=jnp.float32
+    ).reshape(3, slabs * panel_order, 128)
+    wide = (terms[0] + terms[1]) + terms[2]
     total = lookup.shape[0]
     out_rows = total // pack
     chunks = 2

time: 135 us -> 136 us (level)
  other arithmetic: 5.85 us -> 8.92 us
  matrix products: 17.5 us -> 15.1 us
    add x1, other arithmetic: 0.01 us -> 2.96 us  [gathered_rows(): wide = terms[0] + terms[1] + terms[2]]
    dot_general x3 -> x1, matrix products: 4.28 us -> 1.85 us  [gathered_rows(): lax.dot_general(jnp.concatenate(parts, axis=0), spread, (((1,), (0,)), ((...]
where the time goes in v13:
time: 136 us; the launch traced here: 135 us
  waiting for transfers between devices  44.5 us (33%)
  starting transfers between devices  33.7 us (25%)
  Pallas kernels  27.6 us (20%)
  matrix products  15.1 us (11%)
  other arithmetic  8.92 us (7%)
  local copies, waits for them, and re-layouts  4.26 us (3%)
    pallas_call x1, Pallas kernels, gathered_rows(): pl.pallas_call(gather_kernel, out_shape=jax.ShapeDtypeStruct((out_rows, 1...  27.6 us
    ppermute x1, waiting for transfers between devices, interface_chain(): lax.ppermute(offset, 'grp', [(g, g + 1) for g in range(1, levels - 1, 2)])  26.6 us
    all_to_all x1, starting transfers between devices, on_device(): lax.all_to_all(copies, 'dev', split_axis=0, concat_axis=0, tiled=True)  13.2 us
    all_to_all x1, waiting for transfers between devices, on_device(): lax.all_to_all(triple, 'dev', split_axis=0, concat_axis=0, tiled=True)  9.79 us
    all_to_all x1, starting transfers between devices, on_device(): lax.all_to_all(triple, 'dev', split_axis=0, concat_axis=0, tiled=True)  7.81 us
    dot_general x11, matrix products, product(): jnp.dot(left, right, precision=exact_mode, preferred_element_type=jnp.flo...  5.4 us
    dot_general x1, matrix products, on_device(): forces = jnp.einsum('ij,jab->iab', stiffness, motion, precision=exact_mode)  5.01 us
    ppermute x1, waiting for transfers between devices, on_device(): lax.ppermute(to_left, 'dev', [(i + 1, i) for i in range(count - 1)])  4.23 us
  transfers between devices with their start and end apart: 12, of which 4 were waited for; matrix products, arithmetic and copies ran while one was open for 2% of the time, Pallas kernels for 0%

profile of v13, /device:TPU:40, one launch (start us, length us, event | category | flops | bytes accessed | tf_op | source)
XLA Modules:
  0.0 135.3 jit_solution(2445744323338968911)
XLA Ops:
  0.7 0.9 copy-done
  1.6 1.3 convolution_negate_fusion
  2.9 0.9 fusion.25
  3.9 1.7 %collective-permute-start = (f32[136,256]{1,0:T(8,128)S(1)}, f32[136,256]{1,0:T(8,128)S(1)}, u32[]{:S(2)}, u32[]{:S(2)}) collective-permute-start(f32[136,256]{1,0:T(8,128)S(1)} %get-tuple-element.37), channel_id=1, source_target_pairs={{0,32},{64,96},{128,160},{192,224},{256,288},{320,352},{384,416},{... | collective-permute-start | bytes 417800 | tf_op jit(solution)/shard_map/ppermute | solution.py:56
  5.7 1.3 collective-permute-start.1
  7.0 0.9 select_reduce_fusion.1
  8.0 0.2 convolution_add_fusion.4
  8.2 0.4 fusion.21
  8.6 0.7 collective-permute-start.2
  9.3 0.1 multiply_reduce_fusion
  9.4 0.7 collective-permute-start.3
  10.1 0.2 convolution_add_fusion.3
  10.4 0.4 fusion.19
  10.8 0.7 collective-permute-start.4
  11.5 0.7 collective-permute-start.6
  12.5 0.2 convolution_add_fusion.2
  12.7 0.7 collective-permute-start.5
  13.4 0.4 fusion.17
  13.8 0.2 convolution_add_fusion.1
  14.0 1.3 collective-permute-start.7
  15.3 26.6 %collective-permute-done.7 = f32[16,256]{1,0:T(8,128)S(1)} collective-permute-done((f32[16,256]{1,0:T(8,128)S(1)}, f32[16,256]{1,0:T(8,128)S(1)}, u32[]{:S(2)}, u32[]{:S(2)}) %collective-permute-start.7) | collective-permute-done | bytes 16416 | tf_op jit(solution)/shard_map/ppermute | solution.py:74
  41.9 0.2 convolution_add_fusion
  42.2 0.9 broadcast_in_dim.160
  43.0 13.2 %all-to-all-start = ((f32[32,16,256]{2,1,0:T(8,128)}), f32[32,16,256]{2,1,0:T(8,128)S(1)}, u32[]{:S(2)}, u32[]{:S(2)}) async-start(f32[32,16,256]{2,1,0:T(8,128)} %broadcast_in_dim.160), calls=%async_computation | async-start | bytes 1048576 | tf_op jit(solution)/shard_map/all_to_all | solution.py:209
  56.2 3.7 %collective-permute-start.8 = (f32[19,128]{1,0:T(8,128)S(1)}, f32[19,128]{1,0:T(8,128)S(1)}, u32[]{:S(2)}, u32[]{:S(2)}) collective-permute-start(f32[19,128]{1,0:T(8,128)S(1)} %get-tuple-element.14), channel_id=1, source_target_pairs={{0,1},{1,2},{2,3},{3,4},{4,5},{5,6},{6,7},{7,8},{8,9},{9,10},{10,1... | collective-permute-start | bytes 29192 | tf_op jit(solution)/shard_map/ppermute | solution.py:230
  60.0 0.7 add.177.lookup_ref
  60.6 1.3 collective-permute-start.9
  62.0 4.2 %collective-permute-done.9 = f32[19,128]{1,0:T(8,128)S(1)} collective-permute-done((f32[19,128]{1,0:T(8,128)S(1)}, f32[19,128]{1,0:T(8,128)S(1)}, u32[]{:S(2)}, u32[]{:S(2)}) %collective-permute-start.9) | collective-permute-done | bytes 9760 | tf_op jit(solution)/shard_map/ppermute | solution.py:231
  66.3 3.8 %all-to-all-done = f32[32,16,256]{2,1,0:T(8,128)S(1)} async-done(((f32[32,16,256]{2,1,0:T(8,128)}), f32[32,16,256]{2,1,0:T(8,128)S(1)}, u32[]{:S(2)}, u32[]{:S(2)}) %all-to-all-start) | async-done | bytes 524320 | tf_op jit(solution)/shard_map/all_to_all | solution.py:209
  70.0 0.1 reduce-precision_convert_fusion.1
  70.2 1.9 %fusion.9 = f32[96,256,128]{2,1,0:T(8,128)S(1)} fusion(bf16[32,16,256]{2,1,0:T(8,128)(2,1)S(1)} %get-tuple-element.30, bf16[32,16,256]{2,1,0:T(8,128)(2,1)S(1)} %get-tuple-element.31, bf16[32,16,256]{2,1,0:T(8,128)(2,1)S(1)} %get-tuple-element.29, s32[128]{0:T(128)S(1)} %get-tuple-element.63, s32[128]{0:T(128)S(1)} %get-tuple-element.64, ...), kind=kOutput, calls=%fused_computation.23 | convolution fusion | flops 101457920 | bytes 13370496 | tf_op jit(solution)/shard_map/dot_general | solution.py:145
  72.0 3.0 %slice_add_fusion = f32[32,256,128]{2,1,0:T(8,128)} fusion(f32[96,256,128]{2,1,0:T(8,128)S(1)} %fusion.9), kind=kLoop, calls=%fused_computation | loop fusion | flops 2097152 | bytes 16777216 | tf_op jit(solution)/shard_map/add | solution.py:148
  75.0 27.6 %shard_map.131 = f32[3072,128]{1,0:T(8,128)} custom-call(s32[24576]{0:T(1024)} %add.177.lookup_ref, f32[8192,128]{1,0:T(8,128)} %bitcast.103), custom_call_target="tpu_custom_call" | custom-call | bytes 5767168 | tf_op jit(solution)/shard_map/pallas_call | solution.py:153
  102.6 5.0 %fusion.3 = f32[128,128]{1,0:T(8,128)S(1)} fusion(f32[24,128,128]{2,1,0:T(8,128)} %bitcast.104, f32[24,24]{1,0:T(8,128)S(1)} %copy-done.7), kind=kOutput, calls=%fused_computation.8 | convolution fusion | flops 114016256 | bytes 1640704 | tf_op jit(solution)/shard_map/ij,jab->iab/dot_general | solution.py:216
  107.6 0.1 copy.25
  107.7 0.1 copy.26
  107.8 0.1 reshape.226
  107.9 3.1 %select_reduce_fusion = f32[2048]{0:T(1024)S(1)} fusion(f32[128]{0:T(128)S(1)} %get-tuple-element.54, f32[128]{0:T(128)S(1)} %get-tuple-element.55, f32[128]{0:T(128)S(1)} %get-tuple-element.56, f32[128]{0:T(128)S(1)} %get-tuple-element.57, f32[128]{0:T(128)S(1)} %get-tuple-element.58, f32[128]{0:T(128)S(1)} %get-tuple-element.59, ...), kind=kLoop, calls=%fused_computation.21 | loop fusion | flops 4716544 | bytes 36864 | tf_op jit(solution)/shard_map/reduce_sum | solution.py:88
  111.2 0.1 stack_reshape.3
  111.3 0.7 reshape.247
  112.0 7.8 %all-to-all-start.1 = ((f32[32,1,192]{2,1,0:T(1,128)}), f32[32,1,192]{2,1,0:T(1,128)S(1)}, u32[]{:S(2)}, u32[]{:S(2)}) async-start(f32[32,1,192]{2,1,0:T(1,128)} %reshape.247), calls=%async_computation.1 | async-start | bytes 65536 | tf_op jit(solution)/shard_map/all_to_all | solution.py:242
  119.9 9.8 %all-to-all-done.1 = f32[32,1,192]{2,1,0:T(1,128)S(1)} async-done(((f32[32,1,192]{2,1,0:T(1,128)}), f32[32,1,192]{2,1,0:T(1,128)S(1)}, u32[]{:S(2)}, u32[]{:S(2)}) %all-to-all-start.1) | async-done | bytes 24608 | tf_op jit(solution)/shard_map/all_to_all | solution.py:242
  129.7 0.5 broadcast.407
  130.2 0.7 reduce.12
  130.9 0.1 reshape.248
  131.0 0.1 slice_reduce_fusion.2
  131.4 2.8 %fusion = f32[134,128]{1,0:T(8,128)S(1)} fusion(s32[6144]{0:T(1024)S(1)} %get-tuple-element.61, f32[6144]{0:T(1024)S(1)} %pad_maximum_fusion.10, s32[6144]{0:T(1024)S(1)} %get-tuple-element.62), kind=kOutput, calls=%fused_computation.3 | convolution fusion | flops 1266978816 | bytes 142336 | tf_op jit(solution)/shard_map/dot_general | solution.py:98
  134.2 1.0 fusion.8
  (69 shorter events, 1.0 us)
Async XLA Ops:
  0.6 1.0 copy-start
  0.6 11.5 %copy-start.9 = (s32[1,1,1024]{2,1,0:T(1,128)S(1)}, s32[1,1,1024]{2,1,0:T(1,128)}, u32[]{:S(2)}) copy-start(s32[1,1,1024]{2,1,0:T(1,128)} %param.16) | copy-start | bytes 12292
  0.7 11.6 %copy-start.6 = (s32[1,1,32,64]{3,2,1,0:T(8,128)S(1)}, s32[1,1,32,64]{3,2,1,0:T(8,128)}, u32[]{:S(2)}) copy-start(s32[1,1,32,64]{3,2,1,0:T(8,128)} %param.19) | copy-start | bytes 24580
  0.7 9.7 %copy-start.3 = (s32[1,1,32,64]{3,2,1,0:T(8,128)S(1)}, s32[1,1,32,64]{3,2,1,0:T(8,128)}, u32[]{:S(2)}) copy-start(s32[1,1,32,64]{3,2,1,0:T(8,128)} %param.20) | copy-start | bytes 24580
  0.7 11.8 %copy-start.10 = (f32[1,1,128,128]{3,2,1,0:T(8,128)S(1)}, f32[1,1,128,128]{3,2,1,0:T(8,128)}, u32[]{:S(2)}) copy-start(f32[1,1,128,128]{3,2,1,0:T(8,128)} %param.21) | copy-start | bytes 196612
  3.9 4.0 %collective-permute-start = (f32[136,256]{1,0:T(8,128)S(1)}, f32[136,256]{1,0:T(8,128)S(1)}, u32[]{:S(2)}, u32[]{:S(2)}) collective-permute-start(f32[136,256]{1,0:T(8,128)S(1)} %get-tuple-element.37), channel_id=1, source_target_pairs={{0,32},{64,96},{128,160},{192,224},{256,288},{320,352},{384,416},{... | collective-permute-start | bytes 417800 | tf_op jit(solution)/shard_map/ppermute | solution.py:56
  5.7 2.5 %collective-permute-start.1 = (f32[136,256]{1,0:T(8,128)S(1)}, f32[136,256]{1,0:T(8,128)S(1)}, u32[]{:S(2)}, u32[]{:S(2)}) collective-permute-start(f32[136,256]{1,0:T(8,128)S(1)} %get-tuple-element.36), channel_id=1, source_target_pairs={{0,32},{64,96},{128,160},{192,224},{256,288},{320,352},{384,416},{... | collective-permute-start | bytes 417800 | tf_op jit(solution)/shard_map/ppermute | solution.py:56
  8.6 51.4 %copy-start.1 = (s32[1,1,24,1024]{3,2,1,0:T(8,128)S(1)}, s32[1,1,24,1024]{3,2,1,0:T(8,128)}, u32[]{:S(2)}) copy-start(s32[1,1,24,1024]{3,2,1,0:T(8,128)} %param.17) | copy-start | bytes 294916
  8.6 1.5 %collective-permute-start.2 = (f32[136,256]{1,0:T(8,128)S(1)}, f32[136,256]{1,0:T(8,128)S(1)}, u32[]{:S(2)}, u32[]{:S(2)}) collective-permute-start(f32[136,256]{1,0:T(8,128)S(1)} %get-tuple-element.35), channel_id=1, source_target_pairs={{32,96},{96,160},{160,224},{224,288},{288,352},{352,416},{416,480}... | collective-permute-start | bytes 417800 | tf_op jit(solution)/shard_map/ppermute | solution.py:56
  9.4 1.0 collective-permute-start.3
  10.8 1.6 %collective-permute-start.4 = (f32[136,256]{1,0:T(8,128)S(1)}, f32[136,256]{1,0:T(8,128)S(1)}, u32[]{:S(2)}, u32[]{:S(2)}) collective-permute-start(f32[136,256]{1,0:T(8,128)S(1)} %get-tuple-element.33), channel_id=1, source_target_pairs={{32,160},{96,224},{160,288},{224,352},{288,416},{352,480},{33,161}... | collective-permute-start | bytes 417800 | tf_op jit(solution)/shard_map/ppermute | solution.py:56
  11.5 1.9 %collective-permute-start.6 = (f32[136,256]{1,0:T(8,128)S(1)}, f32[136,256]{1,0:T(8,128)S(1)}, u32[]{:S(2)}, u32[]{:S(2)}) collective-permute-start(f32[136,256]{1,0:T(8,128)S(1)} %get-tuple-element.32), channel_id=1, source_target_pairs={{32,160},{96,224},{160,288},{224,352},{288,416},{352,480},{33,161}... | collective-permute-start | bytes 417800 | tf_op jit(solution)/shard_map/ppermute | solution.py:56
  12.7 1.1 collective-permute-start.5
  14.0 27.9 %collective-permute-start.7 = (f32[16,256]{1,0:T(8,128)S(1)}, f32[16,256]{1,0:T(8,128)S(1)}, u32[]{:S(2)}, u32[]{:S(2)}) collective-permute-start(f32[16,256]{1,0:T(8,128)S(1)} %convolution_add_fusion.1), channel_id=1, source_target_pairs={{32,64},{96,128},{160,192},{224,256},{288,320},{352,384},{416,448}... | collective-permute-start | bytes 49160 | tf_op jit(solution)/shard_map/ppermute | solution.py:74
  42.1 29.9 %copy-start.2 = (f32[16,256]{1,0:T(8,128)}, f32[16,256]{1,0:T(8,128)S(1)}, u32[]{:S(2)}) copy-start(f32[16,256]{1,0:T(8,128)S(1)} %convolution_add_fusion) | copy-start | bytes 49156
  43.0 27.0 %all-to-all-start = ((f32[32,16,256]{2,1,0:T(8,128)}), f32[32,16,256]{2,1,0:T(8,128)S(1)}, u32[]{:S(2)}, u32[]{:S(2)}) async-start(f32[32,16,256]{2,1,0:T(8,128)} %broadcast_in_dim.160), calls=%async_computation | async-start | bytes 1048576 | tf_op jit(solution)/shard_map/all_to_all | solution.py:209
  56.2 5.7 %collective-permute-start.8 = (f32[19,128]{1,0:T(8,128)S(1)}, f32[19,128]{1,0:T(8,128)S(1)}, u32[]{:S(2)}, u32[]{:S(2)}) collective-permute-start(f32[19,128]{1,0:T(8,128)S(1)} %get-tuple-element.14), channel_id=1, source_target_pairs={{0,1},{1,2},{2,3},{3,4},{4,5},{5,6},{6,7},{7,8},{8,9},{9,10},{10,1... | collective-permute-start | bytes 29192 | tf_op jit(solution)/shard_map/ppermute | solution.py:230
  60.6 5.6 %collective-permute-start.9 = (f32[19,128]{1,0:T(8,128)S(1)}, f32[19,128]{1,0:T(8,128)S(1)}, u32[]{:S(2)}, u32[]{:S(2)}) collective-permute-start(f32[19,128]{1,0:T(8,128)S(1)} %get-tuple-element.15), channel_id=1, source_target_pairs={{1,0},{2,1},{3,2},{4,3},{5,4},{6,5},{7,6},{8,7},{9,8},{10,9},{11,1... | collective-permute-start | bytes 29192 | tf_op jit(solution)/shard_map/ppermute | solution.py:231
  61.9 57.9 %copy-start.4 = (f32[19,128]{1,0:T(8,128)}, f32[19,128]{1,0:T(8,128)S(1)}, u32[]{:S(2)}) copy-start(f32[19,128]{1,0:T(8,128)S(1)} %collective-permute-done.8) | copy-start | bytes 29188
  66.2 53.7 %copy-start.5 = (f32[19,128]{1,0:T(8,128)}, f32[19,128]{1,0:T(8,128)S(1)}, u32[]{:S(2)}) copy-start(f32[19,128]{1,0:T(8,128)S(1)} %collective-permute-done.9) | copy-start | bytes 29188
  75.0 27.6 %copy-start.7 = (f32[24,24]{1,0:T(8,128)S(1)}, f32[24,24]{1,0:T(8,128)}, u32[]{:S(2)}) copy-start(f32[24,24]{1,0:T(8,128)} %param.15) | copy-start | bytes 6916
  75.0 32.9 %copy-start.8 = (f32[1,1,1024]{2,1,0:T(1,128)S(1)}, f32[1,1,1024]{2,1,0:T(1,128)}, u32[]{:S(2)}) copy-start(f32[1,1,1024]{2,1,0:T(1,128)} %param.18) | copy-start | bytes 12292
  112.0 17.7 %all-to-all-start.1 = ((f32[32,1,192]{2,1,0:T(1,128)}), f32[32,1,192]{2,1,0:T(1,128)S(1)}, u32[]{:S(2)}, u32[]{:S(2)}) async-start(f32[32,1,192]{2,1,0:T(1,128)} %reshape.247), calls=%async_computation.1 | async-start | bytes 65536 | tf_op jit(solution)/shard_map/all_to_all | solution.py:242
  119.9 14.3 %slice-start = ((f32[19,128]{1,0:T(8,128)}), f32[3,128]{1,0:T(4,128)S(1)}, s32[]{:S(2)}) async-start(f32[19,128]{1,0:T(8,128)} %copy-done.4), calls=%async_computation.2 | async-start | bytes 4096 | tf_op jit(solution)/shard_map/slice | solution.py:235
  119.9 14.3 %slice-start.1 = ((f32[19,128]{1,0:T(8,128)}), f32[3,128]{1,0:T(4,128)S(1)}, s32[]{:S(2)}) async-start(f32[19,128]{1,0:T(8,128)} %copy-done.5), calls=%async_computation.3 | async-start | bytes 4096 | tf_op jit(solution)/shard_map/slice | solution.py:235

commit v14 on v11

--- a/solution.py
+++ b/solution.py
@@ -212,7 +212,7 @@
     dofs, elements = lookup.shape
     pack = 128 // order
     motion = gathered_rows(panels, lookup.reshape(-1)).reshape(dofs, elements // pack, 128)
-    forces = jnp.einsum("ij,jab->iab", stiffness, motion, precision=exact_mode)
+    forces = jnp.einsum("ij,jab->iab", stiffness, motion, precision=lax.Precision.HIGH)
     energy = jnp.sum(jnp.sum(motion * forces, axis=0).reshape(elements // pack, pack, order), axis=2)
     energy = energy.reshape(elements)
     density = element_density[0, 0]

time: 135 us -> 134 us (level)
  no operation moved by 1% of the time
where the time goes in v14:
time: 134 us
  waiting for transfers between devices  44.3 us (33%)
  starting transfers between devices  33.8 us (25%)
  Pallas kernels  27.6 us (21%)
  matrix products  16.7 us (12%)
  other arithmetic  5.85 us (4%)
  local copies, waits for them, and re-layouts  4.25 us (3%)
    pallas_call x1, Pallas kernels, gathered_rows(): pl.pallas_call(gather_kernel, out_shape=jax.ShapeDtypeStruct((out_rows, 1...  27.6 us
    ppermute x1, waiting for transfers between devices, interface_chain(): lax.ppermute(offset, 'grp', [(g, g + 1) for g in range(1, levels - 1, 2)])  26.6 us
    all_to_all x1, starting transfers between devices, on_device(): lax.all_to_all(copies, 'dev', split_axis=0, concat_axis=0, tiled=True)  13.2 us
    all_to_all x1, waiting for transfers between devices, on_device(): lax.all_to_all(triple, 'dev', split_axis=0, concat_axis=0, tiled=True)  9.61 us
    all_to_all x1, starting transfers between devices, on_device(): lax.all_to_all(triple, 'dev', split_axis=0, concat_axis=0, tiled=True)  7.99 us
    dot_general x11, matrix products, product(): jnp.dot(left, right, precision=exact_mode, preferred_element_type=jnp.flo...  5.41 us
    dot_general x3, matrix products, gathered_rows(): lax.dot_general(part, spread, (((1,), (0,)), ((), ())), preferred_element...  4.28 us
    ppermute x1, waiting for transfers between devices, on_device(): lax.ppermute(to_left, 'dev', [(i + 1, i) for i in range(count - 1)])  4.23 us
  transfers between devices with their start and end apart: 12, of which 4 were waited for; matrix products, arithmetic and copies ran while one was open for 2% of the time, Pallas kernels for 0%

profile of v14, /device:TPU:40, one launch (start us, length us, event | category | flops | bytes accessed | tf_op | source)
XLA Modules:
  0.0 133.8 jit_solution(9812782443481004625)
XLA Ops:
  0.7 0.9 copy-done
  1.6 1.3 convolution_negate_fusion
  2.9 0.9 fusion.22
  3.9 1.7 %collective-permute-start = (f32[136,256]{1,0:T(8,128)S(1)}, f32[136,256]{1,0:T(8,128)S(1)}, u32[]{:S(2)}, u32[]{:S(2)}) collective-permute-start(f32[136,256]{1,0:T(8,128)S(1)} %get-tuple-element.34), channel_id=1, source_target_pairs={{0,32},{64,96},{128,160},{192,224},{256,288},{320,352},{384,416},{... | collective-permute-start | bytes 417800 | tf_op jit(solution)/shard_map/ppermute | solution.py:56
  5.7 1.3 collective-permute-start.1
  7.0 0.9 select_reduce_fusion.1
  8.0 0.2 convolution_add_fusion.4
  8.2 0.4 fusion.18
  8.6 0.7 collective-permute-start.2
  9.3 0.1 multiply_reduce_fusion
  9.4 0.7 collective-permute-start.3
  10.1 0.2 convolution_add_fusion.3
  10.4 0.4 fusion.16
  10.8 0.7 collective-permute-start.4
  11.5 0.7 collective-permute-start.6
  12.5 0.2 convolution_add_fusion.2
  12.7 0.7 collective-permute-start.5
  13.4 0.4 fusion.14
  13.8 0.2 convolution_add_fusion.1
  14.0 1.3 collective-permute-start.7
  15.3 26.6 %collective-permute-done.7 = f32[16,256]{1,0:T(8,128)S(1)} collective-permute-done((f32[16,256]{1,0:T(8,128)S(1)}, f32[16,256]{1,0:T(8,128)S(1)}, u32[]{:S(2)}, u32[]{:S(2)}) %collective-permute-start.7) | collective-permute-done | bytes 16416 | tf_op jit(solution)/shard_map/ppermute | solution.py:74
  41.9 0.2 convolution_add_fusion
  42.2 0.9 broadcast_in_dim.160
  43.0 13.2 %all-to-all-start = ((f32[32,16,256]{2,1,0:T(8,128)}), f32[32,16,256]{2,1,0:T(8,128)S(1)}, u32[]{:S(2)}, u32[]{:S(2)}) async-start(f32[32,16,256]{2,1,0:T(8,128)} %broadcast_in_dim.160), calls=%async_computation | async-start | bytes 1048576 | tf_op jit(solution)/shard_map/all_to_all | solution.py:208
  56.2 3.7 %collective-permute-start.8 = (f32[19,128]{1,0:T(8,128)S(1)}, f32[19,128]{1,0:T(8,128)S(1)}, u32[]{:S(2)}, u32[]{:S(2)}) collective-permute-start(f32[19,128]{1,0:T(8,128)S(1)} %get-tuple-element.14), channel_id=1, source_target_pairs={{0,1},{1,2},{2,3},{3,4},{4,5},{5,6},{6,7},{7,8},{8,9},{9,10},{10,1... | collective-permute-start | bytes 29192 | tf_op jit(solution)/shard_map/ppermute | solution.py:229
  60.0 0.7 add.178.lookup_ref
  60.6 1.3 collective-permute-start.9
  62.0 4.2 %collective-permute-done.9 = f32[19,128]{1,0:T(8,128)S(1)} collective-permute-done((f32[19,128]{1,0:T(8,128)S(1)}, f32[19,128]{1,0:T(8,128)S(1)}, u32[]{:S(2)}, u32[]{:S(2)}) %collective-permute-start.9) | collective-permute-done | bytes 9760 | tf_op jit(solution)/shard_map/ppermute | solution.py:230
  66.2 3.8 %all-to-all-done = f32[32,16,256]{2,1,0:T(8,128)S(1)} async-done(((f32[32,16,256]{2,1,0:T(8,128)}), f32[32,16,256]{2,1,0:T(8,128)S(1)}, u32[]{:S(2)}, u32[]{:S(2)}) %all-to-all-start) | async-done | bytes 524320 | tf_op jit(solution)/shard_map/all_to_all | solution.py:208
  70.0 0.8 fusion.12
  70.8 0.8 fusion.13
  71.6 2.8 %add_add_fusion = f32[32,256,128]{2,1,0:T(8,128)} fusion(f32[32,256,128]{2,1,0:T(8,128)S(1)} %fusion.12, f32[32,256,128]{2,1,0:T(8,128)S(1)} %fusion.13, f32[32,16,256]{2,1,0:T(8,128)S(1)} %all-to-all-done, s32[128]{0:T(128)S(1)} %iota_and_fusion, s32[128]{0:T(128)S(1)} %broadcast_add_fusion, pred[128]{0:T(512)(128)(4,1)S(1)} %compare_and_fusion), kind=kOutput, calls=%fused_computation | convolution fusion | flops 36446208 | bytes 13108352 | tf_op jit(solution)/shard_map/dot_general | solution.py:145
  74.3 27.6 %shard_map.131 = f32[3072,128]{1,0:T(8,128)} custom-call(s32[24576]{0:T(1024)} %add.178.lookup_ref, f32[8192,128]{1,0:T(8,128)} %bitcast.105), custom_call_target="tpu_custom_call" | custom-call | bytes 5767168 | tf_op jit(solution)/shard_map/pallas_call | solution.py:152
  101.9 4.2 %fusion.3 = f32[128,128]{1,0:T(8,128)S(1)} fusion(f32[24,128,128]{2,1,0:T(8,128)} %bitcast.106, f32[24,24]{1,0:T(8,128)S(1)} %copy-done.7), kind=kOutput, calls=%fused_computation.7 | convolution fusion | flops 57393152 | bytes 1640704 | tf_op jit(solution)/shard_map/ij,jab->iab/dot_general | solution.py:215
  106.1 0.1 copy.25
  106.3 0.1 copy.26
  106.4 0.1 reshape.221
  106.5 3.1 %select_reduce_fusion = f32[2048]{0:T(1024)S(1)} fusion(f32[128]{0:T(128)S(1)} %get-tuple-element.51, f32[128]{0:T(128)S(1)} %get-tuple-element.52, f32[128]{0:T(128)S(1)} %get-tuple-element.53, f32[128]{0:T(128)S(1)} %get-tuple-element.54, f32[128]{0:T(128)S(1)} %get-tuple-element.55, f32[128]{0:T(128)S(1)} %get-tuple-element.56, ...), kind=kLoop, calls=%fused_computation.20 | loop fusion | flops 4716544 | bytes 36864 | tf_op jit(solution)/shard_map/reduce_sum | solution.py:88
  109.7 0.1 stack_reshape.3
  109.9 0.7 reshape.242
  110.6 8.0 %all-to-all-start.1 = ((f32[32,1,192]{2,1,0:T(1,128)}), f32[32,1,192]{2,1,0:T(1,128)S(1)}, u32[]{:S(2)}, u32[]{:S(2)}) async-start(f32[32,1,192]{2,1,0:T(1,128)} %reshape.242), calls=%async_computation.1 | async-start | bytes 65536 | tf_op jit(solution)/shard_map/all_to_all | solution.py:241
  118.6 9.6 %all-to-all-done.1 = f32[32,1,192]{2,1,0:T(1,128)S(1)} async-done(((f32[32,1,192]{2,1,0:T(1,128)}), f32[32,1,192]{2,1,0:T(1,128)S(1)}, u32[]{:S(2)}, u32[]{:S(2)}) %all-to-all-start.1) | async-done | bytes 24608 | tf_op jit(solution)/shard_map/all_to_all | solution.py:241
  128.2 0.5 broadcast.407
  128.8 0.7 reduce.12
  129.5 0.1 reshape.243
  129.6 0.1 slice_reduce_fusion.2
  129.9 2.8 %fusion = f32[134,128]{1,0:T(8,128)S(1)} fusion(s32[6144]{0:T(1024)S(1)} %get-tuple-element.58, f32[6144]{0:T(1024)S(1)} %pad_maximum_fusion.10, s32[6144]{0:T(1024)S(1)} %get-tuple-element.59), kind=kOutput, calls=%fused_computation.2 | convolution fusion | flops 1266978816 | bytes 142336 | tf_op jit(solution)/shard_map/dot_general | solution.py:98
  132.8 1.0 fusion.8
  (70 shorter events, 1.0 us)
Async XLA Ops:
  0.6 1.0 copy-start
  0.6 11.6 %copy-start.9 = (s32[1,1,1024]{2,1,0:T(1,128)S(1)}, s32[1,1,1024]{2,1,0:T(1,128)}, u32[]{:S(2)}) copy-start(s32[1,1,1024]{2,1,0:T(1,128)} %param.16) | copy-start | bytes 12292
  0.7 11.6 %copy-start.6 = (s32[1,1,32,64]{3,2,1,0:T(8,128)S(1)}, s32[1,1,32,64]{3,2,1,0:T(8,128)}, u32[]{:S(2)}) copy-start(s32[1,1,32,64]{3,2,1,0:T(8,128)} %param.19) | copy-start | bytes 24580
  0.7 9.7 %copy-start.3 = (s32[1,1,32,64]{3,2,1,0:T(8,128)S(1)}, s32[1,1,32,64]{3,2,1,0:T(8,128)}, u32[]{:S(2)}) copy-start(s32[1,1,32,64]{3,2,1,0:T(8,128)} %param.20) | copy-start | bytes 24580
  0.7 11.8 %copy-start.10 = (f32[1,1,128,128]{3,2,1,0:T(8,128)S(1)}, f32[1,1,128,128]{3,2,1,0:T(8,128)}, u32[]{:S(2)}) copy-start(f32[1,1,128,128]{3,2,1,0:T(8,128)} %param.21) | copy-start | bytes 196612
  3.9 4.0 %collective-permute-start = (f32[136,256]{1,0:T(8,128)S(1)}, f32[136,256]{1,0:T(8,128)S(1)}, u32[]{:S(2)}, u32[]{:S(2)}) collective-permute-start(f32[136,256]{1,0:T(8,128)S(1)} %get-tuple-element.34), channel_id=1, source_target_pairs={{0,32},{64,96},{128,160},{192,224},{256,288},{320,352},{384,416},{... | collective-permute-start | bytes 417800 | tf_op jit(solution)/shard_map/ppermute | solution.py:56
  5.7 2.5 %collective-permute-start.1 = (f32[136,256]{1,0:T(8,128)S(1)}, f32[136,256]{1,0:T(8,128)S(1)}, u32[]{:S(2)}, u32[]{:S(2)}) collective-permute-start(f32[136,256]{1,0:T(8,128)S(1)} %get-tuple-element.33), channel_id=1, source_target_pairs={{0,32},{64,96},{128,160},{192,224},{256,288},{320,352},{384,416},{... | collective-permute-start | bytes 417800 | tf_op jit(solution)/shard_map/ppermute | solution.py:56
  8.6 51.3 %copy-start.1 = (s32[1,1,24,1024]{3,2,1,0:T(8,128)S(1)}, s32[1,1,24,1024]{3,2,1,0:T(8,128)}, u32[]{:S(2)}) copy-start(s32[1,1,24,1024]{3,2,1,0:T(8,128)} %param.17) | copy-start | bytes 294916
  8.6 1.5 %collective-permute-start.2 = (f32[136,256]{1,0:T(8,128)S(1)}, f32[136,256]{1,0:T(8,128)S(1)}, u32[]{:S(2)}, u32[]{:S(2)}) collective-permute-start(f32[136,256]{1,0:T(8,128)S(1)} %get-tuple-element.32), channel_id=1, source_target_pairs={{32,96},{96,160},{160,224},{224,288},{288,352},{352,416},{416,480}... | collective-permute-start | bytes 417800 | tf_op jit(solution)/shard_map/ppermute | solution.py:56
  9.4 1.0 collective-permute-start.3
  10.8 1.6 %collective-permute-start.4 = (f32[136,256]{1,0:T(8,128)S(1)}, f32[136,256]{1,0:T(8,128)S(1)}, u32[]{:S(2)}, u32[]{:S(2)}) collective-permute-start(f32[136,256]{1,0:T(8,128)S(1)} %get-tuple-element.30), channel_id=1, source_target_pairs={{32,160},{96,224},{160,288},{224,352},{288,416},{352,480},{33,161}... | collective-permute-start | bytes 417800 | tf_op jit(solution)/shard_map/ppermute | solution.py:56
  11.5 1.9 %collective-permute-start.6 = (f32[136,256]{1,0:T(8,128)S(1)}, f32[136,256]{1,0:T(8,128)S(1)}, u32[]{:S(2)}, u32[]{:S(2)}) collective-permute-start(f32[136,256]{1,0:T(8,128)S(1)} %get-tuple-element.29), channel_id=1, source_target_pairs={{32,160},{96,224},{160,288},{224,352},{288,416},{352,480},{33,161}... | collective-permute-start | bytes 417800 | tf_op jit(solution)/shard_map/ppermute | solution.py:56
  12.7 1.1 collective-permute-start.5
  14.0 27.9 %collective-permute-start.7 = (f32[16,256]{1,0:T(8,128)S(1)}, f32[16,256]{1,0:T(8,128)S(1)}, u32[]{:S(2)}, u32[]{:S(2)}) collective-permute-start(f32[16,256]{1,0:T(8,128)S(1)} %convolution_add_fusion.1), channel_id=1, source_target_pairs={{32,64},{96,128},{160,192},{224,256},{288,320},{352,384},{416,448}... | collective-permute-start | bytes 49160 | tf_op jit(solution)/shard_map/ppermute | solution.py:74
  42.1 28.7 %copy-start.2 = (f32[16,256]{1,0:T(8,128)}, f32[16,256]{1,0:T(8,128)S(1)}, u32[]{:S(2)}) copy-start(f32[16,256]{1,0:T(8,128)S(1)} %convolution_add_fusion) | copy-start | bytes 49156
  43.0 27.0 %all-to-all-start = ((f32[32,16,256]{2,1,0:T(8,128)}), f32[32,16,256]{2,1,0:T(8,128)S(1)}, u32[]{:S(2)}, u32[]{:S(2)}) async-start(f32[32,16,256]{2,1,0:T(8,128)} %broadcast_in_dim.160), calls=%async_computation | async-start | bytes 1048576 | tf_op jit(solution)/shard_map/all_to_all | solution.py:208
  56.2 5.7 %collective-permute-start.8 = (f32[19,128]{1,0:T(8,128)S(1)}, f32[19,128]{1,0:T(8,128)S(1)}, u32[]{:S(2)}, u32[]{:S(2)}) collective-permute-start(f32[19,128]{1,0:T(8,128)S(1)} %get-tuple-element.14), channel_id=1, source_target_pairs={{0,1},{1,2},{2,3},{3,4},{4,5},{5,6},{6,7},{7,8},{8,9},{9,10},{10,1... | collective-permute-start | bytes 29192 | tf_op jit(solution)/shard_map/ppermute | solution.py:229
  60.6 5.6 %collective-permute-start.9 = (f32[19,128]{1,0:T(8,128)S(1)}, f32[19,128]{1,0:T(8,128)S(1)}, u32[]{:S(2)}, u32[]{:S(2)}) collective-permute-start(f32[19,128]{1,0:T(8,128)S(1)} %get-tuple-element.15), channel_id=1, source_target_pairs={{1,0},{2,1},{3,2},{4,3},{5,4},{6,5},{7,6},{8,7},{9,8},{10,9},{11,1... | collective-permute-start | bytes 29192 | tf_op jit(solution)/shard_map/ppermute | solution.py:230
  61.9 56.7 %copy-start.4 = (f32[19,128]{1,0:T(8,128)}, f32[19,128]{1,0:T(8,128)S(1)}, u32[]{:S(2)}) copy-start(f32[19,128]{1,0:T(8,128)S(1)} %collective-permute-done.8) | copy-start | bytes 29188
  66.2 52.4 %copy-start.5 = (f32[19,128]{1,0:T(8,128)}, f32[19,128]{1,0:T(8,128)S(1)}, u32[]{:S(2)}) copy-start(f32[19,128]{1,0:T(8,128)S(1)} %collective-permute-done.9) | copy-start | bytes 29188
  74.3 27.6 %copy-start.7 = (f32[24,24]{1,0:T(8,128)S(1)}, f32[24,24]{1,0:T(8,128)}, u32[]{:S(2)}) copy-start(f32[24,24]{1,0:T(8,128)} %param.15) | copy-start | bytes 6916
  74.3 32.1 %copy-start.8 = (f32[1,1,1024]{2,1,0:T(1,128)S(1)}, f32[1,1,1024]{2,1,0:T(1,128)}, u32[]{:S(2)}) copy-start(f32[1,1,1024]{2,1,0:T(1,128)} %param.18) | copy-start | bytes 12292
  110.6 17.7 %all-to-all-start.1 = ((f32[32,1,192]{2,1,0:T(1,128)}), f32[32,1,192]{2,1,0:T(1,128)S(1)}, u32[]{:S(2)}, u32[]{:S(2)}) async-start(f32[32,1,192]{2,1,0:T(1,128)} %reshape.242), calls=%async_computation.1 | async-start | bytes 65536 | tf_op jit(solution)/shard_map/all_to_all | solution.py:241
  118.6 14.1 %slice-start = ((f32[19,128]{1,0:T(8,128)}), f32[3,128]{1,0:T(4,128)S(1)}, s32[]{:S(2)}) async-start(f32[19,128]{1,0:T(8,128)} %copy-done.4), calls=%async_computation.2 | async-start | bytes 4096 | tf_op jit(solution)/shard_map/slice | solution.py:234
  118.6 14.1 %slice-start.1 = ((f32[19,128]{1,0:T(8,128)}), f32[3,128]{1,0:T(4,128)S(1)}, s32[]{:S(2)}) async-start(f32[19,128]{1,0:T(8,128)} %copy-done.5), calls=%async_computation.3 | async-start | bytes 4096 | tf_op jit(solution)/shard_map/slice | solution.py:234

commit v15 on v14

--- a/solution.py
+++ b/solution.py
@@ -125,7 +125,7 @@
         out_ref[pl.ds(row, 1), :] = packed_row
         return carry
 
-    lax.fori_loop(0, rows, body, 0, unroll=8)
+    lax.fori_loop(0, rows, body, 0, unroll=16)
 
 
 def gathered_rows(panels, lookup):

time: 134 us -> 134 us (level)
  no operation moved by 1% of the time
where the time goes in v15:
time: 134 us; the launch traced here: 133 us
  waiting for transfers between devices  44.3 us (33%)
  starting transfers between devices  33.8 us (25%)
  Pallas kernels  26.7 us (20%)
  matrix products  16.7 us (12%)
  other arithmetic  5.85 us (4%)
  local copies, waits for them, and re-layouts  4.25 us (3%)
    pallas_call x1, Pallas kernels, gathered_rows(): pl.pallas_call(gather_kernel, out_shape=jax.ShapeDtypeStruct((out_rows, 1...  26.7 us
    ppermute x1, waiting for transfers between devices, interface_chain(): lax.ppermute(offset, 'grp', [(g, g + 1) for g in range(1, levels - 1, 2)])  26.6 us
    all_to_all x1, starting transfers between devices, on_device(): lax.all_to_all(copies, 'dev', split_axis=0, concat_axis=0, tiled=True)  13.2 us
    all_to_all x1, waiting for transfers between devices, on_device(): lax.all_to_all(triple, 'dev', split_axis=0, concat_axis=0, tiled=True)  9.61 us
    all_to_all x1, starting transfers between devices, on_device(): lax.all_to_all(triple, 'dev', split_axis=0, concat_axis=0, tiled=True)  7.99 us
    dot_general x11, matrix products, product(): jnp.dot(left, right, precision=exact_mode, preferred_element_type=jnp.flo...  5.41 us
    dot_general x3, matrix products, gathered_rows(): lax.dot_general(part, spread, (((1,), (0,)), ((), ())), preferred_element...  4.28 us
    ppermute x1, waiting for transfers between devices, on_device(): lax.ppermute(to_left, 'dev', [(i + 1, i) for i in range(count - 1)])  4.23 us
  transfers between devices with their start and end apart: 12, of which 4 were waited for; matrix products, arithmetic and copies ran while one was open for 2% of the time, Pallas kernels for 0%

profile of v15, /device:TPU:40, one launch (start us, length us, event | category | flops | bytes accessed | tf_op | source)
XLA Modules:
  0.0 132.9 jit_solution(9988773924477562649)
XLA Ops:
  0.7 0.9 copy-done
  1.6 1.3 convolution_negate_fusion
  2.9 0.9 fusion.22
  3.9 1.7 %collective-permute-start = (f32[136,256]{1,0:T(8,128)S(1)}, f32[136,256]{1,0:T(8,128)S(1)}, u32[]{:S(2)}, u32[]{:S(2)}) collective-permute-start(f32[136,256]{1,0:T(8,128)S(1)} %get-tuple-element.34), channel_id=1, source_target_pairs={{0,32},{64,96},{128,160},{192,224},{256,288},{320,352},{384,416},{... | collective-permute-start | bytes 417800 | tf_op jit(solution)/shard_map/ppermute | solution.py:56
  5.7 1.3 collective-permute-start.1
  7.0 0.9 select_reduce_fusion.1
  8.0 0.2 convolution_add_fusion.4
  8.2 0.4 fusion.18
  8.6 0.7 collective-permute-start.2
  9.3 0.1 multiply_reduce_fusion
  9.4 0.7 collective-permute-start.3
  10.1 0.2 convolution_add_fusion.3
  10.4 0.4 fusion.16
  10.8 0.7 collective-permute-start.4
  11.5 0.7 collective-permute-start.6
  12.5 0.2 convolution_add_fusion.2
  12.7 0.7 collective-permute-start.5
  13.4 0.4 fusion.14
  13.8 0.2 convolution_add_fusion.1
  14.0 1.3 collective-permute-start.7
  15.3 26.6 %collective-permute-done.7 = f32[16,256]{1,0:T(8,128)S(1)} collective-permute-done((f32[16,256]{1,0:T(8,128)S(1)}, f32[16,256]{1,0:T(8,128)S(1)}, u32[]{:S(2)}, u32[]{:S(2)}) %collective-permute-start.7) | collective-permute-done | bytes 16416 | tf_op jit(solution)/shard_map/ppermute | solution.py:74
  41.9 0.2 convolution_add_fusion
  42.2 0.9 broadcast_in_dim.160
  43.0 13.2 %all-to-all-start = ((f32[32,16,256]{2,1,0:T(8,128)}), f32[32,16,256]{2,1,0:T(8,128)S(1)}, u32[]{:S(2)}, u32[]{:S(2)}) async-start(f32[32,16,256]{2,1,0:T(8,128)} %broadcast_in_dim.160), calls=%async_computation | async-start | bytes 1048576 | tf_op jit(solution)/shard_map/all_to_all | solution.py:208
  56.2 3.7 %collective-permute-start.8 = (f32[19,128]{1,0:T(8,128)S(1)}, f32[19,128]{1,0:T(8,128)S(1)}, u32[]{:S(2)}, u32[]{:S(2)}) collective-permute-start(f32[19,128]{1,0:T(8,128)S(1)} %get-tuple-element.14), channel_id=1, source_target_pairs={{0,1},{1,2},{2,3},{3,4},{4,5},{5,6},{6,7},{7,8},{8,9},{9,10},{10,1... | collective-permute-start | bytes 29192 | tf_op jit(solution)/shard_map/ppermute | solution.py:229
  60.0 0.7 add.178.lookup_ref
  60.6 1.3 collective-permute-start.9
  62.0 4.2 %collective-permute-done.9 = f32[19,128]{1,0:T(8,128)S(1)} collective-permute-done((f32[19,128]{1,0:T(8,128)S(1)}, f32[19,128]{1,0:T(8,128)S(1)}, u32[]{:S(2)}, u32[]{:S(2)}) %collective-permute-start.9) | collective-permute-done | bytes 9760 | tf_op jit(solution)/shard_map/ppermute | solution.py:230
  66.2 3.8 %all-to-all-done = f32[32,16,256]{2,1,0:T(8,128)S(1)} async-done(((f32[32,16,256]{2,1,0:T(8,128)}), f32[32,16,256]{2,1,0:T(8,128)S(1)}, u32[]{:S(2)}, u32[]{:S(2)}) %all-to-all-start) | async-done | bytes 524320 | tf_op jit(solution)/shard_map/all_to_all | solution.py:208
  70.0 0.8 fusion.12
  70.8 0.8 fusion.13
  71.6 2.8 %add_add_fusion = f32[32,256,128]{2,1,0:T(8,128)} fusion(f32[32,256,128]{2,1,0:T(8,128)S(1)} %fusion.12, f32[32,256,128]{2,1,0:T(8,128)S(1)} %fusion.13, f32[32,16,256]{2,1,0:T(8,128)S(1)} %all-to-all-done, s32[128]{0:T(128)S(1)} %iota_and_fusion, s32[128]{0:T(128)S(1)} %broadcast_add_fusion, pred[128]{0:T(512)(128)(4,1)S(1)} %compare_and_fusion), kind=kOutput, calls=%fused_computation | convolution fusion | flops 36446208 | bytes 13108352 | tf_op jit(solution)/shard_map/dot_general | solution.py:145
  74.3 26.7 %shard_map.131 = f32[3072,128]{1,0:T(8,128)} custom-call(s32[24576]{0:T(1024)} %add.178.lookup_ref, f32[8192,128]{1,0:T(8,128)} %bitcast.105), custom_call_target="tpu_custom_call" | custom-call | bytes 5767168 | tf_op jit(solution)/shard_map/pallas_call | solution.py:152
  101.0 4.2 %fusion.3 = f32[128,128]{1,0:T(8,128)S(1)} fusion(f32[24,128,128]{2,1,0:T(8,128)} %bitcast.106, f32[24,24]{1,0:T(8,128)S(1)} %copy-done.7), kind=kOutput, calls=%fused_computation.7 | convolution fusion | flops 57393152 | bytes 1640704 | tf_op jit(solution)/shard_map/ij,jab->iab/dot_general | solution.py:215
  105.2 0.1 copy.25
  105.3 0.1 copy.26
  105.4 0.1 reshape.221
  105.6 3.1 %select_reduce_fusion = f32[2048]{0:T(1024)S(1)} fusion(f32[128]{0:T(128)S(1)} %get-tuple-element.51, f32[128]{0:T(128)S(1)} %get-tuple-element.52, f32[128]{0:T(128)S(1)} %get-tuple-element.53, f32[128]{0:T(128)S(1)} %get-tuple-element.54, f32[128]{0:T(128)S(1)} %get-tuple-element.55, f32[128]{0:T(128)S(1)} %get-tuple-element.56, ...), kind=kLoop, calls=%fused_computation.20 | loop fusion | flops 4716544 | bytes 36864 | tf_op jit(solution)/shard_map/reduce_sum | solution.py:88
  108.8 0.1 stack_reshape.3
  109.0 0.7 reshape.242
  109.7 8.0 %all-to-all-start.1 = ((f32[32,1,192]{2,1,0:T(1,128)}), f32[32,1,192]{2,1,0:T(1,128)S(1)}, u32[]{:S(2)}, u32[]{:S(2)}) async-start(f32[32,1,192]{2,1,0:T(1,128)} %reshape.242), calls=%async_computation.1 | async-start | bytes 65536 | tf_op jit(solution)/shard_map/all_to_all | solution.py:241
  117.7 9.6 %all-to-all-done.1 = f32[32,1,192]{2,1,0:T(1,128)S(1)} async-done(((f32[32,1,192]{2,1,0:T(1,128)}), f32[32,1,192]{2,1,0:T(1,128)S(1)}, u32[]{:S(2)}, u32[]{:S(2)}) %all-to-all-start.1) | async-done | bytes 24608 | tf_op jit(solution)/shard_map/all_to_all | solution.py:241
  127.3 0.5 broadcast.407
  127.8 0.7 reduce.12
  128.6 0.1 reshape.243
  128.7 0.1 slice_reduce_fusion.2
  129.0 2.8 %fusion = f32[134,128]{1,0:T(8,128)S(1)} fusion(s32[6144]{0:T(1024)S(1)} %get-tuple-element.58, f32[6144]{0:T(1024)S(1)} %pad_maximum_fusion.10, s32[6144]{0:T(1024)S(1)} %get-tuple-element.59), kind=kOutput, calls=%fused_computation.2 | convolution fusion | flops 1266978816 | bytes 142336 | tf_op jit(solution)/shard_map/dot_general | solution.py:98
  131.8 1.0 fusion.8
  (70 shorter events, 1.0 us)
Async XLA Ops:
  0.6 1.0 copy-start
  0.6 11.6 %copy-start.9 = (s32[1,1,1024]{2,1,0:T(1,128)S(1)}, s32[1,1,1024]{2,1,0:T(1,128)}, u32[]{:S(2)}) copy-start(s32[1,1,1024]{2,1,0:T(1,128)} %param.16) | copy-start | bytes 12292
  0.7 11.6 %copy-start.6 = (s32[1,1,32,64]{3,2,1,0:T(8,128)S(1)}, s32[1,1,32,64]{3,2,1,0:T(8,128)}, u32[]{:S(2)}) copy-start(s32[1,1,32,64]{3,2,1,0:T(8,128)} %param.19) | copy-start | bytes 24580
  0.7 9.7 %copy-start.3 = (s32[1,1,32,64]{3,2,1,0:T(8,128)S(1)}, s32[1,1,32,64]{3,2,1,0:T(8,128)}, u32[]{:S(2)}) copy-start(s32[1,1,32,64]{3,2,1,0:T(8,128)} %param.20) | copy-start | bytes 24580
  0.7 11.8 %copy-start.10 = (f32[1,1,128,128]{3,2,1,0:T(8,128)S(1)}, f32[1,1,128,128]{3,2,1,0:T(8,128)}, u32[]{:S(2)}) copy-start(f32[1,1,128,128]{3,2,1,0:T(8,128)} %param.21) | copy-start | bytes 196612
  3.9 4.0 %collective-permute-start = (f32[136,256]{1,0:T(8,128)S(1)}, f32[136,256]{1,0:T(8,128)S(1)}, u32[]{:S(2)}, u32[]{:S(2)}) collective-permute-start(f32[136,256]{1,0:T(8,128)S(1)} %get-tuple-element.34), channel_id=1, source_target_pairs={{0,32},{64,96},{128,160},{192,224},{256,288},{320,352},{384,416},{... | collective-permute-start | bytes 417800 | tf_op jit(solution)/shard_map/ppermute | solution.py:56
  5.7 2.5 %collective-permute-start.1 = (f32[136,256]{1,0:T(8,128)S(1)}, f32[136,256]{1,0:T(8,128)S(1)}, u32[]{:S(2)}, u32[]{:S(2)}) collective-permute-start(f32[136,256]{1,0:T(8,128)S(1)} %get-tuple-element.33), channel_id=1, source_target_pairs={{0,32},{64,96},{128,160},{192,224},{256,288},{320,352},{384,416},{... | collective-permute-start | bytes 417800 | tf_op jit(solution)/shard_map/ppermute | solution.py:56
  8.6 51.3 %copy-start.1 = (s32[1,1,24,1024]{3,2,1,0:T(8,128)S(1)}, s32[1,1,24,1024]{3,2,1,0:T(8,128)}, u32[]{:S(2)}) copy-start(s32[1,1,24,1024]{3,2,1,0:T(8,128)} %param.17) | copy-start | bytes 294916
  8.6 1.5 %collective-permute-start.2 = (f32[136,256]{1,0:T(8,128)S(1)}, f32[136,256]{1,0:T(8,128)S(1)}, u32[]{:S(2)}, u32[]{:S(2)}) collective-permute-start(f32[136,256]{1,0:T(8,128)S(1)} %get-tuple-element.32), channel_id=1, source_target_pairs={{32,96},{96,160},{160,224},{224,288},{288,352},{352,416},{416,480}... | collective-permute-start | bytes 417800 | tf_op jit(solution)/shard_map/ppermute | solution.py:56
  9.4 1.0 collective-permute-start.3
  10.8 1.6 %collective-permute-start.4 = (f32[136,256]{1,0:T(8,128)S(1)}, f32[136,256]{1,0:T(8,128)S(1)}, u32[]{:S(2)}, u32[]{:S(2)}) collective-permute-start(f32[136,256]{1,0:T(8,128)S(1)} %get-tuple-element.30), channel_id=1, source_target_pairs={{32,160},{96,224},{160,288},{224,352},{288,416},{352,480},{33,161}... | collective-permute-start | bytes 417800 | tf_op jit(solution)/shard_map/ppermute | solution.py:56
  11.5 1.9 %collective-permute-start.6 = (f32[136,256]{1,0:T(8,128)S(1)}, f32[136,256]{1,0:T(8,128)S(1)}, u32[]{:S(2)}, u32[]{:S(2)}) collective-permute-start(f32[136,256]{1,0:T(8,128)S(1)} %get-tuple-element.29), channel_id=1, source_target_pairs={{32,160},{96,224},{160,288},{224,352},{288,416},{352,480},{33,161}... | collective-permute-start | bytes 417800 | tf_op jit(solution)/shard_map/ppermute | solution.py:56
  12.7 1.1 collective-permute-start.5
  14.0 27.9 %collective-permute-start.7 = (f32[16,256]{1,0:T(8,128)S(1)}, f32[16,256]{1,0:T(8,128)S(1)}, u32[]{:S(2)}, u32[]{:S(2)}) collective-permute-start(f32[16,256]{1,0:T(8,128)S(1)} %convolution_add_fusion.1), channel_id=1, source_target_pairs={{32,64},{96,128},{160,192},{224,256},{288,320},{352,384},{416,448}... | collective-permute-start | bytes 49160 | tf_op jit(solution)/shard_map/ppermute | solution.py:74
  42.1 28.7 %copy-start.2 = (f32[16,256]{1,0:T(8,128)}, f32[16,256]{1,0:T(8,128)S(1)}, u32[]{:S(2)}) copy-start(f32[16,256]{1,0:T(8,128)S(1)} %convolution_add_fusion) | copy-start | bytes 49156
  43.0 27.0 %all-to-all-start = ((f32[32,16,256]{2,1,0:T(8,128)}), f32[32,16,256]{2,1,0:T(8,128)S(1)}, u32[]{:S(2)}, u32[]{:S(2)}) async-start(f32[32,16,256]{2,1,0:T(8,128)} %broadcast_in_dim.160), calls=%async_computation | async-start | bytes 1048576 | tf_op jit(solution)/shard_map/all_to_all | solution.py:208
  56.2 5.7 %collective-permute-start.8 = (f32[19,128]{1,0:T(8,128)S(1)}, f32[19,128]{1,0:T(8,128)S(1)}, u32[]{:S(2)}, u32[]{:S(2)}) collective-permute-start(f32[19,128]{1,0:T(8,128)S(1)} %get-tuple-element.14), channel_id=1, source_target_pairs={{0,1},{1,2},{2,3},{3,4},{4,5},{5,6},{6,7},{7,8},{8,9},{9,10},{10,1... | collective-permute-start | bytes 29192 | tf_op jit(solution)/shard_map/ppermute | solution.py:229
  60.6 5.6 %collective-permute-start.9 = (f32[19,128]{1,0:T(8,128)S(1)}, f32[19,128]{1,0:T(8,128)S(1)}, u32[]{:S(2)}, u32[]{:S(2)}) collective-permute-start(f32[19,128]{1,0:T(8,128)S(1)} %get-tuple-element.15), channel_id=1, source_target_pairs={{1,0},{2,1},{3,2},{4,3},{5,4},{6,5},{7,6},{8,7},{9,8},{10,9},{11,1... | collective-permute-start | bytes 29192 | tf_op jit(solution)/shard_map/ppermute | solution.py:230
  61.9 55.8 %copy-start.4 = (f32[19,128]{1,0:T(8,128)}, f32[19,128]{1,0:T(8,128)S(1)}, u32[]{:S(2)}) copy-start(f32[19,128]{1,0:T(8,128)S(1)} %collective-permute-done.8) | copy-start | bytes 29188
  66.2 51.5 %copy-start.5 = (f32[19,128]{1,0:T(8,128)}, f32[19,128]{1,0:T(8,128)S(1)}, u32[]{:S(2)}) copy-start(f32[19,128]{1,0:T(8,128)S(1)} %collective-permute-done.9) | copy-start | bytes 29188
  74.3 26.7 %copy-start.7 = (f32[24,24]{1,0:T(8,128)S(1)}, f32[24,24]{1,0:T(8,128)}, u32[]{:S(2)}) copy-start(f32[24,24]{1,0:T(8,128)} %param.15) | copy-start | bytes 6916
  74.3 31.2 %copy-start.8 = (f32[1,1,1024]{2,1,0:T(1,128)S(1)}, f32[1,1,1024]{2,1,0:T(1,128)}, u32[]{:S(2)}) copy-start(f32[1,1,1024]{2,1,0:T(1,128)} %param.18) | copy-start | bytes 12292
  109.7 17.7 %all-to-all-start.1 = ((f32[32,1,192]{2,1,0:T(1,128)}), f32[32,1,192]{2,1,0:T(1,128)S(1)}, u32[]{:S(2)}, u32[]{:S(2)}) async-start(f32[32,1,192]{2,1,0:T(1,128)} %reshape.242), calls=%async_computation.1 | async-start | bytes 65536 | tf_op jit(solution)/shard_map/all_to_all | solution.py:241
  117.7 14.1 %slice-start = ((f32[19,128]{1,0:T(8,128)}), f32[3,128]{1,0:T(4,128)S(1)}, s32[]{:S(2)}) async-start(f32[19,128]{1,0:T(8,128)} %copy-done.4), calls=%async_computation.2 | async-start | bytes 4096 | tf_op jit(solution)/shard_map/slice | solution.py:234
  117.7 14.1 %slice-start.1 = ((f32[19,128]{1,0:T(8,128)}), f32[3,128]{1,0:T(4,128)S(1)}, s32[]{:S(2)}) async-start(f32[19,128]{1,0:T(8,128)} %copy-done.5), calls=%async_computation.3 | async-start | bytes 4096 | tf_op jit(solution)/shard_map/slice | solution.py:234

commit v16 on v15

--- a/solution.py
+++ b/solution.py
@@ -125,7 +125,7 @@
         out_ref[pl.ds(row, 1), :] = packed_row
         return carry
 
-    lax.fori_loop(0, rows, body, 0, unroll=16)
+    lax.fori_loop(0, rows, body, 0, unroll=32)
 
 
 def gathered_rows(panels, lookup):

time: 134 us -> 133 us (level)
  no operation moved by 1% of the time
where the time goes in v16:
time: 133 us; the launch traced here: 132 us
  waiting for transfers between devices  44.3 us (33%)
  starting transfers between devices  33.8 us (25%)
  Pallas kernels  26.2 us (20%)
  matrix products  16.7 us (13%)
  other arithmetic  5.85 us (4%)
  local copies, waits for them, and re-layouts  4.25 us (3%)
  between operations  1.33 us (1%)
    ppermute x1, waiting for transfers between devices, interface_chain(): lax.ppermute(offset, 'grp', [(g, g + 1) for g in range(1, levels - 1, 2)])  26.6 us
    pallas_call x1, Pallas kernels, gathered_rows(): pl.pallas_call(gather_kernel, out_shape=jax.ShapeDtypeStruct((out_rows, 1...  26.2 us
    all_to_all x1, starting transfers between devices, on_device(): lax.all_to_all(copies, 'dev', split_axis=0, concat_axis=0, tiled=True)  13.2 us
    all_to_all x1, waiting for transfers between devices, on_device(): lax.all_to_all(triple, 'dev', split_axis=0, concat_axis=0, tiled=True)  9.61 us
    all_to_all x1, starting transfers between devices, on_device(): lax.all_to_all(triple, 'dev', split_axis=0, concat_axis=0, tiled=True)  7.99 us
    dot_general x11, matrix products, product(): jnp.dot(left, right, precision=exact_mode, preferred_element_type=jnp.flo...  5.41 us
    dot_general x3, matrix products, gathered_rows(): lax.dot_general(part, spread, (((1,), (0,)), ((), ())), preferred_element...  4.28 us
    ppermute x1, waiting for transfers between devices, on_device(): lax.ppermute(to_left, 'dev', [(i + 1, i) for i in range(count - 1)])  4.23 us
  transfers between devices with their start and end apart: 12, of which 4 were waited for; matrix products, arithmetic and copies ran while one was open for 2% of the time, Pallas kernels for 0%

profile of v16, /device:TPU:40, one launch (start us, length us, event | category | flops | bytes accessed | tf_op | source)
XLA Modules:
  0.0 132.4 jit_solution(15261746767375182638)
XLA Ops:
  0.7 0.9 copy-done
  1.6 1.3 %convolution_negate_fusion = f32[256,256]{1,0:T(8,128)S(1)} fusion(f32[1,1,256,256]{3,2,1,0:T(8,128)} %param.13, f32[1,1,256,256]{3,2,1,0:T(8,128)S(1)} %copy-done), kind=kOutput, calls=%fused_computation.12 | convolution fusion | flops 201392128 | bytes 786432 | tf_op jit(solution)/shard_map/dot_general | solution.py:41
  2.9 0.9 fusion.22
  3.9 1.7 %collective-permute-start = (f32[136,256]{1,0:T(8,128)S(1)}, f32[136,256]{1,0:T(8,128)S(1)}, u32[]{:S(2)}, u32[]{:S(2)}) collective-permute-start(f32[136,256]{1,0:T(8,128)S(1)} %get-tuple-element.34), channel_id=1, source_target_pairs={{0,32},{64,96},{128,160},{192,224},{256,288},{320,352},{384,416},{... | collective-permute-start | bytes 417800 | tf_op jit(solution)/shard_map/ppermute | solution.py:56
  5.7 1.3 collective-permute-start.1
  7.0 0.9 select_reduce_fusion.1
  8.0 0.2 convolution_add_fusion.4
  8.2 0.4 fusion.18
  8.6 0.7 collective-permute-start.2
  9.3 0.1 multiply_reduce_fusion
  9.4 0.7 collective-permute-start.3
  10.1 0.2 convolution_add_fusion.3
  10.4 0.4 fusion.16
  10.8 0.7 collective-permute-start.4
  11.5 0.7 collective-permute-start.6
  12.5 0.2 convolution_add_fusion.2
  12.7 0.7 collective-permute-start.5
  13.4 0.4 fusion.14
  13.8 0.2 convolution_add_fusion.1
  14.0 1.3 collective-permute-start.7
  15.3 26.6 %collective-permute-done.7 = f32[16,256]{1,0:T(8,128)S(1)} collective-permute-done((f32[16,256]{1,0:T(8,128)S(1)}, f32[16,256]{1,0:T(8,128)S(1)}, u32[]{:S(2)}, u32[]{:S(2)}) %collective-permute-start.7) | collective-permute-done | bytes 16416 | tf_op jit(solution)/shard_map/ppermute | solution.py:74
  41.9 0.2 convolution_add_fusion
  42.2 0.9 broadcast_in_dim.160
  43.0 13.2 %all-to-all-start = ((f32[32,16,256]{2,1,0:T(8,128)}), f32[32,16,256]{2,1,0:T(8,128)S(1)}, u32[]{:S(2)}, u32[]{:S(2)}) async-start(f32[32,16,256]{2,1,0:T(8,128)} %broadcast_in_dim.160), calls=%async_computation | async-start | bytes 1048576 | tf_op jit(solution)/shard_map/all_to_all | solution.py:208
  56.2 3.7 %collective-permute-start.8 = (f32[19,128]{1,0:T(8,128)S(1)}, f32[19,128]{1,0:T(8,128)S(1)}, u32[]{:S(2)}, u32[]{:S(2)}) collective-permute-start(f32[19,128]{1,0:T(8,128)S(1)} %get-tuple-element.14), channel_id=1, source_target_pairs={{0,1},{1,2},{2,3},{3,4},{4,5},{5,6},{6,7},{7,8},{8,9},{9,10},{10,1... | collective-permute-start | bytes 29192 | tf_op jit(solution)/shard_map/ppermute | solution.py:229
  60.0 0.7 add.178.lookup_ref
  60.6 1.3 collective-permute-start.9
  62.0 4.2 %collective-permute-done.9 = f32[19,128]{1,0:T(8,128)S(1)} collective-permute-done((f32[19,128]{1,0:T(8,128)S(1)}, f32[19,128]{1,0:T(8,128)S(1)}, u32[]{:S(2)}, u32[]{:S(2)}) %collective-permute-start.9) | collective-permute-done | bytes 9760 | tf_op jit(solution)/shard_map/ppermute | solution.py:230
  66.2 3.8 %all-to-all-done = f32[32,16,256]{2,1,0:T(8,128)S(1)} async-done(((f32[32,16,256]{2,1,0:T(8,128)}), f32[32,16,256]{2,1,0:T(8,128)S(1)}, u32[]{:S(2)}, u32[]{:S(2)}) %all-to-all-start) | async-done | bytes 524320 | tf_op jit(solution)/shard_map/all_to_all | solution.py:208
  70.0 0.8 fusion.12
  70.8 0.8 fusion.13
  71.6 2.8 %add_add_fusion = f32[32,256,128]{2,1,0:T(8,128)} fusion(f32[32,256,128]{2,1,0:T(8,128)S(1)} %fusion.12, f32[32,256,128]{2,1,0:T(8,128)S(1)} %fusion.13, f32[32,16,256]{2,1,0:T(8,128)S(1)} %all-to-all-done, s32[128]{0:T(128)S(1)} %iota_and_fusion, s32[128]{0:T(128)S(1)} %broadcast_add_fusion, pred[128]{0:T(512)(128)(4,1)S(1)} %compare_and_fusion), kind=kOutput, calls=%fused_computation | convolution fusion | flops 36446208 | bytes 13108352 | tf_op jit(solution)/shard_map/dot_general | solution.py:145
  74.3 26.2 %shard_map.131 = f32[3072,128]{1,0:T(8,128)} custom-call(s32[24576]{0:T(1024)} %add.178.lookup_ref, f32[8192,128]{1,0:T(8,128)} %bitcast.105), custom_call_target="tpu_custom_call" | custom-call | bytes 5767168 | tf_op jit(solution)/shard_map/pallas_call | solution.py:152
  100.5 4.2 %fusion.3 = f32[128,128]{1,0:T(8,128)S(1)} fusion(f32[24,128,128]{2,1,0:T(8,128)} %bitcast.106, f32[24,24]{1,0:T(8,128)S(1)} %copy-done.7), kind=kOutput, calls=%fused_computation.7 | convolution fusion | flops 57393152 | bytes 1640704 | tf_op jit(solution)/shard_map/ij,jab->iab/dot_general | solution.py:215
  104.8 0.1 copy.25
  104.9 0.1 copy.26
  105.0 0.1 reshape.221
  105.1 3.1 %select_reduce_fusion = f32[2048]{0:T(1024)S(1)} fusion(f32[128]{0:T(128)S(1)} %get-tuple-element.51, f32[128]{0:T(128)S(1)} %get-tuple-element.52, f32[128]{0:T(128)S(1)} %get-tuple-element.53, f32[128]{0:T(128)S(1)} %get-tuple-element.54, f32[128]{0:T(128)S(1)} %get-tuple-element.55, f32[128]{0:T(128)S(1)} %get-tuple-element.56, ...), kind=kLoop, calls=%fused_computation.20 | loop fusion | flops 4716544 | bytes 36864 | tf_op jit(solution)/shard_map/reduce_sum | solution.py:88
  108.3 0.1 stack_reshape.3
  108.5 0.7 reshape.242
  109.2 8.0 %all-to-all-start.1 = ((f32[32,1,192]{2,1,0:T(1,128)}), f32[32,1,192]{2,1,0:T(1,128)S(1)}, u32[]{:S(2)}, u32[]{:S(2)}) async-start(f32[32,1,192]{2,1,0:T(1,128)} %reshape.242), calls=%async_computation.1 | async-start | bytes 65536 | tf_op jit(solution)/shard_map/all_to_all | solution.py:241
  117.3 9.6 %all-to-all-done.1 = f32[32,1,192]{2,1,0:T(1,128)S(1)} async-done(((f32[32,1,192]{2,1,0:T(1,128)}), f32[32,1,192]{2,1,0:T(1,128)S(1)}, u32[]{:S(2)}, u32[]{:S(2)}) %all-to-all-start.1) | async-done | bytes 24608 | tf_op jit(solution)/shard_map/all_to_all | solution.py:241
  126.9 0.5 broadcast.407
  127.4 0.7 reduce.12
  128.1 0.1 reshape.243
  128.2 0.1 slice_reduce_fusion.2
  128.6 2.8 %fusion = f32[134,128]{1,0:T(8,128)S(1)} fusion(s32[6144]{0:T(1024)S(1)} %get-tuple-element.58, f32[6144]{0:T(1024)S(1)} %pad_maximum_fusion.10, s32[6144]{0:T(1024)S(1)} %get-tuple-element.59), kind=kOutput, calls=%fused_computation.2 | convolution fusion | flops 1266978816 | bytes 142336 | tf_op jit(solution)/shard_map/dot_general | solution.py:98
  131.4 1.0 fusion.8
  (70 shorter events, 1.0 us)
Async XLA Ops:
  0.6 1.0 copy-start
  0.6 11.6 %copy-start.9 = (s32[1,1,1024]{2,1,0:T(1,128)S(1)}, s32[1,1,1024]{2,1,0:T(1,128)}, u32[]{:S(2)}) copy-start(s32[1,1,1024]{2,1,0:T(1,128)} %param.16) | copy-start | bytes 12292
  0.7 11.6 %copy-start.6 = (s32[1,1,32,64]{3,2,1,0:T(8,128)S(1)}, s32[1,1,32,64]{3,2,1,0:T(8,128)}, u32[]{:S(2)}) copy-start(s32[1,1,32,64]{3,2,1,0:T(8,128)} %param.19) | copy-start | bytes 24580
  0.7 9.7 %copy-start.3 = (s32[1,1,32,64]{3,2,1,0:T(8,128)S(1)}, s32[1,1,32,64]{3,2,1,0:T(8,128)}, u32[]{:S(2)}) copy-start(s32[1,1,32,64]{3,2,1,0:T(8,128)} %param.20) | copy-start | bytes 24580
  0.7 11.8 %copy-start.10 = (f32[1,1,128,128]{3,2,1,0:T(8,128)S(1)}, f32[1,1,128,128]{3,2,1,0:T(8,128)}, u32[]{:S(2)}) copy-start(f32[1,1,128,128]{3,2,1,0:T(8,128)} %param.21) | copy-start | bytes 196612
  3.9 4.0 %collective-permute-start = (f32[136,256]{1,0:T(8,128)S(1)}, f32[136,256]{1,0:T(8,128)S(1)}, u32[]{:S(2)}, u32[]{:S(2)}) collective-permute-start(f32[136,256]{1,0:T(8,128)S(1)} %get-tuple-element.34), channel_id=1, source_target_pairs={{0,32},{64,96},{128,160},{192,224},{256,288},{320,352},{384,416},{... | collective-permute-start | bytes 417800 | tf_op jit(solution)/shard_map/ppermute | solution.py:56
  5.7 2.5 %collective-permute-start.1 = (f32[136,256]{1,0:T(8,128)S(1)}, f32[136,256]{1,0:T(8,128)S(1)}, u32[]{:S(2)}, u32[]{:S(2)}) collective-permute-start(f32[136,256]{1,0:T(8,128)S(1)} %get-tuple-element.33), channel_id=1, source_target_pairs={{0,32},{64,96},{128,160},{192,224},{256,288},{320,352},{384,416},{... | collective-permute-start | bytes 417800 | tf_op jit(solution)/shard_map/ppermute | solution.py:56
  8.6 51.3 %copy-start.1 = (s32[1,1,24,1024]{3,2,1,0:T(8,128)S(1)}, s32[1,1,24,1024]{3,2,1,0:T(8,128)}, u32[]{:S(2)}) copy-start(s32[1,1,24,1024]{3,2,1,0:T(8,128)} %param.17) | copy-start | bytes 294916
  8.6 1.5 %collective-permute-start.2 = (f32[136,256]{1,0:T(8,128)S(1)}, f32[136,256]{1,0:T(8,128)S(1)}, u32[]{:S(2)}, u32[]{:S(2)}) collective-permute-start(f32[136,256]{1,0:T(8,128)S(1)} %get-tuple-element.32), channel_id=1, source_target_pairs={{32,96},{96,160},{160,224},{224,288},{288,352},{352,416},{416,480}... | collective-permute-start | bytes 417800 | tf_op jit(solution)/shard_map/ppermute | solution.py:56
  9.4 1.0 collective-permute-start.3
  10.8 1.6 %collective-permute-start.4 = (f32[136,256]{1,0:T(8,128)S(1)}, f32[136,256]{1,0:T(8,128)S(1)}, u32[]{:S(2)}, u32[]{:S(2)}) collective-permute-start(f32[136,256]{1,0:T(8,128)S(1)} %get-tuple-element.30), channel_id=1, source_target_pairs={{32,160},{96,224},{160,288},{224,352},{288,416},{352,480},{33,161}... | collective-permute-start | bytes 417800 | tf_op jit(solution)/shard_map/ppermute | solution.py:56
  11.5 1.9 %collective-permute-start.6 = (f32[136,256]{1,0:T(8,128)S(1)}, f32[136,256]{1,0:T(8,128)S(1)}, u32[]{:S(2)}, u32[]{:S(2)}) collective-permute-start(f32[136,256]{1,0:T(8,128)S(1)} %get-tuple-element.29), channel_id=1, source_target_pairs={{32,160},{96,224},{160,288},{224,352},{288,416},{352,480},{33,161}... | collective-permute-start | bytes 417800 | tf_op jit(solution)/shard_map/ppermute | solution.py:56
  12.7 1.1 collective-permute-start.5
  14.0 27.9 %collective-permute-start.7 = (f32[16,256]{1,0:T(8,128)S(1)}, f32[16,256]{1,0:T(8,128)S(1)}, u32[]{:S(2)}, u32[]{:S(2)}) collective-permute-start(f32[16,256]{1,0:T(8,128)S(1)} %convolution_add_fusion.1), channel_id=1, source_target_pairs={{32,64},{96,128},{160,192},{224,256},{288,320},{352,384},{416,448}... | collective-permute-start | bytes 49160 | tf_op jit(solution)/shard_map/ppermute | solution.py:74
  42.1 28.7 %copy-start.2 = (f32[16,256]{1,0:T(8,128)}, f32[16,256]{1,0:T(8,128)S(1)}, u32[]{:S(2)}) copy-start(f32[16,256]{1,0:T(8,128)S(1)} %convolution_add_fusion) | copy-start | bytes 49156
  43.0 27.0 %all-to-all-start = ((f32[32,16,256]{2,1,0:T(8,128)}), f32[32,16,256]{2,1,0:T(8,128)S(1)}, u32[]{:S(2)}, u32[]{:S(2)}) async-start(f32[32,16,256]{2,1,0:T(8,128)} %broadcast_in_dim.160), calls=%async_computation | async-start | bytes 1048576 | tf_op jit(solution)/shard_map/all_to_all | solution.py:208
  56.2 5.7 %collective-permute-start.8 = (f32[19,128]{1,0:T(8,128)S(1)}, f32[19,128]{1,0:T(8,128)S(1)}, u32[]{:S(2)}, u32[]{:S(2)}) collective-permute-start(f32[19,128]{1,0:T(8,128)S(1)} %get-tuple-element.14), channel_id=1, source_target_pairs={{0,1},{1,2},{2,3},{3,4},{4,5},{5,6},{6,7},{7,8},{8,9},{9,10},{10,1... | collective-permute-start | bytes 29192 | tf_op jit(solution)/shard_map/ppermute | solution.py:229
  60.6 5.6 %collective-permute-start.9 = (f32[19,128]{1,0:T(8,128)S(1)}, f32[19,128]{1,0:T(8,128)S(1)}, u32[]{:S(2)}, u32[]{:S(2)}) collective-permute-start(f32[19,128]{1,0:T(8,128)S(1)} %get-tuple-element.15), channel_id=1, source_target_pairs={{1,0},{2,1},{3,2},{4,3},{5,4},{6,5},{7,6},{8,7},{9,8},{10,9},{11,1... | collective-permute-start | bytes 29192 | tf_op jit(solution)/shard_map/ppermute | solution.py:230
  61.9 55.3 %copy-start.4 = (f32[19,128]{1,0:T(8,128)}, f32[19,128]{1,0:T(8,128)S(1)}, u32[]{:S(2)}) copy-start(f32[19,128]{1,0:T(8,128)S(1)} %collective-permute-done.8) | copy-start | bytes 29188
  66.2 51.0 %copy-start.5 = (f32[19,128]{1,0:T(8,128)}, f32[19,128]{1,0:T(8,128)S(1)}, u32[]{:S(2)}) copy-start(f32[19,128]{1,0:T(8,128)S(1)} %collective-permute-done.9) | copy-start | bytes 29188
  74.3 26.2 %copy-start.7 = (f32[24,24]{1,0:T(8,128)S(1)}, f32[24,24]{1,0:T(8,128)}, u32[]{:S(2)}) copy-start(f32[24,24]{1,0:T(8,128)} %param.15) | copy-start | bytes 6916
  74.3 30.8 %copy-start.8 = (f32[1,1,1024]{2,1,0:T(1,128)S(1)}, f32[1,1,1024]{2,1,0:T(1,128)}, u32[]{:S(2)}) copy-start(f32[1,1,1024]{2,1,0:T(1,128)} %param.18) | copy-start | bytes 12292
  109.2 17.7 %all-to-all-start.1 = ((f32[32,1,192]{2,1,0:T(1,128)}), f32[32,1,192]{2,1,0:T(1,128)S(1)}, u32[]{:S(2)}, u32[]{:S(2)}) async-start(f32[32,1,192]{2,1,0:T(1,128)} %reshape.242), calls=%async_computation.1 | async-start | bytes 65536 | tf_op jit(solution)/shard_map/all_to_all | solution.py:241
  117.2 14.1 %slice-start = ((f32[19,128]{1,0:T(8,128)}), f32[3,128]{1,0:T(4,128)S(1)}, s32[]{:S(2)}) async-start(f32[19,128]{1,0:T(8,128)} %copy-done.4), calls=%async_computation.2 | async-start | bytes 4096 | tf_op jit(solution)/shard_map/slice | solution.py:234
  117.3 14.1 %slice-start.1 = ((f32[19,128]{1,0:T(8,128)}), f32[3,128]{1,0:T(4,128)S(1)}, s32[]{:S(2)}) async-start(f32[19,128]{1,0:T(8,128)} %copy-done.5), calls=%async_computation.3 | async-start | bytes 4096 | tf_op jit(solution)/shard_map/slice | solution.py:234

commit v17 on v16

--- a/solution.py
+++ b/solution.py
@@ -138,7 +138,7 @@
     spread = spread.astype(jnp.bfloat16)
     rest = panels
     wide = None
-    for _ in range(3):
+    for _ in range(2):
         rounded = lax.reduce_precision(rest, exponent_bits=8, mantissa_bits=7)
         rest = rest - rounded
         part = rounded.astype(jnp.bfloat16)

time: 133 us -> 132 us (level)
    dot_general x3 -> x2, matrix products: 4.28 us -> 3.5 us  [gathered_rows(): lax.dot_general(part, spread, (((1,), (0,)), ((), ())), preferred_element...]
where the time goes in v17:
time: 132 us
  waiting for transfers between devices  44.3 us (34%)
  starting transfers between devices  33.8 us (26%)
  Pallas kernels  26.2 us (20%)
  matrix products  15.9 us (12%)
  other arithmetic  5.85 us (4%)
  local copies, waits for them, and re-layouts  4.25 us (3%)
  between operations  1.33 us (1%)
    ppermute x1, waiting for transfers between devices, interface_chain(): lax.ppermute(offset, 'grp', [(g, g + 1) for g in range(1, levels - 1, 2)])  26.6 us
    pallas_call x1, Pallas kernels, gathered_rows(): pl.pallas_call(gather_kernel, out_shape=jax.ShapeDtypeStruct((out_rows, 1...  26.2 us
    all_to_all x1, starting transfers between devices, on_device(): lax.all_to_all(copies, 'dev', split_axis=0, concat_axis=0, tiled=True)  13.2 us
    all_to_all x1, waiting for transfers between devices, on_device(): lax.all_to_all(triple, 'dev', split_axis=0, concat_axis=0, tiled=True)  9.61 us
    all_to_all x1, starting transfers between devices, on_device(): lax.all_to_all(triple, 'dev', split_axis=0, concat_axis=0, tiled=True)  7.99 us
    dot_general x11, matrix products, product(): jnp.dot(left, right, precision=exact_mode, preferred_element_type=jnp.flo...  5.41 us
    ppermute x1, waiting for transfers between devices, on_device(): lax.ppermute(to_left, 'dev', [(i + 1, i) for i in range(count - 1)])  4.23 us
    dot_general x1, matrix products, on_device(): jnp.einsum('ij,jab->iab', stiffness, motion, precision=lax.Precision.HIGH)  4.22 us
  transfers between devices with their start and end apart: 12, of which 4 were waited for; matrix products, arithmetic and copies ran while one was open for 2% of the time, Pallas kernels for 0%

profile of v17, /device:TPU:40, one launch (start us, length us, event | category | flops | bytes accessed | tf_op | source)
XLA Modules:
  0.0 131.6 jit_solution(5615597940084035013)
XLA Ops:
  0.7 0.9 copy-done
  1.6 1.3 %convolution_negate_fusion = f32[256,256]{1,0:T(8,128)S(1)} fusion(f32[1,1,256,256]{3,2,1,0:T(8,128)} %param.13, f32[1,1,256,256]{3,2,1,0:T(8,128)S(1)} %copy-done), kind=kOutput, calls=%fused_computation.12 | convolution fusion | flops 201392128 | bytes 786432 | tf_op jit(solution)/shard_map/dot_general | solution.py:41
  2.9 0.9 fusion.21
  3.9 1.7 %collective-permute-start = (f32[136,256]{1,0:T(8,128)S(1)}, f32[136,256]{1,0:T(8,128)S(1)}, u32[]{:S(2)}, u32[]{:S(2)}) collective-permute-start(f32[136,256]{1,0:T(8,128)S(1)} %get-tuple-element.34), channel_id=1, source_target_pairs={{0,32},{64,96},{128,160},{192,224},{256,288},{320,352},{384,416},{... | collective-permute-start | bytes 417800 | tf_op jit(solution)/shard_map/ppermute | solution.py:56
  5.7 1.3 collective-permute-start.1
  7.0 0.9 select_reduce_fusion.1
  8.0 0.2 convolution_add_fusion.5
  8.2 0.4 fusion.17
  8.6 0.7 collective-permute-start.2
  9.3 0.1 multiply_reduce_fusion
  9.4 0.7 collective-permute-start.3
  10.1 0.2 convolution_add_fusion.4
  10.4 0.1 squeeze.25
  10.4 0.4 fusion.15
  10.8 0.7 collective-permute-start.4
  11.5 0.7 collective-permute-start.6
  12.5 0.2 convolution_add_fusion.3
  12.7 0.7 collective-permute-start.5
  13.4 0.4 fusion.13
  13.8 0.2 convolution_add_fusion.2
  14.0 1.3 collective-permute-start.7
  15.3 26.6 %collective-permute-done.7 = f32[16,256]{1,0:T(8,128)S(1)} collective-permute-done((f32[16,256]{1,0:T(8,128)S(1)}, f32[16,256]{1,0:T(8,128)S(1)}, u32[]{:S(2)}, u32[]{:S(2)}) %collective-permute-start.7) | collective-permute-done | bytes 16416 | tf_op jit(solution)/shard_map/ppermute | solution.py:74
  41.9 0.2 convolution_add_fusion.1
  42.2 0.9 broadcast_in_dim.160
  43.0 13.2 %all-to-all-start = ((f32[32,16,256]{2,1,0:T(8,128)}), f32[32,16,256]{2,1,0:T(8,128)S(1)}, u32[]{:S(2)}, u32[]{:S(2)}) async-start(f32[32,16,256]{2,1,0:T(8,128)} %broadcast_in_dim.160), calls=%async_computation | async-start | bytes 1048576 | tf_op jit(solution)/shard_map/all_to_all | solution.py:208
  56.2 3.7 %collective-permute-start.8 = (f32[19,128]{1,0:T(8,128)S(1)}, f32[19,128]{1,0:T(8,128)S(1)}, u32[]{:S(2)}, u32[]{:S(2)}) collective-permute-start(f32[19,128]{1,0:T(8,128)S(1)} %get-tuple-element.14), channel_id=1, source_target_pairs={{0,1},{1,2},{2,3},{3,4},{4,5},{5,6},{6,7},{7,8},{8,9},{9,10},{10,1... | collective-permute-start | bytes 29192 | tf_op jit(solution)/shard_map/ppermute | solution.py:229
  60.0 0.7 add.173.lookup_ref
  60.6 1.3 collective-permute-start.9
  62.0 4.2 %collective-permute-done.9 = f32[19,128]{1,0:T(8,128)S(1)} collective-permute-done((f32[19,128]{1,0:T(8,128)S(1)}, f32[19,128]{1,0:T(8,128)S(1)}, u32[]{:S(2)}, u32[]{:S(2)}) %collective-permute-start.9) | collective-permute-done | bytes 9760 | tf_op jit(solution)/shard_map/ppermute | solution.py:230
  66.2 3.8 %all-to-all-done = f32[32,16,256]{2,1,0:T(8,128)S(1)} async-done(((f32[32,16,256]{2,1,0:T(8,128)}), f32[32,16,256]{2,1,0:T(8,128)S(1)}, u32[]{:S(2)}, u32[]{:S(2)}) %all-to-all-start) | async-done | bytes 524320 | tf_op jit(solution)/shard_map/all_to_all | solution.py:208
  70.0 0.8 fusion.12
  70.8 2.7 %convolution_add_fusion = f32[32,256,128]{2,1,0:T(8,128)} fusion(f32[32,256,128]{2,1,0:T(8,128)S(1)} %fusion.12, f32[32,16,256]{2,1,0:T(8,128)S(1)} %all-to-all-done, s32[128]{0:T(128)S(1)} %iota_and_fusion, s32[128]{0:T(128)S(1)} %broadcast_add_fusion, pred[128]{0:T(512)(128)(4,1)S(1)} %compare_and_fusion), kind=kOutput, calls=%fused_computation.4 | convolution fusion | flops 35135488 | bytes 8914048 | tf_op jit(solution)/shard_map/dot_general | solution.py:145
  73.5 26.2 %shard_map.131 = f32[3072,128]{1,0:T(8,128)} custom-call(s32[24576]{0:T(1024)} %add.173.lookup_ref, f32[8192,128]{1,0:T(8,128)} %bitcast.104), custom_call_target="tpu_custom_call" | custom-call | bytes 5767168 | tf_op jit(solution)/shard_map/pallas_call | solution.py:152
  99.7 4.2 %fusion.3 = f32[128,128]{1,0:T(8,128)S(1)} fusion(f32[24,128,128]{2,1,0:T(8,128)} %bitcast.105, f32[24,24]{1,0:T(8,128)S(1)} %copy-done.7), kind=kOutput, calls=%fused_computation.7 | convolution fusion | flops 57393152 | bytes 1640704 | tf_op jit(solution)/shard_map/ij,jab->iab/dot_general | solution.py:215
  104.0 0.1 copy.25
  104.1 0.1 copy.26
  104.2 0.1 reshape.221
  104.3 3.1 %select_reduce_fusion = f32[2048]{0:T(1024)S(1)} fusion(f32[128]{0:T(128)S(1)} %get-tuple-element.51, f32[128]{0:T(128)S(1)} %get-tuple-element.52, f32[128]{0:T(128)S(1)} %get-tuple-element.53, f32[128]{0:T(128)S(1)} %get-tuple-element.54, f32[128]{0:T(128)S(1)} %get-tuple-element.55, f32[128]{0:T(128)S(1)} %get-tuple-element.56, ...), kind=kLoop, calls=%fused_computation.20 | loop fusion | flops 4716544 | bytes 36864 | tf_op jit(solution)/shard_map/reduce_sum | solution.py:88
  107.5 0.1 stack_reshape.3
  107.7 0.7 reshape.242
  108.4 8.0 %all-to-all-start.1 = ((f32[32,1,192]{2,1,0:T(1,128)}), f32[32,1,192]{2,1,0:T(1,128)S(1)}, u32[]{:S(2)}, u32[]{:S(2)}) async-start(f32[32,1,192]{2,1,0:T(1,128)} %reshape.242), calls=%async_computation.1 | async-start | bytes 65536 | tf_op jit(solution)/shard_map/all_to_all | solution.py:241
  116.5 9.6 %all-to-all-done.1 = f32[32,1,192]{2,1,0:T(1,128)S(1)} async-done(((f32[32,1,192]{2,1,0:T(1,128)}), f32[32,1,192]{2,1,0:T(1,128)S(1)}, u32[]{:S(2)}, u32[]{:S(2)}) %all-to-all-start.1) | async-done | bytes 24608 | tf_op jit(solution)/shard_map/all_to_all | solution.py:241
  126.1 0.5 broadcast.407
  126.6 0.7 reduce.12
  127.3 0.1 reshape.243
  127.4 0.1 slice_reduce_fusion.2
  127.8 2.8 %fusion = f32[134,128]{1,0:T(8,128)S(1)} fusion(s32[6144]{0:T(1024)S(1)} %get-tuple-element.58, f32[6144]{0:T(1024)S(1)} %pad_maximum_fusion.10, s32[6144]{0:T(1024)S(1)} %get-tuple-element.59), kind=kOutput, calls=%fused_computation.1 | convolution fusion | flops 1266978816 | bytes 142336 | tf_op jit(solution)/shard_map/dot_general | solution.py:98
  130.6 1.0 fusion.8
  (69 shorter events, 1.0 us)
Async XLA Ops:
  0.6 1.0 copy-start
  0.6 11.6 %copy-start.9 = (s32[1,1,1024]{2,1,0:T(1,128)S(1)}, s32[1,1,1024]{2,1,0:T(1,128)}, u32[]{:S(2)}) copy-start(s32[1,1,1024]{2,1,0:T(1,128)} %param.16) | copy-start | bytes 12292
  0.7 11.6 %copy-start.6 = (s32[1,1,32,64]{3,2,1,0:T(8,128)S(1)}, s32[1,1,32,64]{3,2,1,0:T(8,128)}, u32[]{:S(2)}) copy-start(s32[1,1,32,64]{3,2,1,0:T(8,128)} %param.19) | copy-start | bytes 24580
  0.7 9.7 %copy-start.3 = (s32[1,1,32,64]{3,2,1,0:T(8,128)S(1)}, s32[1,1,32,64]{3,2,1,0:T(8,128)}, u32[]{:S(2)}) copy-start(s32[1,1,32,64]{3,2,1,0:T(8,128)} %param.20) | copy-start | bytes 24580
  0.7 11.8 %copy-start.10 = (f32[1,1,128,128]{3,2,1,0:T(8,128)S(1)}, f32[1,1,128,128]{3,2,1,0:T(8,128)}, u32[]{:S(2)}) copy-start(f32[1,1,128,128]{3,2,1,0:T(8,128)} %param.21) | copy-start | bytes 196612
  3.9 4.0 %collective-permute-start = (f32[136,256]{1,0:T(8,128)S(1)}, f32[136,256]{1,0:T(8,128)S(1)}, u32[]{:S(2)}, u32[]{:S(2)}) collective-permute-start(f32[136,256]{1,0:T(8,128)S(1)} %get-tuple-element.34), channel_id=1, source_target_pairs={{0,32},{64,96},{128,160},{192,224},{256,288},{320,352},{384,416},{... | collective-permute-start | bytes 417800 | tf_op jit(solution)/shard_map/ppermute | solution.py:56
  5.7 2.5 %collective-permute-start.1 = (f32[136,256]{1,0:T(8,128)S(1)}, f32[136,256]{1,0:T(8,128)S(1)}, u32[]{:S(2)}, u32[]{:S(2)}) collective-permute-start(f32[136,256]{1,0:T(8,128)S(1)} %get-tuple-element.33), channel_id=1, source_target_pairs={{0,32},{64,96},{128,160},{192,224},{256,288},{320,352},{384,416},{... | collective-permute-start | bytes 417800 | tf_op jit(solution)/shard_map/ppermute | solution.py:56
  8.6 51.3 %copy-start.1 = (s32[1,1,24,1024]{3,2,1,0:T(8,128)S(1)}, s32[1,1,24,1024]{3,2,1,0:T(8,128)}, u32[]{:S(2)}) copy-start(s32[1,1,24,1024]{3,2,1,0:T(8,128)} %param.17) | copy-start | bytes 294916
  8.6 1.5 %collective-permute-start.2 = (f32[136,256]{1,0:T(8,128)S(1)}, f32[136,256]{1,0:T(8,128)S(1)}, u32[]{:S(2)}, u32[]{:S(2)}) collective-permute-start(f32[136,256]{1,0:T(8,128)S(1)} %get-tuple-element.32), channel_id=1, source_target_pairs={{32,96},{96,160},{160,224},{224,288},{288,352},{352,416},{416,480}... | collective-permute-start | bytes 417800 | tf_op jit(solution)/shard_map/ppermute | solution.py:56
  9.4 1.0 collective-permute-start.3
  10.8 1.6 %collective-permute-start.4 = (f32[136,256]{1,0:T(8,128)S(1)}, f32[136,256]{1,0:T(8,128)S(1)}, u32[]{:S(2)}, u32[]{:S(2)}) collective-permute-start(f32[136,256]{1,0:T(8,128)S(1)} %get-tuple-element.30), channel_id=1, source_target_pairs={{32,160},{96,224},{160,288},{224,352},{288,416},{352,480},{33,161}... | collective-permute-start | bytes 417800 | tf_op jit(solution)/shard_map/ppermute | solution.py:56
  11.5 1.9 %collective-permute-start.6 = (f32[136,256]{1,0:T(8,128)S(1)}, f32[136,256]{1,0:T(8,128)S(1)}, u32[]{:S(2)}, u32[]{:S(2)}) collective-permute-start(f32[136,256]{1,0:T(8,128)S(1)} %get-tuple-element.29), channel_id=1, source_target_pairs={{32,160},{96,224},{160,288},{224,352},{288,416},{352,480},{33,161}... | collective-permute-start | bytes 417800 | tf_op jit(solution)/shard_map/ppermute | solution.py:56
  12.7 1.1 collective-permute-start.5
  14.0 27.9 %collective-permute-start.7 = (f32[16,256]{1,0:T(8,128)S(1)}, f32[16,256]{1,0:T(8,128)S(1)}, u32[]{:S(2)}, u32[]{:S(2)}) collective-permute-start(f32[16,256]{1,0:T(8,128)S(1)} %convolution_add_fusion.2), channel_id=1, source_target_pairs={{32,64},{96,128},{160,192},{224,256},{288,320},{352,384},{416,448}... | collective-permute-start | bytes 49160 | tf_op jit(solution)/shard_map/ppermute | solution.py:74
  42.1 28.7 %copy-start.2 = (f32[16,256]{1,0:T(8,128)}, f32[16,256]{1,0:T(8,128)S(1)}, u32[]{:S(2)}) copy-start(f32[16,256]{1,0:T(8,128)S(1)} %convolution_add_fusion.1) | copy-start | bytes 49156
  43.0 27.0 %all-to-all-start = ((f32[32,16,256]{2,1,0:T(8,128)}), f32[32,16,256]{2,1,0:T(8,128)S(1)}, u32[]{:S(2)}, u32[]{:S(2)}) async-start(f32[32,16,256]{2,1,0:T(8,128)} %broadcast_in_dim.160), calls=%async_computation | async-start | bytes 1048576 | tf_op jit(solution)/shard_map/all_to_all | solution.py:208
  56.2 5.7 %collective-permute-start.8 = (f32[19,128]{1,0:T(8,128)S(1)}, f32[19,128]{1,0:T(8,128)S(1)}, u32[]{:S(2)}, u32[]{:S(2)}) collective-permute-start(f32[19,128]{1,0:T(8,128)S(1)} %get-tuple-element.14), channel_id=1, source_target_pairs={{0,1},{1,2},{2,3},{3,4},{4,5},{5,6},{6,7},{7,8},{8,9},{9,10},{10,1... | collective-permute-start | bytes 29192 | tf_op jit(solution)/shard_map/ppermute | solution.py:229
  60.6 5.6 %collective-permute-start.9 = (f32[19,128]{1,0:T(8,128)S(1)}, f32[19,128]{1,0:T(8,128)S(1)}, u32[]{:S(2)}, u32[]{:S(2)}) collective-permute-start(f32[19,128]{1,0:T(8,128)S(1)} %get-tuple-element.15), channel_id=1, source_target_pairs={{1,0},{2,1},{3,2},{4,3},{5,4},{6,5},{7,6},{8,7},{9,8},{10,9},{11,1... | collective-permute-start | bytes 29192 | tf_op jit(solution)/shard_map/ppermute | solution.py:230
  61.9 54.5 %copy-start.4 = (f32[19,128]{1,0:T(8,128)}, f32[19,128]{1,0:T(8,128)S(1)}, u32[]{:S(2)}) copy-start(f32[19,128]{1,0:T(8,128)S(1)} %collective-permute-done.8) | copy-start | bytes 29188
  66.2 50.2 %copy-start.5 = (f32[19,128]{1,0:T(8,128)}, f32[19,128]{1,0:T(8,128)S(1)}, u32[]{:S(2)}) copy-start(f32[19,128]{1,0:T(8,128)S(1)} %collective-permute-done.9) | copy-start | bytes 29188
  73.5 26.2 %copy-start.7 = (f32[24,24]{1,0:T(8,128)S(1)}, f32[24,24]{1,0:T(8,128)}, u32[]{:S(2)}) copy-start(f32[24,24]{1,0:T(8,128)} %param.15) | copy-start | bytes 6916
  73.5 30.8 %copy-start.8 = (f32[1,1,1024]{2,1,0:T(1,128)S(1)}, f32[1,1,1024]{2,1,0:T(1,128)}, u32[]{:S(2)}) copy-start(f32[1,1,1024]{2,1,0:T(1,128)} %param.18) | copy-start | bytes 12292
  108.4 17.7 %all-to-all-start.1 = ((f32[32,1,192]{2,1,0:T(1,128)}), f32[32,1,192]{2,1,0:T(1,128)S(1)}, u32[]{:S(2)}, u32[]{:S(2)}) async-start(f32[32,1,192]{2,1,0:T(1,128)} %reshape.242), calls=%async_computation.1 | async-start | bytes 65536 | tf_op jit(solution)/shard_map/all_to_all | solution.py:241
  116.5 14.1 %slice-start = ((f32[19,128]{1,0:T(8,128)}), f32[3,128]{1,0:T(4,128)S(1)}, s32[]{:S(2)}) async-start(f32[19,128]{1,0:T(8,128)} %copy-done.4), calls=%async_computation.2 | async-start | bytes 4096 | tf_op jit(solution)/shard_map/slice | solution.py:234
  116.5 14.1 %slice-start.1 = ((f32[19,128]{1,0:T(8,128)}), f32[3,128]{1,0:T(4,128)S(1)}, s32[]{:S(2)}) async-start(f32[19,128]{1,0:T(8,128)} %copy-done.5), calls=%async_computation.3 | async-start | bytes 4096 | tf_op jit(solution)/shard_map/slice | solution.py:234

commit v18 on v17

--- a/solution.py
+++ b/solution.py
@@ -99,7 +99,7 @@
         rows_hot,
         cols_hot,
         (((0,), (0,)), ((), ())),
-        precision=exact_mode,
+        precision=lax.Precision.HIGH,
         preferred_element_type=jnp.float32,
     )
 

time: 132 us -> 132 us (level)
  no operation moved by 1% of the time
where the time goes in v18:
time: 132 us; the launch traced here: 131 us
  waiting for transfers between devices  44.3 us (34%)
  starting transfers between devices  33.8 us (26%)
  Pallas kernels  26.2 us (20%)
  matrix products  15.4 us (12%)
  other arithmetic  5.85 us (4%)
  local copies, waits for them, and re-layouts  4.25 us (3%)
  between operations  1.33 us (1%)
    ppermute x1, waiting for transfers between devices, interface_chain(): lax.ppermute(offset, 'grp', [(g, g + 1) for g in range(1, levels - 1, 2)])  26.6 us
    pallas_call x1, Pallas kernels, gathered_rows(): pl.pallas_call(gather_kernel, out_shape=jax.ShapeDtypeStruct((out_rows, 1...  26.2 us
    all_to_all x1, starting transfers between devices, on_device(): lax.all_to_all(copies, 'dev', split_axis=0, concat_axis=0, tiled=True)  13.2 us
    all_to_all x1, waiting for transfers between devices, on_device(): lax.all_to_all(triple, 'dev', split_axis=0, concat_axis=0, tiled=True)  9.61 us
    all_to_all x1, starting transfers between devices, on_device(): lax.all_to_all(triple, 'dev', split_axis=0, concat_axis=0, tiled=True)  7.99 us
    dot_general x11, matrix products, product(): jnp.dot(left, right, precision=exact_mode, preferred_element_type=jnp.flo...  5.41 us
    ppermute x1, waiting for transfers between devices, on_device(): lax.ppermute(to_left, 'dev', [(i + 1, i) for i in range(count - 1)])  4.23 us
    dot_general x1, matrix products, on_device(): jnp.einsum('ij,jab->iab', stiffness, motion, precision=lax.Precision.HIGH)  4.22 us
  transfers between devices with their start and end apart: 12, of which 4 were waited for; matrix products, arithmetic and copies ran while one was open for 2% of the time, Pallas kernels for 0%

profile of v18, /device:TPU:40, one launch (start us, length us, event | category | flops | bytes accessed | tf_op | source)
XLA Modules:
  0.0 131.1 jit_solution(3812029147451458782)
XLA Ops:
  0.7 0.9 copy-done
  1.6 1.3 %convolution_negate_fusion = f32[256,256]{1,0:T(8,128)S(1)} fusion(f32[1,1,256,256]{3,2,1,0:T(8,128)} %param.13, f32[1,1,256,256]{3,2,1,0:T(8,128)S(1)} %copy-done), kind=kOutput, calls=%fused_computation.12 | convolution fusion | flops 201392128 | bytes 786432 | tf_op jit(solution)/shard_map/dot_general | solution.py:41
  2.9 0.9 fusion.21
  3.9 1.7 %collective-permute-start = (f32[136,256]{1,0:T(8,128)S(1)}, f32[136,256]{1,0:T(8,128)S(1)}, u32[]{:S(2)}, u32[]{:S(2)}) collective-permute-start(f32[136,256]{1,0:T(8,128)S(1)} %get-tuple-element.34), channel_id=1, source_target_pairs={{0,32},{64,96},{128,160},{192,224},{256,288},{320,352},{384,416},{... | collective-permute-start | bytes 417800 | tf_op jit(solution)/shard_map/ppermute | solution.py:56
  5.7 1.3 collective-permute-start.1
  7.0 0.9 select_reduce_fusion.1
  8.0 0.2 convolution_add_fusion.5
  8.2 0.4 fusion.17
  8.6 0.7 collective-permute-start.2
  9.3 0.1 multiply_reduce_fusion
  9.4 0.7 collective-permute-start.3
  10.1 0.2 convolution_add_fusion.4
  10.4 0.1 squeeze.25
  10.4 0.4 fusion.15
  10.8 0.7 collective-permute-start.4
  11.5 0.7 collective-permute-start.6
  12.5 0.2 convolution_add_fusion.3
  12.7 0.7 collective-permute-start.5
  13.4 0.4 fusion.13
  13.8 0.2 convolution_add_fusion.2
  14.0 1.3 collective-permute-start.7
  15.3 26.6 %collective-permute-done.7 = f32[16,256]{1,0:T(8,128)S(1)} collective-permute-done((f32[16,256]{1,0:T(8,128)S(1)}, f32[16,256]{1,0:T(8,128)S(1)}, u32[]{:S(2)}, u32[]{:S(2)}) %collective-permute-start.7) | collective-permute-done | bytes 16416 | tf_op jit(solution)/shard_map/ppermute | solution.py:74
  41.9 0.2 convolution_add_fusion.1
  42.2 0.9 broadcast_in_dim.160
  43.0 13.2 %all-to-all-start = ((f32[32,16,256]{2,1,0:T(8,128)}), f32[32,16,256]{2,1,0:T(8,128)S(1)}, u32[]{:S(2)}, u32[]{:S(2)}) async-start(f32[32,16,256]{2,1,0:T(8,128)} %broadcast_in_dim.160), calls=%async_computation | async-start | bytes 1048576 | tf_op jit(solution)/shard_map/all_to_all | solution.py:208
  56.2 3.7 %collective-permute-start.8 = (f32[19,128]{1,0:T(8,128)S(1)}, f32[19,128]{1,0:T(8,128)S(1)}, u32[]{:S(2)}, u32[]{:S(2)}) collective-permute-start(f32[19,128]{1,0:T(8,128)S(1)} %get-tuple-element.14), channel_id=1, source_target_pairs={{0,1},{1,2},{2,3},{3,4},{4,5},{5,6},{6,7},{7,8},{8,9},{9,10},{10,1... | collective-permute-start | bytes 29192 | tf_op jit(solution)/shard_map/ppermute | solution.py:229
  60.0 0.7 add.173.lookup_ref
  60.6 1.3 collective-permute-start.9
  62.0 4.2 %collective-permute-done.9 = f32[19,128]{1,0:T(8,128)S(1)} collective-permute-done((f32[19,128]{1,0:T(8,128)S(1)}, f32[19,128]{1,0:T(8,128)S(1)}, u32[]{:S(2)}, u32[]{:S(2)}) %collective-permute-start.9) | collective-permute-done | bytes 9760 | tf_op jit(solution)/shard_map/ppermute | solution.py:230
  66.2 3.8 %all-to-all-done = f32[32,16,256]{2,1,0:T(8,128)S(1)} async-done(((f32[32,16,256]{2,1,0:T(8,128)}), f32[32,16,256]{2,1,0:T(8,128)S(1)}, u32[]{:S(2)}, u32[]{:S(2)}) %all-to-all-start) | async-done | bytes 524320 | tf_op jit(solution)/shard_map/all_to_all | solution.py:208
  70.0 0.8 fusion.12
  70.8 2.7 %convolution_add_fusion = f32[32,256,128]{2,1,0:T(8,128)} fusion(f32[32,256,128]{2,1,0:T(8,128)S(1)} %fusion.12, f32[32,16,256]{2,1,0:T(8,128)S(1)} %all-to-all-done, s32[128]{0:T(128)S(1)} %iota_and_fusion, s32[128]{0:T(128)S(1)} %broadcast_add_fusion, pred[128]{0:T(512)(128)(4,1)S(1)} %compare_and_fusion), kind=kOutput, calls=%fused_computation.4 | convolution fusion | flops 35135488 | bytes 8914048 | tf_op jit(solution)/shard_map/dot_general | solution.py:145
  73.5 26.2 %shard_map.131 = f32[3072,128]{1,0:T(8,128)} custom-call(s32[24576]{0:T(1024)} %add.173.lookup_ref, f32[8192,128]{1,0:T(8,128)} %bitcast.104), custom_call_target="tpu_custom_call" | custom-call | bytes 5767168 | tf_op jit(solution)/shard_map/pallas_call | solution.py:152
  99.7 4.2 %fusion.3 = f32[128,128]{1,0:T(8,128)S(1)} fusion(f32[24,128,128]{2,1,0:T(8,128)} %bitcast.105, f32[24,24]{1,0:T(8,128)S(1)} %copy-done.7), kind=kOutput, calls=%fused_computation.7 | convolution fusion | flops 57393152 | bytes 1640704 | tf_op jit(solution)/shard_map/ij,jab->iab/dot_general | solution.py:215
  104.0 0.1 copy.25
  104.1 0.1 copy.26
  104.2 0.1 reshape.221
  104.3 3.1 %select_reduce_fusion = f32[2048]{0:T(1024)S(1)} fusion(f32[128]{0:T(128)S(1)} %get-tuple-element.51, f32[128]{0:T(128)S(1)} %get-tuple-element.52, f32[128]{0:T(128)S(1)} %get-tuple-element.53, f32[128]{0:T(128)S(1)} %get-tuple-element.54, f32[128]{0:T(128)S(1)} %get-tuple-element.55, f32[128]{0:T(128)S(1)} %get-tuple-element.56, ...), kind=kLoop, calls=%fused_computation.20 | loop fusion | flops 4716544 | bytes 36864 | tf_op jit(solution)/shard_map/reduce_sum | solution.py:88
  107.5 0.1 stack_reshape.3
  107.7 0.7 reshape.242
  108.4 8.0 %all-to-all-start.1 = ((f32[32,1,192]{2,1,0:T(1,128)}), f32[32,1,192]{2,1,0:T(1,128)S(1)}, u32[]{:S(2)}, u32[]{:S(2)}) async-start(f32[32,1,192]{2,1,0:T(1,128)} %reshape.242), calls=%async_computation.1 | async-start | bytes 65536 | tf_op jit(solution)/shard_map/all_to_all | solution.py:241
  116.5 9.6 %all-to-all-done.1 = f32[32,1,192]{2,1,0:T(1,128)S(1)} async-done(((f32[32,1,192]{2,1,0:T(1,128)}), f32[32,1,192]{2,1,0:T(1,128)S(1)}, u32[]{:S(2)}, u32[]{:S(2)}) %all-to-all-start.1) | async-done | bytes 24608 | tf_op jit(solution)/shard_map/all_to_all | solution.py:241
  126.1 0.5 broadcast.407
  126.6 0.7 reduce.12
  127.3 0.1 reshape.243
  127.4 0.1 slice_reduce_fusion.2
  127.8 2.3 %fusion = f32[134,128]{1,0:T(8,128)S(1)} fusion(s32[6144]{0:T(1024)S(1)} %get-tuple-element.58, f32[6144]{0:T(1024)S(1)} %pad_maximum_fusion.10, s32[6144]{0:T(1024)S(1)} %get-tuple-element.59), kind=kOutput, calls=%fused_computation.1 | convolution fusion | flops 634687488 | bytes 142336 | tf_op jit(solution)/shard_map/dot_general | solution.py:98
  130.1 1.0 fusion.8
  (69 shorter events, 1.0 us)
Async XLA Ops:
  0.6 1.0 copy-start
  0.6 11.6 %copy-start.9 = (s32[1,1,1024]{2,1,0:T(1,128)S(1)}, s32[1,1,1024]{2,1,0:T(1,128)}, u32[]{:S(2)}) copy-start(s32[1,1,1024]{2,1,0:T(1,128)} %param.16) | copy-start | bytes 12292
  0.7 11.6 %copy-start.6 = (s32[1,1,32,64]{3,2,1,0:T(8,128)S(1)}, s32[1,1,32,64]{3,2,1,0:T(8,128)}, u32[]{:S(2)}) copy-start(s32[1,1,32,64]{3,2,1,0:T(8,128)} %param.19) | copy-start | bytes 24580
  0.7 9.7 %copy-start.3 = (s32[1,1,32,64]{3,2,1,0:T(8,128)S(1)}, s32[1,1,32,64]{3,2,1,0:T(8,128)}, u32[]{:S(2)}) copy-start(s32[1,1,32,64]{3,2,1,0:T(8,128)} %param.20) | copy-start | bytes 24580
  0.7 11.8 %copy-start.10 = (f32[1,1,128,128]{3,2,1,0:T(8,128)S(1)}, f32[1,1,128,128]{3,2,1,0:T(8,128)}, u32[]{:S(2)}) copy-start(f32[1,1,128,128]{3,2,1,0:T(8,128)} %param.21) | copy-start | bytes 196612
  3.9 4.0 %collective-permute-start = (f32[136,256]{1,0:T(8,128)S(1)}, f32[136,256]{1,0:T(8,128)S(1)}, u32[]{:S(2)}, u32[]{:S(2)}) collective-permute-start(f32[136,256]{1,0:T(8,128)S(1)} %get-tuple-element.34), channel_id=1, source_target_pairs={{0,32},{64,96},{128,160},{192,224},{256,288},{320,352},{384,416},{... | collective-permute-start | bytes 417800 | tf_op jit(solution)/shard_map/ppermute | solution.py:56
  5.7 2.5 %collective-permute-start.1 = (f32[136,256]{1,0:T(8,128)S(1)}, f32[136,256]{1,0:T(8,128)S(1)}, u32[]{:S(2)}, u32[]{:S(2)}) collective-permute-start(f32[136,256]{1,0:T(8,128)S(1)} %get-tuple-element.33), channel_id=1, source_target_pairs={{0,32},{64,96},{128,160},{192,224},{256,288},{320,352},{384,416},{... | collective-permute-start | bytes 417800 | tf_op jit(solution)/shard_map/ppermute | solution.py:56
  8.6 51.3 %copy-start.1 = (s32[1,1,24,1024]{3,2,1,0:T(8,128)S(1)}, s32[1,1,24,1024]{3,2,1,0:T(8,128)}, u32[]{:S(2)}) copy-start(s32[1,1,24,1024]{3,2,1,0:T(8,128)} %param.17) | copy-start | bytes 294916
  8.6 1.5 %collective-permute-start.2 = (f32[136,256]{1,0:T(8,128)S(1)}, f32[136,256]{1,0:T(8,128)S(1)}, u32[]{:S(2)}, u32[]{:S(2)}) collective-permute-start(f32[136,256]{1,0:T(8,128)S(1)} %get-tuple-element.32), channel_id=1, source_target_pairs={{32,96},{96,160},{160,224},{224,288},{288,352},{352,416},{416,480}... | collective-permute-start | bytes 417800 | tf_op jit(solution)/shard_map/ppermute | solution.py:56
  9.4 1.0 collective-permute-start.3
  10.8 1.6 %collective-permute-start.4 = (f32[136,256]{1,0:T(8,128)S(1)}, f32[136,256]{1,0:T(8,128)S(1)}, u32[]{:S(2)}, u32[]{:S(2)}) collective-permute-start(f32[136,256]{1,0:T(8,128)S(1)} %get-tuple-element.30), channel_id=1, source_target_pairs={{32,160},{96,224},{160,288},{224,352},{288,416},{352,480},{33,161}... | collective-permute-start | bytes 417800 | tf_op jit(solution)/shard_map/ppermute | solution.py:56
  11.5 1.9 %collective-permute-start.6 = (f32[136,256]{1,0:T(8,128)S(1)}, f32[136,256]{1,0:T(8,128)S(1)}, u32[]{:S(2)}, u32[]{:S(2)}) collective-permute-start(f32[136,256]{1,0:T(8,128)S(1)} %get-tuple-element.29), channel_id=1, source_target_pairs={{32,160},{96,224},{160,288},{224,352},{288,416},{352,480},{33,161}... | collective-permute-start | bytes 417800 | tf_op jit(solution)/shard_map/ppermute | solution.py:56
  12.7 1.1 collective-permute-start.5
  14.0 27.9 %collective-permute-start.7 = (f32[16,256]{1,0:T(8,128)S(1)}, f32[16,256]{1,0:T(8,128)S(1)}, u32[]{:S(2)}, u32[]{:S(2)}) collective-permute-start(f32[16,256]{1,0:T(8,128)S(1)} %convolution_add_fusion.2), channel_id=1, source_target_pairs={{32,64},{96,128},{160,192},{224,256},{288,320},{352,384},{416,448}... | collective-permute-start | bytes 49160 | tf_op jit(solution)/shard_map/ppermute | solution.py:74
  42.1 28.7 %copy-start.2 = (f32[16,256]{1,0:T(8,128)}, f32[16,256]{1,0:T(8,128)S(1)}, u32[]{:S(2)}) copy-start(f32[16,256]{1,0:T(8,128)S(1)} %convolution_add_fusion.1) | copy-start | bytes 49156
  43.0 27.0 %all-to-all-start = ((f32[32,16,256]{2,1,0:T(8,128)}), f32[32,16,256]{2,1,0:T(8,128)S(1)}, u32[]{:S(2)}, u32[]{:S(2)}) async-start(f32[32,16,256]{2,1,0:T(8,128)} %broadcast_in_dim.160), calls=%async_computation | async-start | bytes 1048576 | tf_op jit(solution)/shard_map/all_to_all | solution.py:208
  56.2 5.7 %collective-permute-start.8 = (f32[19,128]{1,0:T(8,128)S(1)}, f32[19,128]{1,0:T(8,128)S(1)}, u32[]{:S(2)}, u32[]{:S(2)}) collective-permute-start(f32[19,128]{1,0:T(8,128)S(1)} %get-tuple-element.14), channel_id=1, source_target_pairs={{0,1},{1,2},{2,3},{3,4},{4,5},{5,6},{6,7},{7,8},{8,9},{9,10},{10,1... | collective-permute-start | bytes 29192 | tf_op jit(solution)/shard_map/ppermute | solution.py:229
  60.6 5.6 %collective-permute-start.9 = (f32[19,128]{1,0:T(8,128)S(1)}, f32[19,128]{1,0:T(8,128)S(1)}, u32[]{:S(2)}, u32[]{:S(2)}) collective-permute-start(f32[19,128]{1,0:T(8,128)S(1)} %get-tuple-element.15), channel_id=1, source_target_pairs={{1,0},{2,1},{3,2},{4,3},{5,4},{6,5},{7,6},{8,7},{9,8},{10,9},{11,1... | collective-permute-start | bytes 29192 | tf_op jit(solution)/shard_map/ppermute | solution.py:230
  61.9 54.5 %copy-start.4 = (f32[19,128]{1,0:T(8,128)}, f32[19,128]{1,0:T(8,128)S(1)}, u32[]{:S(2)}) copy-start(f32[19,128]{1,0:T(8,128)S(1)} %collective-permute-done.8) | copy-start | bytes 29188
  66.2 50.2 %copy-start.5 = (f32[19,128]{1,0:T(8,128)}, f32[19,128]{1,0:T(8,128)S(1)}, u32[]{:S(2)}) copy-start(f32[19,128]{1,0:T(8,128)S(1)} %collective-permute-done.9) | copy-start | bytes 29188
  73.5 26.2 %copy-start.7 = (f32[24,24]{1,0:T(8,128)S(1)}, f32[24,24]{1,0:T(8,128)}, u32[]{:S(2)}) copy-start(f32[24,24]{1,0:T(8,128)} %param.15) | copy-start | bytes 6916
  73.5 30.8 %copy-start.8 = (f32[1,1,1024]{2,1,0:T(1,128)S(1)}, f32[1,1,1024]{2,1,0:T(1,128)}, u32[]{:S(2)}) copy-start(f32[1,1,1024]{2,1,0:T(1,128)} %param.18) | copy-start | bytes 12292
  108.4 17.7 %all-to-all-start.1 = ((f32[32,1,192]{2,1,0:T(1,128)}), f32[32,1,192]{2,1,0:T(1,128)S(1)}, u32[]{:S(2)}, u32[]{:S(2)}) async-start(f32[32,1,192]{2,1,0:T(1,128)} %reshape.242), calls=%async_computation.1 | async-start | bytes 65536 | tf_op jit(solution)/shard_map/all_to_all | solution.py:241
  116.5 13.6 %slice-start = ((f32[19,128]{1,0:T(8,128)}), f32[3,128]{1,0:T(4,128)S(1)}, s32[]{:S(2)}) async-start(f32[19,128]{1,0:T(8,128)} %copy-done.4), calls=%async_computation.2 | async-start | bytes 4096 | tf_op jit(solution)/shard_map/slice | solution.py:234
  116.5 13.6 %slice-start.1 = ((f32[19,128]{1,0:T(8,128)}), f32[3,128]{1,0:T(4,128)S(1)}, s32[]{:S(2)}) async-start(f32[19,128]{1,0:T(8,128)} %copy-done.5), calls=%async_computation.3 | async-start | bytes 4096 | tf_op jit(solution)/shard_map/slice | solution.py:234

commit v19 on v18

--- a/solution.py
+++ b/solution.py
@@ -262,7 +262,7 @@
     padded_global = lax.axis_index("dev") * row_count - RADIUS + jnp.arange(padded_rows, dtype=jnp.int32)
     valid = ((padded_global >= 0) & (padded_global < total_rows)).astype(jnp.float32)
     weight_sum = jnp.sum(band * valid[None, :], axis=1)
-    accum = product(band, padded)
+    accum = jnp.dot(band, padded, precision=lax.Precision.HIGH, preferred_element_type=jnp.float32)
     filtered = accum / (owned * weight_sum[:, None])
     return (solved[None, None], filtered[None, None])
 

time: 132 us -> 132 us (level)
    dot_general x11 -> x10, matrix products: 5.41 us -> 4.37 us  [product(): jnp.dot(left, right, precision=exact_mode, preferred_element_type=jnp.flo...]
where the time goes in v19:
time: 132 us; the launch traced here: 131 us
  waiting for transfers between devices  44.4 us (34%)
  starting transfers between devices  33.7 us (26%)
  Pallas kernels  26.2 us (20%)
  matrix products  15.3 us (12%)
  other arithmetic  5.85 us (4%)
  local copies, waits for them, and re-layouts  4.25 us (3%)
  between operations  1.33 us (1%)
    ppermute x1, waiting for transfers between devices, interface_chain(): lax.ppermute(offset, 'grp', [(g, g + 1) for g in range(1, levels - 1, 2)])  26.6 us
    pallas_call x1, Pallas kernels, gathered_rows(): pl.pallas_call(gather_kernel, out_shape=jax.ShapeDtypeStruct((out_rows, 1...  26.2 us
    all_to_all x1, starting transfers between devices, on_device(): lax.all_to_all(copies, 'dev', split_axis=0, concat_axis=0, tiled=True)  13.2 us
    all_to_all x1, waiting for transfers between devices, on_device(): lax.all_to_all(triple, 'dev', split_axis=0, concat_axis=0, tiled=True)  9.79 us
    all_to_all x1, starting transfers between devices, on_device(): lax.all_to_all(triple, 'dev', split_axis=0, concat_axis=0, tiled=True)  7.81 us
    dot_general x10, matrix products, product(): jnp.dot(left, right, precision=exact_mode, preferred_element_type=jnp.flo...  4.37 us
    ppermute x1, waiting for transfers between devices, on_device(): lax.ppermute(to_left, 'dev', [(i + 1, i) for i in range(count - 1)])  4.23 us
    dot_general x1, matrix products, on_device(): jnp.einsum('ij,jab->iab', stiffness, motion, precision=lax.Precision.HIGH)  4.22 us
  transfers between devices with their start and end apart: 12, of which 4 were waited for; matrix products, arithmetic and copies ran while one was open for 2% of the time, Pallas kernels for 0%

profile of v19, /device:TPU:40, one launch (start us, length us, event | category | flops | bytes accessed | tf_op | source)
XLA Modules:
  0.0 131.0 jit_solution(14581452823099995851)
XLA Ops:
  0.7 0.9 copy-done
  1.6 1.3 %convolution_negate_fusion = f32[256,256]{1,0:T(8,128)S(1)} fusion(f32[1,1,256,256]{3,2,1,0:T(8,128)} %param.13, f32[1,1,256,256]{3,2,1,0:T(8,128)S(1)} %copy-done), kind=kOutput, calls=%fused_computation.12 | convolution fusion | flops 201392128 | bytes 786432 | tf_op jit(solution)/shard_map/dot_general | solution.py:41
  2.9 0.9 fusion.21
  3.9 1.7 %collective-permute-start = (f32[136,256]{1,0:T(8,128)S(1)}, f32[136,256]{1,0:T(8,128)S(1)}, u32[]{:S(2)}, u32[]{:S(2)}) collective-permute-start(f32[136,256]{1,0:T(8,128)S(1)} %get-tuple-element.34), channel_id=1, source_target_pairs={{0,32},{64,96},{128,160},{192,224},{256,288},{320,352},{384,416},{... | collective-permute-start | bytes 417800 | tf_op jit(solution)/shard_map/ppermute | solution.py:56
  5.7 1.3 collective-permute-start.1
  7.0 0.9 select_reduce_fusion.1
  8.0 0.2 convolution_add_fusion.5
  8.2 0.4 fusion.17
  8.6 0.7 collective-permute-start.2
  9.3 0.1 multiply_reduce_fusion
  9.4 0.7 collective-permute-start.3
  10.1 0.2 convolution_add_fusion.4
  10.4 0.4 fusion.15
  10.8 0.7 collective-permute-start.4
  11.5 0.7 collective-permute-start.6
  12.5 0.2 convolution_add_fusion.3
  12.7 0.7 collective-permute-start.5
  13.4 0.4 fusion.13
  13.8 0.2 convolution_add_fusion.2
  14.0 1.3 collective-permute-start.7
  15.3 26.6 %collective-permute-done.7 = f32[16,256]{1,0:T(8,128)S(1)} collective-permute-done((f32[16,256]{1,0:T(8,128)S(1)}, f32[16,256]{1,0:T(8,128)S(1)}, u32[]{:S(2)}, u32[]{:S(2)}) %collective-permute-start.7) | collective-permute-done | bytes 16416 | tf_op jit(solution)/shard_map/ppermute | solution.py:74
  41.9 0.2 convolution_add_fusion.1
  42.2 0.9 broadcast_in_dim.160
  43.0 13.2 %all-to-all-start = ((f32[32,16,256]{2,1,0:T(8,128)}), f32[32,16,256]{2,1,0:T(8,128)S(1)}, u32[]{:S(2)}, u32[]{:S(2)}) async-start(f32[32,16,256]{2,1,0:T(8,128)} %broadcast_in_dim.160), calls=%async_computation | async-start | bytes 1048576 | tf_op jit(solution)/shard_map/all_to_all | solution.py:208
  56.2 3.7 %collective-permute-start.8 = (f32[19,128]{1,0:T(8,128)S(1)}, f32[19,128]{1,0:T(8,128)S(1)}, u32[]{:S(2)}, u32[]{:S(2)}) collective-permute-start(f32[19,128]{1,0:T(8,128)S(1)} %get-tuple-element.14), channel_id=1, source_target_pairs={{0,1},{1,2},{2,3},{3,4},{4,5},{5,6},{6,7},{7,8},{8,9},{9,10},{10,1... | collective-permute-start | bytes 29192 | tf_op jit(solution)/shard_map/ppermute | solution.py:229
  60.0 0.7 add.173.lookup_ref
  60.6 1.3 collective-permute-start.9
  62.0 4.2 %collective-permute-done.9 = f32[19,128]{1,0:T(8,128)S(1)} collective-permute-done((f32[19,128]{1,0:T(8,128)S(1)}, f32[19,128]{1,0:T(8,128)S(1)}, u32[]{:S(2)}, u32[]{:S(2)}) %collective-permute-start.9) | collective-permute-done | bytes 9760 | tf_op jit(solution)/shard_map/ppermute | solution.py:230
  66.3 3.8 %all-to-all-done = f32[32,16,256]{2,1,0:T(8,128)S(1)} async-done(((f32[32,16,256]{2,1,0:T(8,128)}), f32[32,16,256]{2,1,0:T(8,128)S(1)}, u32[]{:S(2)}, u32[]{:S(2)}) %all-to-all-start) | async-done | bytes 524320 | tf_op jit(solution)/shard_map/all_to_all | solution.py:208
  70.0 0.8 fusion.12
  70.8 2.7 %convolution_add_fusion = f32[32,256,128]{2,1,0:T(8,128)} fusion(f32[32,256,128]{2,1,0:T(8,128)S(1)} %fusion.12, f32[32,16,256]{2,1,0:T(8,128)S(1)} %all-to-all-done, s32[128]{0:T(128)S(1)} %iota_and_fusion, s32[128]{0:T(128)S(1)} %broadcast_add_fusion, pred[128]{0:T(512)(128)(4,1)S(1)} %compare_and_fusion), kind=kOutput, calls=%fused_computation.4 | convolution fusion | flops 35135488 | bytes 8914048 | tf_op jit(solution)/shard_map/dot_general | solution.py:145
  73.5 26.2 %shard_map.131 = f32[3072,128]{1,0:T(8,128)} custom-call(s32[24576]{0:T(1024)} %add.173.lookup_ref, f32[8192,128]{1,0:T(8,128)} %bitcast.104), custom_call_target="tpu_custom_call" | custom-call | bytes 5767168 | tf_op jit(solution)/shard_map/pallas_call | solution.py:152
  99.8 4.2 %fusion.3 = f32[128,128]{1,0:T(8,128)S(1)} fusion(f32[24,128,128]{2,1,0:T(8,128)} %bitcast.105, f32[24,24]{1,0:T(8,128)S(1)} %copy-done.7), kind=kOutput, calls=%fused_computation.7 | convolution fusion | flops 57393152 | bytes 1640704 | tf_op jit(solution)/shard_map/ij,jab->iab/dot_general | solution.py:215
  104.0 0.1 copy.25
  104.1 0.1 copy.26
  104.2 0.1 reshape.221
  104.3 3.1 %select_reduce_fusion = f32[2048]{0:T(1024)S(1)} fusion(f32[128]{0:T(128)S(1)} %get-tuple-element.51, f32[128]{0:T(128)S(1)} %get-tuple-element.52, f32[128]{0:T(128)S(1)} %get-tuple-element.53, f32[128]{0:T(128)S(1)} %get-tuple-element.54, f32[128]{0:T(128)S(1)} %get-tuple-element.55, f32[128]{0:T(128)S(1)} %get-tuple-element.56, ...), kind=kLoop, calls=%fused_computation.20 | loop fusion | flops 4716544 | bytes 36864 | tf_op jit(solution)/shard_map/reduce_sum | solution.py:88
  107.5 0.1 stack_reshape.3
  107.7 0.7 reshape.242
  108.4 7.8 %all-to-all-start.1 = ((f32[32,1,192]{2,1,0:T(1,128)}), f32[32,1,192]{2,1,0:T(1,128)S(1)}, u32[]{:S(2)}, u32[]{:S(2)}) async-start(f32[32,1,192]{2,1,0:T(1,128)} %reshape.242), calls=%async_computation.1 | async-start | bytes 65536 | tf_op jit(solution)/shard_map/all_to_all | solution.py:241
  116.3 9.8 %all-to-all-done.1 = f32[32,1,192]{2,1,0:T(1,128)S(1)} async-done(((f32[32,1,192]{2,1,0:T(1,128)}), f32[32,1,192]{2,1,0:T(1,128)S(1)}, u32[]{:S(2)}, u32[]{:S(2)}) %all-to-all-start.1) | async-done | bytes 24608 | tf_op jit(solution)/shard_map/all_to_all | solution.py:241
  126.1 0.5 broadcast.407
  126.6 0.7 reduce.12
  127.3 0.1 reshape.243
  127.4 0.1 slice_reduce_fusion.2
  127.6 0.1 reshape_squeeze.13
  127.8 2.3 %fusion = f32[134,128]{1,0:T(8,128)S(1)} fusion(s32[6144]{0:T(1024)S(1)} %get-tuple-element.58, f32[6144]{0:T(1024)S(1)} %pad_maximum_fusion.10, s32[6144]{0:T(1024)S(1)} %get-tuple-element.59), kind=kOutput, calls=%fused_computation.1 | convolution fusion | flops 634687488 | bytes 142336 | tf_op jit(solution)/shard_map/dot_general | solution.py:98
  130.1 0.9 fusion.8
  (69 shorter events, 1.0 us)
Async XLA Ops:
  0.6 1.0 copy-start
  0.6 11.6 %copy-start.9 = (s32[1,1,1024]{2,1,0:T(1,128)S(1)}, s32[1,1,1024]{2,1,0:T(1,128)}, u32[]{:S(2)}) copy-start(s32[1,1,1024]{2,1,0:T(1,128)} %param.16) | copy-start | bytes 12292
  0.7 11.6 %copy-start.6 = (s32[1,1,32,64]{3,2,1,0:T(8,128)S(1)}, s32[1,1,32,64]{3,2,1,0:T(8,128)}, u32[]{:S(2)}) copy-start(s32[1,1,32,64]{3,2,1,0:T(8,128)} %param.19) | copy-start | bytes 24580
  0.7 9.7 %copy-start.3 = (s32[1,1,32,64]{3,2,1,0:T(8,128)S(1)}, s32[1,1,32,64]{3,2,1,0:T(8,128)}, u32[]{:S(2)}) copy-start(s32[1,1,32,64]{3,2,1,0:T(8,128)} %param.20) | copy-start | bytes 24580
  0.7 11.8 %copy-start.10 = (f32[1,1,128,128]{3,2,1,0:T(8,128)S(1)}, f32[1,1,128,128]{3,2,1,0:T(8,128)}, u32[]{:S(2)}) copy-start(f32[1,1,128,128]{3,2,1,0:T(8,128)} %param.21) | copy-start | bytes 196612
  3.9 4.0 %collective-permute-start = (f32[136,256]{1,0:T(8,128)S(1)}, f32[136,256]{1,0:T(8,128)S(1)}, u32[]{:S(2)}, u32[]{:S(2)}) collective-permute-start(f32[136,256]{1,0:T(8,128)S(1)} %get-tuple-element.34), channel_id=1, source_target_pairs={{0,32},{64,96},{128,160},{192,224},{256,288},{320,352},{384,416},{... | collective-permute-start | bytes 417800 | tf_op jit(solution)/shard_map/ppermute | solution.py:56
  5.7 2.5 %collective-permute-start.1 = (f32[136,256]{1,0:T(8,128)S(1)}, f32[136,256]{1,0:T(8,128)S(1)}, u32[]{:S(2)}, u32[]{:S(2)}) collective-permute-start(f32[136,256]{1,0:T(8,128)S(1)} %get-tuple-element.33), channel_id=1, source_target_pairs={{0,32},{64,96},{128,160},{192,224},{256,288},{320,352},{384,416},{... | collective-permute-start | bytes 417800 | tf_op jit(solution)/shard_map/ppermute | solution.py:56
  8.6 51.3 %copy-start.1 = (s32[1,1,24,1024]{3,2,1,0:T(8,128)S(1)}, s32[1,1,24,1024]{3,2,1,0:T(8,128)}, u32[]{:S(2)}) copy-start(s32[1,1,24,1024]{3,2,1,0:T(8,128)} %param.17) | copy-start | bytes 294916
  8.6 1.5 %collective-permute-start.2 = (f32[136,256]{1,0:T(8,128)S(1)}, f32[136,256]{1,0:T(8,128)S(1)}, u32[]{:S(2)}, u32[]{:S(2)}) collective-permute-start(f32[136,256]{1,0:T(8,128)S(1)} %get-tuple-element.32), channel_id=1, source_target_pairs={{32,96},{96,160},{160,224},{224,288},{288,352},{352,416},{416,480}... | collective-permute-start | bytes 417800 | tf_op jit(solution)/shard_map/ppermute | solution.py:56
  9.4 1.0 collective-permute-start.3
  10.8 1.6 %collective-permute-start.4 = (f32[136,256]{1,0:T(8,128)S(1)}, f32[136,256]{1,0:T(8,128)S(1)}, u32[]{:S(2)}, u32[]{:S(2)}) collective-permute-start(f32[136,256]{1,0:T(8,128)S(1)} %get-tuple-element.30), channel_id=1, source_target_pairs={{32,160},{96,224},{160,288},{224,352},{288,416},{352,480},{33,161}... | collective-permute-start | bytes 417800 | tf_op jit(solution)/shard_map/ppermute | solution.py:56
  11.5 1.9 %collective-permute-start.6 = (f32[136,256]{1,0:T(8,128)S(1)}, f32[136,256]{1,0:T(8,128)S(1)}, u32[]{:S(2)}, u32[]{:S(2)}) collective-permute-start(f32[136,256]{1,0:T(8,128)S(1)} %get-tuple-element.29), channel_id=1, source_target_pairs={{32,160},{96,224},{160,288},{224,352},{288,416},{352,480},{33,161}... | collective-permute-start | bytes 417800 | tf_op jit(solution)/shard_map/ppermute | solution.py:56
  12.7 1.1 collective-permute-start.5
  14.0 27.9 %collective-permute-start.7 = (f32[16,256]{1,0:T(8,128)S(1)}, f32[16,256]{1,0:T(8,128)S(1)}, u32[]{:S(2)}, u32[]{:S(2)}) collective-permute-start(f32[16,256]{1,0:T(8,128)S(1)} %convolution_add_fusion.2), channel_id=1, source_target_pairs={{32,64},{96,128},{160,192},{224,256},{288,320},{352,384},{416,448}... | collective-permute-start | bytes 49160 | tf_op jit(solution)/shard_map/ppermute | solution.py:74
  42.1 28.7 %copy-start.2 = (f32[16,256]{1,0:T(8,128)}, f32[16,256]{1,0:T(8,128)S(1)}, u32[]{:S(2)}) copy-start(f32[16,256]{1,0:T(8,128)S(1)} %convolution_add_fusion.1) | copy-start | bytes 49156
  43.0 27.0 %all-to-all-start = ((f32[32,16,256]{2,1,0:T(8,128)}), f32[32,16,256]{2,1,0:T(8,128)S(1)}, u32[]{:S(2)}, u32[]{:S(2)}) async-start(f32[32,16,256]{2,1,0:T(8,128)} %broadcast_in_dim.160), calls=%async_computation | async-start | bytes 1048576 | tf_op jit(solution)/shard_map/all_to_all | solution.py:208
  56.2 5.7 %collective-permute-start.8 = (f32[19,128]{1,0:T(8,128)S(1)}, f32[19,128]{1,0:T(8,128)S(1)}, u32[]{:S(2)}, u32[]{:S(2)}) collective-permute-start(f32[19,128]{1,0:T(8,128)S(1)} %get-tuple-element.14), channel_id=1, source_target_pairs={{0,1},{1,2},{2,3},{3,4},{4,5},{5,6},{6,7},{7,8},{8,9},{9,10},{10,1... | collective-permute-start | bytes 29192 | tf_op jit(solution)/shard_map/ppermute | solution.py:229
  60.6 5.6 %collective-permute-start.9 = (f32[19,128]{1,0:T(8,128)S(1)}, f32[19,128]{1,0:T(8,128)S(1)}, u32[]{:S(2)}, u32[]{:S(2)}) collective-permute-start(f32[19,128]{1,0:T(8,128)S(1)} %get-tuple-element.15), channel_id=1, source_target_pairs={{1,0},{2,1},{3,2},{4,3},{5,4},{6,5},{7,6},{8,7},{9,8},{10,9},{11,1... | collective-permute-start | bytes 29192 | tf_op jit(solution)/shard_map/ppermute | solution.py:230
  61.9 54.3 %copy-start.4 = (f32[19,128]{1,0:T(8,128)}, f32[19,128]{1,0:T(8,128)S(1)}, u32[]{:S(2)}) copy-start(f32[19,128]{1,0:T(8,128)S(1)} %collective-permute-done.8) | copy-start | bytes 29188
  66.2 50.1 %copy-start.5 = (f32[19,128]{1,0:T(8,128)}, f32[19,128]{1,0:T(8,128)S(1)}, u32[]{:S(2)}) copy-start(f32[19,128]{1,0:T(8,128)S(1)} %collective-permute-done.9) | copy-start | bytes 29188
  73.5 26.2 %copy-start.7 = (f32[24,24]{1,0:T(8,128)S(1)}, f32[24,24]{1,0:T(8,128)}, u32[]{:S(2)}) copy-start(f32[24,24]{1,0:T(8,128)} %param.15) | copy-start | bytes 6916
  73.5 30.8 %copy-start.8 = (f32[1,1,1024]{2,1,0:T(1,128)S(1)}, f32[1,1,1024]{2,1,0:T(1,128)}, u32[]{:S(2)}) copy-start(f32[1,1,1024]{2,1,0:T(1,128)} %param.18) | copy-start | bytes 12292
  108.4 17.7 %all-to-all-start.1 = ((f32[32,1,192]{2,1,0:T(1,128)}), f32[32,1,192]{2,1,0:T(1,128)S(1)}, u32[]{:S(2)}, u32[]{:S(2)}) async-start(f32[32,1,192]{2,1,0:T(1,128)} %reshape.242), calls=%async_computation.1 | async-start | bytes 65536 | tf_op jit(solution)/shard_map/all_to_all | solution.py:241
  116.3 13.8 %slice-start = ((f32[19,128]{1,0:T(8,128)}), f32[3,128]{1,0:T(4,128)S(1)}, s32[]{:S(2)}) async-start(f32[19,128]{1,0:T(8,128)} %copy-done.4), calls=%async_computation.2 | async-start | bytes 4096 | tf_op jit(solution)/shard_map/slice | solution.py:234
  116.3 13.8 %slice-start.1 = ((f32[19,128]{1,0:T(8,128)}), f32[3,128]{1,0:T(4,128)S(1)}, s32[]{:S(2)}) async-start(f32[19,128]{1,0:T(8,128)} %copy-done.5), calls=%async_computation.3 | async-start | bytes 4096 | tf_op jit(solution)/shard_map/slice | solution.py:234
